TPU v7x, 32 devices: a whole 2x2x4 slice. The times are simulated.
32 devices in a mesh: groups: 2 (over x), seq: 8 (over z, y), tgrp: 2 (over core).
Axes of the slice: x: 2, y: 2, z: 4, core: 2. Of those that a mesh axis runs over, the one named last changes fastest.
Arguments:
- student_hidden: bfloat16 [8192, 4096], P(('groups', 'seq'), 'tgrp'), parts along dimension 0, may hold values from -6 to 6
- teacher_hidden: bfloat16 [8192, 8192], P(('groups', 'seq'), 'tgrp'), parts along dimension 0, may hold values from -6 to 6
- student_proj: bfloat16 [4096, 128], P('tgrp'), may hold values from -0.09375 to 0.09375
- teacher_proj: bfloat16 [8192, 128], P('tgrp'), may hold values from -0.0625 to 0.0625
- student_chars: int32 [8192], P(('groups', 'seq')), parts along dimension 0, may hold values from 0 to 18427, as said below
- teacher_chars: int32 [8192], P(('groups', 'seq')), parts along dimension 0, may hold values from 0 to 18427, as said below
- band: int32 [16, 2], P(('groups', 'seq')), parts along dimension 0, may hold values from 0 to 1, as said below
Outputs:
- aligned: bfloat16 [8192, 8192], P(('groups', 'seq'), 'tgrp'), parts along dimension 0
There are 2 independent parts, one for each index of `groups`. A program takes and returns all parts, laid end to end along the dimension named above; an argument that names none is the same for every part. Nothing has to cross between parts.
Inputs may be any that keep to these rules, and one draw needn't show every extreme that they name: `student_chars`: offsets of consecutive tokens rise by 1 to 8; the first token's offset is 0 and the last one's is 18427. `teacher_chars`: offsets of consecutive tokens rise by 1 to 8; the first token's offset is 0 and the last one's is 18427. `band`: every row has at least one 1; the first row's column 0 and the last row's column 1 are 0.
All inputs are finite; a program needn't handle non-finite values.
Results may differ from a plain program's by a relative error of at most 0.008.
Values may be sent and summed in bfloat16 or wider, within the bound.
No kernel may reach another device: no remote copies, remote signals or barrier semaphores. Data moves between devices by JAX's collectives and lax.ppermute only.
A program may use at most 64 MiB of HBM per device.

v0:
```python
import math

import jax
import jax.numpy as jnp
from jax import lax
from jax.sharding import PartitionSpec as P

ITERS = 4


norm_eps = 1e-05


def shifted(block, axis, distance):
    devices = range(lax.axis_size(axis))
    route = [(i - distance, i) for i in devices if i - distance in devices]
    return lax.ppermute(block, axis, route)


def unit_rows(features):
    factor = lax.rsqrt(jnp.mean(features * features, axis=-1, keepdims=True) + norm_eps)
    return (features * factor).astype(jnp.bfloat16)


def body(
    student_hidden, teacher_hidden, student_proj, teacher_proj, student_chars, teacher_chars, band
):
    block_rows = student_hidden.shape[0]
    proj_width = student_proj.shape[1]
    s_part = jnp.dot(student_hidden, student_proj, preferred_element_type=jnp.float32)
    t_part = jnp.dot(teacher_hidden, teacher_proj, preferred_element_type=jnp.float32)
    s_feat, t_feat = lax.psum((s_part, t_part), "tgrp")
    s_unit = unit_rows(s_feat)
    t_unit = unit_rows(t_feat)
    left_rows, left_unit, left_chars = shifted((teacher_hidden, t_unit, teacher_chars), "seq", 1)
    right_rows, right_unit, right_chars = shifted(
        (teacher_hidden, t_unit, teacher_chars), "seq", -1
    )
    near_unit = jnp.stack([left_unit, t_unit, right_unit])
    near_pos = jnp.stack([left_chars, teacher_chars, right_chars]).astype(jnp.float32)
    s_pos = student_chars.astype(jnp.float32)
    flags = band[0]
    slot_mask = jnp.stack([flags[0], jnp.ones((), jnp.int32), flags[1]]).astype(jnp.float32)
    scores = jnp.einsum(
        "ip,kjp->kij", s_unit, near_unit, preferred_element_type=jnp.float32
    ) / math.sqrt(proj_width)
    distance = jnp.abs(s_pos[None, :, None] - near_pos[:, None, :]) / (4.0 * block_rows)
    kernel = jnp.exp(scores - distance) * slot_mask[:, None, None]
    row_scale = jnp.ones((block_rows,), jnp.float32)
    col_scale = jnp.zeros((3, block_rows), jnp.float32)
    for iteration in range(ITERS):
        partial_cols = jnp.sum(row_scale[None, :, None] * kernel, axis=1)
        left_one = shifted(partial_cols[1:], "seq", 1)
        left_two = shifted(partial_cols[2:], "seq", 2)
        right_one = shifted(partial_cols[:2], "seq", -1)
        right_two = shifted(partial_cols[:1], "seq", -2)
        column_total = jnp.stack(
            [
                left_two[0] + left_one[0] + partial_cols[0],
                left_one[1] + partial_cols[1] + right_one[0],
                partial_cols[2] + right_one[1] + right_two[0],
            ]
        )
        col_scale = slot_mask[:, None] / jnp.where(slot_mask[:, None] > 0.0, column_total, 1.0)
        row_scale = 1.0 / jnp.sum(kernel * col_scale[:, None, :], axis=(0, 2))
    plan = (row_scale[None, :, None] * kernel * col_scale[:, None, :]).astype(jnp.bfloat16)
    aligned = jnp.dot(plan[0], left_rows, preferred_element_type=jnp.float32)
    aligned = aligned + jnp.dot(plan[1], teacher_hidden, preferred_element_type=jnp.float32)
    aligned = aligned + jnp.dot(plan[2], right_rows, preferred_element_type=jnp.float32)
    return aligned.astype(jnp.bfloat16)


def solution(mesh):
    return jax.shard_map(
        body,
        mesh=mesh,
        in_specs=(
            P(("groups", "seq"), "tgrp"),
            P(("groups", "seq"), "tgrp"),
            P("tgrp", None),
            P("tgrp", None),
            P(("groups", "seq")),
            P(("groups", "seq")),
            P(("groups", "seq"), None),
        ),
        out_specs=P(("groups", "seq"), "tgrp"),
        check_vma=False,
    )
```

profile of v0, /device:TPU:0, one launch (start us, length us, event | category | flops | bytes accessed | tf_op | source)
XLA Modules:
  0.0 300.3 jit_solution(8330264855214489857)
XLA Ops:
  6.5 1.6 copy-done
  8.1 2.5 fusion.40
  10.6 4.5 %fusion.39 = f32[512,128]{1,0:T(8,128)} fusion(bf16[512,4096]{1,0:T(8,128)(2,1)} %param.8, bf16[4096,128]{1,0:T(8,128)(2,1)} %param.10), kind=kOutput, calls=%fused_computation.82 | convolution fusion | flops 536870912 | bytes 5505024 | tf_op jit(solution)/shard_map/dot_general | solution.py:31
  15.1 0.0 all-reduce.3.cloned.1.call-update
  15.1 4.9 %collective-permute-start.2 = (s32[512]{0:T(512)S(1)}, s32[512]{0:T(512)S(1)}, u32[]{:S(2)}, u32[]{:S(2)}) collective-permute-start(s32[512]{0:T(512)S(1)} %copy-done.2), channel_id=1, source_target_pairs={{0,2},{2,4},{4,6},{6,8},{8,10},{10,12},{12,14},{1,3},{3,5},{5,7},{... | collective-permute-start | bytes 6152 | tf_op jit(solution)/shard_map/ppermute | solution.py:17
  20.0 1.3 collective-permute-start.3
  21.3 0.7 fusion.37
  22.0 1.5 broadcast_compare_fusion
  23.4 2.0 collective-permute-done.3
  25.5 11.3 %all-reduce.3.cloned.1.call-done = (f32[512,128]{1,0:T(8,128)}, f32[512,128]{1,0:T(8,128)}) async-done(((f32[512,128]{1,0:T(8,128)}, f32[512,128]{1,0:T(8,128)}), (f32[512,128]{1,0:T(8,128)}, f32[512,128]{1,0:T(8,128)})) %all-reduce.3.cloned.1.call-update) | async-done | bytes 524304 | tf_op jit(solution)/shard_map/psum | solution.py:32
  36.8 1.1 multiply_reduce_fusion.8
  37.9 1.1 multiply_convert_fusion.2
  39.0 1.1 fusion.48
  40.0 1.3 collective-permute-start.1
  41.3 4.6 %collective-permute-start = (bf16[512,128]{1,0:T(8,128)(2,1)S(1)}, bf16[512,128]{1,0:T(8,128)(2,1)S(1)}, u32[]{:S(2)}, u32[]{:S(2)}) collective-permute-start(bf16[512,128]{1,0:T(8,128)(2,1)S(1)} %multiply_convert_fusion.2), channel_id=1, source_target_pairs={{0,2},{2,4},{4,6},{6,8},{8,10},{10,12},{12,14},{1,3},{3,5},{5,7},{... | collective-permute-start | bytes 393224 | tf_op jit(solution)/shard_map/ppermute | solution.py:17
  45.9 1.1 multiply_reduce_fusion.7
  47.0 0.6 collective-permute-done.1
  47.6 3.0 collective-permute-done
  50.6 2.2 fusion.38
  52.8 4.4 %collective-permute-start.5 = (f32[2,512]{1,0:T(2,128)S(1)}, f32[2,512]{1,0:T(2,128)S(1)}, u32[]{:S(2)}, u32[]{:S(2)}) collective-permute-start(f32[2,512]{1,0:T(2,128)S(1)} %get-tuple-element.35), channel_id=1, source_target_pairs={{0,2},{2,4},{4,6},{6,8},{8,10},{10,12},{12,14},{1,3},{3,5},{5,7},{... | collective-permute-start | bytes 12296 | tf_op jit(solution)/shard_map/ppermute | solution.py:17
  57.2 1.3 collective-permute-start.6
  58.5 5.7 %collective-permute-start.4 = (f32[1,512]{1,0:T(1,128)S(1)}, f32[1,512]{1,0:T(1,128)S(1)}, u32[]{:S(2)}, u32[]{:S(2)}) collective-permute-start(f32[1,512]{1,0:T(1,128)S(1)} %get-tuple-element.33), channel_id=1, source_target_pairs={{0,4},{2,6},{4,8},{6,10},{8,12},{10,14},{1,5},{3,7},{5,9},{7,11},{... | collective-permute-start | bytes 6152 | tf_op jit(solution)/shard_map/ppermute | solution.py:17
  64.3 1.3 collective-permute-start.7
  65.6 4.2 %collective-permute-done.7 = f32[1,512]{1,0:T(1,128)S(1)} collective-permute-done((f32[1,512]{1,0:T(1,128)S(1)}, f32[1,512]{1,0:T(1,128)S(1)}, u32[]{:S(2)}, u32[]{:S(2)}) %collective-permute-start.7) | collective-permute-done | bytes 2080 | tf_op jit(solution)/shard_map/ppermute | solution.py:17
  69.8 0.0 collective-permute-done.6
  69.8 0.1 fusion.16
  69.9 0.3 multiply_reduce_fusion.6
  70.2 0.3 multiply_reduce_fusion.5
  70.5 2.3 collective-permute-start.9
  72.8 1.3 collective-permute-start.10
  74.1 6.6 %collective-permute-start.8 = (f32[1,512]{1,0:T(1,128)S(1)}, f32[1,512]{1,0:T(1,128)S(1)}, u32[]{:S(2)}, u32[]{:S(2)}) collective-permute-start(f32[1,512]{1,0:T(1,128)S(1)} %get-tuple-element.29), channel_id=1, source_target_pairs={{0,4},{2,6},{4,8},{6,10},{8,12},{10,14},{1,5},{3,7},{5,9},{7,11},{... | collective-permute-start | bytes 6152 | tf_op jit(solution)/shard_map/ppermute | solution.py:17
  80.8 1.3 collective-permute-start.11
  82.1 2.2 collective-permute-start.20
  84.3 0.0 collective-permute-done.8
  84.3 1.3 collective-permute-start.21
  85.6 0.6 collective-permute-done.11
  86.3 0.0 collective-permute-done.9
  86.3 0.1 fusion.17
  86.4 0.3 multiply_reduce_fusion.4
  86.7 0.3 multiply_reduce_fusion.3
  87.0 7.2 %collective-permute-start.12 = (f32[1,512]{1,0:T(1,128)S(1)}, f32[1,512]{1,0:T(1,128)S(1)}, u32[]{:S(2)}, u32[]{:S(2)}) collective-permute-start(f32[1,512]{1,0:T(1,128)S(1)} %get-tuple-element.25), channel_id=1, source_target_pairs={{0,4},{2,6},{4,8},{6,10},{8,12},{10,14},{1,5},{3,7},{5,9},{7,11},{... | collective-permute-start | bytes 6152 | tf_op jit(solution)/shard_map/ppermute | solution.py:17
  94.2 1.9 collective-permute-start.13
  96.1 1.3 collective-permute-start.14
  97.4 1.3 collective-permute-start.15
  98.7 79.1 %collective-permute-done.15 = f32[1,512]{1,0:T(1,128)S(1)} collective-permute-done((f32[1,512]{1,0:T(1,128)S(1)}, f32[1,512]{1,0:T(1,128)S(1)}, u32[]{:S(2)}, u32[]{:S(2)}) %collective-permute-start.15) | collective-permute-done | bytes 2080 | tf_op jit(solution)/shard_map/ppermute | solution.py:17
  177.9 82.8 %collective-permute-done.13 = f32[2,512]{1,0:T(2,128)S(1)} collective-permute-done((f32[2,512]{1,0:T(2,128)S(1)}, f32[2,512]{1,0:T(2,128)S(1)}, u32[]{:S(2)}, u32[]{:S(2)}) %collective-permute-start.13) | collective-permute-done | bytes 4128 | tf_op jit(solution)/shard_map/ppermute | solution.py:17
  260.7 0.0 collective-permute-done.14
  260.7 0.1 fusion.18
  260.8 0.3 multiply_reduce_fusion.2
  261.1 0.3 multiply_reduce_fusion.1
  261.4 7.4 %collective-permute-start.16 = (f32[1,512]{1,0:T(1,128)S(1)}, f32[1,512]{1,0:T(1,128)S(1)}, u32[]{:S(2)}, u32[]{:S(2)}) collective-permute-start(f32[1,512]{1,0:T(1,128)S(1)} %get-tuple-element.21), channel_id=1, source_target_pairs={{0,4},{2,6},{4,8},{6,10},{8,12},{10,14},{1,5},{3,7},{5,9},{7,11},{... | collective-permute-start | bytes 6152 | tf_op jit(solution)/shard_map/ppermute | solution.py:17
  268.8 1.4 collective-permute-start.17
  270.2 1.3 collective-permute-start.18
  271.5 1.5 collective-permute-start.19
  273.0 7.5 %collective-permute-done.19 = f32[1,512]{1,0:T(1,128)S(1)} collective-permute-done((f32[1,512]{1,0:T(1,128)S(1)}, f32[1,512]{1,0:T(1,128)S(1)}, u32[]{:S(2)}, u32[]{:S(2)}) %collective-permute-start.19) | collective-permute-done | bytes 2080 | tf_op jit(solution)/shard_map/ppermute | solution.py:17
  280.5 0.0 collective-permute-done.17
  280.5 0.0 collective-permute-done.18
  280.6 0.1 fusion.19
  280.6 0.3 multiply_reduce_fusion
  280.9 0.4 multiply_convert_fusion
  281.3 2.5 fusion.3
  283.8 0.0 collective-permute-done.20
  283.8 2.5 fusion.4
  286.3 7.2 %add_convert_fusion = bf16[512,4096]{1,0:T(8,128)(2,1)} fusion(f32[512,4096]{1,0:T(8,128)S(1)} %fusion.4, f32[512,4096]{1,0:T(8,128)S(1)} %fusion.3, bf16[512,4096]{1,0:T(8,128)(2,1)} %collective-permute-done.21, bf16[3,512,512]{1,2,0:T(8,128)(2,1)S(1)} %multiply_convert_fusion), kind=kOutput, calls=%fused_computation | convolution fusion | flops 2153775104 | bytes 25690112 | tf_op jit(solution)/shard_map/dot_general | solution.py:69
  (37 shorter events, 0.2 us)
Async XLA Ops:
  6.5 1.6 copy-start
  6.5 30.2 %all-reduce.3.cloned.1.call-start = ((), (), s32[]{:S(2)}) async-start(), calls=%async_computation | async-start | bytes 1048576 | tf_op jit(solution)/shard_map/psum | solution.py:32
  10.6 4.5 %copy-start.2 = (s32[512]{0:T(512)S(1)}, s32[512]{0:T(512)}, u32[]{:S(2)}) copy-start(s32[512]{0:T(512)} %param.12) | copy-start | bytes 6148
  10.6 10.7 %copy-start.4 = (s32[1,2]{1,0:T(1,128)S(1)}, s32[1,2]{1,0:T(1,128)}, u32[]{:S(2)}) copy-start(s32[1,2]{1,0:T(1,128)} %param.13) | copy-start | bytes 28
  10.6 12.8 %copy-start.3 = (s32[512]{0:T(512)S(1)}, s32[512]{0:T(512)}, u32[]{:S(2)}) copy-start(s32[512]{0:T(512)} %param.11) | copy-start | bytes 6148
  15.1 8.3 %collective-permute-start.2 = (s32[512]{0:T(512)S(1)}, s32[512]{0:T(512)S(1)}, u32[]{:S(2)}, u32[]{:S(2)}) collective-permute-start(s32[512]{0:T(512)S(1)} %copy-done.2), channel_id=1, source_target_pairs={{0,2},{2,4},{4,6},{6,8},{8,10},{10,12},{12,14},{1,3},{3,5},{5,7},{... | collective-permute-start | bytes 6152 | tf_op jit(solution)/shard_map/ppermute | solution.py:17
  20.0 5.5 %collective-permute-start.3 = (s32[512]{0:T(512)S(1)}, s32[512]{0:T(512)S(1)}, u32[]{:S(2)}, u32[]{:S(2)}) collective-permute-start(s32[512]{0:T(512)S(1)} %copy-done.2), channel_id=1, source_target_pairs={{2,0},{4,2},{6,4},{8,6},{10,8},{12,10},{14,12},{3,1},{5,3},{7,5},{... | collective-permute-start | bytes 6152 | tf_op jit(solution)/shard_map/ppermute | solution.py:17
  40.0 7.6 %collective-permute-start.1 = (bf16[512,128]{1,0:T(8,128)(2,1)S(1)}, bf16[512,128]{1,0:T(8,128)(2,1)S(1)}, u32[]{:S(2)}, u32[]{:S(2)}) collective-permute-start(bf16[512,128]{1,0:T(8,128)(2,1)S(1)} %multiply_convert_fusion.2), channel_id=1, source_target_pairs={{2,0},{4,2},{6,4},{8,6},{10,8},{12,10},{14,12},{3,1},{5,3},{7,5},{... | collective-permute-start | bytes 393224 | tf_op jit(solution)/shard_map/ppermute | solution.py:17
  41.3 9.3 %collective-permute-start = (bf16[512,128]{1,0:T(8,128)(2,1)S(1)}, bf16[512,128]{1,0:T(8,128)(2,1)S(1)}, u32[]{:S(2)}, u32[]{:S(2)}) collective-permute-start(bf16[512,128]{1,0:T(8,128)(2,1)S(1)} %multiply_convert_fusion.2), channel_id=1, source_target_pairs={{0,2},{2,4},{4,6},{6,8},{8,10},{10,12},{12,14},{1,3},{3,5},{5,7},{... | collective-permute-start | bytes 393224 | tf_op jit(solution)/shard_map/ppermute | solution.py:17
  52.8 16.9 %collective-permute-start.5 = (f32[2,512]{1,0:T(2,128)S(1)}, f32[2,512]{1,0:T(2,128)S(1)}, u32[]{:S(2)}, u32[]{:S(2)}) collective-permute-start(f32[2,512]{1,0:T(2,128)S(1)} %get-tuple-element.35), channel_id=1, source_target_pairs={{0,2},{2,4},{4,6},{6,8},{8,10},{10,12},{12,14},{1,3},{3,5},{5,7},{... | collective-permute-start | bytes 12296 | tf_op jit(solution)/shard_map/ppermute | solution.py:17
  57.2 12.6 %collective-permute-start.6 = (f32[2,512]{1,0:T(2,128)S(1)}, f32[2,512]{1,0:T(2,128)S(1)}, u32[]{:S(2)}, u32[]{:S(2)}) collective-permute-start(f32[2,512]{1,0:T(2,128)S(1)} %get-tuple-element.36), channel_id=1, source_target_pairs={{2,0},{4,2},{6,4},{8,6},{10,8},{12,10},{14,12},{3,1},{5,3},{7,5},{... | collective-permute-start | bytes 12296 | tf_op jit(solution)/shard_map/ppermute | solution.py:17
  58.5 7.1 %collective-permute-start.4 = (f32[1,512]{1,0:T(1,128)S(1)}, f32[1,512]{1,0:T(1,128)S(1)}, u32[]{:S(2)}, u32[]{:S(2)}) collective-permute-start(f32[1,512]{1,0:T(1,128)S(1)} %get-tuple-element.33), channel_id=1, source_target_pairs={{0,4},{2,6},{4,8},{6,10},{8,12},{10,14},{1,5},{3,7},{5,9},{7,11},{... | collective-permute-start | bytes 6152 | tf_op jit(solution)/shard_map/ppermute | solution.py:17
  64.3 5.5 %collective-permute-start.7 = (f32[1,512]{1,0:T(1,128)S(1)}, f32[1,512]{1,0:T(1,128)S(1)}, u32[]{:S(2)}, u32[]{:S(2)}) collective-permute-start(f32[1,512]{1,0:T(1,128)S(1)} %get-tuple-element.34), channel_id=1, source_target_pairs={{4,0},{6,2},{8,4},{10,6},{12,8},{14,10},{5,1},{7,3},{9,5},{11,7},{... | collective-permute-start | bytes 6152 | tf_op jit(solution)/shard_map/ppermute | solution.py:17
  69.9 12.2 %copy-start.1 = (bf16[512,4096]{1,0:T(8,128)(2,1)S(1)}, bf16[512,4096]{1,0:T(8,128)(2,1)}, u32[]{:S(2)}) copy-start(bf16[512,4096]{1,0:T(8,128)(2,1)} %param.8) | copy-start | bytes 12582916
  70.5 15.8 %collective-permute-start.9 = (f32[2,512]{1,0:T(2,128)S(1)}, f32[2,512]{1,0:T(2,128)S(1)}, u32[]{:S(2)}, u32[]{:S(2)}) collective-permute-start(f32[2,512]{1,0:T(2,128)S(1)} %get-tuple-element.31), channel_id=1, source_target_pairs={{0,2},{2,4},{4,6},{6,8},{8,10},{10,12},{12,14},{1,3},{3,5},{5,7},{... | collective-permute-start | bytes 12296 | tf_op jit(solution)/shard_map/ppermute | solution.py:17
  72.8 13.4 %collective-permute-start.10 = (f32[2,512]{1,0:T(2,128)S(1)}, f32[2,512]{1,0:T(2,128)S(1)}, u32[]{:S(2)}, u32[]{:S(2)}) collective-permute-start(f32[2,512]{1,0:T(2,128)S(1)} %get-tuple-element.32), channel_id=1, source_target_pairs={{2,0},{4,2},{6,4},{8,6},{10,8},{12,10},{14,12},{3,1},{5,3},{7,5},{... | collective-permute-start | bytes 12296 | tf_op jit(solution)/shard_map/ppermute | solution.py:17
  74.1 10.2 %collective-permute-start.8 = (f32[1,512]{1,0:T(1,128)S(1)}, f32[1,512]{1,0:T(1,128)S(1)}, u32[]{:S(2)}, u32[]{:S(2)}) collective-permute-start(f32[1,512]{1,0:T(1,128)S(1)} %get-tuple-element.29), channel_id=1, source_target_pairs={{0,4},{2,6},{4,8},{6,10},{8,12},{10,14},{1,5},{3,7},{5,9},{7,11},{... | collective-permute-start | bytes 6152 | tf_op jit(solution)/shard_map/ppermute | solution.py:17
  80.8 5.5 %collective-permute-start.11 = (f32[1,512]{1,0:T(1,128)S(1)}, f32[1,512]{1,0:T(1,128)S(1)}, u32[]{:S(2)}, u32[]{:S(2)}) collective-permute-start(f32[1,512]{1,0:T(1,128)S(1)} %get-tuple-element.30), channel_id=1, source_target_pairs={{4,0},{6,2},{8,4},{10,6},{12,8},{14,10},{5,1},{7,3},{9,5},{11,7},{... | collective-permute-start | bytes 6152 | tf_op jit(solution)/shard_map/ppermute | solution.py:17
  82.1 201.7 %collective-permute-start.20 = (bf16[512,4096]{1,0:T(8,128)(2,1)S(1)}, bf16[512,4096]{1,0:T(8,128)(2,1)S(1)}, u32[]{:S(2)}, u32[]{:S(2)}) collective-permute-start(bf16[512,4096]{1,0:T(8,128)(2,1)S(1)} %copy-done.1), channel_id=1, source_target_pairs={{0,2},{2,4},{4,6},{6,8},{8,10},{10,12},{12,14},{1,3},{3,5},{5,7},{... | collective-permute-start | bytes 12582920 | tf_op jit(solution)/shard_map/ppermute | solution.py:17
  84.3 201.9 %collective-permute-start.21 = (bf16[512,4096]{1,0:T(8,128)(2,1)S(1)}, bf16[512,4096]{1,0:T(8,128)(2,1)}, u32[]{:S(2)}, u32[]{:S(2)}) collective-permute-start(bf16[512,4096]{1,0:T(8,128)(2,1)S(1)} %copy-done.1), channel_id=1, source_target_pairs={{2,0},{4,2},{6,4},{8,6},{10,8},{12,10},{14,12},{3,1},{5,3},{7,5},{... | collective-permute-start | bytes 12582920 | tf_op jit(solution)/shard_map/ppermute | solution.py:17
  87.0 10.5 %collective-permute-start.12 = (f32[1,512]{1,0:T(1,128)S(1)}, f32[1,512]{1,0:T(1,128)S(1)}, u32[]{:S(2)}, u32[]{:S(2)}) collective-permute-start(f32[1,512]{1,0:T(1,128)S(1)} %get-tuple-element.25), channel_id=1, source_target_pairs={{0,4},{2,6},{4,8},{6,10},{8,12},{10,14},{1,5},{3,7},{5,9},{7,11},{... | collective-permute-start | bytes 6152 | tf_op jit(solution)/shard_map/ppermute | solution.py:17
  94.2 166.5 %collective-permute-start.13 = (f32[2,512]{1,0:T(2,128)S(1)}, f32[2,512]{1,0:T(2,128)S(1)}, u32[]{:S(2)}, u32[]{:S(2)}) collective-permute-start(f32[2,512]{1,0:T(2,128)S(1)} %get-tuple-element.27), channel_id=1, source_target_pairs={{0,2},{2,4},{4,6},{6,8},{8,10},{10,12},{12,14},{1,3},{3,5},{5,7},{... | collective-permute-start | bytes 12296 | tf_op jit(solution)/shard_map/ppermute | solution.py:17
  96.1 164.6 %collective-permute-start.14 = (f32[2,512]{1,0:T(2,128)S(1)}, f32[2,512]{1,0:T(2,128)S(1)}, u32[]{:S(2)}, u32[]{:S(2)}) collective-permute-start(f32[2,512]{1,0:T(2,128)S(1)} %get-tuple-element.28), channel_id=1, source_target_pairs={{2,0},{4,2},{6,4},{8,6},{10,8},{12,10},{14,12},{3,1},{5,3},{7,5},{... | collective-permute-start | bytes 12296 | tf_op jit(solution)/shard_map/ppermute | solution.py:17
  97.4 80.4 %collective-permute-start.15 = (f32[1,512]{1,0:T(1,128)S(1)}, f32[1,512]{1,0:T(1,128)S(1)}, u32[]{:S(2)}, u32[]{:S(2)}) collective-permute-start(f32[1,512]{1,0:T(1,128)S(1)} %get-tuple-element.26), channel_id=1, source_target_pairs={{4,0},{6,2},{8,4},{10,6},{12,8},{14,10},{5,1},{7,3},{9,5},{11,7},{... | collective-permute-start | bytes 6152 | tf_op jit(solution)/shard_map/ppermute | solution.py:17
  261.4 10.1 %collective-permute-start.16 = (f32[1,512]{1,0:T(1,128)S(1)}, f32[1,512]{1,0:T(1,128)S(1)}, u32[]{:S(2)}, u32[]{:S(2)}) collective-permute-start(f32[1,512]{1,0:T(1,128)S(1)} %get-tuple-element.21), channel_id=1, source_target_pairs={{0,4},{2,6},{4,8},{6,10},{8,12},{10,14},{1,5},{3,7},{5,9},{7,11},{... | collective-permute-start | bytes 6152 | tf_op jit(solution)/shard_map/ppermute | solution.py:17
  268.8 11.7 %collective-permute-start.17 = (f32[2,512]{1,0:T(2,128)S(1)}, f32[2,512]{1,0:T(2,128)S(1)}, u32[]{:S(2)}, u32[]{:S(2)}) collective-permute-start(f32[2,512]{1,0:T(2,128)S(1)} %get-tuple-element.23), channel_id=1, source_target_pairs={{0,2},{2,4},{4,6},{6,8},{8,10},{10,12},{12,14},{1,3},{3,5},{5,7},{... | collective-permute-start | bytes 12296 | tf_op jit(solution)/shard_map/ppermute | solution.py:17
  270.2 10.3 %collective-permute-start.18 = (f32[2,512]{1,0:T(2,128)S(1)}, f32[2,512]{1,0:T(2,128)S(1)}, u32[]{:S(2)}, u32[]{:S(2)}) collective-permute-start(f32[2,512]{1,0:T(2,128)S(1)} %get-tuple-element.24), channel_id=1, source_target_pairs={{2,0},{4,2},{6,4},{8,6},{10,8},{12,10},{14,12},{3,1},{5,3},{7,5},{... | collective-permute-start | bytes 12296 | tf_op jit(solution)/shard_map/ppermute | solution.py:17
  271.5 9.0 %collective-permute-start.19 = (f32[1,512]{1,0:T(1,128)S(1)}, f32[1,512]{1,0:T(1,128)S(1)}, u32[]{:S(2)}, u32[]{:S(2)}) collective-permute-start(f32[1,512]{1,0:T(1,128)S(1)} %get-tuple-element.22), channel_id=1, source_target_pairs={{4,0},{6,2},{8,4},{10,6},{12,8},{14,10},{5,1},{7,3},{9,5},{11,7},{... | collective-permute-start | bytes 6152 | tf_op jit(solution)/shard_map/ppermute | solution.py:17
Sparse Core Ops, SparseCore 0:
  15.2 21.4 all-reduce.2
where the time goes:
time: 301 us; the launch traced here: 300 us
  waiting for transfers between devices  191 us (63%)
  starting transfers between devices  63.1 us (21%)
  matrix products  21.3 us (7%)
  between operations  13.8 us (5%)
  other arithmetic  8.61 us (3%)
    ppermute x22, waiting for transfers between devices, shifted(): return lax.ppermute(block, axis, route)  180 us
    ppermute x22, starting transfers between devices, shifted(): return lax.ppermute(block, axis, route)  63.1 us
    psum x1, waiting for transfers between devices, body(): s_feat, t_feat = lax.psum((s_part, t_part), 'tgrp')  11.3 us
    dot_general x1, matrix products, body(): jnp.dot(plan[2], right_rows, preferred_element_type=jnp.float32)  7.2 us
  transfers between devices with their start and end apart: 23, of which 9 were waited for; matrix products, arithmetic and copies ran while one was open for 3% of the time, Pallas kernels for 0%

commit v1 on v0

--- a/solution.py
+++ b/solution.py
@@ -7,6 +7,7 @@
 
 ITERS = 4
 
+LOCAL_KERNEL_BYTES = 24 * 2**20
 
 norm_eps = 1e-05
 
@@ -22,7 +23,85 @@
     return (features * factor).astype(jnp.bfloat16)
 
 
-def body(
+def beside(values):
+    zero_row = jnp.zeros_like(values[:1])
+    from_left = jnp.concatenate([zero_row, values[:-1]], 0)
+    from_right = jnp.concatenate([values[1:], zero_row], 0)
+    return jnp.stack([from_left, values, from_right], 1)
+
+
+def tgrp_sum(value):
+    if lax.axis_size("tgrp") == 2:
+        return value + lax.ppermute(value, "tgrp", [(0, 1), (1, 0)])
+    return lax.psum(value, "tgrp")
+
+
+def body_local(
+    student_hidden, teacher_hidden, student_proj, teacher_proj, student_chars, teacher_chars, band
+):
+    rows = student_hidden.shape[0]
+    proj_width = student_proj.shape[1]
+    blocks = lax.axis_size("seq")
+    me = lax.axis_index("seq")
+
+    s_part = jnp.dot(student_hidden, student_proj, preferred_element_type=jnp.float32)
+    t_part = jnp.dot(teacher_hidden, teacher_proj, preferred_element_type=jnp.float32)
+    feats = tgrp_sum(jnp.concatenate([s_part, t_part], 1))
+    units = jnp.concatenate(
+        [unit_rows(feats[:, :proj_width]), unit_rows(feats[:, proj_width:])], 1
+    )
+    ints = jnp.concatenate([student_chars, teacher_chars, band[0]])
+    all_units = lax.all_gather(units, "seq")
+    all_ints = lax.all_gather(ints, "seq")
+
+    teacher_rows, all_units, all_ints = lax.optimization_barrier((teacher_hidden, all_units, all_ints))
+    left_rows = shifted(teacher_rows, "seq", 1)
+    right_rows = shifted(teacher_rows, "seq", -1)
+
+    s_unit = all_units[:, :, :proj_width]
+    t_unit = all_units[:, :, proj_width:]
+    s_pos = all_ints[:, :rows].astype(jnp.float32)
+    t_pos = beside(all_ints[:, rows : 2 * rows].astype(jnp.float32))
+    flags = all_ints[:, 2 * rows :]
+    ones_col = jnp.ones((blocks,), jnp.int32)
+    slot_mask = jnp.stack([flags[:, 0], ones_col, flags[:, 1]], 1).astype(jnp.float32)
+    scores = jnp.einsum(
+        "bkjp,bip->bkji", beside(t_unit), s_unit, preferred_element_type=jnp.float32
+    ) / math.sqrt(proj_width)
+    distance = jnp.abs(s_pos[:, None, None, :] - t_pos[:, :, :, None]) / (4.0 * rows)
+    kernel = jnp.exp(scores - distance) * slot_mask[:, :, None, None]
+
+    def iterate(iteration, scales):
+        row_scale, col_scale = scales
+        partial_cols = jnp.sum(row_scale[:, None, None, :] * kernel, axis=3)
+        zero_row = jnp.zeros_like(partial_cols[:1, 0])
+        column_total = (
+            partial_cols[:, 1]
+            + jnp.concatenate([zero_row, partial_cols[:-1, 2]], 0)
+            + jnp.concatenate([partial_cols[1:, 0], zero_row], 0)
+        )
+        col_scale = beside(1.0 / column_total)
+        row_scale = 1.0 / jnp.sum(kernel * col_scale[:, :, :, None], axis=(1, 2))
+        return row_scale, col_scale
+
+    row_scale, col_scale = lax.fori_loop(
+        0,
+        ITERS,
+        iterate,
+        (jnp.ones((blocks, rows), jnp.float32), jnp.zeros((blocks, 3, rows), jnp.float32)),
+    )
+    own_kernel = lax.dynamic_index_in_dim(kernel, me, 0, keepdims=False)
+    own_row = lax.dynamic_index_in_dim(row_scale, me, 0, keepdims=False)
+    own_col = lax.dynamic_index_in_dim(col_scale, me, 0, keepdims=False)
+    plan = (own_row[None, None, :] * own_kernel * own_col[:, :, None]).astype(jnp.bfloat16)
+    along_j = (((0,), (0,)), ((), ()))
+    aligned = lax.dot_general(plan[1], teacher_hidden, along_j, preferred_element_type=jnp.float32)
+    aligned = aligned + lax.dot_general(plan[0], left_rows, along_j, preferred_element_type=jnp.float32)
+    aligned = aligned + lax.dot_general(plan[2], right_rows, along_j, preferred_element_type=jnp.float32)
+    return aligned.astype(jnp.bfloat16)
+
+
+def body_banded(
     student_hidden, teacher_hidden, student_proj, teacher_proj, student_chars, teacher_chars, band
 ):
     block_rows = student_hidden.shape[0]
@@ -71,6 +150,14 @@
 
 
 def solution(mesh):
+    blocks = mesh.shape["seq"]
+
+    def body(*args):
+        rows = args[0].shape[0]
+        if blocks * 3 * rows * rows * 4 <= LOCAL_KERNEL_BYTES:
+            return body_local(*args)
+        return body_banded(*args)
+
     return jax.shard_map(
         body,
         mesh=mesh,

time: 301 us -> 281 us (0.934)
  waiting for transfers between devices: 191 us -> 101 us
  starting transfers between devices: 63.1 us -> 7.26 us
  other arithmetic: 8.61 us -> 50.8 us
  blocking collectives: 0 us -> 39.7 us
  local copies, waits for them, and re-layouts: 2.32 us -> 33.7 us
  matrix products: 21.3 us -> 33.3 us
    ppermute x22 -> x2, waiting for transfers between devices: 180 us -> 86.9 us  [shifted(): return lax.ppermute(block, axis, route)]
    ppermute x22 -> x2, starting transfers between devices: 63.1 us -> 6.74 us  [shifted(): return lax.ppermute(block, axis, route)]
    reduce_sum x7 -> x8, other arithmetic: 2.04 us -> 47.3 us  [the longest x4 38.4 us: iterate(): partial_cols = jnp.sum(row_scale[:, None, None, :] * kernel, axis=3)]
    unnamed x0 -> x1, blocking collectives: none -> 39.7 us
    while x0 -> x16, local copies, waits for them, and re-layouts: none -> 22.4 us
    all_gather x0 -> x1, waiting for transfers between devices: none -> 12.7 us  [body_local(): all_units = lax.all_gather(units, 'seq')]
    dot_general x6, matrix products: 21.3 us -> 33.3 us  [the longest x1 10.8 us: body_local(): jnp.einsum('bkjp,bip->bkji', beside(t_unit), s_unit, preferred_element_ty...]
    psum x1 -> x0, waiting for transfers between devices: 11.3 us -> none  [body(): s_feat, t_feat = lax.psum((s_part, t_part), 'tgrp')]
  transfers between devices with their start and end apart: 23 -> 4, of which waited for: 9 -> 3; matrix products, arithmetic and copies ran while one was open for 3% -> 26% of each run, Pallas kernels for 0% -> 0%
where the time goes in v1:
time: 281 us
  waiting for transfers between devices  101 us (36%)
  other arithmetic  50.8 us (18%)
  blocking collectives  39.7 us (14%)
  local copies, waits for them, and re-layouts  33.7 us (12%)
  matrix products  33.3 us (12%)
  between operations  14.4 us (5%)
  starting transfers between devices  7.26 us (3%)
    ppermute x2, waiting for transfers between devices, shifted(): return lax.ppermute(block, axis, route)  86.9 us
    unnamed x1, blocking collectives  39.7 us
    reduce_sum x4, other arithmetic, iterate(): partial_cols = jnp.sum(row_scale[:, None, None, :] * kernel, axis=3)  38.4 us
    while x16, local copies, waits for them, and re-layouts  22.4 us
    all_gather x1, waiting for transfers between devices, body_local(): all_units = lax.all_gather(units, 'seq')  12.7 us
    dot_general x1, matrix products, body_local(): jnp.einsum('bkjp,bip->bkji', beside(t_unit), s_unit, preferred_element_ty...  10.8 us
    reduce_sum x4, other arithmetic, iterate(): row_scale = 1.0 / jnp.sum(kernel * col_scale[:, :, :, None], axis=(1, 2))  8.94 us
    dot_general x1, matrix products, body_local(): lax.dot_general(plan[2], right_rows, along_j, preferred_element_type=jnp....  7.35 us
  transfers between devices with their start and end apart: 4, of which 3 were waited for; matrix products, arithmetic and copies ran while one was open for 26% of the time, Pallas kernels for 0%

profile of v1, /device:TPU:0, one launch (start us, length us, event | category | flops | bytes accessed | tf_op | source)
XLA Modules:
  0.0 280.8 jit_solution(9486870150378005238)
XLA Ops:
  6.5 0.0 copy-start
  6.5 0.0 all-gather.4.cloned.1.call-start
  6.5 1.6 copy-done
  8.1 1.9 fusion.20
  10.0 4.0 %fusion.21 = f32[512,128]{0,1:T(8,128)S(1)} fusion(bf16[512,4096]{1,0:T(8,128)(2,1)} %param.10, bf16[4096,128]{1,0:T(8,128)(2,1)} %param.12), kind=kOutput, calls=%fused_computation.59 | convolution fusion | flops 536870912 | bytes 5505024 | tf_op jit(solution)/shard_map/dot_general | solution.py:48
  14.0 0.0 copy-start.7
  14.0 0.0 copy-start.4
  14.0 0.0 copy-start.5
  14.0 0.0 copy-start.6
  14.1 0.5 collective-permute-start
  14.6 1.5 collective-permute-done
  16.1 0.1 fusion.14
  16.2 0.1 multiply_reduce_fusion.3
  16.3 0.1 multiply_convert_fusion.1
  16.4 0.7 pad_maximum_fusion.2
  17.1 0.0 all-gather.4.cloned.1.call-update
  17.1 0.0 copy-done.7
  17.2 0.6 dynamic-slice
  18.5 0.0 copy-done.4
  18.5 0.0 copy-done.5
  18.5 0.0 copy-done.6
  18.5 0.1 add_dynamic-update-slice_fusion
  18.7 39.7 %all-reduce.8 = s32[8208]{0:T(1024)S(1)} all-reduce(s32[8208]{0:T(1024)S(1)} %add_dynamic-update-slice_fusion), channel_id=3, replica_groups=mesh['groups'=2,'seq'=8,'tgrp'=2] {'seq'}, use_global_device_ids=true, to_apply=%add.8 | all-reduce | flops 8208 | bytes 65664
  58.4 0.1 reshape.44
  58.5 0.1 pad.12.clone
  58.5 12.7 %all-gather.4.cloned.1.call-done = bf16[4096,256]{0,1:T(8,128)(2,1)} async-done(((bf16[512,256]{0,1:T(8,128)(2,1)}), bf16[4096,256]{0,1:T(8,128)(2,1)}) %all-gather.4.cloned.1.call-update) | async-done | bytes 2097168 | tf_op jit(solution)/shard_map/all_gather | solution.py:54
  71.2 3.8 %copy.28 = bf16[32,8,8,512]{3,2,1,0:T(8,128)(2,1)} copy(bf16[32,8,8,512]{3,1,2,0:T(8,128)(2,1)} %bitcast.79) | data formatting | bytes 4194304
  75.0 0.1 fusion.18
  75.1 3.0 %copy.18 = bf16[8,512,256]{2,1,0:T(8,128)(2,1)S(1)} copy(bf16[8,512,256]{1,0,2:T(8,128)(2,1)} %bitcast.77) | data formatting | bytes 4194304 | tf_op jit(solution)/shard_map/optimization_barrier | solution.py:57
  78.1 0.4 fusion.17
  78.5 0.2 slice_bitcast_fusion.2
  78.7 5.3 %collective-permute-start.1 = (bf16[512,4096]{1,0:T(8,128)(2,1)}, bf16[512,4096]{1,0:T(8,128)(2,1)}, u32[]{:S(2)}, u32[]{:S(2)}) collective-permute-start(bf16[512,4096]{1,0:T(8,128)(2,1)} %param.10), channel_id=1, source_target_pairs={{0,2},{2,4},{4,6},{6,8},{8,10},{10,12},{12,14},{1,3},{3,5},{5,7},{... | collective-permute-start | bytes 12582920 | tf_op jit(solution)/shard_map/ppermute | solution.py:18
  84.0 1.5 collective-permute-start.2
  85.5 0.1 pad_bitcast_fusion.2
  85.6 0.1 pad_bitcast_fusion.3
  85.7 0.1 add_convert_fusion.1
  85.8 10.8 %exponential_multiply_fusion = f32[8,3,512,512]{3,2,1,0:T(8,128)} fusion(f32[8,3]{1,0:T(8,128)S(1)} %add_convert_fusion.1, f32[8,3,512]{2,1,0:T(4,128)S(1)} %copy.22, f32[8,512]{1,0:T(8,128)S(1)} %get-tuple-element.69, bf16[8,1,512,128]{3,2,1,0:T(8,128)(2,1)S(1)} %pad_bitcast_fusion.2, bf16[8,1,512,128]{3,2,1,0:T(8,128)(2,1)S(1)} %slice_bitcast_fusion.2, ...), kind=kOutput, calls=%fused_computation.13 | convolution fusion | flops 1651507200 | bytes 29446144 | tf_op jit(solution)/shard_map/bkjp,bip->bkji/dot_general | solution.py:68
  96.6 70.8 %while.13 = (s32[]{:T(128)}, f32[8,512]{1,0:T(8,128)S(1)}, f32[8,3,512]{2,0,1:T(8,128)}, f32[8,3,512,512]{3,2,1,0:T(8,128)}, s32[]{:T(128)}, /*index=5*/s32[]{:T(128)}) while((s32[]{:T(128)}, f32[8,512]{1,0:T(8,128)S(1)}, f32[8,3,512]{2,0,1:T(8,128)}, f32[8,3,512,512]{3,2,1,0:T(8,128)}, s32[]{:T(128)}, /*index=5*/s32[]{:T(128)}) %tuple.41), condition=%wide.region_5.0_spmd.clone, body=%wide.region_2.0_spmd.clone.sunk | while | flops 25194500 | bytes 151912576 | solution.py:87
  96.6 9.6 %multiply_reduce_fusion.6 = f32[8,3,512]{2,1,0:T(4,128)S(1)} fusion(f32[8,3,512,512]{3,2,1,0:T(8,128)} %get-tuple-element.128, f32[8,512]{1,0:T(8,128)S(1)} %broadcast_select_fusion.2), kind=kLoop, calls=%fused_computation.1.clone.1 | loop fusion | flops 12570624 | bytes 25231360 | tf_op jit(solution)/shard_map/while/body/eval_jaxpr/reduce_sum | solution.py:76
  106.3 0.0 copy-start.3
  106.4 5.6 %copy-done.2 = f32[8,3,512,512]{3,2,1,0:T(8,128)S(1)} copy-done((f32[8,3,512,512]{3,2,1,0:T(8,128)S(1)}, f32[8,3,512,512]{3,2,1,0:T(8,128)}, u32[]{:S(2)}) %copy-start.2) | copy-done | bytes 25165848 | tf_op jit(solution)/shard_map/while
  112.0 2.2 multiply_reduce_fusion.7
  114.3 0.0 copy-start.2
  114.3 9.6 %multiply_reduce_fusion.6 = f32[8,3,512]{2,1,0:T(4,128)S(1)} fusion(f32[8,3,512,512]{3,2,1,0:T(8,128)} %get-tuple-element.128, f32[8,512]{1,0:T(8,128)S(1)} %broadcast_select_fusion.2), kind=kLoop, calls=%fused_computation.1.clone.1 | loop fusion | flops 12570624 | bytes 25231360 | tf_op jit(solution)/shard_map/while/body/eval_jaxpr/reduce_sum | solution.py:76
  124.1 5.6 %copy-done.2 = f32[8,3,512,512]{3,2,1,0:T(8,128)S(1)} copy-done((f32[8,3,512,512]{3,2,1,0:T(8,128)S(1)}, f32[8,3,512,512]{3,2,1,0:T(8,128)}, u32[]{:S(2)}) %copy-start.2) | copy-done | bytes 25165848 | tf_op jit(solution)/shard_map/while
  129.7 2.2 multiply_reduce_fusion.7
  132.0 0.0 copy-start.2
  132.0 9.6 %multiply_reduce_fusion.6 = f32[8,3,512]{2,1,0:T(4,128)S(1)} fusion(f32[8,3,512,512]{3,2,1,0:T(8,128)} %get-tuple-element.128, f32[8,512]{1,0:T(8,128)S(1)} %broadcast_select_fusion.2), kind=kLoop, calls=%fused_computation.1.clone.1 | loop fusion | flops 12570624 | bytes 25231360 | tf_op jit(solution)/shard_map/while/body/eval_jaxpr/reduce_sum | solution.py:76
  141.8 0.0 copy-start.3
  141.8 5.6 %copy-done.2 = f32[8,3,512,512]{3,2,1,0:T(8,128)S(1)} copy-done((f32[8,3,512,512]{3,2,1,0:T(8,128)S(1)}, f32[8,3,512,512]{3,2,1,0:T(8,128)}, u32[]{:S(2)}) %copy-start.2) | copy-done | bytes 25165848 | tf_op jit(solution)/shard_map/while
  147.4 2.2 multiply_reduce_fusion.7
  149.7 9.6 %multiply_reduce_fusion.6 = f32[8,3,512]{2,1,0:T(4,128)S(1)} fusion(f32[8,3,512,512]{3,2,1,0:T(8,128)} %get-tuple-element.128, f32[8,512]{1,0:T(8,128)S(1)} %broadcast_select_fusion.2), kind=kLoop, calls=%fused_computation.1.clone.1 | loop fusion | flops 12570624 | bytes 25231360 | tf_op jit(solution)/shard_map/while/body/eval_jaxpr/reduce_sum | solution.py:76
  159.5 5.6 %copy-done.2 = f32[8,3,512,512]{3,2,1,0:T(8,128)S(1)} copy-done((f32[8,3,512,512]{3,2,1,0:T(8,128)S(1)}, f32[8,3,512,512]{3,2,1,0:T(8,128)}, u32[]{:S(2)}) %copy-start.2) | copy-done | bytes 25165848 | tf_op jit(solution)/shard_map/while
  165.1 2.2 multiply_reduce_fusion.7
  167.4 0.0 copy-done.3
  167.4 0.8 constant_dynamic-slice_fusion
  168.2 2.2 fusion.9
  170.5 4.6 %fusion.11 = f32[512,4096]{1,0:T(8,128)S(1)} fusion(bf16[512,4096]{1,0:T(8,128)(2,1)} %param.10, bf16[3,512,512]{2,1,0:T(8,128)(2,1)S(1)} %fusion.9), kind=kOutput, calls=%fused_computation.31 | convolution fusion | flops 2147483648 | bytes 13107200 | tf_op jit(solution)/shard_map/dot_general | solution.py:98
  175.1 86.9 %collective-permute-done.1 = bf16[512,4096]{1,0:T(8,128)(2,1)} collective-permute-done((bf16[512,4096]{1,0:T(8,128)(2,1)}, bf16[512,4096]{1,0:T(8,128)(2,1)}, u32[]{:S(2)}, u32[]{:S(2)}) %collective-permute-start.1) | collective-permute-done | bytes 4194336 | tf_op jit(solution)/shard_map/ppermute | solution.py:18
  262.0 4.6 %fusion.10 = f32[512,4096]{1,0:T(8,128)S(1)} fusion(bf16[512,4096]{1,0:T(8,128)(2,1)} %collective-permute-done.1, bf16[3,512,512]{2,1,0:T(8,128)(2,1)S(1)} %fusion.9), kind=kOutput, calls=%fused_computation.29 | convolution fusion | flops 2147483648 | bytes 13107200 | tf_op jit(solution)/shard_map/dot_general | solution.py:99
  266.6 0.0 collective-permute-done.2
  266.6 0.0 copy-start.1
  266.6 7.3 %add_convert_fusion = bf16[512,4096]{1,0:T(8,128)(2,1)} fusion(f32[512,4096]{1,0:T(8,128)S(1)} %fusion.11, f32[512,4096]{1,0:T(8,128)S(1)} %fusion.10, bf16[512,4096]{1,0:T(8,128)(2,1)} %collective-permute-done.2, bf16[3,512,512]{2,1,0:T(8,128)(2,1)S(1)} %fusion.9), kind=kOutput, calls=%fused_computation.14 | convolution fusion | flops 2153775104 | bytes 25690112 | tf_op jit(solution)/shard_map/dot_general | solution.py:100
  274.0 0.0 copy-done.1
  (64 shorter events, 0.7 us)
Async XLA Ops:
  6.5 1.6 copy-start
  6.5 64.7 %all-gather.4.cloned.1.call-start = ((), (), s32[]{:S(2)}) async-start(), calls=%async_computation | async-start | bytes 2359296 | tf_op jit(solution)/shard_map/all_gather | solution.py:54
  14.0 3.2 %copy-start.7 = (u32[32]{0:T(128)S(1)}, u32[32]{0:T(128)}, u32[]{:S(2)}) copy-start(u32[32]{0:T(128)} %constant.71) | copy-start | bytes 388
  14.0 4.5 %copy-start.4 = (s32[512]{0:T(512)S(1)}, s32[512]{0:T(512)}, u32[]{:S(2)}) copy-start(s32[512]{0:T(512)} %param.14) | copy-start | bytes 6148
  14.0 4.5 %copy-start.5 = (s32[512]{0:T(512)S(1)}, s32[512]{0:T(512)}, u32[]{:S(2)}) copy-start(s32[512]{0:T(512)} %param.13) | copy-start | bytes 6148
  14.0 4.5 %copy-start.6 = (s32[1,2]{1,0:T(1,128)S(1)}, s32[1,2]{1,0:T(1,128)}, u32[]{:S(2)}) copy-start(s32[1,2]{1,0:T(1,128)} %param.15) | copy-start | bytes 28
  14.1 2.1 collective-permute-start
  78.7 183.3 %collective-permute-start.1 = (bf16[512,4096]{1,0:T(8,128)(2,1)}, bf16[512,4096]{1,0:T(8,128)(2,1)}, u32[]{:S(2)}, u32[]{:S(2)}) collective-permute-start(bf16[512,4096]{1,0:T(8,128)(2,1)} %param.10), channel_id=1, source_target_pairs={{0,2},{2,4},{4,6},{6,8},{8,10},{10,12},{12,14},{1,3},{3,5},{5,7},{... | collective-permute-start | bytes 12582920 | tf_op jit(solution)/shard_map/ppermute | solution.py:18
  84.0 182.7 %collective-permute-start.2 = (bf16[512,4096]{1,0:T(8,128)(2,1)}, bf16[512,4096]{1,0:T(8,128)(2,1)}, u32[]{:S(2)}, u32[]{:S(2)}) collective-permute-start(bf16[512,4096]{1,0:T(8,128)(2,1)} %param.10), channel_id=1, source_target_pairs={{2,0},{4,2},{6,4},{8,6},{10,8},{12,10},{14,12},{3,1},{5,3},{7,5},{... | collective-permute-start | bytes 12582920 | tf_op jit(solution)/shard_map/ppermute | solution.py:18
  96.6 15.4 %copy-start.2 = (f32[8,3,512,512]{3,2,1,0:T(8,128)S(1)}, f32[8,3,512,512]{3,2,1,0:T(8,128)}, u32[]{:S(2)}) copy-start(f32[8,3,512,512]{3,2,1,0:T(8,128)} %get-tuple-element.128) | copy-start | bytes 75497472 | tf_op jit(solution)/shard_map/while
  106.3 7.9 %copy-start.3 = (f32[8,3,512]{2,0,1:T(8,128)}, f32[8,3,512]{2,0,1:T(8,128)S(1)}, u32[]{:S(2)}) copy-start(f32[8,3,512]{2,0,1:T(8,128)S(1)} %pad_maximum_fusion.5) | copy-start | bytes 147460 | tf_op jit(solution)/shard_map/while
  114.3 15.4 %copy-start.2 = (f32[8,3,512,512]{3,2,1,0:T(8,128)S(1)}, f32[8,3,512,512]{3,2,1,0:T(8,128)}, u32[]{:S(2)}) copy-start(f32[8,3,512,512]{3,2,1,0:T(8,128)} %get-tuple-element.128) | copy-start | bytes 75497472 | tf_op jit(solution)/shard_map/while
  124.1 7.9 %copy-start.3 = (f32[8,3,512]{2,0,1:T(8,128)}, f32[8,3,512]{2,0,1:T(8,128)S(1)}, u32[]{:S(2)}) copy-start(f32[8,3,512]{2,0,1:T(8,128)S(1)} %pad_maximum_fusion.5) | copy-start | bytes 147460 | tf_op jit(solution)/shard_map/while
  132.0 15.4 %copy-start.2 = (f32[8,3,512,512]{3,2,1,0:T(8,128)S(1)}, f32[8,3,512,512]{3,2,1,0:T(8,128)}, u32[]{:S(2)}) copy-start(f32[8,3,512,512]{3,2,1,0:T(8,128)} %get-tuple-element.128) | copy-start | bytes 75497472 | tf_op jit(solution)/shard_map/while
  141.8 7.9 %copy-start.3 = (f32[8,3,512]{2,0,1:T(8,128)}, f32[8,3,512]{2,0,1:T(8,128)S(1)}, u32[]{:S(2)}) copy-start(f32[8,3,512]{2,0,1:T(8,128)S(1)} %pad_maximum_fusion.5) | copy-start | bytes 147460 | tf_op jit(solution)/shard_map/while
  149.7 15.4 %copy-start.2 = (f32[8,3,512,512]{3,2,1,0:T(8,128)S(1)}, f32[8,3,512,512]{3,2,1,0:T(8,128)}, u32[]{:S(2)}) copy-start(f32[8,3,512,512]{3,2,1,0:T(8,128)} %get-tuple-element.128) | copy-start | bytes 75497472 | tf_op jit(solution)/shard_map/while
  159.5 7.9 %copy-start.3 = (f32[8,3,512]{2,0,1:T(8,128)}, f32[8,3,512]{2,0,1:T(8,128)S(1)}, u32[]{:S(2)}) copy-start(f32[8,3,512]{2,0,1:T(8,128)S(1)} %pad_maximum_fusion.5) | copy-start | bytes 147460 | tf_op jit(solution)/shard_map/while
  266.6 7.4 %copy-start.1 = (bf16[512,2048]{1,0:T(8,128)(2,1)S(1)}, bf16[512,2048]{1,0:T(8,128)(2,1)}, u32[]{:S(2)}) copy-start(bf16[512,2048]{1,0:T(8,128)(2,1)} %param.9) | copy-start | bytes 6291460
Sparse Core Ops, SparseCore 0:
  17.2 53.9 all-gather.3

commit v2 on v1

--- a/solution.py
+++ b/solution.py
@@ -50,19 +50,26 @@
     units = jnp.concatenate(
         [unit_rows(feats[:, :proj_width]), unit_rows(feats[:, proj_width:])], 1
     )
-    ints = jnp.concatenate([student_chars, teacher_chars, band[0]])
-    all_units = lax.all_gather(units, "seq")
-    all_ints = lax.all_gather(ints, "seq")
+    digits = jnp.stack([student_chars, teacher_chars])
+    digits = jnp.stack([digits // 4096, digits // 64 % 64, digits % 64], 1)
+    digit_rows = digits.reshape(-1, units.shape[1]).astype(jnp.bfloat16)
+    flag_row = jnp.zeros((1, units.shape[1]), jnp.bfloat16).at[0, :2].set(band[0].astype(jnp.bfloat16))
+    extra = jnp.concatenate([digit_rows, flag_row], 0)
+    pad = -(rows + extra.shape[0]) % 16
+    packed = jnp.concatenate([units, extra, jnp.zeros((pad, units.shape[1]), jnp.bfloat16)], 0)
+    gathered = lax.all_gather(packed, "seq")
 
-    teacher_rows, all_units, all_ints = lax.optimization_barrier((teacher_hidden, all_units, all_ints))
+    teacher_rows, gathered = lax.optimization_barrier((teacher_hidden, gathered))
     left_rows = shifted(teacher_rows, "seq", 1)
     right_rows = shifted(teacher_rows, "seq", -1)
 
-    s_unit = all_units[:, :, :proj_width]
-    t_unit = all_units[:, :, proj_width:]
-    s_pos = all_ints[:, :rows].astype(jnp.float32)
-    t_pos = beside(all_ints[:, rows : 2 * rows].astype(jnp.float32))
-    flags = all_ints[:, 2 * rows :]
+    s_unit = gathered[:, :rows, :proj_width]
+    t_unit = gathered[:, :rows, proj_width:]
+    got = gathered[:, rows : rows + digit_rows.shape[0]].astype(jnp.float32).reshape(blocks, 2, 3, rows)
+    chars = got[:, :, 0] * 4096.0 + got[:, :, 1] * 64.0 + got[:, :, 2]
+    s_pos = chars[:, 0]
+    t_pos = beside(chars[:, 1])
+    flags = gathered[:, rows + digit_rows.shape[0], :2].astype(jnp.int32)
     ones_col = jnp.ones((blocks,), jnp.int32)
     slot_mask = jnp.stack([flags[:, 0], ones_col, flags[:, 1]], 1).astype(jnp.float32)
     scores = jnp.einsum(

time: 281 us -> 301 us (1.071)
  blocking collectives: 39.7 us -> 0 us
  waiting for transfers between devices: 101 us -> 136 us
  local copies, waits for them, and re-layouts: 33.7 us -> 54.5 us
    all_gather x1, waiting for transfers between devices: 12.7 us -> 52.4 us  [body_local(): gathered = lax.all_gather(packed, 'seq')]
    unnamed x1 -> x0, blocking collectives: 39.7 us -> none
    optimization_barrier x1, local copies, waits for them, and re-layouts: 2.99 us -> 24.5 us  [body_local(): lax.optimization_barrier((teacher_hidden, gathered))]
    unnamed x16, local copies, waits for them, and re-layouts: 6.08 us -> 1.65 us
  transfers between devices with their start and end apart: 4 -> 4, of which waited for: 3 -> 2; matrix products, arithmetic and copies ran while one was open for 26% -> 25% of each run, Pallas kernels for 0% -> 0%
where the time goes in v2:
time: 301 us; the launch traced here: 299 us
  waiting for transfers between devices  136 us (45%)
  local copies, waits for them, and re-layouts  54.5 us (18%)
  other arithmetic  53.1 us (18%)
  matrix products  34.3 us (11%)
  between operations  13.7 us (5%)
  starting transfers between devices  6.52 us (2%)
    ppermute x2, waiting for transfers between devices, shifted(): return lax.ppermute(block, axis, route)  83.9 us
    all_gather x1, waiting for transfers between devices, body_local(): gathered = lax.all_gather(packed, 'seq')  52.4 us
    reduce_sum x4, other arithmetic, iterate(): partial_cols = jnp.sum(row_scale[:, None, None, :] * kernel, axis=3)  38.4 us
    optimization_barrier x1, local copies, waits for them, and re-layouts, body_local(): lax.optimization_barrier((teacher_hidden, gathered))  24.5 us
    while x16, local copies, waits for them, and re-layouts  22.4 us
    dot_general x1, matrix products, body_local(): jnp.einsum('bkjp,bip->bkji', beside(t_unit), s_unit, preferred_element_ty...  11.8 us
    reduce_sum x4, other arithmetic, iterate(): row_scale = 1.0 / jnp.sum(kernel * col_scale[:, :, :, None], axis=(1, 2))  8.94 us
    dot_general x1, matrix products, body_local(): lax.dot_general(plan[2], right_rows, along_j, preferred_element_type=jnp....  7.35 us
  transfers between devices with their start and end apart: 4, of which 2 were waited for; matrix products, arithmetic and copies ran while one was open for 25% of the time, Pallas kernels for 0%

profile of v2, /device:TPU:0, one launch (start us, length us, event | category | flops | bytes accessed | tf_op | source)
XLA Modules:
  0.0 298.9 jit_solution(17479440184776834803)
XLA Ops:
  6.5 0.0 copy-start
  6.5 1.6 copy-done
  8.1 1.9 fusion.32
  10.0 0.0 copy-start.4
  10.0 0.0 copy-start.5
  10.0 0.0 copy-start.6
  10.0 4.0 %fusion.33 = f32[512,128]{0,1:T(8,128)S(1)} fusion(bf16[512,4096]{1,0:T(8,128)(2,1)} %param.12, bf16[4096,128]{1,0:T(8,128)(2,1)} %param.14), kind=kOutput, calls=%fused_computation.93 | convolution fusion | flops 536870912 | bytes 5505024 | tf_op jit(solution)/shard_map/dot_general | solution.py:48
  14.1 0.5 collective-permute-start
  14.6 0.0 copy-done.5
  14.6 0.1 fusion.19
  14.7 0.1 copy.44
  14.9 0.0 copy-done.6
  14.9 0.1 copy.43
  15.0 0.1 pad.29.clone
  15.1 0.6 compare_reduce_fusion
  15.7 0.6 broadcast_select_fusion.1
  16.4 0.0 collective-permute-done
  16.4 0.1 fusion.25
  16.5 0.1 multiply_reduce_fusion.3
  16.6 0.1 multiply_convert_fusion.1
  16.6 0.1 fusion.17
  16.7 0.9 copy.45
  17.6 0.0 all-gather.3.cloned.1.call-update
  17.7 0.1 pad.17.clone
  17.7 52.4 %all-gather.3.cloned.1.call-done = bf16[4224,256]{1,0:T(8,128)(2,1)} async-done(((bf16[528,256]{1,0:T(8,128)(2,1)}), bf16[4224,256]{1,0:T(8,128)(2,1)}) %all-gather.3.cloned.1.call-update) | async-done | bytes 2162704 | tf_op jit(solution)/shard_map/all_gather | solution.py:60
  70.1 24.5 %copy.49 = bf16[8,528,256]{0,2,1:T(8,128)(2,1)} copy(bf16[8,528,256]{2,1,0:T(8,128)(2,1)} %bitcast.89) | data formatting | bytes 4325376 | tf_op jit(solution)/shard_map/optimization_barrier | solution.py:62
  94.6 0.8 slice_convert_fusion
  95.5 0.1 reshape.423
  95.6 0.1 slice_add_fusion
  95.7 1.7 fusion.28
  97.4 1.3 slice_bitcast_fusion
  98.7 4.5 %collective-permute-start.1 = (bf16[512,4096]{1,0:T(8,128)(2,1)}, bf16[512,4096]{1,0:T(8,128)(2,1)}, u32[]{:S(2)}, u32[]{:S(2)}) collective-permute-start(bf16[512,4096]{1,0:T(8,128)(2,1)} %param.12), channel_id=1, source_target_pairs={{0,2},{2,4},{4,6},{6,8},{8,10},{10,12},{12,14},{1,3},{3,5},{5,7},{... | collective-permute-start | bytes 12582920 | tf_op jit(solution)/shard_map/ppermute | solution.py:18
  103.3 1.5 collective-permute-start.2
  104.8 0.6 fusion.23
  105.4 0.1 add_convert_fusion.1
  105.5 0.1 copy.50
  105.6 0.1 pad_bitcast_fusion.2
  105.7 0.1 pad_bitcast_fusion.3
  105.8 11.8 %exponential_multiply_fusion = f32[8,3,512,512]{3,2,1,0:T(8,128)} fusion(f32[8,3]{1,0:T(8,128)S(1)} %copy.50, f32[8,3,512]{2,1,0:T(4,128)S(1)} %copy.48, f32[8,512]{1,0:T(8,128)S(1)} %bitcast.100, bf16[8,1,512,128]{3,2,1,0:T(8,128)(2,1)S(1)} %pad_bitcast_fusion.2, bf16[8,1,512,128]{3,2,1,0:T(8,128)(2,1)S(1)} %slice_bitcast_fusion, ...), kind=kOutput, calls=%fused_computation.13 | convolution fusion | flops 1651507200 | bytes 29425760 | tf_op jit(solution)/shard_map/bkjp,bip->bkji/dot_general | solution.py:75
  117.7 70.8 %while.14 = (s32[]{:T(128)}, f32[8,512]{1,0:T(8,128)S(1)}, f32[8,3,512]{2,0,1:T(8,128)}, f32[8,3,512,512]{3,2,1,0:T(8,128)}, s32[]{:T(128)}, /*index=5*/s32[]{:T(128)}) while((s32[]{:T(128)}, f32[8,512]{1,0:T(8,128)S(1)}, f32[8,3,512]{2,0,1:T(8,128)}, f32[8,3,512,512]{3,2,1,0:T(8,128)}, s32[]{:T(128)}, /*index=5*/s32[]{:T(128)}) %tuple.46), condition=%wide.region_6.7_spmd.clone, body=%wide.region_3.6_spmd.clone.sunk | while | flops 25194500 | bytes 151912576 | solution.py:94
  117.7 9.6 %multiply_reduce_fusion.6 = f32[8,3,512]{2,1,0:T(4,128)S(1)} fusion(f32[8,3,512,512]{3,2,1,0:T(8,128)} %get-tuple-element.140, f32[8,512]{1,0:T(8,128)S(1)} %broadcast_select_fusion.3), kind=kLoop, calls=%fused_computation.1.clone.1 | loop fusion | flops 12570624 | bytes 25231360 | tf_op jit(solution)/shard_map/while/body/eval_jaxpr/reduce_sum | solution.py:83
  127.5 5.6 %copy-done.2 = f32[8,3,512,512]{3,2,1,0:T(8,128)S(1)} copy-done((f32[8,3,512,512]{3,2,1,0:T(8,128)S(1)}, f32[8,3,512,512]{3,2,1,0:T(8,128)}, u32[]{:S(2)}) %copy-start.2) | copy-done | bytes 25165848 | tf_op jit(solution)/shard_map/while
  133.1 2.2 multiply_reduce_fusion.7
  135.4 9.6 %multiply_reduce_fusion.6 = f32[8,3,512]{2,1,0:T(4,128)S(1)} fusion(f32[8,3,512,512]{3,2,1,0:T(8,128)} %get-tuple-element.140, f32[8,512]{1,0:T(8,128)S(1)} %broadcast_select_fusion.3), kind=kLoop, calls=%fused_computation.1.clone.1 | loop fusion | flops 12570624 | bytes 25231360 | tf_op jit(solution)/shard_map/while/body/eval_jaxpr/reduce_sum | solution.py:83
  145.2 5.6 %copy-done.2 = f32[8,3,512,512]{3,2,1,0:T(8,128)S(1)} copy-done((f32[8,3,512,512]{3,2,1,0:T(8,128)S(1)}, f32[8,3,512,512]{3,2,1,0:T(8,128)}, u32[]{:S(2)}) %copy-start.2) | copy-done | bytes 25165848 | tf_op jit(solution)/shard_map/while
  150.8 2.2 multiply_reduce_fusion.7
  153.1 0.0 copy-start.2
  153.1 9.6 %multiply_reduce_fusion.6 = f32[8,3,512]{2,1,0:T(4,128)S(1)} fusion(f32[8,3,512,512]{3,2,1,0:T(8,128)} %get-tuple-element.140, f32[8,512]{1,0:T(8,128)S(1)} %broadcast_select_fusion.3), kind=kLoop, calls=%fused_computation.1.clone.1 | loop fusion | flops 12570624 | bytes 25231360 | tf_op jit(solution)/shard_map/while/body/eval_jaxpr/reduce_sum | solution.py:83
  162.9 5.6 %copy-done.2 = f32[8,3,512,512]{3,2,1,0:T(8,128)S(1)} copy-done((f32[8,3,512,512]{3,2,1,0:T(8,128)S(1)}, f32[8,3,512,512]{3,2,1,0:T(8,128)}, u32[]{:S(2)}) %copy-start.2) | copy-done | bytes 25165848 | tf_op jit(solution)/shard_map/while
  168.5 2.2 multiply_reduce_fusion.7
  170.8 0.0 copy-start.2
  170.8 9.6 %multiply_reduce_fusion.6 = f32[8,3,512]{2,1,0:T(4,128)S(1)} fusion(f32[8,3,512,512]{3,2,1,0:T(8,128)} %get-tuple-element.140, f32[8,512]{1,0:T(8,128)S(1)} %broadcast_select_fusion.3), kind=kLoop, calls=%fused_computation.1.clone.1 | loop fusion | flops 12570624 | bytes 25231360 | tf_op jit(solution)/shard_map/while/body/eval_jaxpr/reduce_sum | solution.py:83
  180.5 0.0 copy-start.3
  180.6 5.6 %copy-done.2 = f32[8,3,512,512]{3,2,1,0:T(8,128)S(1)} copy-done((f32[8,3,512,512]{3,2,1,0:T(8,128)S(1)}, f32[8,3,512,512]{3,2,1,0:T(8,128)}, u32[]{:S(2)}) %copy-start.2) | copy-done | bytes 25165848 | tf_op jit(solution)/shard_map/while
  186.2 2.2 multiply_reduce_fusion.7
  188.5 0.8 constant_dynamic-slice_fusion
  189.3 2.2 fusion.9
  191.5 4.6 %fusion.15 = f32[512,4096]{1,0:T(8,128)S(1)} fusion(bf16[512,4096]{1,0:T(8,128)(2,1)} %param.12, bf16[3,512,512]{2,1,0:T(8,128)(2,1)S(1)} %fusion.9), kind=kOutput, calls=%fused_computation.36 | convolution fusion | flops 2147483648 | bytes 13107200 | tf_op jit(solution)/shard_map/dot_general | solution.py:105
  196.2 83.9 %collective-permute-done.1 = bf16[512,4096]{1,0:T(8,128)(2,1)} collective-permute-done((bf16[512,4096]{1,0:T(8,128)(2,1)}, bf16[512,4096]{1,0:T(8,128)(2,1)}, u32[]{:S(2)}, u32[]{:S(2)}) %collective-permute-start.1) | collective-permute-done | bytes 4194336 | tf_op jit(solution)/shard_map/ppermute | solution.py:18
  280.1 4.6 %fusion.14 = f32[512,4096]{1,0:T(8,128)S(1)} fusion(bf16[512,4096]{1,0:T(8,128)(2,1)} %collective-permute-done.1, bf16[3,512,512]{2,1,0:T(8,128)(2,1)S(1)} %fusion.9), kind=kOutput, calls=%fused_computation.34 | convolution fusion | flops 2147483648 | bytes 13107200 | tf_op jit(solution)/shard_map/dot_general | solution.py:106
  284.7 0.0 collective-permute-done.2
  284.7 0.0 copy-start.1
  284.7 7.4 %add_convert_fusion = bf16[512,4096]{1,0:T(8,128)(2,1)} fusion(f32[512,4096]{1,0:T(8,128)S(1)} %fusion.15, f32[512,4096]{1,0:T(8,128)S(1)} %fusion.14, bf16[512,4096]{1,0:T(8,128)(2,1)} %collective-permute-done.2, bf16[3,512,512]{2,1,0:T(8,128)(2,1)S(1)} %fusion.9), kind=kOutput, calls=%fused_computation.14 | convolution fusion | flops 2153775104 | bytes 25690112 | tf_op jit(solution)/shard_map/dot_general | solution.py:107
  292.1 0.0 copy-done.1
  (78 shorter events, 0.8 us)
Async XLA Ops:
  6.5 1.6 copy-start
  6.5 63.6 %all-gather.3.cloned.1.call-start = ((), (), s32[]{:S(2)}) async-start(), calls=%async_computation | async-start | bytes 2433024 | tf_op jit(solution)/shard_map/all_gather | solution.py:60
  10.0 4.6 %copy-start.4 = (s32[512]{0:T(512)S(1)}, s32[512]{0:T(512)}, u32[]{:S(2)}) copy-start(s32[512]{0:T(512)} %param.16) | copy-start | bytes 6148
  10.0 4.6 %copy-start.5 = (s32[512]{0:T(512)S(1)}, s32[512]{0:T(512)}, u32[]{:S(2)}) copy-start(s32[512]{0:T(512)} %param.15) | copy-start | bytes 6148
  10.0 4.9 %copy-start.6 = (s32[1,2]{1,0:T(1,128)S(1)}, s32[1,2]{1,0:T(1,128)}, u32[]{:S(2)}) copy-start(s32[1,2]{1,0:T(1,128)} %param.17) | copy-start | bytes 28
  14.1 2.3 collective-permute-start
  98.7 181.3 %collective-permute-start.1 = (bf16[512,4096]{1,0:T(8,128)(2,1)}, bf16[512,4096]{1,0:T(8,128)(2,1)}, u32[]{:S(2)}, u32[]{:S(2)}) collective-permute-start(bf16[512,4096]{1,0:T(8,128)(2,1)} %param.12), channel_id=1, source_target_pairs={{0,2},{2,4},{4,6},{6,8},{8,10},{10,12},{12,14},{1,3},{3,5},{5,7},{... | collective-permute-start | bytes 12582920 | tf_op jit(solution)/shard_map/ppermute | solution.py:18
  103.3 181.4 %collective-permute-start.2 = (bf16[512,4096]{1,0:T(8,128)(2,1)}, bf16[512,4096]{1,0:T(8,128)(2,1)}, u32[]{:S(2)}, u32[]{:S(2)}) collective-permute-start(bf16[512,4096]{1,0:T(8,128)(2,1)} %param.12), channel_id=1, source_target_pairs={{2,0},{4,2},{6,4},{8,6},{10,8},{12,10},{14,12},{3,1},{5,3},{7,5},{... | collective-permute-start | bytes 12582920 | tf_op jit(solution)/shard_map/ppermute | solution.py:18
  117.7 15.4 %copy-start.2 = (f32[8,3,512,512]{3,2,1,0:T(8,128)S(1)}, f32[8,3,512,512]{3,2,1,0:T(8,128)}, u32[]{:S(2)}) copy-start(f32[8,3,512,512]{3,2,1,0:T(8,128)} %get-tuple-element.140) | copy-start | bytes 75497472 | tf_op jit(solution)/shard_map/while
  127.4 7.9 %copy-start.3 = (f32[8,3,512]{2,0,1:T(8,128)}, f32[8,3,512]{2,0,1:T(8,128)S(1)}, u32[]{:S(2)}) copy-start(f32[8,3,512]{2,0,1:T(8,128)S(1)} %pad_maximum_fusion.5) | copy-start | bytes 147460 | tf_op jit(solution)/shard_map/while
  135.4 15.4 %copy-start.2 = (f32[8,3,512,512]{3,2,1,0:T(8,128)S(1)}, f32[8,3,512,512]{3,2,1,0:T(8,128)}, u32[]{:S(2)}) copy-start(f32[8,3,512,512]{3,2,1,0:T(8,128)} %get-tuple-element.140) | copy-start | bytes 75497472 | tf_op jit(solution)/shard_map/while
  145.1 7.9 %copy-start.3 = (f32[8,3,512]{2,0,1:T(8,128)}, f32[8,3,512]{2,0,1:T(8,128)S(1)}, u32[]{:S(2)}) copy-start(f32[8,3,512]{2,0,1:T(8,128)S(1)} %pad_maximum_fusion.5) | copy-start | bytes 147460 | tf_op jit(solution)/shard_map/while
  153.1 15.4 %copy-start.2 = (f32[8,3,512,512]{3,2,1,0:T(8,128)S(1)}, f32[8,3,512,512]{3,2,1,0:T(8,128)}, u32[]{:S(2)}) copy-start(f32[8,3,512,512]{3,2,1,0:T(8,128)} %get-tuple-element.140) | copy-start | bytes 75497472 | tf_op jit(solution)/shard_map/while
  162.8 7.9 %copy-start.3 = (f32[8,3,512]{2,0,1:T(8,128)}, f32[8,3,512]{2,0,1:T(8,128)S(1)}, u32[]{:S(2)}) copy-start(f32[8,3,512]{2,0,1:T(8,128)S(1)} %pad_maximum_fusion.5) | copy-start | bytes 147460 | tf_op jit(solution)/shard_map/while
  170.8 15.4 %copy-start.2 = (f32[8,3,512,512]{3,2,1,0:T(8,128)S(1)}, f32[8,3,512,512]{3,2,1,0:T(8,128)}, u32[]{:S(2)}) copy-start(f32[8,3,512,512]{3,2,1,0:T(8,128)} %get-tuple-element.140) | copy-start | bytes 75497472 | tf_op jit(solution)/shard_map/while
  180.5 7.9 %copy-start.3 = (f32[8,3,512]{2,0,1:T(8,128)}, f32[8,3,512]{2,0,1:T(8,128)S(1)}, u32[]{:S(2)}) copy-start(f32[8,3,512]{2,0,1:T(8,128)S(1)} %pad_maximum_fusion.5) | copy-start | bytes 147460 | tf_op jit(solution)/shard_map/while
  284.7 7.4 %copy-start.1 = (bf16[512,2048]{1,0:T(8,128)(2,1)S(1)}, bf16[512,2048]{1,0:T(8,128)(2,1)}, u32[]{:S(2)}) copy-start(bf16[512,2048]{1,0:T(8,128)(2,1)} %param.11) | copy-start | bytes 6291460
Sparse Core Ops, SparseCore 0:
  17.7 52.3 all-gather.2

commit v3 on v2

--- a/solution.py
+++ b/solution.py
@@ -59,9 +59,8 @@
     packed = jnp.concatenate([units, extra, jnp.zeros((pad, units.shape[1]), jnp.bfloat16)], 0)
     gathered = lax.all_gather(packed, "seq")
 
-    teacher_rows, gathered = lax.optimization_barrier((teacher_hidden, gathered))
-    left_rows = shifted(teacher_rows, "seq", 1)
-    right_rows = shifted(teacher_rows, "seq", -1)
+    left_rows = shifted(teacher_hidden, "seq", 1)
+    right_rows = shifted(teacher_hidden, "seq", -1)
 
     s_unit = gathered[:, :rows, :proj_width]
     t_unit = gathered[:, :rows, proj_width:]
@@ -69,9 +68,9 @@
     chars = got[:, :, 0] * 4096.0 + got[:, :, 1] * 64.0 + got[:, :, 2]
     s_pos = chars[:, 0]
     t_pos = beside(chars[:, 1])
-    flags = gathered[:, rows + digit_rows.shape[0], :2].astype(jnp.int32)
-    ones_col = jnp.ones((blocks,), jnp.int32)
-    slot_mask = jnp.stack([flags[:, 0], ones_col, flags[:, 1]], 1).astype(jnp.float32)
+    flags = gathered[:, rows + digit_rows.shape[0]].astype(jnp.float32)
+    ones_col = jnp.ones((blocks,), jnp.float32)
+    slot_mask = jnp.stack([flags[:, 0], ones_col, flags[:, 1]], 1)
     scores = jnp.einsum(
         "bkjp,bip->bkji", beside(t_unit), s_unit, preferred_element_type=jnp.float32
     ) / math.sqrt(proj_width)

time: 301 us -> 282 us (0.937)
  local copies, waits for them, and re-layouts: 54.5 us -> 28.9 us
  waiting for transfers between devices: 136 us -> 146 us
  matrix products: 34.3 us -> 31.1 us
    all_gather x1, waiting for transfers between devices: 52.4 us -> 146 us  [body_local(): gathered = lax.all_gather(packed, 'seq')]
    ppermute x2, waiting for transfers between devices: 83.9 us -> 0.01 us  [shifted(): return lax.ppermute(block, axis, route)]
    optimization_barrier x1 -> x0, local copies, waits for them, and re-layouts: 24.5 us -> none  [body_local(): lax.optimization_barrier((teacher_hidden, gathered))]
  transfers between devices with their start and end apart: 4 -> 4, of which waited for: 2 -> 1; matrix products, arithmetic and copies ran while one was open for 25% -> 27% of each run, Pallas kernels for 0% -> 0%
where the time goes in v3:
time: 282 us
  waiting for transfers between devices  146 us (52%)
  other arithmetic  53.6 us (19%)
  matrix products  31.1 us (11%)
  local copies, waits for them, and re-layouts  28.9 us (10%)
  between operations  13.8 us (5%)
  starting transfers between devices  8.52 us (3%)
    all_gather x1, waiting for transfers between devices, body_local(): gathered = lax.all_gather(packed, 'seq')  146 us
    reduce_sum x4, other arithmetic, iterate(): partial_cols = jnp.sum(row_scale[:, None, None, :] * kernel, axis=3)  38.4 us
    while x16, local copies, waits for them, and re-layouts  22.4 us
    dot_general x1, matrix products, body_local(): jnp.einsum('bkjp,bip->bkji', beside(t_unit), s_unit, preferred_element_ty...  10.8 us
    reduce_sum x4, other arithmetic, iterate(): row_scale = 1.0 / jnp.sum(kernel * col_scale[:, :, :, None], axis=(1, 2))  8.94 us
    ppermute x2, starting transfers between devices, shifted(): return lax.ppermute(block, axis, route)  8 us
    dot_general x1, matrix products, body_local(): lax.dot_general(plan[2], right_rows, along_j, preferred_element_type=jnp....  7.35 us
  transfers between devices with their start and end apart: 4, of which 1 were waited for; matrix products, arithmetic and copies ran while one was open for 27% of the time, Pallas kernels for 0%

profile of v3, /device:TPU:0, one launch (start us, length us, event | category | flops | bytes accessed | tf_op | source)
XLA Modules:
  0.0 282.0 jit_solution(3589763353587103050)
XLA Ops:
  6.5 0.0 copy-start
  6.5 0.0 all-gather.3.cloned.1.call-start
  6.5 1.6 copy-done
  8.1 1.9 fusion.29
  10.0 0.0 copy-start.6
  10.0 0.0 copy-start.7
  10.0 0.0 copy-start.8
  10.0 4.0 %fusion.30 = f32[512,128]{0,1:T(8,128)S(1)} fusion(bf16[512,4096]{1,0:T(8,128)(2,1)} %param.12, bf16[4096,128]{1,0:T(8,128)(2,1)} %param.14), kind=kOutput, calls=%fused_computation.92 | convolution fusion | flops 536870912 | bytes 5505024 | tf_op jit(solution)/shard_map/dot_general | solution.py:48
  14.1 0.5 collective-permute-start
  14.6 0.0 copy-done.6
  14.6 0.0 copy-done.7
  14.6 0.1 fusion.17
  14.7 0.1 copy.30
  14.9 0.1 copy.29
  15.0 0.1 pad.29.clone
  15.1 0.6 compare_reduce_fusion
  15.7 0.6 broadcast_select_fusion.1
  16.4 0.0 collective-permute-done
  16.4 0.1 fusion.22
  16.5 0.1 multiply_reduce_fusion.3
  16.6 0.1 multiply_convert_fusion.1
  16.6 0.1 fusion.15
  16.7 0.9 copy.31
  17.6 0.0 all-gather.3.cloned.1.call-update
  17.6 6.5 %collective-permute-start.1 = (bf16[512,4096]{1,0:T(8,128)(2,1)}, bf16[512,4096]{1,0:T(8,128)(2,1)}, u32[]{:S(2)}, u32[]{:S(2)}) collective-permute-start(bf16[512,4096]{1,0:T(8,128)(2,1)} %param.12), channel_id=1, source_target_pairs={{0,2},{2,4},{4,6},{6,8},{8,10},{10,12},{12,14},{1,3},{3,5},{5,7},{... | collective-permute-start | bytes 12582920 | tf_op jit(solution)/shard_map/ppermute | solution.py:18
  24.2 1.5 collective-permute-start.2
  25.7 0.1 pad.17.clone
  25.7 145.6 %all-gather.3.cloned.1.call-done = bf16[4224,256]{1,0:T(8,128)(2,1)} async-done(((bf16[528,256]{1,0:T(8,128)(2,1)}), bf16[4224,256]{1,0:T(8,128)(2,1)}) %all-gather.3.cloned.1.call-update) | async-done | bytes 2162704 | tf_op jit(solution)/shard_map/all_gather | solution.py:60
  171.3 0.8 slice_convert_fusion
  172.2 0.1 reshape.405
  172.3 0.1 slice_add_fusion
  172.4 0.9 slice_convert_fusion.1
  173.3 1.6 fusion.25
  174.9 0.2 slice_bitcast_fusion.2
  175.3 0.1 fusion.28
  175.3 0.1 pad_bitcast_fusion.2
  175.4 0.1 pad_bitcast_fusion.3
  175.5 0.1 pad_maximum_fusion.4
  175.6 10.8 %exponential_multiply_fusion = f32[8,3,512,512]{3,2,1,0:T(8,128)} fusion(f32[8,3]{1,0:T(8,128)S(1)} %pad_maximum_fusion.4, f32[8,3,512]{2,1,0:T(4,128)S(1)} %copy.34, f32[8,512]{1,0:T(8,128)S(1)} %bitcast.99, bf16[8,1,512,128]{3,2,1,0:T(8,128)(2,1)S(1)} %pad_bitcast_fusion.2, bf16[8,1,512,128]{3,2,1,0:T(8,128)(2,1)S(1)} %slice_bitcast_fusion.2, ...), kind=kOutput, calls=%fused_computation.13 | convolution fusion | flops 1651507200 | bytes 29446144 | tf_op jit(solution)/shard_map/bkjp,bip->bkji/dot_general | solution.py:74
  186.4 70.8 %while.14 = (s32[]{:T(128)}, f32[8,512]{1,0:T(8,128)S(1)}, f32[8,3,512]{2,0,1:T(8,128)}, f32[8,3,512,512]{3,2,1,0:T(8,128)}, s32[]{:T(128)}, /*index=5*/s32[]{:T(128)}) while((s32[]{:T(128)}, f32[8,512]{1,0:T(8,128)S(1)}, f32[8,3,512]{2,0,1:T(8,128)}, f32[8,3,512,512]{3,2,1,0:T(8,128)}, s32[]{:T(128)}, /*index=5*/s32[]{:T(128)}) %tuple.44), condition=%wide.region_6.7_spmd.clone, body=%wide.region_3.6_spmd.clone.sunk | while | flops 25194500 | bytes 151912576 | solution.py:93
  186.4 9.6 %multiply_reduce_fusion.6 = f32[8,3,512]{2,1,0:T(4,128)S(1)} fusion(f32[8,3,512,512]{3,2,1,0:T(8,128)} %get-tuple-element.136, f32[8,512]{1,0:T(8,128)S(1)} %broadcast_select_fusion.3), kind=kLoop, calls=%fused_computation.1.clone.1 | loop fusion | flops 12570624 | bytes 25231360 | tf_op jit(solution)/shard_map/while/body/eval_jaxpr/reduce_sum | solution.py:82
  196.2 5.6 %copy-done.2 = f32[8,3,512,512]{3,2,1,0:T(8,128)S(1)} copy-done((f32[8,3,512,512]{3,2,1,0:T(8,128)S(1)}, f32[8,3,512,512]{3,2,1,0:T(8,128)}, u32[]{:S(2)}) %copy-start.2) | copy-done | bytes 25165848 | tf_op jit(solution)/shard_map/while
  201.8 2.2 multiply_reduce_fusion.7
  204.1 0.0 copy-done.5
  204.1 9.6 %multiply_reduce_fusion.6 = f32[8,3,512]{2,1,0:T(4,128)S(1)} fusion(f32[8,3,512,512]{3,2,1,0:T(8,128)} %get-tuple-element.136, f32[8,512]{1,0:T(8,128)S(1)} %broadcast_select_fusion.3), kind=kLoop, calls=%fused_computation.1.clone.1 | loop fusion | flops 12570624 | bytes 25231360 | tf_op jit(solution)/shard_map/while/body/eval_jaxpr/reduce_sum | solution.py:82
  213.9 5.6 %copy-done.2 = f32[8,3,512,512]{3,2,1,0:T(8,128)S(1)} copy-done((f32[8,3,512,512]{3,2,1,0:T(8,128)S(1)}, f32[8,3,512,512]{3,2,1,0:T(8,128)}, u32[]{:S(2)}) %copy-start.2) | copy-done | bytes 25165848 | tf_op jit(solution)/shard_map/while
  219.5 2.2 multiply_reduce_fusion.7
  221.8 9.6 %multiply_reduce_fusion.6 = f32[8,3,512]{2,1,0:T(4,128)S(1)} fusion(f32[8,3,512,512]{3,2,1,0:T(8,128)} %get-tuple-element.136, f32[8,512]{1,0:T(8,128)S(1)} %broadcast_select_fusion.3), kind=kLoop, calls=%fused_computation.1.clone.1 | loop fusion | flops 12570624 | bytes 25231360 | tf_op jit(solution)/shard_map/while/body/eval_jaxpr/reduce_sum | solution.py:82
  231.6 5.6 %copy-done.2 = f32[8,3,512,512]{3,2,1,0:T(8,128)S(1)} copy-done((f32[8,3,512,512]{3,2,1,0:T(8,128)S(1)}, f32[8,3,512,512]{3,2,1,0:T(8,128)}, u32[]{:S(2)}) %copy-start.2) | copy-done | bytes 25165848 | tf_op jit(solution)/shard_map/while
  237.2 2.2 multiply_reduce_fusion.7
  239.5 0.0 copy-start.2
  239.5 9.6 %multiply_reduce_fusion.6 = f32[8,3,512]{2,1,0:T(4,128)S(1)} fusion(f32[8,3,512,512]{3,2,1,0:T(8,128)} %get-tuple-element.136, f32[8,512]{1,0:T(8,128)S(1)} %broadcast_select_fusion.3), kind=kLoop, calls=%fused_computation.1.clone.1 | loop fusion | flops 12570624 | bytes 25231360 | tf_op jit(solution)/shard_map/while/body/eval_jaxpr/reduce_sum | solution.py:82
  249.3 5.6 %copy-done.2 = f32[8,3,512,512]{3,2,1,0:T(8,128)S(1)} copy-done((f32[8,3,512,512]{3,2,1,0:T(8,128)S(1)}, f32[8,3,512,512]{3,2,1,0:T(8,128)}, u32[]{:S(2)}) %copy-start.2) | copy-done | bytes 25165848 | tf_op jit(solution)/shard_map/while
  254.9 2.2 multiply_reduce_fusion.7
  257.2 0.0 copy-start.3
  257.2 1.0 constant_dynamic-slice_fusion
  258.2 2.5 fusion.9
  260.7 2.5 fusion.13
  263.2 0.0 collective-permute-done.1
  263.2 4.6 %fusion.12 = f32[512,4096]{1,0:T(8,128)S(1)} fusion(bf16[512,4096]{1,0:T(8,128)(2,1)} %collective-permute-done.1, bf16[3,512,512]{2,1,0:T(8,128)(2,1)S(1)} %fusion.9), kind=kOutput, calls=%fused_computation.33 | convolution fusion | flops 2147483648 | bytes 13107200 | tf_op jit(solution)/shard_map/dot_general | solution.py:105
  267.8 0.0 collective-permute-done.2
  267.8 0.0 copy-start.1
  267.8 7.3 %add_convert_fusion = bf16[512,4096]{1,0:T(8,128)(2,1)} fusion(f32[512,4096]{1,0:T(8,128)S(1)} %fusion.13, f32[512,4096]{1,0:T(8,128)S(1)} %fusion.12, bf16[512,4096]{1,0:T(8,128)(2,1)} %collective-permute-done.2, bf16[3,512,512]{2,1,0:T(8,128)(2,1)S(1)} %fusion.9), kind=kOutput, calls=%fused_computation.14 | convolution fusion | flops 2153775104 | bytes 25690112 | tf_op jit(solution)/shard_map/dot_general | solution.py:106
  275.2 0.0 copy-done.1
  (81 shorter events, 0.8 us)
Async XLA Ops:
  6.5 1.6 copy-start
  6.5 164.8 %all-gather.3.cloned.1.call-start = ((), (), s32[]{:S(2)}) async-start(), calls=%async_computation | async-start | bytes 2433024 | tf_op jit(solution)/shard_map/all_gather | solution.py:60
  10.0 4.6 %copy-start.6 = (s32[512]{0:T(512)S(1)}, s32[512]{0:T(512)}, u32[]{:S(2)}) copy-start(s32[512]{0:T(512)} %param.16) | copy-start | bytes 6148
  10.0 4.6 %copy-start.7 = (s32[512]{0:T(512)S(1)}, s32[512]{0:T(512)}, u32[]{:S(2)}) copy-start(s32[512]{0:T(512)} %param.15) | copy-start | bytes 6148
  10.0 4.9 %copy-start.8 = (s32[1,2]{1,0:T(1,128)S(1)}, s32[1,2]{1,0:T(1,128)}, u32[]{:S(2)}) copy-start(s32[1,2]{1,0:T(1,128)} %param.17) | copy-start | bytes 28
  14.1 2.3 collective-permute-start
  17.6 245.6 %collective-permute-start.1 = (bf16[512,4096]{1,0:T(8,128)(2,1)}, bf16[512,4096]{1,0:T(8,128)(2,1)}, u32[]{:S(2)}, u32[]{:S(2)}) collective-permute-start(bf16[512,4096]{1,0:T(8,128)(2,1)} %param.12), channel_id=1, source_target_pairs={{0,2},{2,4},{4,6},{6,8},{8,10},{10,12},{12,14},{1,3},{3,5},{5,7},{... | collective-permute-start | bytes 12582920 | tf_op jit(solution)/shard_map/ppermute | solution.py:18
  24.2 243.7 %collective-permute-start.2 = (bf16[512,4096]{1,0:T(8,128)(2,1)}, bf16[512,4096]{1,0:T(8,128)(2,1)}, u32[]{:S(2)}, u32[]{:S(2)}) collective-permute-start(bf16[512,4096]{1,0:T(8,128)(2,1)} %param.12), channel_id=1, source_target_pairs={{2,0},{4,2},{6,4},{8,6},{10,8},{12,10},{14,12},{3,1},{5,3},{7,5},{... | collective-permute-start | bytes 12582920 | tf_op jit(solution)/shard_map/ppermute | solution.py:18
  172.2 2.7 copy-start.4
  186.4 15.4 %copy-start.2 = (f32[8,3,512,512]{3,2,1,0:T(8,128)S(1)}, f32[8,3,512,512]{3,2,1,0:T(8,128)}, u32[]{:S(2)}) copy-start(f32[8,3,512,512]{3,2,1,0:T(8,128)} %get-tuple-element.136) | copy-start | bytes 75497472 | tf_op jit(solution)/shard_map/while
  196.2 7.9 %copy-start.5 = (f32[8,3,512]{2,0,1:T(8,128)}, f32[8,3,512]{2,0,1:T(8,128)S(1)}, u32[]{:S(2)}) copy-start(f32[8,3,512]{2,0,1:T(8,128)S(1)} %pad_maximum_fusion.6) | copy-start | bytes 147460 | tf_op jit(solution)/shard_map/while
  204.1 15.4 %copy-start.2 = (f32[8,3,512,512]{3,2,1,0:T(8,128)S(1)}, f32[8,3,512,512]{3,2,1,0:T(8,128)}, u32[]{:S(2)}) copy-start(f32[8,3,512,512]{3,2,1,0:T(8,128)} %get-tuple-element.136) | copy-start | bytes 75497472 | tf_op jit(solution)/shard_map/while
  213.9 7.9 %copy-start.5 = (f32[8,3,512]{2,0,1:T(8,128)}, f32[8,3,512]{2,0,1:T(8,128)S(1)}, u32[]{:S(2)}) copy-start(f32[8,3,512]{2,0,1:T(8,128)S(1)} %pad_maximum_fusion.6) | copy-start | bytes 147460 | tf_op jit(solution)/shard_map/while
  221.8 15.4 %copy-start.2 = (f32[8,3,512,512]{3,2,1,0:T(8,128)S(1)}, f32[8,3,512,512]{3,2,1,0:T(8,128)}, u32[]{:S(2)}) copy-start(f32[8,3,512,512]{3,2,1,0:T(8,128)} %get-tuple-element.136) | copy-start | bytes 75497472 | tf_op jit(solution)/shard_map/while
  231.6 7.9 %copy-start.5 = (f32[8,3,512]{2,0,1:T(8,128)}, f32[8,3,512]{2,0,1:T(8,128)S(1)}, u32[]{:S(2)}) copy-start(f32[8,3,512]{2,0,1:T(8,128)S(1)} %pad_maximum_fusion.6) | copy-start | bytes 147460 | tf_op jit(solution)/shard_map/while
  239.5 15.4 %copy-start.2 = (f32[8,3,512,512]{3,2,1,0:T(8,128)S(1)}, f32[8,3,512,512]{3,2,1,0:T(8,128)}, u32[]{:S(2)}) copy-start(f32[8,3,512,512]{3,2,1,0:T(8,128)} %get-tuple-element.136) | copy-start | bytes 75497472 | tf_op jit(solution)/shard_map/while
  249.3 7.9 %copy-start.5 = (f32[8,3,512]{2,0,1:T(8,128)}, f32[8,3,512]{2,0,1:T(8,128)S(1)}, u32[]{:S(2)}) copy-start(f32[8,3,512]{2,0,1:T(8,128)S(1)} %pad_maximum_fusion.6) | copy-start | bytes 147460 | tf_op jit(solution)/shard_map/while
  257.2 3.5 %copy-start.3 = (bf16[512,4096]{1,0:T(8,128)(2,1)S(1)}, bf16[512,4096]{1,0:T(8,128)(2,1)}, u32[]{:S(2)}) copy-start(bf16[512,4096]{1,0:T(8,128)(2,1)} %param.12) | copy-start | bytes 12582916
  267.8 7.4 %copy-start.1 = (bf16[512,2048]{1,0:T(8,128)(2,1)S(1)}, bf16[512,2048]{1,0:T(8,128)(2,1)}, u32[]{:S(2)}) copy-start(bf16[512,2048]{1,0:T(8,128)(2,1)} %param.11) | copy-start | bytes 6291460
Sparse Core Ops, SparseCore 0:
  17.7 153.5 all-gather.2

commit v4 on v3

--- a/solution.py
+++ b/solution.py
@@ -36,6 +36,19 @@
     return lax.psum(value, "tgrp")
 
 
+def gather_halves(packed):
+    if lax.axis_size("tgrp") != 2:
+        return lax.all_gather(packed, "seq")
+    half = packed.shape[1] // 2
+    core = lax.axis_index("tgrp")
+    mine = lax.dynamic_slice_in_dim(packed, core * half, half, 1)
+    got = lax.all_gather(mine, "seq")
+    theirs = lax.ppermute(got, "tgrp", [(0, 1), (1, 0)])
+    first = jnp.where(core == 0, got, theirs)
+    second = jnp.where(core == 0, theirs, got)
+    return jnp.concatenate([first, second], 2)
+
+
 def body_local(
     student_hidden, teacher_hidden, student_proj, teacher_proj, student_chars, teacher_chars, band
 ):
@@ -57,10 +70,11 @@
     extra = jnp.concatenate([digit_rows, flag_row], 0)
     pad = -(rows + extra.shape[0]) % 16
     packed = jnp.concatenate([units, extra, jnp.zeros((pad, units.shape[1]), jnp.bfloat16)], 0)
-    gathered = lax.all_gather(packed, "seq")
+    gathered = gather_halves(packed)
 
-    left_rows = shifted(teacher_hidden, "seq", 1)
-    right_rows = shifted(teacher_hidden, "seq", -1)
+    teacher_rows, gathered = lax.optimization_barrier((teacher_hidden, gathered))
+    left_rows = shifted(teacher_rows, "seq", 1)
+    right_rows = shifted(teacher_rows, "seq", -1)
 
     s_unit = gathered[:, :rows, :proj_width]
     t_unit = gathered[:, :rows, proj_width:]

time: 282 us -> 269 us (0.954)
  waiting for transfers between devices: 146 us -> 134 us
    all_gather x1, waiting for transfers between devices: 146 us -> 42.9 us  [gather_halves(): got = lax.all_gather(mine, 'seq')]
    ppermute x2, waiting for transfers between devices: 0.01 us -> 87.9 us  [shifted(): return lax.ppermute(block, axis, route)]
    ppermute x0 -> x1, waiting for transfers between devices: none -> 2.84 us  [gather_halves(): theirs = lax.ppermute(got, 'tgrp', [(0, 1), (1, 0)])]
  transfers between devices with their start and end apart: 4 -> 5, of which waited for: 1 -> 3; matrix products, arithmetic and copies ran while one was open for 27% -> 27% of each run, Pallas kernels for 0% -> 0%
where the time goes in v4:
time: 269 us
  waiting for transfers between devices  134 us (50%)
  other arithmetic  54.2 us (20%)
  matrix products  32.1 us (12%)
  local copies, waits for them, and re-layouts  28.4 us (11%)
  between operations  13.8 us (5%)
  starting transfers between devices  6.42 us (2%)
    ppermute x2, waiting for transfers between devices, shifted(): return lax.ppermute(block, axis, route)  87.9 us
    all_gather x1, waiting for transfers between devices, gather_halves(): got = lax.all_gather(mine, 'seq')  42.9 us
    reduce_sum x4, other arithmetic, iterate(): partial_cols = jnp.sum(row_scale[:, None, None, :] * kernel, axis=3)  38.4 us
    while x16, local copies, waits for them, and re-layouts  22.4 us
    dot_general x1, matrix products, body_local(): jnp.einsum('bkjp,bip->bkji', beside(t_unit), s_unit, preferred_element_ty...  11.8 us
    reduce_sum x4, other arithmetic, iterate(): row_scale = 1.0 / jnp.sum(kernel * col_scale[:, :, :, None], axis=(1, 2))  8.94 us
    dot_general x1, matrix products, body_local(): lax.dot_general(plan[2], right_rows, along_j, preferred_element_type=jnp....  7.35 us
    ppermute x2, starting transfers between devices, shifted(): return lax.ppermute(block, axis, route)  5.89 us
  transfers between devices with their start and end apart: 5, of which 3 were waited for; matrix products, arithmetic and copies ran while one was open for 27% of the time, Pallas kernels for 0%

profile of v4, /device:TPU:0, one launch (start us, length us, event | category | flops | bytes accessed | tf_op | source)
XLA Modules:
  0.0 269.0 jit_solution(7988195209815630302)
XLA Ops:
  6.5 0.0 copy-start
  6.5 1.6 copy-done
  8.1 1.9 fusion.28
  10.0 0.0 copy-start.6
  10.0 0.0 copy-start.7
  10.0 0.0 copy-start.8
  10.0 4.0 %fusion.29 = f32[512,128]{0,1:T(8,128)S(1)} fusion(bf16[512,4096]{1,0:T(8,128)(2,1)} %param.12, bf16[4096,128]{1,0:T(8,128)(2,1)} %param.14), kind=kOutput, calls=%fused_computation.98 | convolution fusion | flops 536870912 | bytes 5505024 | tf_op jit(solution)/shard_map/dot_general | solution.py:61
  14.1 0.5 collective-permute-start
  14.6 0.1 fusion.17
  14.7 0.1 copy.31
  14.9 0.1 copy.30
  15.0 0.1 pad.31.clone
  15.1 0.6 compare_reduce_fusion
  15.7 0.6 broadcast_select_fusion.3
  16.4 0.0 collective-permute-done
  16.4 0.1 fusion.21
  16.5 0.1 multiply_reduce_fusion.2
  16.6 0.1 multiply_convert_fusion
  16.6 0.1 fusion.13
  16.8 0.8 copy.32
  17.5 0.0 all-gather.3.cloned.1.call-update
  17.6 42.9 %all-gather.3.cloned.1.call-done = bf16[4224,128]{1,0:T(8,128)(2,1)} async-done(((bf16[528,128]{1,0:T(8,128)(2,1)}), bf16[4224,128]{1,0:T(8,128)(2,1)}) %all-gather.3.cloned.1.call-update) | async-done | bytes 1081360 | tf_op jit(solution)/shard_map/all_gather | solution.py:45
  60.4 0.0 collective-permute-start.1
  60.4 0.1 pad.17.clone
  60.5 2.8 %collective-permute-done.1 = bf16[8,528,128]{2,1,0:T(8,128)(2,1)S(1)} collective-permute-done((bf16[8,528,128]{2,1,0:T(8,128)(2,1)}, bf16[8,528,128]{2,1,0:T(8,128)(2,1)S(1)}, u32[]{:S(2)}, u32[]{:S(2)}) %collective-permute-start.1) | collective-permute-done | bytes 1081376 | tf_op jit(solution)/shard_map/ppermute | solution.py:46
  63.3 1.4 broadcast_select_fusion.2
  64.7 0.2 pad_maximum_fusion.2
  65.0 0.0 copy-start.4
  65.0 0.4 fusion.24
  65.3 0.2 slice_bitcast_fusion
  65.5 0.8 copy-done.4
  66.3 0.1 reshape.405
  66.4 0.1 slice_add_fusion
  66.6 0.8 slice_convert_fusion.1
  67.3 4.4 %collective-permute-start.2 = (bf16[512,4096]{1,0:T(8,128)(2,1)}, bf16[512,4096]{1,0:T(8,128)(2,1)}, u32[]{:S(2)}, u32[]{:S(2)}) collective-permute-start(bf16[512,4096]{1,0:T(8,128)(2,1)} %param.12), channel_id=1, source_target_pairs={{0,2},{2,4},{4,6},{6,8},{8,10},{10,12},{12,14},{1,3},{3,5},{5,7},{... | collective-permute-start | bytes 12582920 | tf_op jit(solution)/shard_map/ppermute | solution.py:18
  71.8 1.5 collective-permute-start.3
  73.2 0.1 pad_bitcast_fusion.2
  73.3 0.1 pad_bitcast_fusion.3
  73.5 0.1 fusion.27
  73.6 0.1 pad_maximum_fusion.6
  73.7 11.8 %exponential_multiply_fusion = f32[8,3,512,512]{3,2,1,0:T(8,128)} fusion(f32[8,3]{1,0:T(8,128)S(1)} %pad_maximum_fusion.6, f32[8,3,512]{2,1,0:T(4,128)S(1)} %copy.36, f32[8,512]{1,0:T(8,128)S(1)} %bitcast.96, bf16[8,528,256]{2,1,0:T(8,128)(2,1)} %copy-done.4, bf16[8,1,512,128]{3,2,0,1:T(8,128)(2,1)S(1)} %pad_bitcast_fusion.2, ...), kind=kOutput, calls=%fused_computation.13 | convolution fusion | flops 1651507200 | bytes 29425760 | tf_op jit(solution)/shard_map/bkjp,bip->bkji/dot_general | solution.py:88
  85.5 70.8 %while.14 = (s32[]{:T(128)}, f32[8,512]{1,0:T(8,128)S(1)}, f32[8,3,512]{2,0,1:T(8,128)}, f32[8,3,512,512]{3,2,1,0:T(8,128)}, s32[]{:T(128)}, /*index=5*/s32[]{:T(128)}) while((s32[]{:T(128)}, f32[8,512]{1,0:T(8,128)S(1)}, f32[8,3,512]{2,0,1:T(8,128)}, f32[8,3,512,512]{3,2,1,0:T(8,128)}, s32[]{:T(128)}, /*index=5*/s32[]{:T(128)}) %tuple.47), condition=%wide.region_6.7_spmd.clone, body=%wide.region_3.6_spmd.clone.sunk | while | flops 25194500 | bytes 151912576 | solution.py:107
  85.5 9.6 %multiply_reduce_fusion.6 = f32[8,3,512]{2,1,0:T(4,128)S(1)} fusion(f32[8,3,512,512]{3,2,1,0:T(8,128)} %get-tuple-element.142, f32[8,512]{1,0:T(8,128)S(1)} %broadcast_select_fusion.5), kind=kLoop, calls=%fused_computation.1.clone.1 | loop fusion | flops 12570624 | bytes 25231360 | tf_op jit(solution)/shard_map/while/body/eval_jaxpr/reduce_sum | solution.py:96
  95.3 5.6 %copy-done.2 = f32[8,3,512,512]{3,2,1,0:T(8,128)S(1)} copy-done((f32[8,3,512,512]{3,2,1,0:T(8,128)S(1)}, f32[8,3,512,512]{3,2,1,0:T(8,128)}, u32[]{:S(2)}) %copy-start.2) | copy-done | bytes 25165848 | tf_op jit(solution)/shard_map/while
  100.9 2.2 multiply_reduce_fusion.7
  103.1 0.0 copy-done.5
  103.2 9.6 %multiply_reduce_fusion.6 = f32[8,3,512]{2,1,0:T(4,128)S(1)} fusion(f32[8,3,512,512]{3,2,1,0:T(8,128)} %get-tuple-element.142, f32[8,512]{1,0:T(8,128)S(1)} %broadcast_select_fusion.5), kind=kLoop, calls=%fused_computation.1.clone.1 | loop fusion | flops 12570624 | bytes 25231360 | tf_op jit(solution)/shard_map/while/body/eval_jaxpr/reduce_sum | solution.py:96
  113.0 5.6 %copy-done.2 = f32[8,3,512,512]{3,2,1,0:T(8,128)S(1)} copy-done((f32[8,3,512,512]{3,2,1,0:T(8,128)S(1)}, f32[8,3,512,512]{3,2,1,0:T(8,128)}, u32[]{:S(2)}) %copy-start.2) | copy-done | bytes 25165848 | tf_op jit(solution)/shard_map/while
  118.6 2.2 multiply_reduce_fusion.7
  120.9 9.6 %multiply_reduce_fusion.6 = f32[8,3,512]{2,1,0:T(4,128)S(1)} fusion(f32[8,3,512,512]{3,2,1,0:T(8,128)} %get-tuple-element.142, f32[8,512]{1,0:T(8,128)S(1)} %broadcast_select_fusion.5), kind=kLoop, calls=%fused_computation.1.clone.1 | loop fusion | flops 12570624 | bytes 25231360 | tf_op jit(solution)/shard_map/while/body/eval_jaxpr/reduce_sum | solution.py:96
  130.7 5.6 %copy-done.2 = f32[8,3,512,512]{3,2,1,0:T(8,128)S(1)} copy-done((f32[8,3,512,512]{3,2,1,0:T(8,128)S(1)}, f32[8,3,512,512]{3,2,1,0:T(8,128)}, u32[]{:S(2)}) %copy-start.2) | copy-done | bytes 25165848 | tf_op jit(solution)/shard_map/while
  136.3 2.2 multiply_reduce_fusion.7
  138.6 9.6 %multiply_reduce_fusion.6 = f32[8,3,512]{2,1,0:T(4,128)S(1)} fusion(f32[8,3,512,512]{3,2,1,0:T(8,128)} %get-tuple-element.142, f32[8,512]{1,0:T(8,128)S(1)} %broadcast_select_fusion.5), kind=kLoop, calls=%fused_computation.1.clone.1 | loop fusion | flops 12570624 | bytes 25231360 | tf_op jit(solution)/shard_map/while/body/eval_jaxpr/reduce_sum | solution.py:96
  148.4 5.6 %copy-done.2 = f32[8,3,512,512]{3,2,1,0:T(8,128)S(1)} copy-done((f32[8,3,512,512]{3,2,1,0:T(8,128)S(1)}, f32[8,3,512,512]{3,2,1,0:T(8,128)}, u32[]{:S(2)}) %copy-start.2) | copy-done | bytes 25165848 | tf_op jit(solution)/shard_map/while
  154.0 2.2 multiply_reduce_fusion.7
  156.3 0.0 copy-start.3
  156.3 1.0 constant_dynamic-slice_fusion
  157.3 2.5 fusion.4
  159.8 2.5 fusion.9
  162.2 87.9 %collective-permute-done.2 = bf16[512,4096]{1,0:T(8,128)(2,1)} collective-permute-done((bf16[512,4096]{1,0:T(8,128)(2,1)}, bf16[512,4096]{1,0:T(8,128)(2,1)}, u32[]{:S(2)}, u32[]{:S(2)}) %collective-permute-start.2) | collective-permute-done | bytes 4194336 | tf_op jit(solution)/shard_map/ppermute | solution.py:18
  250.1 4.6 %fusion.8 = f32[512,4096]{1,0:T(8,128)S(1)} fusion(bf16[512,4096]{1,0:T(8,128)(2,1)} %collective-permute-done.2, bf16[3,512,512]{2,1,0:T(8,128)(2,1)S(1)} %fusion.4), kind=kOutput, calls=%fused_computation.30 | convolution fusion | flops 2147483648 | bytes 13107200 | tf_op jit(solution)/shard_map/dot_general | solution.py:119
  254.7 0.0 collective-permute-done.3
  254.7 0.0 copy-start.1
  254.8 7.3 %add_convert_fusion = bf16[512,4096]{1,0:T(8,128)(2,1)} fusion(f32[512,4096]{1,0:T(8,128)S(1)} %fusion.9, f32[512,4096]{1,0:T(8,128)S(1)} %fusion.8, bf16[512,4096]{1,0:T(8,128)(2,1)} %collective-permute-done.3, bf16[3,512,512]{2,1,0:T(8,128)(2,1)S(1)} %fusion.4), kind=kOutput, calls=%fused_computation.14 | convolution fusion | flops 2153775104 | bytes 25690112 | tf_op jit(solution)/shard_map/dot_general | solution.py:120
  (85 shorter events, 0.8 us)
Async XLA Ops:
  6.5 1.6 copy-start
  6.5 53.9 %all-gather.3.cloned.1.call-start = ((), (), s32[]{:S(2)}) async-start(), calls=%async_computation | async-start | bytes 1216512 | tf_op jit(solution)/shard_map/all_gather | solution.py:45
  10.0 4.6 %copy-start.6 = (s32[512]{0:T(512)S(1)}, s32[512]{0:T(512)}, u32[]{:S(2)}) copy-start(s32[512]{0:T(512)} %param.16) | copy-start | bytes 6148
  10.0 4.6 %copy-start.7 = (s32[512]{0:T(512)S(1)}, s32[512]{0:T(512)}, u32[]{:S(2)}) copy-start(s32[512]{0:T(512)} %param.15) | copy-start | bytes 6148
  10.0 4.9 %copy-start.8 = (s32[1,2]{1,0:T(1,128)S(1)}, s32[1,2]{1,0:T(1,128)}, u32[]{:S(2)}) copy-start(s32[1,2]{1,0:T(1,128)} %param.17) | copy-start | bytes 28
  14.1 2.3 collective-permute-start
  60.4 2.9 %collective-permute-start.1 = (bf16[8,528,128]{2,1,0:T(8,128)(2,1)}, bf16[8,528,128]{2,1,0:T(8,128)(2,1)S(1)}, u32[]{:S(2)}, u32[]{:S(2)}) collective-permute-start(bf16[8,528,128]{2,1,0:T(8,128)(2,1)} %bitcast.88), channel_id=1, source_target_pairs={{0,1},{1,0},{2,3},{3,2},{4,5},{5,4},{6,7},{7,6},{8,9},{9,8},{10,11... | collective-permute-start | bytes 3244040 | tf_op jit(solution)/shard_map/ppermute | solution.py:46
  65.0 1.3 copy-start.4
  67.3 182.8 %collective-permute-start.2 = (bf16[512,4096]{1,0:T(8,128)(2,1)}, bf16[512,4096]{1,0:T(8,128)(2,1)}, u32[]{:S(2)}, u32[]{:S(2)}) collective-permute-start(bf16[512,4096]{1,0:T(8,128)(2,1)} %param.12), channel_id=1, source_target_pairs={{0,2},{2,4},{4,6},{6,8},{8,10},{10,12},{12,14},{1,3},{3,5},{5,7},{... | collective-permute-start | bytes 12582920 | tf_op jit(solution)/shard_map/ppermute | solution.py:18
  71.8 183.0 %collective-permute-start.3 = (bf16[512,4096]{1,0:T(8,128)(2,1)}, bf16[512,4096]{1,0:T(8,128)(2,1)}, u32[]{:S(2)}, u32[]{:S(2)}) collective-permute-start(bf16[512,4096]{1,0:T(8,128)(2,1)} %param.12), channel_id=1, source_target_pairs={{2,0},{4,2},{6,4},{8,6},{10,8},{12,10},{14,12},{3,1},{5,3},{7,5},{... | collective-permute-start | bytes 12582920 | tf_op jit(solution)/shard_map/ppermute | solution.py:18
  85.5 15.4 %copy-start.2 = (f32[8,3,512,512]{3,2,1,0:T(8,128)S(1)}, f32[8,3,512,512]{3,2,1,0:T(8,128)}, u32[]{:S(2)}) copy-start(f32[8,3,512,512]{3,2,1,0:T(8,128)} %get-tuple-element.142) | copy-start | bytes 75497472 | tf_op jit(solution)/shard_map/while
  95.2 7.9 %copy-start.5 = (f32[8,3,512]{2,0,1:T(8,128)}, f32[8,3,512]{2,0,1:T(8,128)S(1)}, u32[]{:S(2)}) copy-start(f32[8,3,512]{2,0,1:T(8,128)S(1)} %pad_maximum_fusion.10) | copy-start | bytes 147460 | tf_op jit(solution)/shard_map/while
  103.2 15.4 %copy-start.2 = (f32[8,3,512,512]{3,2,1,0:T(8,128)S(1)}, f32[8,3,512,512]{3,2,1,0:T(8,128)}, u32[]{:S(2)}) copy-start(f32[8,3,512,512]{3,2,1,0:T(8,128)} %get-tuple-element.142) | copy-start | bytes 75497472 | tf_op jit(solution)/shard_map/while
  112.9 7.9 %copy-start.5 = (f32[8,3,512]{2,0,1:T(8,128)}, f32[8,3,512]{2,0,1:T(8,128)S(1)}, u32[]{:S(2)}) copy-start(f32[8,3,512]{2,0,1:T(8,128)S(1)} %pad_maximum_fusion.10) | copy-start | bytes 147460 | tf_op jit(solution)/shard_map/while
  120.9 15.4 %copy-start.2 = (f32[8,3,512,512]{3,2,1,0:T(8,128)S(1)}, f32[8,3,512,512]{3,2,1,0:T(8,128)}, u32[]{:S(2)}) copy-start(f32[8,3,512,512]{3,2,1,0:T(8,128)} %get-tuple-element.142) | copy-start | bytes 75497472 | tf_op jit(solution)/shard_map/while
  130.6 7.9 %copy-start.5 = (f32[8,3,512]{2,0,1:T(8,128)}, f32[8,3,512]{2,0,1:T(8,128)S(1)}, u32[]{:S(2)}) copy-start(f32[8,3,512]{2,0,1:T(8,128)S(1)} %pad_maximum_fusion.10) | copy-start | bytes 147460 | tf_op jit(solution)/shard_map/while
  138.6 15.4 %copy-start.2 = (f32[8,3,512,512]{3,2,1,0:T(8,128)S(1)}, f32[8,3,512,512]{3,2,1,0:T(8,128)}, u32[]{:S(2)}) copy-start(f32[8,3,512,512]{3,2,1,0:T(8,128)} %get-tuple-element.142) | copy-start | bytes 75497472 | tf_op jit(solution)/shard_map/while
  148.3 7.9 %copy-start.5 = (f32[8,3,512]{2,0,1:T(8,128)}, f32[8,3,512]{2,0,1:T(8,128)S(1)}, u32[]{:S(2)}) copy-start(f32[8,3,512]{2,0,1:T(8,128)S(1)} %pad_maximum_fusion.10) | copy-start | bytes 147460 | tf_op jit(solution)/shard_map/while
  156.3 3.5 %copy-start.3 = (bf16[512,4096]{1,0:T(8,128)(2,1)S(1)}, bf16[512,4096]{1,0:T(8,128)(2,1)}, u32[]{:S(2)}) copy-start(bf16[512,4096]{1,0:T(8,128)(2,1)} %param.12) | copy-start | bytes 12582916
  254.7 7.4 %copy-start.1 = (bf16[512,2048]{1,0:T(8,128)(2,1)S(1)}, bf16[512,2048]{1,0:T(8,128)(2,1)}, u32[]{:S(2)}) copy-start(bf16[512,2048]{1,0:T(8,128)(2,1)} %param.11) | copy-start | bytes 6291460
Sparse Core Ops, SparseCore 0:
  17.7 42.6 all-gather.2

commit v5 on v4

--- a/solution.py
+++ b/solution.py
@@ -73,8 +73,13 @@
     gathered = gather_halves(packed)
 
     teacher_rows, gathered = lax.optimization_barrier((teacher_hidden, gathered))
-    left_rows = shifted(teacher_rows, "seq", 1)
-    right_rows = shifted(teacher_rows, "seq", -1)
+    width = teacher_rows.shape[1]
+    pieces = 2 if width % 256 == 0 else 1
+    cut = width // pieces
+    column_pieces = [teacher_rows[:, p * cut : (p + 1) * cut] for p in range(pieces)]
+    near_pieces = [
+        (shifted(piece, "seq", 1), piece, shifted(piece, "seq", -1)) for piece in column_pieces
+    ]
 
     s_unit = gathered[:, :rows, :proj_width]
     t_unit = gathered[:, :rows, proj_width:]
@@ -115,10 +120,15 @@
     own_col = lax.dynamic_index_in_dim(col_scale, me, 0, keepdims=False)
     plan = (own_row[None, None, :] * own_kernel * own_col[:, :, None]).astype(jnp.bfloat16)
     along_j = (((0,), (0,)), ((), ()))
-    aligned = lax.dot_general(plan[1], teacher_hidden, along_j, preferred_element_type=jnp.float32)
-    aligned = aligned + lax.dot_general(plan[0], left_rows, along_j, preferred_element_type=jnp.float32)
-    aligned = aligned + lax.dot_general(plan[2], right_rows, along_j, preferred_element_type=jnp.float32)
-    return aligned.astype(jnp.bfloat16)
+    outs = []
+    for left_rows, own_rows, right_rows in near_pieces:
+        if outs:
+            left_rows, right_rows, outs = lax.optimization_barrier((left_rows, right_rows, outs))
+        aligned = lax.dot_general(plan[1], own_rows, along_j, preferred_element_type=jnp.float32)
+        aligned = aligned + lax.dot_general(plan[0], left_rows, along_j, preferred_element_type=jnp.float32)
+        aligned = aligned + lax.dot_general(plan[2], right_rows, along_j, preferred_element_type=jnp.float32)
+        outs.append(aligned.astype(jnp.bfloat16))
+    return jnp.concatenate(outs, 1)
 
 
 def body_banded(

time: 269 us -> 271 us (level)
  waiting for transfers between devices: 134 us -> 121 us
  starting transfers between devices: 6.42 us -> 13 us
  local copies, waits for them, and re-layouts: 28.4 us -> 33.2 us
    ppermute x2 -> x4, waiting for transfers between devices: 87.9 us -> 75.2 us  [shifted(): return lax.ppermute(block, axis, route)]
    ppermute x2 -> x4, starting transfers between devices: 5.89 us -> 12.5 us  [shifted(): return lax.ppermute(block, axis, route)]
    slice x0 -> x1, local copies, waits for them, and re-layouts: none -> 4.83 us  [body_local(): teacher_rows[:, p * cut:(p + 1) * cut]]
    dot_general x1 -> x2, matrix products: 7.35 us -> 5.97 us  [body_local(): lax.dot_general(plan[2], right_rows, along_j, preferred_element_type=jnp....]
    dot_general x1 -> x2, matrix products: 4.63 us -> 5.73 us  [body_local(): lax.dot_general(plan[0], left_rows, along_j, preferred_element_type=jnp.f...]
  transfers between devices with their start and end apart: 5 -> 7, of which waited for: 3 -> 4; matrix products, arithmetic and copies ran while one was open for 27% -> 27% of each run, Pallas kernels for 0% -> 0%
where the time goes in v5:
time: 271 us; the launch traced here: 270 us
  waiting for transfers between devices  121 us (45%)
  other arithmetic  56.8 us (21%)
  local copies, waits for them, and re-layouts  33.2 us (12%)
  matrix products  31.7 us (12%)
  between operations  13.8 us (5%)
  starting transfers between devices  13 us (5%)
    ppermute x4, waiting for transfers between devices, shifted(): return lax.ppermute(block, axis, route)  75.2 us
    all_gather x1, waiting for transfers between devices, gather_halves(): got = lax.all_gather(mine, 'seq')  42.9 us
    reduce_sum x4, other arithmetic, iterate(): partial_cols = jnp.sum(row_scale[:, None, None, :] * kernel, axis=3)  38.4 us
    while x16, local copies, waits for them, and re-layouts  22.4 us
    ppermute x4, starting transfers between devices, shifted(): return lax.ppermute(block, axis, route)  12.5 us
    dot_general x1, matrix products, body_local(): jnp.einsum('bkjp,bip->bkji', beside(t_unit), s_unit, preferred_element_ty...  11.8 us
    reduce_sum x4, other arithmetic, iterate(): row_scale = 1.0 / jnp.sum(kernel * col_scale[:, :, :, None], axis=(1, 2))  8.94 us
    dot_general x2, matrix products, body_local(): lax.dot_general(plan[2], right_rows, along_j, preferred_element_type=jnp....  5.97 us
  transfers between devices with their start and end apart: 7, of which 4 were waited for; matrix products, arithmetic and copies ran while one was open for 27% of the time, Pallas kernels for 0%

profile of v5, /device:TPU:0, one launch (start us, length us, event | category | flops | bytes accessed | tf_op | source)
XLA Modules:
  0.0 269.9 jit_solution(13784057799785947359)
XLA Ops:
  6.5 1.6 copy-done
  8.1 1.9 fusion.33
  10.0 0.0 copy-start.7
  10.0 0.0 copy-start.8
  10.0 0.0 copy-start.9
  10.0 3.7 %fusion.34 = f32[512,128]{0,1:T(8,128)S(1)} fusion(bf16[512,4096]{1,0:T(8,128)(2,1)} %param.12, bf16[4096,128]{1,0:T(8,128)(2,1)S(1)} %copy-done.6), kind=kOutput, calls=%fused_computation.105 | convolution fusion | flops 536870912 | bytes 5505024 | tf_op jit(solution)/shard_map/dot_general | solution.py:61
  13.8 0.5 collective-permute-start
  14.3 0.1 fusion.19
  14.5 0.1 copy.31
  14.6 0.1 copy.30
  14.7 0.1 pad.33.clone
  14.8 0.6 compare_reduce_fusion
  15.4 0.6 broadcast_select_fusion.3
  16.1 0.1 fusion.23
  16.2 0.1 multiply_reduce_fusion.2
  16.3 0.1 multiply_convert_fusion
  16.3 0.1 fusion.15
  16.5 0.8 copy.32
  17.2 0.0 all-gather.3.cloned.1.call-update
  17.3 42.9 %all-gather.3.cloned.1.call-done = bf16[4224,128]{1,0:T(8,128)(2,1)} async-done(((bf16[528,128]{1,0:T(8,128)(2,1)}), bf16[4224,128]{1,0:T(8,128)(2,1)}) %all-gather.3.cloned.1.call-update) | async-done | bytes 1081360 | tf_op jit(solution)/shard_map/all_gather | solution.py:45
  60.1 0.1 pad.19.clone
  60.2 2.8 %collective-permute-done.1 = bf16[8,528,128]{2,1,0:T(8,128)(2,1)S(1)} collective-permute-done((bf16[8,528,128]{2,1,0:T(8,128)(2,1)}, bf16[8,528,128]{2,1,0:T(8,128)(2,1)S(1)}, u32[]{:S(2)}, u32[]{:S(2)}) %collective-permute-start.1) | collective-permute-done | bytes 1081376 | tf_op jit(solution)/shard_map/ppermute | solution.py:46
  63.0 1.4 broadcast_select_fusion.2
  64.4 0.2 pad_maximum_fusion.3
  64.7 0.4 fusion.29
  65.1 0.2 slice_bitcast_fusion
  65.2 0.8 copy-done.4
  66.0 0.1 reshape.405
  66.1 0.1 slice_add_fusion
  66.3 0.8 slice_convert_fusion.1
  67.0 4.8 %fusion.28 = (bf16[512,2048]{1,0:T(8,128)(2,1)}, bf16[512,2048]{1,0:T(8,128)(2,1)}) fusion(bf16[512,4096]{1,0:T(8,128)(2,1)} %param.12), kind=kLoop, calls=%fused_computation.99 | loop fusion | bytes 8388608 | tf_op jit(solution)/shard_map/slice | solution.py:79
  71.9 3.9 %collective-permute-start.4 = (bf16[512,2048]{1,0:T(8,128)(2,1)}, bf16[512,2048]{1,0:T(8,128)(2,1)}, u32[]{:S(2)}, u32[]{:S(2)}) collective-permute-start(bf16[512,2048]{1,0:T(8,128)(2,1)} %get-tuple-element.83), channel_id=1, source_target_pairs={{0,2},{2,4},{4,6},{6,8},{8,10},{10,12},{12,14},{1,3},{3,5},{5,7},{... | collective-permute-start | bytes 6291464 | tf_op jit(solution)/shard_map/ppermute | solution.py:18
  75.7 1.3 collective-permute-start.5
  77.0 5.9 %collective-permute-start.2 = (bf16[512,2048]{1,0:T(8,128)(2,1)}, bf16[512,2048]{1,0:T(8,128)(2,1)}, u32[]{:S(2)}, u32[]{:S(2)}) collective-permute-start(bf16[512,2048]{1,0:T(8,128)(2,1)} %get-tuple-element.84), channel_id=1, source_target_pairs={{0,2},{2,4},{4,6},{6,8},{8,10},{10,12},{12,14},{1,3},{3,5},{5,7},{... | collective-permute-start | bytes 6291464 | tf_op jit(solution)/shard_map/ppermute | solution.py:18
  82.9 1.5 collective-permute-start.3
  84.4 0.1 pad_bitcast_fusion.2
  84.5 0.1 pad_bitcast_fusion.3
  84.7 0.1 fusion.32
  84.8 0.1 pad_maximum_fusion.7
  84.8 11.8 %exponential_multiply_fusion = f32[8,3,512,512]{3,2,1,0:T(8,128)} fusion(f32[8,3]{1,0:T(8,128)S(1)} %pad_maximum_fusion.7, f32[8,3,512]{2,1,0:T(4,128)S(1)} %copy.36, f32[8,512]{1,0:T(8,128)S(1)} %bitcast.100, bf16[8,528,256]{2,1,0:T(8,128)(2,1)} %copy-done.4, bf16[8,1,512,128]{3,2,0,1:T(8,128)(2,1)S(1)} %pad_bitcast_fusion.2, ...), kind=kOutput, calls=%fused_computation.13 | convolution fusion | flops 1651507200 | bytes 29425760 | tf_op jit(solution)/shard_map/bkjp,bip->bkji/dot_general | solution.py:93
  96.7 70.8 %while.14 = (s32[]{:T(128)}, f32[8,512]{1,0:T(8,128)S(1)}, f32[8,3,512]{2,0,1:T(8,128)}, f32[8,3,512,512]{3,2,1,0:T(8,128)}, s32[]{:T(128)}, /*index=5*/s32[]{:T(128)}) while((s32[]{:T(128)}, f32[8,512]{1,0:T(8,128)S(1)}, f32[8,3,512]{2,0,1:T(8,128)}, f32[8,3,512,512]{3,2,1,0:T(8,128)}, s32[]{:T(128)}, /*index=5*/s32[]{:T(128)}) %tuple.50), condition=%wide.region_6.7_spmd.clone, body=%wide.region_3.6_spmd.clone.sunk | while | flops 25194500 | bytes 151912576 | solution.py:112
  96.7 9.6 %multiply_reduce_fusion.6 = f32[8,3,512]{2,1,0:T(4,128)S(1)} fusion(f32[8,3,512,512]{3,2,1,0:T(8,128)} %get-tuple-element.150, f32[8,512]{1,0:T(8,128)S(1)} %broadcast_select_fusion.5), kind=kLoop, calls=%fused_computation.1.clone.1 | loop fusion | flops 12570624 | bytes 25231360 | tf_op jit(solution)/shard_map/while/body/eval_jaxpr/reduce_sum | solution.py:101
  106.5 5.6 %copy-done.2 = f32[8,3,512,512]{3,2,1,0:T(8,128)S(1)} copy-done((f32[8,3,512,512]{3,2,1,0:T(8,128)S(1)}, f32[8,3,512,512]{3,2,1,0:T(8,128)}, u32[]{:S(2)}) %copy-start.2) | copy-done | bytes 25165848 | tf_op jit(solution)/shard_map/while
  112.1 2.2 multiply_reduce_fusion.7
  114.4 9.6 %multiply_reduce_fusion.6 = f32[8,3,512]{2,1,0:T(4,128)S(1)} fusion(f32[8,3,512,512]{3,2,1,0:T(8,128)} %get-tuple-element.150, f32[8,512]{1,0:T(8,128)S(1)} %broadcast_select_fusion.5), kind=kLoop, calls=%fused_computation.1.clone.1 | loop fusion | flops 12570624 | bytes 25231360 | tf_op jit(solution)/shard_map/while/body/eval_jaxpr/reduce_sum | solution.py:101
  124.2 5.6 %copy-done.2 = f32[8,3,512,512]{3,2,1,0:T(8,128)S(1)} copy-done((f32[8,3,512,512]{3,2,1,0:T(8,128)S(1)}, f32[8,3,512,512]{3,2,1,0:T(8,128)}, u32[]{:S(2)}) %copy-start.2) | copy-done | bytes 25165848 | tf_op jit(solution)/shard_map/while
  129.8 2.2 multiply_reduce_fusion.7
  132.1 9.6 %multiply_reduce_fusion.6 = f32[8,3,512]{2,1,0:T(4,128)S(1)} fusion(f32[8,3,512,512]{3,2,1,0:T(8,128)} %get-tuple-element.150, f32[8,512]{1,0:T(8,128)S(1)} %broadcast_select_fusion.5), kind=kLoop, calls=%fused_computation.1.clone.1 | loop fusion | flops 12570624 | bytes 25231360 | tf_op jit(solution)/shard_map/while/body/eval_jaxpr/reduce_sum | solution.py:101
  141.9 5.6 %copy-done.2 = f32[8,3,512,512]{3,2,1,0:T(8,128)S(1)} copy-done((f32[8,3,512,512]{3,2,1,0:T(8,128)S(1)}, f32[8,3,512,512]{3,2,1,0:T(8,128)}, u32[]{:S(2)}) %copy-start.2) | copy-done | bytes 25165848 | tf_op jit(solution)/shard_map/while
  147.5 2.2 multiply_reduce_fusion.7
  149.8 9.6 %multiply_reduce_fusion.6 = f32[8,3,512]{2,1,0:T(4,128)S(1)} fusion(f32[8,3,512,512]{3,2,1,0:T(8,128)} %get-tuple-element.150, f32[8,512]{1,0:T(8,128)S(1)} %broadcast_select_fusion.5), kind=kLoop, calls=%fused_computation.1.clone.1 | loop fusion | flops 12570624 | bytes 25231360 | tf_op jit(solution)/shard_map/while/body/eval_jaxpr/reduce_sum | solution.py:101
  159.6 5.6 %copy-done.2 = f32[8,3,512,512]{3,2,1,0:T(8,128)S(1)} copy-done((f32[8,3,512,512]{3,2,1,0:T(8,128)S(1)}, f32[8,3,512,512]{3,2,1,0:T(8,128)}, u32[]{:S(2)}) %copy-start.2) | copy-done | bytes 25165848 | tf_op jit(solution)/shard_map/while
  165.2 2.2 multiply_reduce_fusion.7
  167.5 1.0 constant_dynamic-slice_fusion
  168.5 2.5 fusion.4
  171.0 1.3 fusion.9
  172.3 1.3 fusion.8
  173.6 36.9 %collective-permute-done.4 = bf16[512,2048]{1,0:T(8,128)(2,1)} collective-permute-done((bf16[512,2048]{1,0:T(8,128)(2,1)}, bf16[512,2048]{1,0:T(8,128)(2,1)}, u32[]{:S(2)}, u32[]{:S(2)}) %collective-permute-start.4) | collective-permute-done | bytes 2097184 | tf_op jit(solution)/shard_map/ppermute | solution.py:18
  210.5 2.9 %fusion.11 = f32[512,2048]{1,0:T(8,128)S(1)} fusion(bf16[512,2048]{1,0:T(8,128)(2,1)} %collective-permute-done.4, bf16[3,512,512]{2,1,0:T(8,128)(2,1)S(1)} %fusion.4), kind=kOutput, calls=%fused_computation.39 | convolution fusion | flops 1073741824 | bytes 6815744 | tf_op jit(solution)/shard_map/dot_general | solution.py:128
  213.4 2.9 %add_convert_fusion.1 = bf16[512,2048]{1,0:T(8,128)(2,1)S(1)} fusion(f32[512,2048]{1,0:T(8,128)S(1)} %fusion.9, f32[512,2048]{1,0:T(8,128)S(1)} %fusion.11, bf16[512,2048]{1,0:T(8,128)(2,1)} %collective-permute-done.5, bf16[3,512,512]{2,1,0:T(8,128)(2,1)S(1)} %fusion.4), kind=kOutput, calls=%fused_computation.16 | convolution fusion | flops 1076887552 | bytes 13107200 | tf_op jit(solution)/shard_map/dot_general | solution.py:129
  216.3 38.3 %collective-permute-done.2 = bf16[512,2048]{1,0:T(8,128)(2,1)} collective-permute-done((bf16[512,2048]{1,0:T(8,128)(2,1)}, bf16[512,2048]{1,0:T(8,128)(2,1)}, u32[]{:S(2)}, u32[]{:S(2)}) %collective-permute-start.2) | collective-permute-done | bytes 2097184 | tf_op jit(solution)/shard_map/ppermute | solution.py:18
  254.6 2.9 %fusion.10 = f32[512,2048]{1,0:T(8,128)S(1)} fusion(bf16[512,2048]{1,0:T(8,128)(2,1)} %collective-permute-done.2, bf16[3,512,512]{2,1,0:T(8,128)(2,1)S(1)} %fusion.4), kind=kOutput, calls=%fused_computation.38 | convolution fusion | flops 1073741824 | bytes 6815744 | tf_op jit(solution)/shard_map/dot_general | solution.py:128
  257.5 3.1 %add_convert_fusion = bf16[512,2048]{1,0:T(8,128)(2,1)S(1)} fusion(f32[512,2048]{1,0:T(8,128)S(1)} %fusion.8, f32[512,2048]{1,0:T(8,128)S(1)} %fusion.10, bf16[512,2048]{1,0:T(8,128)(2,1)} %collective-permute-done.3, bf16[3,512,512]{2,1,0:T(8,128)(2,1)S(1)} %fusion.4), kind=kOutput, calls=%fused_computation.15 | convolution fusion | flops 1076887552 | bytes 13107200 | tf_op jit(solution)/shard_map/dot_general | solution.py:129
  260.6 2.5 pad_maximum_fusion.1
  (96 shorter events, 0.9 us)
Async XLA Ops:
  6.5 1.6 copy-start
  6.5 3.5 %copy-start.6 = (bf16[4096,128]{1,0:T(8,128)(2,1)S(1)}, bf16[4096,128]{1,0:T(8,128)(2,1)}, u32[]{:S(2)}) copy-start(bf16[4096,128]{1,0:T(8,128)(2,1)} %param.14) | copy-start | bytes 3145732
  6.5 53.6 %all-gather.3.cloned.1.call-start = ((), (), s32[]{:S(2)}) async-start(), calls=%async_computation | async-start | bytes 1216512 | tf_op jit(solution)/shard_map/all_gather | solution.py:45
  10.0 4.3 %copy-start.7 = (s32[512]{0:T(512)S(1)}, s32[512]{0:T(512)}, u32[]{:S(2)}) copy-start(s32[512]{0:T(512)} %param.16) | copy-start | bytes 6148
  10.0 4.3 %copy-start.8 = (s32[512]{0:T(512)S(1)}, s32[512]{0:T(512)}, u32[]{:S(2)}) copy-start(s32[512]{0:T(512)} %param.15) | copy-start | bytes 6148
  10.0 4.6 %copy-start.9 = (s32[1,2]{1,0:T(1,128)S(1)}, s32[1,2]{1,0:T(1,128)}, u32[]{:S(2)}) copy-start(s32[1,2]{1,0:T(1,128)} %param.17) | copy-start | bytes 28
  13.8 2.3 collective-permute-start
  60.1 2.9 %collective-permute-start.1 = (bf16[8,528,128]{2,1,0:T(8,128)(2,1)}, bf16[8,528,128]{2,1,0:T(8,128)(2,1)S(1)}, u32[]{:S(2)}, u32[]{:S(2)}) collective-permute-start(bf16[8,528,128]{2,1,0:T(8,128)(2,1)} %bitcast.92), channel_id=1, source_target_pairs={{0,1},{1,0},{2,3},{3,2},{4,5},{5,4},{6,7},{7,6},{8,9},{9,8},{10,11... | collective-permute-start | bytes 3244040 | tf_op jit(solution)/shard_map/ppermute | solution.py:46
  64.7 1.3 copy-start.4
  71.9 138.6 %collective-permute-start.4 = (bf16[512,2048]{1,0:T(8,128)(2,1)}, bf16[512,2048]{1,0:T(8,128)(2,1)}, u32[]{:S(2)}, u32[]{:S(2)}) collective-permute-start(bf16[512,2048]{1,0:T(8,128)(2,1)} %get-tuple-element.83), channel_id=1, source_target_pairs={{0,2},{2,4},{4,6},{6,8},{8,10},{10,12},{12,14},{1,3},{3,5},{5,7},{... | collective-permute-start | bytes 6291464 | tf_op jit(solution)/shard_map/ppermute | solution.py:18
  75.7 137.6 %collective-permute-start.5 = (bf16[512,2048]{1,0:T(8,128)(2,1)}, bf16[512,2048]{1,0:T(8,128)(2,1)}, u32[]{:S(2)}, u32[]{:S(2)}) collective-permute-start(bf16[512,2048]{1,0:T(8,128)(2,1)} %get-tuple-element.83), channel_id=1, source_target_pairs={{2,0},{4,2},{6,4},{8,6},{10,8},{12,10},{14,12},{3,1},{5,3},{7,5},{... | collective-permute-start | bytes 6291464 | tf_op jit(solution)/shard_map/ppermute | solution.py:18
  77.0 177.6 %collective-permute-start.2 = (bf16[512,2048]{1,0:T(8,128)(2,1)}, bf16[512,2048]{1,0:T(8,128)(2,1)}, u32[]{:S(2)}, u32[]{:S(2)}) collective-permute-start(bf16[512,2048]{1,0:T(8,128)(2,1)} %get-tuple-element.84), channel_id=1, source_target_pairs={{0,2},{2,4},{4,6},{6,8},{8,10},{10,12},{12,14},{1,3},{3,5},{5,7},{... | collective-permute-start | bytes 6291464 | tf_op jit(solution)/shard_map/ppermute | solution.py:18
  82.9 171.7 %collective-permute-start.3 = (bf16[512,2048]{1,0:T(8,128)(2,1)}, bf16[512,2048]{1,0:T(8,128)(2,1)}, u32[]{:S(2)}, u32[]{:S(2)}) collective-permute-start(bf16[512,2048]{1,0:T(8,128)(2,1)} %get-tuple-element.84), channel_id=1, source_target_pairs={{2,0},{4,2},{6,4},{8,6},{10,8},{12,10},{14,12},{3,1},{5,3},{7,5},{... | collective-permute-start | bytes 6291464 | tf_op jit(solution)/shard_map/ppermute | solution.py:18
  96.7 15.4 %copy-start.2 = (f32[8,3,512,512]{3,2,1,0:T(8,128)S(1)}, f32[8,3,512,512]{3,2,1,0:T(8,128)}, u32[]{:S(2)}) copy-start(f32[8,3,512,512]{3,2,1,0:T(8,128)} %get-tuple-element.150) | copy-start | bytes 75497472 | tf_op jit(solution)/shard_map/while
  106.4 7.9 %copy-start.5 = (f32[8,3,512]{2,0,1:T(8,128)}, f32[8,3,512]{2,0,1:T(8,128)S(1)}, u32[]{:S(2)}) copy-start(f32[8,3,512]{2,0,1:T(8,128)S(1)} %pad_maximum_fusion.11) | copy-start | bytes 147460 | tf_op jit(solution)/shard_map/while
  114.4 15.4 %copy-start.2 = (f32[8,3,512,512]{3,2,1,0:T(8,128)S(1)}, f32[8,3,512,512]{3,2,1,0:T(8,128)}, u32[]{:S(2)}) copy-start(f32[8,3,512,512]{3,2,1,0:T(8,128)} %get-tuple-element.150) | copy-start | bytes 75497472 | tf_op jit(solution)/shard_map/while
  124.1 7.9 %copy-start.5 = (f32[8,3,512]{2,0,1:T(8,128)}, f32[8,3,512]{2,0,1:T(8,128)S(1)}, u32[]{:S(2)}) copy-start(f32[8,3,512]{2,0,1:T(8,128)S(1)} %pad_maximum_fusion.11) | copy-start | bytes 147460 | tf_op jit(solution)/shard_map/while
  132.1 15.4 %copy-start.2 = (f32[8,3,512,512]{3,2,1,0:T(8,128)S(1)}, f32[8,3,512,512]{3,2,1,0:T(8,128)}, u32[]{:S(2)}) copy-start(f32[8,3,512,512]{3,2,1,0:T(8,128)} %get-tuple-element.150) | copy-start | bytes 75497472 | tf_op jit(solution)/shard_map/while
  141.8 7.9 %copy-start.5 = (f32[8,3,512]{2,0,1:T(8,128)}, f32[8,3,512]{2,0,1:T(8,128)S(1)}, u32[]{:S(2)}) copy-start(f32[8,3,512]{2,0,1:T(8,128)S(1)} %pad_maximum_fusion.11) | copy-start | bytes 147460 | tf_op jit(solution)/shard_map/while
  149.8 15.4 %copy-start.2 = (f32[8,3,512,512]{3,2,1,0:T(8,128)S(1)}, f32[8,3,512,512]{3,2,1,0:T(8,128)}, u32[]{:S(2)}) copy-start(f32[8,3,512,512]{3,2,1,0:T(8,128)} %get-tuple-element.150) | copy-start | bytes 75497472 | tf_op jit(solution)/shard_map/while
  159.5 7.9 %copy-start.5 = (f32[8,3,512]{2,0,1:T(8,128)}, f32[8,3,512]{2,0,1:T(8,128)S(1)}, u32[]{:S(2)}) copy-start(f32[8,3,512]{2,0,1:T(8,128)S(1)} %pad_maximum_fusion.11) | copy-start | bytes 147460 | tf_op jit(solution)/shard_map/while
  167.5 3.5 %copy-start.3 = (bf16[512,4096]{1,0:T(8,128)(2,1)S(1)}, bf16[512,4096]{1,0:T(8,128)(2,1)}, u32[]{:S(2)}) copy-start(bf16[512,4096]{1,0:T(8,128)(2,1)} %param.12) | copy-start | bytes 12582916
  257.5 5.6 %copy-start.1 = (bf16[512,2048]{1,0:T(8,128)(2,1)S(1)}, bf16[512,2048]{1,0:T(8,128)(2,1)}, u32[]{:S(2)}) copy-start(bf16[512,2048]{1,0:T(8,128)(2,1)} %param.11) | copy-start | bytes 6291460
Sparse Core Ops, SparseCore 0:
  17.4 42.6 all-gather.2

commit v6 on v4

--- a/solution.py
+++ b/solution.py
@@ -34,6 +34,22 @@
     if lax.axis_size("tgrp") == 2:
         return value + lax.ppermute(value, "tgrp", [(0, 1), (1, 0)])
     return lax.psum(value, "tgrp")
+
+
+def gather_seq(block):
+    n = lax.axis_size("seq")
+    if n % 2:
+        return lax.all_gather(block, "seq")
+    me = lax.axis_index("seq")
+    pairs = n // 2
+    partner = lax.ppermute(block, "seq", [(i, i ^ 1) for i in range(n)])
+    odd = me % 2 == 1
+    pair = jnp.stack([jnp.where(odd, partner, block), jnp.where(odd, block, partner)])
+    by_offset = [pair]
+    for d in range(1, pairs):
+        by_offset = [shifted(pair, "seq", 2 * d)] + by_offset + [shifted(pair, "seq", -2 * d)]
+    window = lax.dynamic_slice_in_dim(jnp.stack(by_offset), pairs - 1 - me // 2, pairs, 0)
+    return window.reshape((n,) + block.shape)
 
 
 def gather_halves(packed):
@@ -42,7 +58,7 @@
     half = packed.shape[1] // 2
     core = lax.axis_index("tgrp")
     mine = lax.dynamic_slice_in_dim(packed, core * half, half, 1)
-    got = lax.all_gather(mine, "seq")
+    got = gather_seq(mine)
     theirs = lax.ppermute(got, "tgrp", [(0, 1), (1, 0)])
     first = jnp.where(core == 0, got, theirs)
     second = jnp.where(core == 0, theirs, got)

time: 269 us -> 263 us (0.978)
  starting transfers between devices: 6.42 us -> 23.6 us
  between operations: 13.8 us -> 0.55 us
  waiting for transfers between devices: 134 us -> 122 us
    all_gather x1 -> x0, waiting for transfers between devices: 42.9 us -> none  [gather_halves(): got = lax.all_gather(mine, 'seq')]
    ppermute x2 -> x8, waiting for transfers between devices: 87.9 us -> 115 us  [shifted(): return lax.ppermute(block, axis, route)]
    ppermute x2 -> x8, starting transfers between devices: 5.89 us -> 20.3 us  [shifted(): return lax.ppermute(block, axis, route)]
    ppermute x0 -> x1, waiting for transfers between devices: none -> 4.73 us  [gather_seq(): partner = lax.ppermute(block, 'seq', [(i, i ^ 1) for i in range(n)])]
    ppermute x0 -> x1, starting transfers between devices: none -> 2.72 us  [gather_seq(): partner = lax.ppermute(block, 'seq', [(i, i ^ 1) for i in range(n)])]
  transfers between devices with their start and end apart: 5 -> 11, of which waited for: 3 -> 7; matrix products, arithmetic and copies ran while one was open for 27% -> 28% of each run, Pallas kernels for 0% -> 0%
where the time goes in v6:
time: 263 us; the launch traced here: 262 us
  waiting for transfers between devices  122 us (46%)
  other arithmetic  54.4 us (21%)
  matrix products  31.8 us (12%)
  local copies, waits for them, and re-layouts  28.7 us (11%)
  starting transfers between devices  23.6 us (9%)
    ppermute x8, waiting for transfers between devices, shifted(): return lax.ppermute(block, axis, route)  115 us
    reduce_sum x4, other arithmetic, iterate(): partial_cols = jnp.sum(row_scale[:, None, None, :] * kernel, axis=3)  38.4 us
    while x16, local copies, waits for them, and re-layouts  22.4 us
    ppermute x8, starting transfers between devices, shifted(): return lax.ppermute(block, axis, route)  20.3 us
    dot_general x1, matrix products, body_local(): jnp.einsum('bkjp,bip->bkji', beside(t_unit), s_unit, preferred_element_ty...  11.8 us
    reduce_sum x4, other arithmetic, iterate(): row_scale = 1.0 / jnp.sum(kernel * col_scale[:, :, :, None], axis=(1, 2))  8.94 us
    dot_general x1, matrix products, body_local(): lax.dot_general(plan[2], right_rows, along_j, preferred_element_type=jnp....  7.35 us
  transfers between devices with their start and end apart: 11, of which 7 were waited for; matrix products, arithmetic and copies ran while one was open for 28% of the time, Pallas kernels for 0%

profile of v6, /device:TPU:0, one launch (start us, length us, event | category | flops | bytes accessed | tf_op | source)
XLA Modules:
  0.0 262.0 jit_solution(15790225366925037373)
XLA Ops:
  0.0 1.6 copy-done
  1.6 1.9 fusion.28
  3.5 3.7 %fusion.29 = f32[512,128]{0,1:T(8,128)S(1)} fusion(bf16[512,4096]{1,0:T(8,128)(2,1)} %param.12, bf16[4096,128]{1,0:T(8,128)(2,1)S(1)} %copy-done.6), kind=kOutput, calls=%fused_computation.109 | convolution fusion | flops 536870912 | bytes 5505024 | tf_op jit(solution)/shard_map/dot_general | solution.py:77
  7.3 0.5 collective-permute-start
  7.8 0.1 fusion.17
  7.9 0.1 copy.28
  8.1 0.1 copy.27
  8.2 0.1 pad.33.clone
  8.3 0.6 compare_reduce_fusion
  8.9 0.6 broadcast_select_fusion.3
  9.6 0.1 fusion.21
  9.7 0.1 multiply_reduce_fusion.2
  9.8 0.1 fusion.13
  9.9 2.7 %collective-permute-start.1 = (bf16[528,128]{0,1:T(8,128)(2,1)S(1)}, bf16[528,128]{0,1:T(8,128)(2,1)S(1)}, u32[]{:S(2)}, u32[]{:S(2)}) collective-permute-start(bf16[528,128]{0,1:T(8,128)(2,1)S(1)} %fusion.13), channel_id=1, source_target_pairs={{0,2},{2,0},{4,6},{6,4},{8,10},{10,8},{12,14},{14,12},{1,3},{3,1},... | collective-permute-start | bytes 405512 | tf_op jit(solution)/shard_map/ppermute | solution.py:45
  12.7 4.7 %collective-permute-done.1 = bf16[528,128]{0,1:T(8,128)(2,1)S(1)} collective-permute-done((bf16[528,128]{0,1:T(8,128)(2,1)S(1)}, bf16[528,128]{0,1:T(8,128)(2,1)S(1)}, u32[]{:S(2)}, u32[]{:S(2)}) %collective-permute-start.1) | collective-permute-done | bytes 135200 | tf_op jit(solution)/shard_map/ppermute | solution.py:45
  17.5 5.7 %collective-permute-start.2 = (bf16[2,528,128]{1,2,0:T(8,128)(2,1)S(1)}, bf16[2,528,128]{1,2,0:T(8,128)(2,1)S(1)}, u32[]{:S(2)}, u32[]{:S(2)}) collective-permute-start(bf16[2,528,128]{1,2,0:T(8,128)(2,1)S(1)} %pad_maximum_fusion.4), channel_id=1, source_target_pairs={{0,12},{2,14},{1,13},{3,15},{16,28},{18,30},{17,29},{19,31}} | collective-permute-start | bytes 811016 | tf_op jit(solution)/shard_map/ppermute | solution.py:18
  23.2 1.3 collective-permute-start.3
  24.6 2.5 collective-permute-start.4
  27.1 1.3 collective-permute-start.5
  28.4 1.3 collective-permute-start.6
  29.7 1.8 collective-permute-done.2
  31.5 1.3 collective-permute-start.7
  32.8 5.7 %collective-permute-done.3 = bf16[2,528,128]{1,2,0:T(8,128)(2,1)S(1)} collective-permute-done((bf16[2,528,128]{1,2,0:T(8,128)(2,1)S(1)}, bf16[2,528,128]{1,2,0:T(8,128)(2,1)S(1)}, u32[]{:S(2)}, u32[]{:S(2)}) %collective-permute-start.3) | collective-permute-done | bytes 270368 | tf_op jit(solution)/shard_map/ppermute | solution.py:18
  38.5 5.5 %collective-permute-done.4 = bf16[2,528,128]{1,2,0:T(8,128)(2,1)S(1)} collective-permute-done((bf16[2,528,128]{1,2,0:T(8,128)(2,1)S(1)}, bf16[2,528,128]{1,2,0:T(8,128)(2,1)S(1)}, u32[]{:S(2)}, u32[]{:S(2)}) %collective-permute-start.4) | collective-permute-done | bytes 270368 | tf_op jit(solution)/shard_map/ppermute | solution.py:18
  44.2 14.2 %collective-permute-done.6 = bf16[2,528,128]{1,2,0:T(8,128)(2,1)S(1)} collective-permute-done((bf16[2,528,128]{1,2,0:T(8,128)(2,1)S(1)}, bf16[2,528,128]{1,2,0:T(8,128)(2,1)S(1)}, u32[]{:S(2)}, u32[]{:S(2)}) %collective-permute-start.6) | collective-permute-done | bytes 270368 | tf_op jit(solution)/shard_map/ppermute | solution.py:18
  58.5 0.1 constant_dynamic-slice_fusion.2
  58.6 0.8 copy.29
  59.4 0.1 collective-permute-start.8
  59.5 0.1 pad.17.clone
  59.6 2.7 %collective-permute-done.8 = bf16[8,528,128]{2,1,0:T(8,128)(2,1)} collective-permute-done((bf16[8,528,128]{2,1,0:T(8,128)(2,1)S(1)}, bf16[8,528,128]{2,1,0:T(8,128)(2,1)}, u32[]{:S(2)}, u32[]{:S(2)}) %collective-permute-start.8) | collective-permute-done | bytes 1081376 | tf_op jit(solution)/shard_map/ppermute | solution.py:62
  62.3 1.4 broadcast_select_fusion.2
  63.7 0.2 pad_maximum_fusion.2
  63.9 0.4 fusion.24
  64.3 0.2 slice_bitcast_fusion
  64.5 0.8 copy-done.4
  65.3 0.1 reshape.409
  65.3 0.1 slice_add_fusion
  65.5 0.8 slice_convert_fusion.1
  66.3 5.4 %collective-permute-start.9 = (bf16[512,4096]{1,0:T(8,128)(2,1)}, bf16[512,4096]{1,0:T(8,128)(2,1)}, u32[]{:S(2)}, u32[]{:S(2)}) collective-permute-start(bf16[512,4096]{1,0:T(8,128)(2,1)} %param.12), channel_id=1, source_target_pairs={{0,2},{2,4},{4,6},{6,8},{8,10},{10,12},{12,14},{1,3},{3,5},{5,7},{... | collective-permute-start | bytes 12582920 | tf_op jit(solution)/shard_map/ppermute | solution.py:18
  71.7 1.5 collective-permute-start.10
  73.2 0.1 pad_bitcast_fusion.2
  73.2 0.1 pad_bitcast_fusion.3
  73.5 0.1 fusion.27
  73.5 0.1 pad_maximum_fusion.7
  73.6 11.8 %exponential_multiply_fusion = f32[8,3,512,512]{3,2,1,0:T(8,128)} fusion(f32[8,3]{1,0:T(8,128)S(1)} %pad_maximum_fusion.7, f32[8,3,512]{2,1,0:T(4,128)S(1)} %copy.33, f32[8,512]{1,0:T(8,128)S(1)} %bitcast.115, bf16[8,528,256]{2,1,0:T(8,128)(2,1)} %copy-done.4, bf16[8,1,512,128]{3,2,0,1:T(8,128)(2,1)S(1)} %pad_bitcast_fusion.2, ...), kind=kOutput, calls=%fused_computation.13 | convolution fusion | flops 1651507200 | bytes 29425760 | tf_op jit(solution)/shard_map/bkjp,bip->bkji/dot_general | solution.py:104
  85.5 70.8 %while.14 = (s32[]{:T(128)}, f32[8,512]{1,0:T(8,128)S(1)}, f32[8,3,512]{2,0,1:T(8,128)}, f32[8,3,512,512]{3,2,1,0:T(8,128)}, s32[]{:T(128)}, /*index=5*/s32[]{:T(128)}) while((s32[]{:T(128)}, f32[8,512]{1,0:T(8,128)S(1)}, f32[8,3,512]{2,0,1:T(8,128)}, f32[8,3,512,512]{3,2,1,0:T(8,128)}, s32[]{:T(128)}, /*index=5*/s32[]{:T(128)}) %tuple.48), condition=%wide.region_6.7_spmd.clone, body=%wide.region_3.6_spmd.clone.sunk | while | flops 25194500 | bytes 151912576 | solution.py:123
  85.5 9.6 %multiply_reduce_fusion.6 = f32[8,3,512]{2,1,0:T(4,128)S(1)} fusion(f32[8,3,512,512]{3,2,1,0:T(8,128)} %get-tuple-element.144, f32[8,512]{1,0:T(8,128)S(1)} %broadcast_select_fusion.5), kind=kLoop, calls=%fused_computation.1.clone.1 | loop fusion | flops 12570624 | bytes 25231360 | tf_op jit(solution)/shard_map/while/body/eval_jaxpr/reduce_sum | solution.py:112
  95.3 5.6 %copy-done.2 = f32[8,3,512,512]{3,2,1,0:T(8,128)S(1)} copy-done((f32[8,3,512,512]{3,2,1,0:T(8,128)S(1)}, f32[8,3,512,512]{3,2,1,0:T(8,128)}, u32[]{:S(2)}) %copy-start.2) | copy-done | bytes 25165848 | tf_op jit(solution)/shard_map/while
  100.9 2.2 multiply_reduce_fusion.7
  103.2 9.6 %multiply_reduce_fusion.6 = f32[8,3,512]{2,1,0:T(4,128)S(1)} fusion(f32[8,3,512,512]{3,2,1,0:T(8,128)} %get-tuple-element.144, f32[8,512]{1,0:T(8,128)S(1)} %broadcast_select_fusion.5), kind=kLoop, calls=%fused_computation.1.clone.1 | loop fusion | flops 12570624 | bytes 25231360 | tf_op jit(solution)/shard_map/while/body/eval_jaxpr/reduce_sum | solution.py:112
  113.0 5.6 %copy-done.2 = f32[8,3,512,512]{3,2,1,0:T(8,128)S(1)} copy-done((f32[8,3,512,512]{3,2,1,0:T(8,128)S(1)}, f32[8,3,512,512]{3,2,1,0:T(8,128)}, u32[]{:S(2)}) %copy-start.2) | copy-done | bytes 25165848 | tf_op jit(solution)/shard_map/while
  118.6 2.2 multiply_reduce_fusion.7
  120.9 9.6 %multiply_reduce_fusion.6 = f32[8,3,512]{2,1,0:T(4,128)S(1)} fusion(f32[8,3,512,512]{3,2,1,0:T(8,128)} %get-tuple-element.144, f32[8,512]{1,0:T(8,128)S(1)} %broadcast_select_fusion.5), kind=kLoop, calls=%fused_computation.1.clone.1 | loop fusion | flops 12570624 | bytes 25231360 | tf_op jit(solution)/shard_map/while/body/eval_jaxpr/reduce_sum | solution.py:112
  130.7 5.6 %copy-done.2 = f32[8,3,512,512]{3,2,1,0:T(8,128)S(1)} copy-done((f32[8,3,512,512]{3,2,1,0:T(8,128)S(1)}, f32[8,3,512,512]{3,2,1,0:T(8,128)}, u32[]{:S(2)}) %copy-start.2) | copy-done | bytes 25165848 | tf_op jit(solution)/shard_map/while
  136.3 2.2 multiply_reduce_fusion.7
  138.6 9.6 %multiply_reduce_fusion.6 = f32[8,3,512]{2,1,0:T(4,128)S(1)} fusion(f32[8,3,512,512]{3,2,1,0:T(8,128)} %get-tuple-element.144, f32[8,512]{1,0:T(8,128)S(1)} %broadcast_select_fusion.5), kind=kLoop, calls=%fused_computation.1.clone.1 | loop fusion | flops 12570624 | bytes 25231360 | tf_op jit(solution)/shard_map/while/body/eval_jaxpr/reduce_sum | solution.py:112
  148.4 5.6 %copy-done.2 = f32[8,3,512,512]{3,2,1,0:T(8,128)S(1)} copy-done((f32[8,3,512,512]{3,2,1,0:T(8,128)S(1)}, f32[8,3,512,512]{3,2,1,0:T(8,128)}, u32[]{:S(2)}) %copy-start.2) | copy-done | bytes 25165848 | tf_op jit(solution)/shard_map/while
  154.0 2.2 multiply_reduce_fusion.7
  156.3 1.0 constant_dynamic-slice_fusion
  157.2 2.5 fusion.4
  159.8 2.5 fusion.9
  162.2 87.8 %collective-permute-done.9 = bf16[512,4096]{1,0:T(8,128)(2,1)} collective-permute-done((bf16[512,4096]{1,0:T(8,128)(2,1)}, bf16[512,4096]{1,0:T(8,128)(2,1)}, u32[]{:S(2)}, u32[]{:S(2)}) %collective-permute-start.9) | collective-permute-done | bytes 4194336 | tf_op jit(solution)/shard_map/ppermute | solution.py:18
  250.0 4.6 %fusion.8 = f32[512,4096]{1,0:T(8,128)S(1)} fusion(bf16[512,4096]{1,0:T(8,128)(2,1)} %collective-permute-done.9, bf16[3,512,512]{2,1,0:T(8,128)(2,1)S(1)} %fusion.4), kind=kOutput, calls=%fused_computation.30 | convolution fusion | flops 2147483648 | bytes 13107200 | tf_op jit(solution)/shard_map/dot_general | solution.py:135
  254.7 7.4 %add_convert_fusion = bf16[512,4096]{1,0:T(8,128)(2,1)} fusion(f32[512,4096]{1,0:T(8,128)S(1)} %fusion.9, f32[512,4096]{1,0:T(8,128)S(1)} %fusion.8, bf16[512,4096]{1,0:T(8,128)(2,1)} %collective-permute-done.10, bf16[3,512,512]{2,1,0:T(8,128)(2,1)S(1)} %fusion.4), kind=kOutput, calls=%fused_computation.14 | convolution fusion | flops 2153775104 | bytes 25690112 | tf_op jit(solution)/shard_map/dot_general | solution.py:136
  (108 shorter events, 1.3 us)
Async XLA Ops:
  0.0 1.6 copy-start
  0.0 3.5 %copy-start.6 = (bf16[4096,128]{1,0:T(8,128)(2,1)S(1)}, bf16[4096,128]{1,0:T(8,128)(2,1)}, u32[]{:S(2)}) copy-start(bf16[4096,128]{1,0:T(8,128)(2,1)} %param.14) | copy-start | bytes 3145732
  3.5 4.3 %copy-start.7 = (s32[512]{0:T(512)S(1)}, s32[512]{0:T(512)}, u32[]{:S(2)}) copy-start(s32[512]{0:T(512)} %param.16) | copy-start | bytes 6148
  3.5 4.3 %copy-start.8 = (s32[512]{0:T(512)S(1)}, s32[512]{0:T(512)}, u32[]{:S(2)}) copy-start(s32[512]{0:T(512)} %param.15) | copy-start | bytes 6148
  3.5 4.6 %copy-start.9 = (s32[1,2]{1,0:T(1,128)S(1)}, s32[1,2]{1,0:T(1,128)}, u32[]{:S(2)}) copy-start(s32[1,2]{1,0:T(1,128)} %param.17) | copy-start | bytes 28
  7.3 2.3 collective-permute-start
  9.9 7.4 %collective-permute-start.1 = (bf16[528,128]{0,1:T(8,128)(2,1)S(1)}, bf16[528,128]{0,1:T(8,128)(2,1)S(1)}, u32[]{:S(2)}, u32[]{:S(2)}) collective-permute-start(bf16[528,128]{0,1:T(8,128)(2,1)S(1)} %fusion.13), channel_id=1, source_target_pairs={{0,2},{2,0},{4,6},{6,4},{8,10},{10,8},{12,14},{14,12},{1,3},{3,1},... | collective-permute-start | bytes 405512 | tf_op jit(solution)/shard_map/ppermute | solution.py:45
  17.5 14.0 %collective-permute-start.2 = (bf16[2,528,128]{1,2,0:T(8,128)(2,1)S(1)}, bf16[2,528,128]{1,2,0:T(8,128)(2,1)S(1)}, u32[]{:S(2)}, u32[]{:S(2)}) collective-permute-start(bf16[2,528,128]{1,2,0:T(8,128)(2,1)S(1)} %pad_maximum_fusion.4), channel_id=1, source_target_pairs={{0,12},{2,14},{1,13},{3,15},{16,28},{18,30},{17,29},{19,31}} | collective-permute-start | bytes 811016 | tf_op jit(solution)/shard_map/ppermute | solution.py:18
  23.2 15.2 %collective-permute-start.3 = (bf16[2,528,128]{1,2,0:T(8,128)(2,1)S(1)}, bf16[2,528,128]{1,2,0:T(8,128)(2,1)S(1)}, u32[]{:S(2)}, u32[]{:S(2)}) collective-permute-start(bf16[2,528,128]{1,2,0:T(8,128)(2,1)S(1)} %pad_maximum_fusion.4), channel_id=1, source_target_pairs={{0,8},{2,10},{4,12},{6,14},{1,9},{3,11},{5,13},{7,15},{16,24},{18,... | collective-permute-start | bytes 811016 | tf_op jit(solution)/shard_map/ppermute | solution.py:18
  24.6 19.4 %collective-permute-start.4 = (bf16[2,528,128]{1,2,0:T(8,128)(2,1)S(1)}, bf16[2,528,128]{1,2,0:T(8,128)(2,1)S(1)}, u32[]{:S(2)}, u32[]{:S(2)}) collective-permute-start(bf16[2,528,128]{1,2,0:T(8,128)(2,1)S(1)} %pad_maximum_fusion.4), channel_id=1, source_target_pairs={{0,4},{2,6},{4,8},{6,10},{8,12},{10,14},{1,5},{3,7},{5,9},{7,11},{... | collective-permute-start | bytes 811016 | tf_op jit(solution)/shard_map/ppermute | solution.py:18
  27.1 17.1 %collective-permute-start.5 = (bf16[2,528,128]{1,2,0:T(8,128)(2,1)S(1)}, bf16[2,528,128]{1,2,0:T(8,128)(2,1)S(1)}, u32[]{:S(2)}, u32[]{:S(2)}) collective-permute-start(bf16[2,528,128]{1,2,0:T(8,128)(2,1)S(1)} %pad_maximum_fusion.4), channel_id=1, source_target_pairs={{4,0},{6,2},{8,4},{10,6},{12,8},{14,10},{5,1},{7,3},{9,5},{11,7},{... | collective-permute-start | bytes 811016 | tf_op jit(solution)/shard_map/ppermute | solution.py:18
  28.4 30.0 %collective-permute-start.6 = (bf16[2,528,128]{1,2,0:T(8,128)(2,1)S(1)}, bf16[2,528,128]{1,2,0:T(8,128)(2,1)S(1)}, u32[]{:S(2)}, u32[]{:S(2)}) collective-permute-start(bf16[2,528,128]{1,2,0:T(8,128)(2,1)S(1)} %pad_maximum_fusion.4), channel_id=1, source_target_pairs={{8,0},{10,2},{12,4},{14,6},{9,1},{11,3},{13,5},{15,7},{24,16},{26,... | collective-permute-start | bytes 811016 | tf_op jit(solution)/shard_map/ppermute | solution.py:18
  31.5 26.9 %collective-permute-start.7 = (bf16[2,528,128]{1,2,0:T(8,128)(2,1)S(1)}, bf16[2,528,128]{1,2,0:T(8,128)(2,1)S(1)}, u32[]{:S(2)}, u32[]{:S(2)}) collective-permute-start(bf16[2,528,128]{1,2,0:T(8,128)(2,1)S(1)} %pad_maximum_fusion.4), channel_id=1, source_target_pairs={{12,0},{14,2},{13,1},{15,3},{28,16},{30,18},{29,17},{31,19}} | collective-permute-start | bytes 811016 | tf_op jit(solution)/shard_map/ppermute | solution.py:18
  59.4 2.9 %collective-permute-start.8 = (bf16[8,528,128]{2,1,0:T(8,128)(2,1)S(1)}, bf16[8,528,128]{2,1,0:T(8,128)(2,1)}, u32[]{:S(2)}, u32[]{:S(2)}) collective-permute-start(bf16[8,528,128]{2,1,0:T(8,128)(2,1)S(1)} %bitcast.108), channel_id=1, source_target_pairs={{0,1},{1,0},{2,3},{3,2},{4,5},{5,4},{6,7},{7,6},{8,9},{9,8},{10,11... | collective-permute-start | bytes 3244040 | tf_op jit(solution)/shard_map/ppermute | solution.py:62
  63.9 1.3 copy-start.4
  66.3 183.7 %collective-permute-start.9 = (bf16[512,4096]{1,0:T(8,128)(2,1)}, bf16[512,4096]{1,0:T(8,128)(2,1)}, u32[]{:S(2)}, u32[]{:S(2)}) collective-permute-start(bf16[512,4096]{1,0:T(8,128)(2,1)} %param.12), channel_id=1, source_target_pairs={{0,2},{2,4},{4,6},{6,8},{8,10},{10,12},{12,14},{1,3},{3,5},{5,7},{... | collective-permute-start | bytes 12582920 | tf_op jit(solution)/shard_map/ppermute | solution.py:18
  71.7 183.0 %collective-permute-start.10 = (bf16[512,4096]{1,0:T(8,128)(2,1)}, bf16[512,4096]{1,0:T(8,128)(2,1)}, u32[]{:S(2)}, u32[]{:S(2)}) collective-permute-start(bf16[512,4096]{1,0:T(8,128)(2,1)} %param.12), channel_id=1, source_target_pairs={{2,0},{4,2},{6,4},{8,6},{10,8},{12,10},{14,12},{3,1},{5,3},{7,5},{... | collective-permute-start | bytes 12582920 | tf_op jit(solution)/shard_map/ppermute | solution.py:18
  85.5 15.4 %copy-start.2 = (f32[8,3,512,512]{3,2,1,0:T(8,128)S(1)}, f32[8,3,512,512]{3,2,1,0:T(8,128)}, u32[]{:S(2)}) copy-start(f32[8,3,512,512]{3,2,1,0:T(8,128)} %get-tuple-element.144) | copy-start | bytes 75497472 | tf_op jit(solution)/shard_map/while
  95.2 7.9 %copy-start.5 = (f32[8,3,512]{2,0,1:T(8,128)}, f32[8,3,512]{2,0,1:T(8,128)S(1)}, u32[]{:S(2)}) copy-start(f32[8,3,512]{2,0,1:T(8,128)S(1)} %pad_maximum_fusion.11) | copy-start | bytes 147460 | tf_op jit(solution)/shard_map/while
  103.2 15.4 %copy-start.2 = (f32[8,3,512,512]{3,2,1,0:T(8,128)S(1)}, f32[8,3,512,512]{3,2,1,0:T(8,128)}, u32[]{:S(2)}) copy-start(f32[8,3,512,512]{3,2,1,0:T(8,128)} %get-tuple-element.144) | copy-start | bytes 75497472 | tf_op jit(solution)/shard_map/while
  112.9 7.9 %copy-start.5 = (f32[8,3,512]{2,0,1:T(8,128)}, f32[8,3,512]{2,0,1:T(8,128)S(1)}, u32[]{:S(2)}) copy-start(f32[8,3,512]{2,0,1:T(8,128)S(1)} %pad_maximum_fusion.11) | copy-start | bytes 147460 | tf_op jit(solution)/shard_map/while
  120.9 15.4 %copy-start.2 = (f32[8,3,512,512]{3,2,1,0:T(8,128)S(1)}, f32[8,3,512,512]{3,2,1,0:T(8,128)}, u32[]{:S(2)}) copy-start(f32[8,3,512,512]{3,2,1,0:T(8,128)} %get-tuple-element.144) | copy-start | bytes 75497472 | tf_op jit(solution)/shard_map/while
  130.6 7.9 %copy-start.5 = (f32[8,3,512]{2,0,1:T(8,128)}, f32[8,3,512]{2,0,1:T(8,128)S(1)}, u32[]{:S(2)}) copy-start(f32[8,3,512]{2,0,1:T(8,128)S(1)} %pad_maximum_fusion.11) | copy-start | bytes 147460 | tf_op jit(solution)/shard_map/while
  138.6 15.4 %copy-start.2 = (f32[8,3,512,512]{3,2,1,0:T(8,128)S(1)}, f32[8,3,512,512]{3,2,1,0:T(8,128)}, u32[]{:S(2)}) copy-start(f32[8,3,512,512]{3,2,1,0:T(8,128)} %get-tuple-element.144) | copy-start | bytes 75497472 | tf_op jit(solution)/shard_map/while
  148.3 7.9 %copy-start.5 = (f32[8,3,512]{2,0,1:T(8,128)}, f32[8,3,512]{2,0,1:T(8,128)S(1)}, u32[]{:S(2)}) copy-start(f32[8,3,512]{2,0,1:T(8,128)S(1)} %pad_maximum_fusion.11) | copy-start | bytes 147460 | tf_op jit(solution)/shard_map/while
  156.2 3.5 %copy-start.3 = (bf16[512,4096]{1,0:T(8,128)(2,1)S(1)}, bf16[512,4096]{1,0:T(8,128)(2,1)}, u32[]{:S(2)}) copy-start(bf16[512,4096]{1,0:T(8,128)(2,1)} %param.12) | copy-start | bytes 12582916
  254.7 7.4 %copy-start.1 = (bf16[512,2048]{1,0:T(8,128)(2,1)S(1)}, bf16[512,2048]{1,0:T(8,128)(2,1)}, u32[]{:S(2)}) copy-start(bf16[512,2048]{1,0:T(8,128)(2,1)} %param.11) | copy-start | bytes 6291460

commit v7 on v6

--- a/solution.py
+++ b/solution.py
@@ -3,6 +3,7 @@
 import jax
 import jax.numpy as jnp
 from jax import lax
+from jax.experimental import pallas as pl
 from jax.sharding import PartitionSpec as P
 
 ITERS = 4
@@ -131,10 +132,40 @@
     own_col = lax.dynamic_index_in_dim(col_scale, me, 0, keepdims=False)
     plan = (own_row[None, None, :] * own_kernel * own_col[:, :, None]).astype(jnp.bfloat16)
     along_j = (((0,), (0,)), ((), ()))
-    aligned = lax.dot_general(plan[1], teacher_hidden, along_j, preferred_element_type=jnp.float32)
-    aligned = aligned + lax.dot_general(plan[0], left_rows, along_j, preferred_element_type=jnp.float32)
-    aligned = aligned + lax.dot_general(plan[2], right_rows, along_j, preferred_element_type=jnp.float32)
-    return aligned.astype(jnp.bfloat16)
+    center = lax.dot_general(plan[1], teacher_hidden, along_j, preferred_element_type=jnp.float32)
+    sides = jnp.swapaxes(plan[::2], 1, 2)
+    return neighbour_products(sides, left_rows, right_rows, center)
+
+
+def neighbour_kernel(sides_ref, left_ref, right_ref, center_ref, out_ref):
+    total = center_ref[...]
+    total = total + jnp.dot(sides_ref[0], left_ref[...], preferred_element_type=jnp.float32)
+    total = total + jnp.dot(sides_ref[1], right_ref[...], preferred_element_type=jnp.float32)
+    out_ref[...] = total.astype(out_ref.dtype)
+
+
+def neighbour_products(sides, left_rows, right_rows, center):
+    rows, width = center.shape
+    depth = left_rows.shape[0]
+    tile = 512 if width % 512 == 0 else width
+    column = pl.BlockSpec((depth, tile), lambda c: (0, c))
+    return pl.pallas_call(
+        neighbour_kernel,
+        grid=(width // tile,),
+        in_specs=[
+            pl.BlockSpec((2, rows, depth), lambda c: (0, 0, 0)),
+            column,
+            column,
+            pl.BlockSpec((rows, tile), lambda c: (0, c)),
+        ],
+        out_specs=pl.BlockSpec((rows, tile), lambda c: (0, c)),
+        out_shape=jax.ShapeDtypeStruct((rows, width), jnp.bfloat16),
+        cost_estimate=pl.CostEstimate(
+            flops=4 * rows * depth * width,
+            bytes_accessed=2 * rows * depth * 2 + 2 * depth * width * 2 + rows * width * 6,
+            transcendentals=0,
+        ),
+    )(sides, left_rows, right_rows, center)
 
 
 def body_banded(

time: 263 us -> 264 us (level)
  Pallas kernels: 0 us -> 12.5 us
  waiting for transfers between devices: 122 us -> 111 us
  matrix products: 31.8 us -> 23 us
  local copies, waits for them, and re-layouts: 28.7 us -> 37.1 us
    pallas_call x0 -> x1, Pallas kernels: none -> 12.5 us  [neighbour_products(): pl.pallas_call(neighbour_kernel, grid=(width // tile,), in_specs=[pl.Bloc...]
    dot_general x2 -> x0, matrix products: 12 us -> none  [the longest x1 7.35 us: body_local(): lax.dot_general(plan[2], right_rows, along_j, preferred_element_type=jnp....]
    ppermute x8, waiting for transfers between devices: 115 us -> 103 us  [shifted(): return lax.ppermute(block, axis, route)]
    dynamic_slice x0 -> x2, local copies, waits for them, and re-layouts: none -> 7.38 us  [body_local(): own_kernel = lax.dynamic_index_in_dim(kernel, me, 0, keepdims=False)]
    dot_general x1, matrix products: 2.46 us -> 5.66 us  [body_local(): lax.dot_general(plan[1], teacher_hidden, along_j, preferred_element_type=...]
  transfers between devices with their start and end apart: 11 -> 11, of which waited for: 7 -> 7; matrix products, arithmetic and copies ran while one was open for 28% -> 30% of each run, Pallas kernels for 0% -> 0%
where the time goes in v7:
time: 264 us; the launch traced here: 263 us
  waiting for transfers between devices  111 us (42%)
  other arithmetic  54.3 us (21%)
  local copies, waits for them, and re-layouts  37.1 us (14%)
  starting transfers between devices  24.5 us (9%)
  matrix products  23 us (9%)
  Pallas kernels  12.5 us (5%)
    ppermute x8, waiting for transfers between devices, shifted(): return lax.ppermute(block, axis, route)  103 us
    reduce_sum x4, other arithmetic, iterate(): partial_cols = jnp.sum(row_scale[:, None, None, :] * kernel, axis=3)  38.4 us
    while x16, local copies, waits for them, and re-layouts  22.4 us
    ppermute x8, starting transfers between devices, shifted(): return lax.ppermute(block, axis, route)  21.2 us
    pallas_call x1, Pallas kernels, neighbour_products(): pl.pallas_call(neighbour_kernel, grid=(width // tile,), in_specs=[pl.Bloc...  12.5 us
    dot_general x1, matrix products, body_local(): jnp.einsum('bkjp,bip->bkji', beside(t_unit), s_unit, preferred_element_ty...  11.8 us
    reduce_sum x4, other arithmetic, iterate(): row_scale = 1.0 / jnp.sum(kernel * col_scale[:, :, :, None], axis=(1, 2))  8.94 us
    dynamic_slice x2, local copies, waits for them, and re-layouts, body_local(): own_kernel = lax.dynamic_index_in_dim(kernel, me, 0, keepdims=False)  7.38 us
  transfers between devices with their start and end apart: 11, of which 7 were waited for; matrix products, arithmetic and copies ran while one was open for 30% of the time, Pallas kernels for 0%

profile of v7, /device:TPU:0, one launch (start us, length us, event | category | flops | bytes accessed | tf_op | source)
XLA Modules:
  0.0 263.5 jit_solution(5041900642116384514)
XLA Ops:
  0.0 1.6 copy-done
  1.6 1.9 fusion.27
  3.5 3.7 %fusion.28 = f32[512,128]{0,1:T(8,128)S(1)} fusion(bf16[512,4096]{1,0:T(8,128)(2,1)} %param.12, bf16[4096,128]{1,0:T(8,128)(2,1)S(1)} %copy-done.6), kind=kOutput, calls=%fused_computation.107 | convolution fusion | flops 536870912 | bytes 5505024 | tf_op jit(solution)/shard_map/dot_general | solution.py:78
  7.3 0.5 collective-permute-start
  7.9 0.1 copy.30
  8.1 0.1 copy.29
  8.2 0.1 pad.33.clone
  8.3 0.6 compare_reduce_fusion
  8.9 0.6 broadcast_select_fusion.3
  9.6 0.1 fusion.20
  9.7 0.1 multiply_reduce_fusion.2
  9.8 0.1 fusion.12
  9.9 2.7 %collective-permute-start.1 = (bf16[528,128]{0,1:T(8,128)(2,1)S(1)}, bf16[528,128]{0,1:T(8,128)(2,1)S(1)}, u32[]{:S(2)}, u32[]{:S(2)}) collective-permute-start(bf16[528,128]{0,1:T(8,128)(2,1)S(1)} %fusion.12), channel_id=1, source_target_pairs={{0,2},{2,0},{4,6},{6,4},{8,10},{10,8},{12,14},{14,12},{1,3},{3,1},... | collective-permute-start | bytes 405512 | tf_op jit(solution)/shard_map/ppermute | solution.py:46
  12.7 4.7 %collective-permute-done.1 = bf16[528,128]{0,1:T(8,128)(2,1)S(1)} collective-permute-done((bf16[528,128]{0,1:T(8,128)(2,1)S(1)}, bf16[528,128]{0,1:T(8,128)(2,1)S(1)}, u32[]{:S(2)}, u32[]{:S(2)}) %collective-permute-start.1) | collective-permute-done | bytes 135200 | tf_op jit(solution)/shard_map/ppermute | solution.py:46
  17.5 5.7 %collective-permute-start.2 = (bf16[2,528,128]{1,2,0:T(8,128)(2,1)S(1)}, bf16[2,528,128]{1,2,0:T(8,128)(2,1)S(1)}, u32[]{:S(2)}, u32[]{:S(2)}) collective-permute-start(bf16[2,528,128]{1,2,0:T(8,128)(2,1)S(1)} %pad_maximum_fusion.4), channel_id=1, source_target_pairs={{0,12},{2,14},{1,13},{3,15},{16,28},{18,30},{17,29},{19,31}} | collective-permute-start | bytes 811016 | tf_op jit(solution)/shard_map/ppermute | solution.py:19
  23.2 1.3 collective-permute-start.3
  24.6 2.5 collective-permute-start.4
  27.1 1.3 collective-permute-start.5
  28.4 1.3 collective-permute-start.6
  29.7 1.8 collective-permute-done.2
  31.5 1.3 collective-permute-start.7
  32.8 5.7 %collective-permute-done.3 = bf16[2,528,128]{1,2,0:T(8,128)(2,1)S(1)} collective-permute-done((bf16[2,528,128]{1,2,0:T(8,128)(2,1)S(1)}, bf16[2,528,128]{1,2,0:T(8,128)(2,1)S(1)}, u32[]{:S(2)}, u32[]{:S(2)}) %collective-permute-start.3) | collective-permute-done | bytes 270368 | tf_op jit(solution)/shard_map/ppermute | solution.py:19
  38.5 5.5 %collective-permute-done.4 = bf16[2,528,128]{1,2,0:T(8,128)(2,1)S(1)} collective-permute-done((bf16[2,528,128]{1,2,0:T(8,128)(2,1)S(1)}, bf16[2,528,128]{1,2,0:T(8,128)(2,1)S(1)}, u32[]{:S(2)}, u32[]{:S(2)}) %collective-permute-start.4) | collective-permute-done | bytes 270368 | tf_op jit(solution)/shard_map/ppermute | solution.py:19
  44.2 14.2 %collective-permute-done.6 = bf16[2,528,128]{1,2,0:T(8,128)(2,1)S(1)} collective-permute-done((bf16[2,528,128]{1,2,0:T(8,128)(2,1)S(1)}, bf16[2,528,128]{1,2,0:T(8,128)(2,1)S(1)}, u32[]{:S(2)}, u32[]{:S(2)}) %collective-permute-start.6) | collective-permute-done | bytes 270368 | tf_op jit(solution)/shard_map/ppermute | solution.py:19
  58.5 0.1 constant_dynamic-slice_fusion.3
  58.6 0.8 copy.31
  59.4 0.1 collective-permute-start.8
  59.5 0.1 pad.17.clone
  59.6 2.7 %collective-permute-done.8 = bf16[8,528,128]{2,1,0:T(8,128)(2,1)} collective-permute-done((bf16[8,528,128]{2,1,0:T(8,128)(2,1)S(1)}, bf16[8,528,128]{2,1,0:T(8,128)(2,1)}, u32[]{:S(2)}, u32[]{:S(2)}) %collective-permute-start.8) | collective-permute-done | bytes 1081376 | tf_op jit(solution)/shard_map/ppermute | solution.py:63
  62.3 1.4 broadcast_select_fusion.2
  63.7 0.2 pad_maximum_fusion.2
  63.9 0.4 fusion.23
  64.3 0.2 slice_bitcast_fusion.1
  64.5 0.8 copy-done.4
  65.3 0.1 slice_add_fusion
  65.5 0.8 slice_convert_fusion.1
  66.3 1.3 collective-permute-start.10
  67.6 6.5 %collective-permute-start.9 = (bf16[512,4096]{1,0:T(8,128)(2,1)}, bf16[512,4096]{1,0:T(8,128)(2,1)}, u32[]{:S(2)}, u32[]{:S(2)}) collective-permute-start(bf16[512,4096]{1,0:T(8,128)(2,1)} %param.12), channel_id=1, source_target_pairs={{0,2},{2,4},{4,6},{6,8},{8,10},{10,12},{12,14},{1,3},{3,5},{5,7},{... | collective-permute-start | bytes 12582920 | tf_op jit(solution)/shard_map/ppermute | solution.py:19
  74.1 0.1 pad_bitcast_fusion.2
  74.2 0.1 pad_bitcast_fusion.3
  74.4 0.1 fusion.26
  74.5 0.1 pad_maximum_fusion.7
  74.6 11.8 %exponential_multiply_fusion = f32[8,3,512,512]{3,2,1,0:T(8,128)} fusion(f32[8,3]{1,0:T(8,128)S(1)} %pad_maximum_fusion.7, f32[8,3,512]{2,1,0:T(4,128)S(1)} %copy.35, f32[8,512]{1,0:T(8,128)S(1)} %bitcast.109, bf16[8,528,256]{2,1,0:T(8,128)(2,1)} %copy-done.4, bf16[8,1,512,128]{3,2,0,1:T(8,128)(2,1)S(1)} %pad_bitcast_fusion.2, ...), kind=kOutput, calls=%fused_computation.13 | convolution fusion | flops 1651507200 | bytes 29425760 | tf_op jit(solution)/shard_map/bkjp,bip->bkji/dot_general | solution.py:105
  86.4 70.8 %while.14 = (s32[]{:T(128)}, f32[8,512]{1,0:T(8,128)S(1)}, f32[8,3,512]{2,0,1:T(8,128)}, f32[8,3,512,512]{3,2,1,0:T(8,128)}, s32[]{:T(128)}, /*index=5*/s32[]{:T(128)}) while((s32[]{:T(128)}, f32[8,512]{1,0:T(8,128)S(1)}, f32[8,3,512]{2,0,1:T(8,128)}, f32[8,3,512,512]{3,2,1,0:T(8,128)}, s32[]{:T(128)}, /*index=5*/s32[]{:T(128)}) %tuple.48), condition=%wide.region_6.7_spmd.clone, body=%wide.region_3.6_spmd.clone.sunk | while | flops 25194500 | bytes 151912576 | solution.py:124
  86.4 9.6 %multiply_reduce_fusion.6 = f32[8,3,512]{2,1,0:T(4,128)S(1)} fusion(f32[8,3,512,512]{3,2,1,0:T(8,128)} %get-tuple-element.144, f32[8,512]{1,0:T(8,128)S(1)} %broadcast_select_fusion.5), kind=kLoop, calls=%fused_computation.1.clone.1 | loop fusion | flops 12570624 | bytes 25231360 | tf_op jit(solution)/shard_map/while/body/eval_jaxpr/reduce_sum | solution.py:113
  96.2 5.6 %copy-done.2 = f32[8,3,512,512]{3,2,1,0:T(8,128)S(1)} copy-done((f32[8,3,512,512]{3,2,1,0:T(8,128)S(1)}, f32[8,3,512,512]{3,2,1,0:T(8,128)}, u32[]{:S(2)}) %copy-start.2) | copy-done | bytes 25165848 | tf_op jit(solution)/shard_map/while
  101.8 2.2 multiply_reduce_fusion.7
  104.1 9.6 %multiply_reduce_fusion.6 = f32[8,3,512]{2,1,0:T(4,128)S(1)} fusion(f32[8,3,512,512]{3,2,1,0:T(8,128)} %get-tuple-element.144, f32[8,512]{1,0:T(8,128)S(1)} %broadcast_select_fusion.5), kind=kLoop, calls=%fused_computation.1.clone.1 | loop fusion | flops 12570624 | bytes 25231360 | tf_op jit(solution)/shard_map/while/body/eval_jaxpr/reduce_sum | solution.py:113
  113.9 5.6 %copy-done.2 = f32[8,3,512,512]{3,2,1,0:T(8,128)S(1)} copy-done((f32[8,3,512,512]{3,2,1,0:T(8,128)S(1)}, f32[8,3,512,512]{3,2,1,0:T(8,128)}, u32[]{:S(2)}) %copy-start.2) | copy-done | bytes 25165848 | tf_op jit(solution)/shard_map/while
  119.5 2.2 multiply_reduce_fusion.7
  121.8 9.6 %multiply_reduce_fusion.6 = f32[8,3,512]{2,1,0:T(4,128)S(1)} fusion(f32[8,3,512,512]{3,2,1,0:T(8,128)} %get-tuple-element.144, f32[8,512]{1,0:T(8,128)S(1)} %broadcast_select_fusion.5), kind=kLoop, calls=%fused_computation.1.clone.1 | loop fusion | flops 12570624 | bytes 25231360 | tf_op jit(solution)/shard_map/while/body/eval_jaxpr/reduce_sum | solution.py:113
  131.6 5.6 %copy-done.2 = f32[8,3,512,512]{3,2,1,0:T(8,128)S(1)} copy-done((f32[8,3,512,512]{3,2,1,0:T(8,128)S(1)}, f32[8,3,512,512]{3,2,1,0:T(8,128)}, u32[]{:S(2)}) %copy-start.2) | copy-done | bytes 25165848 | tf_op jit(solution)/shard_map/while
  137.2 2.2 multiply_reduce_fusion.7
  139.5 9.6 %multiply_reduce_fusion.6 = f32[8,3,512]{2,1,0:T(4,128)S(1)} fusion(f32[8,3,512,512]{3,2,1,0:T(8,128)} %get-tuple-element.144, f32[8,512]{1,0:T(8,128)S(1)} %broadcast_select_fusion.5), kind=kLoop, calls=%fused_computation.1.clone.1 | loop fusion | flops 12570624 | bytes 25231360 | tf_op jit(solution)/shard_map/while/body/eval_jaxpr/reduce_sum | solution.py:113
  149.3 5.6 %copy-done.2 = f32[8,3,512,512]{3,2,1,0:T(8,128)S(1)} copy-done((f32[8,3,512,512]{3,2,1,0:T(8,128)S(1)}, f32[8,3,512,512]{3,2,1,0:T(8,128)}, u32[]{:S(2)}) %copy-start.2) | copy-done | bytes 25165848 | tf_op jit(solution)/shard_map/while
  154.9 2.2 multiply_reduce_fusion.7
  157.2 3.9 %constant_dynamic-slice_fusion.1 = f32[1,3,512,512]{3,2,1,0:T(8,128)} fusion(f32[8,3,512,512]{3,2,1,0:T(8,128)} %get-tuple-element.147, s32[]{:T(128)S(6)} %select_n.109), kind=kLoop, calls=%fused_computation.94 | loop fusion | bytes 6291460 | tf_op jit(solution)/shard_map/jit(dynamic_index_in_dim)/dynamic_slice | solution.py:130
  161.1 3.5 %copy.36 = f32[1,3,512,512]{2,3,1,0:T(8,128)} copy(f32[1,3,512,512]{3,2,1,0:T(8,128)} %constant_dynamic-slice_fusion.1) | data formatting | bytes 6291456 | tf_op jit(solution)/shard_map/jit(dynamic_index_in_dim)/dynamic_slice | solution.py:130
  164.6 0.8 constant_dynamic-slice_fusion
  165.4 2.4 fusion.4
  167.8 1.1 slice_bitcast_fusion.sides_ref
  169.0 5.7 %fusion.8.center_ref = f32[512,4096]{1,0:T(8,128)} fusion(bf16[512,4096]{1,0:T(8,128)(2,1)S(1)} %copy-done.3, bf16[3,512,512]{1,2,0:T(8,128)(2,1)S(1)} %fusion.4), kind=kOutput, calls=%fused_computation.29 | convolution fusion | flops 2147483648 | bytes 13107200 | tf_op jit(solution)/shard_map/dot_general | solution.py:135
  174.6 76.3 %collective-permute-done.9.left_ref = bf16[512,4096]{1,0:T(8,128)(2,1)} collective-permute-done((bf16[512,4096]{1,0:T(8,128)(2,1)}, bf16[512,4096]{1,0:T(8,128)(2,1)}, u32[]{:S(2)}, u32[]{:S(2)}) %collective-permute-start.9) | collective-permute-done | bytes 4194336 | tf_op jit(solution)/shard_map/ppermute | solution.py:19
  250.9 12.5 %shard_map.73 = bf16[512,4096]{1,0:T(8,128)(2,1)} custom-call(bf16[2,512,512]{2,1,0:T(8,128)(2,1)} %slice_bitcast_fusion.sides_ref, bf16[512,4096]{1,0:T(8,128)(2,1)} %collective-permute-done.9.left_ref, bf16[512,4096]{1,0:T(8,128)(2,1)} %collective-permute-done.10.right_ref, f32[512,4096]{1,0:T(8,128)} %fusion.8.center_ref), custom_call_target="tpu_custom_call" | custom-call | flops 4294967296 | bytes 22020096 | tf_op jit(solution)/shard_map/pallas_call | solution.py:152
  (110 shorter events, 1.4 us)
Async XLA Ops:
  0.0 1.6 copy-start
  0.0 3.5 %copy-start.6 = (bf16[4096,128]{1,0:T(8,128)(2,1)S(1)}, bf16[4096,128]{1,0:T(8,128)(2,1)}, u32[]{:S(2)}) copy-start(bf16[4096,128]{1,0:T(8,128)(2,1)} %param.14) | copy-start | bytes 3145732
  3.5 4.3 %copy-start.7 = (s32[512]{0:T(512)S(1)}, s32[512]{0:T(512)}, u32[]{:S(2)}) copy-start(s32[512]{0:T(512)} %param.16) | copy-start | bytes 6148
  3.5 4.3 %copy-start.8 = (s32[512]{0:T(512)S(1)}, s32[512]{0:T(512)}, u32[]{:S(2)}) copy-start(s32[512]{0:T(512)} %param.15) | copy-start | bytes 6148
  3.5 4.6 %copy-start.9 = (s32[1,2]{1,0:T(1,128)S(1)}, s32[1,2]{1,0:T(1,128)}, u32[]{:S(2)}) copy-start(s32[1,2]{1,0:T(1,128)} %param.17) | copy-start | bytes 28
  7.3 2.3 collective-permute-start
  9.9 7.4 %collective-permute-start.1 = (bf16[528,128]{0,1:T(8,128)(2,1)S(1)}, bf16[528,128]{0,1:T(8,128)(2,1)S(1)}, u32[]{:S(2)}, u32[]{:S(2)}) collective-permute-start(bf16[528,128]{0,1:T(8,128)(2,1)S(1)} %fusion.12), channel_id=1, source_target_pairs={{0,2},{2,0},{4,6},{6,4},{8,10},{10,8},{12,14},{14,12},{1,3},{3,1},... | collective-permute-start | bytes 405512 | tf_op jit(solution)/shard_map/ppermute | solution.py:46
  17.5 14.0 %collective-permute-start.2 = (bf16[2,528,128]{1,2,0:T(8,128)(2,1)S(1)}, bf16[2,528,128]{1,2,0:T(8,128)(2,1)S(1)}, u32[]{:S(2)}, u32[]{:S(2)}) collective-permute-start(bf16[2,528,128]{1,2,0:T(8,128)(2,1)S(1)} %pad_maximum_fusion.4), channel_id=1, source_target_pairs={{0,12},{2,14},{1,13},{3,15},{16,28},{18,30},{17,29},{19,31}} | collective-permute-start | bytes 811016 | tf_op jit(solution)/shard_map/ppermute | solution.py:19
  23.2 15.2 %collective-permute-start.3 = (bf16[2,528,128]{1,2,0:T(8,128)(2,1)S(1)}, bf16[2,528,128]{1,2,0:T(8,128)(2,1)S(1)}, u32[]{:S(2)}, u32[]{:S(2)}) collective-permute-start(bf16[2,528,128]{1,2,0:T(8,128)(2,1)S(1)} %pad_maximum_fusion.4), channel_id=1, source_target_pairs={{0,8},{2,10},{4,12},{6,14},{1,9},{3,11},{5,13},{7,15},{16,24},{18,... | collective-permute-start | bytes 811016 | tf_op jit(solution)/shard_map/ppermute | solution.py:19
  24.6 19.4 %collective-permute-start.4 = (bf16[2,528,128]{1,2,0:T(8,128)(2,1)S(1)}, bf16[2,528,128]{1,2,0:T(8,128)(2,1)S(1)}, u32[]{:S(2)}, u32[]{:S(2)}) collective-permute-start(bf16[2,528,128]{1,2,0:T(8,128)(2,1)S(1)} %pad_maximum_fusion.4), channel_id=1, source_target_pairs={{0,4},{2,6},{4,8},{6,10},{8,12},{10,14},{1,5},{3,7},{5,9},{7,11},{... | collective-permute-start | bytes 811016 | tf_op jit(solution)/shard_map/ppermute | solution.py:19
  27.1 17.1 %collective-permute-start.5 = (bf16[2,528,128]{1,2,0:T(8,128)(2,1)S(1)}, bf16[2,528,128]{1,2,0:T(8,128)(2,1)S(1)}, u32[]{:S(2)}, u32[]{:S(2)}) collective-permute-start(bf16[2,528,128]{1,2,0:T(8,128)(2,1)S(1)} %pad_maximum_fusion.4), channel_id=1, source_target_pairs={{4,0},{6,2},{8,4},{10,6},{12,8},{14,10},{5,1},{7,3},{9,5},{11,7},{... | collective-permute-start | bytes 811016 | tf_op jit(solution)/shard_map/ppermute | solution.py:19
  28.4 30.0 %collective-permute-start.6 = (bf16[2,528,128]{1,2,0:T(8,128)(2,1)S(1)}, bf16[2,528,128]{1,2,0:T(8,128)(2,1)S(1)}, u32[]{:S(2)}, u32[]{:S(2)}) collective-permute-start(bf16[2,528,128]{1,2,0:T(8,128)(2,1)S(1)} %pad_maximum_fusion.4), channel_id=1, source_target_pairs={{8,0},{10,2},{12,4},{14,6},{9,1},{11,3},{13,5},{15,7},{24,16},{26,... | collective-permute-start | bytes 811016 | tf_op jit(solution)/shard_map/ppermute | solution.py:19
  31.5 26.9 %collective-permute-start.7 = (bf16[2,528,128]{1,2,0:T(8,128)(2,1)S(1)}, bf16[2,528,128]{1,2,0:T(8,128)(2,1)S(1)}, u32[]{:S(2)}, u32[]{:S(2)}) collective-permute-start(bf16[2,528,128]{1,2,0:T(8,128)(2,1)S(1)} %pad_maximum_fusion.4), channel_id=1, source_target_pairs={{12,0},{14,2},{13,1},{15,3},{28,16},{30,18},{29,17},{31,19}} | collective-permute-start | bytes 811016 | tf_op jit(solution)/shard_map/ppermute | solution.py:19
  59.4 2.9 %collective-permute-start.8 = (bf16[8,528,128]{2,1,0:T(8,128)(2,1)S(1)}, bf16[8,528,128]{2,1,0:T(8,128)(2,1)}, u32[]{:S(2)}, u32[]{:S(2)}) collective-permute-start(bf16[8,528,128]{2,1,0:T(8,128)(2,1)S(1)} %bitcast.102), channel_id=1, source_target_pairs={{0,1},{1,0},{2,3},{3,2},{4,5},{5,4},{6,7},{7,6},{8,9},{9,8},{10,11... | collective-permute-start | bytes 3244040 | tf_op jit(solution)/shard_map/ppermute | solution.py:63
  63.9 1.3 copy-start.4
  66.3 108.3 %collective-permute-start.10 = (bf16[512,4096]{1,0:T(8,128)(2,1)}, bf16[512,4096]{1,0:T(8,128)(2,1)}, u32[]{:S(2)}, u32[]{:S(2)}) collective-permute-start(bf16[512,4096]{1,0:T(8,128)(2,1)} %param.12), channel_id=1, source_target_pairs={{2,0},{4,2},{6,4},{8,6},{10,8},{12,10},{14,12},{3,1},{5,3},{7,5},{... | collective-permute-start | bytes 12582920 | tf_op jit(solution)/shard_map/ppermute | solution.py:19
  67.6 183.3 %collective-permute-start.9 = (bf16[512,4096]{1,0:T(8,128)(2,1)}, bf16[512,4096]{1,0:T(8,128)(2,1)}, u32[]{:S(2)}, u32[]{:S(2)}) collective-permute-start(bf16[512,4096]{1,0:T(8,128)(2,1)} %param.12), channel_id=1, source_target_pairs={{0,2},{2,4},{4,6},{6,8},{8,10},{10,12},{12,14},{1,3},{3,5},{5,7},{... | collective-permute-start | bytes 12582920 | tf_op jit(solution)/shard_map/ppermute | solution.py:19
  86.4 15.4 %copy-start.2 = (f32[8,3,512,512]{3,2,1,0:T(8,128)S(1)}, f32[8,3,512,512]{3,2,1,0:T(8,128)}, u32[]{:S(2)}) copy-start(f32[8,3,512,512]{3,2,1,0:T(8,128)} %get-tuple-element.144) | copy-start | bytes 75497472 | tf_op jit(solution)/shard_map/while
  96.2 7.9 %copy-start.5 = (f32[8,3,512]{2,0,1:T(8,128)}, f32[8,3,512]{2,0,1:T(8,128)S(1)}, u32[]{:S(2)}) copy-start(f32[8,3,512]{2,0,1:T(8,128)S(1)} %pad_maximum_fusion.11) | copy-start | bytes 147460 | tf_op jit(solution)/shard_map/while
  104.1 15.4 %copy-start.2 = (f32[8,3,512,512]{3,2,1,0:T(8,128)S(1)}, f32[8,3,512,512]{3,2,1,0:T(8,128)}, u32[]{:S(2)}) copy-start(f32[8,3,512,512]{3,2,1,0:T(8,128)} %get-tuple-element.144) | copy-start | bytes 75497472 | tf_op jit(solution)/shard_map/while
  113.9 7.9 %copy-start.5 = (f32[8,3,512]{2,0,1:T(8,128)}, f32[8,3,512]{2,0,1:T(8,128)S(1)}, u32[]{:S(2)}) copy-start(f32[8,3,512]{2,0,1:T(8,128)S(1)} %pad_maximum_fusion.11) | copy-start | bytes 147460 | tf_op jit(solution)/shard_map/while
  121.8 15.4 %copy-start.2 = (f32[8,3,512,512]{3,2,1,0:T(8,128)S(1)}, f32[8,3,512,512]{3,2,1,0:T(8,128)}, u32[]{:S(2)}) copy-start(f32[8,3,512,512]{3,2,1,0:T(8,128)} %get-tuple-element.144) | copy-start | bytes 75497472 | tf_op jit(solution)/shard_map/while
  131.6 7.9 %copy-start.5 = (f32[8,3,512]{2,0,1:T(8,128)}, f32[8,3,512]{2,0,1:T(8,128)S(1)}, u32[]{:S(2)}) copy-start(f32[8,3,512]{2,0,1:T(8,128)S(1)} %pad_maximum_fusion.11) | copy-start | bytes 147460 | tf_op jit(solution)/shard_map/while
  139.5 15.4 %copy-start.2 = (f32[8,3,512,512]{3,2,1,0:T(8,128)S(1)}, f32[8,3,512,512]{3,2,1,0:T(8,128)}, u32[]{:S(2)}) copy-start(f32[8,3,512,512]{3,2,1,0:T(8,128)} %get-tuple-element.144) | copy-start | bytes 75497472 | tf_op jit(solution)/shard_map/while
  149.3 7.9 %copy-start.5 = (f32[8,3,512]{2,0,1:T(8,128)}, f32[8,3,512]{2,0,1:T(8,128)S(1)}, u32[]{:S(2)}) copy-start(f32[8,3,512]{2,0,1:T(8,128)S(1)} %pad_maximum_fusion.11) | copy-start | bytes 147460 | tf_op jit(solution)/shard_map/while
  165.4 3.5 %copy-start.3 = (bf16[512,4096]{1,0:T(8,128)(2,1)S(1)}, bf16[512,4096]{1,0:T(8,128)(2,1)}, u32[]{:S(2)}) copy-start(bf16[512,4096]{1,0:T(8,128)(2,1)} %param.12) | copy-start | bytes 12582916
  250.9 12.5 %copy-start.1 = (bf16[512,2048]{1,0:T(8,128)(2,1)S(1)}, bf16[512,2048]{1,0:T(8,128)(2,1)}, u32[]{:S(2)}) copy-start(bf16[512,2048]{1,0:T(8,128)(2,1)} %param.11) | copy-start | bytes 6291460

commit v8 on v6

--- a/solution.py
+++ b/solution.py
@@ -58,7 +58,8 @@
     half = packed.shape[1] // 2
     core = lax.axis_index("tgrp")
     mine = lax.dynamic_slice_in_dim(packed, core * half, half, 1)
-    got = gather_seq(mine)
+    n = lax.axis_size("seq")
+    got = lax.all_to_all(jnp.broadcast_to(mine, (n,) + mine.shape), "seq", 0, 0, tiled=False)
     theirs = lax.ppermute(got, "tgrp", [(0, 1), (1, 0)])
     first = jnp.where(core == 0, got, theirs)
     second = jnp.where(core == 0, theirs, got)

time: 263 us -> 247 us (0.939)
  blocking collectives: 0 us -> 34.5 us
  waiting for transfers between devices: 122 us -> 90.6 us
  starting transfers between devices: 23.6 us -> 6.56 us
    all_to_all x0 -> x1, blocking collectives: none -> 34.5 us  [gather_halves(): lax.all_to_all(jnp.broadcast_to(mine, (n,) + mine.shape), 'seq', 0, 0, ti...]
    ppermute x8 -> x2, waiting for transfers between devices: 115 us -> 87.9 us  [shifted(): return lax.ppermute(block, axis, route)]
    ppermute x8 -> x2, starting transfers between devices: 20.3 us -> 6.03 us  [shifted(): return lax.ppermute(block, axis, route)]
    ppermute x1 -> x0, waiting for transfers between devices: 4.73 us -> none  [gather_seq(): partner = lax.ppermute(block, 'seq', [(i, i ^ 1) for i in range(n)])]
    ppermute x1 -> x0, starting transfers between devices: 2.72 us -> none  [gather_seq(): partner = lax.ppermute(block, 'seq', [(i, i ^ 1) for i in range(n)])]
  transfers between devices with their start and end apart: 11 -> 4, of which waited for: 7 -> 2; matrix products, arithmetic and copies ran while one was open for 28% -> 29% of each run, Pallas kernels for 0% -> 0%
where the time goes in v8:
time: 247 us
  waiting for transfers between devices  90.6 us (37%)
  other arithmetic  54.2 us (22%)
  blocking collectives  34.5 us (14%)
  matrix products  32.1 us (13%)
  local copies, waits for them, and re-layouts  27.9 us (11%)
  starting transfers between devices  6.56 us (3%)
    ppermute x2, waiting for transfers between devices, shifted(): return lax.ppermute(block, axis, route)  87.9 us
    reduce_sum x4, other arithmetic, iterate(): partial_cols = jnp.sum(row_scale[:, None, None, :] * kernel, axis=3)  38.4 us
    all_to_all x1, blocking collectives, gather_halves(): lax.all_to_all(jnp.broadcast_to(mine, (n,) + mine.shape), 'seq', 0, 0, ti...  34.5 us
    while x16, local copies, waits for them, and re-layouts  22.4 us
    dot_general x1, matrix products, body_local(): jnp.einsum('bkjp,bip->bkji', beside(t_unit), s_unit, preferred_element_ty...  11.8 us
    reduce_sum x4, other arithmetic, iterate(): row_scale = 1.0 / jnp.sum(kernel * col_scale[:, :, :, None], axis=(1, 2))  8.94 us
    dot_general x1, matrix products, body_local(): lax.dot_general(plan[2], right_rows, along_j, preferred_element_type=jnp....  7.35 us
    ppermute x2, starting transfers between devices, shifted(): return lax.ppermute(block, axis, route)  6.03 us
  transfers between devices with their start and end apart: 4, of which 2 were waited for; matrix products, arithmetic and copies ran while one was open for 29% of the time, Pallas kernels for 0%

profile of v8, /device:TPU:0, one launch (start us, length us, event | category | flops | bytes accessed | tf_op | source)
XLA Modules:
  0.0 246.8 jit_solution(4882567834419301606)
XLA Ops:
  0.0 1.6 copy-done
  1.6 1.9 fusion.28
  3.5 0.0 copy-start.6
  3.5 0.0 copy-start.7
  3.5 0.0 copy-start.8
  3.5 4.0 %fusion.29 = f32[512,128]{0,1:T(8,128)S(1)} fusion(bf16[512,4096]{1,0:T(8,128)(2,1)} %param.12, bf16[4096,128]{1,0:T(8,128)(2,1)} %param.14), kind=kOutput, calls=%fused_computation.98 | convolution fusion | flops 536870912 | bytes 5505024 | tf_op jit(solution)/shard_map/dot_general | solution.py:78
  7.6 0.5 collective-permute-start
  8.1 0.1 fusion.17
  8.2 0.1 copy.29
  8.4 0.1 copy.28
  8.5 0.1 pad.31.clone
  8.6 0.6 compare_reduce_fusion
  9.2 0.6 broadcast_select_fusion.3
  9.8 0.0 collective-permute-done
  9.9 0.1 fusion.21
  9.9 0.1 multiply_reduce_fusion.2
  10.0 0.1 multiply_convert_fusion
  10.1 0.1 fusion.13
  10.2 0.1 copy.30
  10.4 0.1 broadcast_in_dim.8
  10.5 34.5 %all_to_all.5 = bf16[8,528,128]{2,1,0:T(8,128)(2,1)S(1)} all-to-all(bf16[8,528,128]{2,1,0:T(8,128)(2,1)S(1)} %broadcast_in_dim.8), channel_id=1, replica_groups=mesh['groups'=2,'seq'=8,'tgrp'=2] {'seq'}, dimensions={0} | all-to-all | bytes 2162688 | tf_op jit(solution)/shard_map/all_to_all | solution.py:62
  45.0 0.0 collective-permute-start.1
  45.0 0.1 pad.17.clone
  45.1 2.8 %collective-permute-done.1 = bf16[8,528,128]{2,1,0:T(8,128)(2,1)} collective-permute-done((bf16[8,528,128]{2,1,0:T(8,128)(2,1)S(1)}, bf16[8,528,128]{2,1,0:T(8,128)(2,1)}, u32[]{:S(2)}, u32[]{:S(2)}) %collective-permute-start.1) | collective-permute-done | bytes 1081376 | tf_op jit(solution)/shard_map/ppermute | solution.py:63
  47.8 1.4 broadcast_select_fusion.2
  49.2 0.2 pad_maximum_fusion.2
  49.5 0.0 copy-start.4
  49.5 0.4 fusion.24
  49.9 0.2 slice_bitcast_fusion
  50.1 0.8 copy-done.4
  50.8 0.1 reshape.405
  50.9 0.1 slice_add_fusion
  51.1 0.8 slice_convert_fusion.1
  51.8 4.6 %collective-permute-start.2 = (bf16[512,4096]{1,0:T(8,128)(2,1)}, bf16[512,4096]{1,0:T(8,128)(2,1)}, u32[]{:S(2)}, u32[]{:S(2)}) collective-permute-start(bf16[512,4096]{1,0:T(8,128)(2,1)} %param.12), channel_id=1, source_target_pairs={{0,2},{2,4},{4,6},{6,8},{8,10},{10,12},{12,14},{1,3},{3,5},{5,7},{... | collective-permute-start | bytes 12582920 | tf_op jit(solution)/shard_map/ppermute | solution.py:18
  56.4 1.5 collective-permute-start.3
  57.9 0.1 pad_bitcast_fusion.2
  58.0 0.1 pad_bitcast_fusion.3
  58.2 0.1 fusion.27
  58.3 0.1 pad_maximum_fusion.6
  58.3 11.8 %exponential_multiply_fusion = f32[8,3,512,512]{3,2,1,0:T(8,128)} fusion(f32[8,3]{1,0:T(8,128)S(1)} %pad_maximum_fusion.6, f32[8,3,512]{2,1,0:T(4,128)S(1)} %copy.34, f32[8,512]{1,0:T(8,128)S(1)} %bitcast.93, bf16[8,528,256]{2,1,0:T(8,128)(2,1)} %copy-done.4, bf16[8,1,512,128]{3,2,0,1:T(8,128)(2,1)S(1)} %pad_bitcast_fusion.2, ...), kind=kOutput, calls=%fused_computation.13 | convolution fusion | flops 1651507200 | bytes 29425760 | tf_op jit(solution)/shard_map/bkjp,bip->bkji/dot_general | solution.py:105
  70.1 70.8 %while.14 = (s32[]{:T(128)}, f32[8,512]{1,0:T(8,128)S(1)}, f32[8,3,512]{2,0,1:T(8,128)}, f32[8,3,512,512]{3,2,1,0:T(8,128)}, s32[]{:T(128)}, /*index=5*/s32[]{:T(128)}) while((s32[]{:T(128)}, f32[8,512]{1,0:T(8,128)S(1)}, f32[8,3,512]{2,0,1:T(8,128)}, f32[8,3,512,512]{3,2,1,0:T(8,128)}, s32[]{:T(128)}, /*index=5*/s32[]{:T(128)}) %tuple.47), condition=%wide.region_6.7_spmd.clone, body=%wide.region_3.6_spmd.clone.sunk | while | flops 25194500 | bytes 151912576 | solution.py:124
  70.1 9.6 %multiply_reduce_fusion.6 = f32[8,3,512]{2,1,0:T(4,128)S(1)} fusion(f32[8,3,512,512]{3,2,1,0:T(8,128)} %get-tuple-element.142, f32[8,512]{1,0:T(8,128)S(1)} %broadcast_select_fusion.5), kind=kLoop, calls=%fused_computation.1.clone.1 | loop fusion | flops 12570624 | bytes 25231360 | tf_op jit(solution)/shard_map/while/body/eval_jaxpr/reduce_sum | solution.py:113
  79.9 5.6 %copy-done.2 = f32[8,3,512,512]{3,2,1,0:T(8,128)S(1)} copy-done((f32[8,3,512,512]{3,2,1,0:T(8,128)S(1)}, f32[8,3,512,512]{3,2,1,0:T(8,128)}, u32[]{:S(2)}) %copy-start.2) | copy-done | bytes 25165848 | tf_op jit(solution)/shard_map/while
  85.5 2.2 multiply_reduce_fusion.7
  87.8 9.6 %multiply_reduce_fusion.6 = f32[8,3,512]{2,1,0:T(4,128)S(1)} fusion(f32[8,3,512,512]{3,2,1,0:T(8,128)} %get-tuple-element.142, f32[8,512]{1,0:T(8,128)S(1)} %broadcast_select_fusion.5), kind=kLoop, calls=%fused_computation.1.clone.1 | loop fusion | flops 12570624 | bytes 25231360 | tf_op jit(solution)/shard_map/while/body/eval_jaxpr/reduce_sum | solution.py:113
  97.6 0.0 copy-start.5
  97.6 5.6 %copy-done.2 = f32[8,3,512,512]{3,2,1,0:T(8,128)S(1)} copy-done((f32[8,3,512,512]{3,2,1,0:T(8,128)S(1)}, f32[8,3,512,512]{3,2,1,0:T(8,128)}, u32[]{:S(2)}) %copy-start.2) | copy-done | bytes 25165848 | tf_op jit(solution)/shard_map/while
  103.2 2.2 multiply_reduce_fusion.7
  105.5 0.0 copy-done.5
  105.6 9.6 %multiply_reduce_fusion.6 = f32[8,3,512]{2,1,0:T(4,128)S(1)} fusion(f32[8,3,512,512]{3,2,1,0:T(8,128)} %get-tuple-element.142, f32[8,512]{1,0:T(8,128)S(1)} %broadcast_select_fusion.5), kind=kLoop, calls=%fused_computation.1.clone.1 | loop fusion | flops 12570624 | bytes 25231360 | tf_op jit(solution)/shard_map/while/body/eval_jaxpr/reduce_sum | solution.py:113
  115.3 5.6 %copy-done.2 = f32[8,3,512,512]{3,2,1,0:T(8,128)S(1)} copy-done((f32[8,3,512,512]{3,2,1,0:T(8,128)S(1)}, f32[8,3,512,512]{3,2,1,0:T(8,128)}, u32[]{:S(2)}) %copy-start.2) | copy-done | bytes 25165848 | tf_op jit(solution)/shard_map/while
  120.9 2.2 multiply_reduce_fusion.7
  123.3 9.6 %multiply_reduce_fusion.6 = f32[8,3,512]{2,1,0:T(4,128)S(1)} fusion(f32[8,3,512,512]{3,2,1,0:T(8,128)} %get-tuple-element.142, f32[8,512]{1,0:T(8,128)S(1)} %broadcast_select_fusion.5), kind=kLoop, calls=%fused_computation.1.clone.1 | loop fusion | flops 12570624 | bytes 25231360 | tf_op jit(solution)/shard_map/while/body/eval_jaxpr/reduce_sum | solution.py:113
  133.1 5.6 %copy-done.2 = f32[8,3,512,512]{3,2,1,0:T(8,128)S(1)} copy-done((f32[8,3,512,512]{3,2,1,0:T(8,128)S(1)}, f32[8,3,512,512]{3,2,1,0:T(8,128)}, u32[]{:S(2)}) %copy-start.2) | copy-done | bytes 25165848 | tf_op jit(solution)/shard_map/while
  138.7 2.2 multiply_reduce_fusion.7
  140.9 0.0 copy-start.3
  140.9 1.0 constant_dynamic-slice_fusion
  141.9 2.5 %fusion.4 = bf16[3,512,512]{2,1,0:T(8,128)(2,1)S(1)} fusion(f32[8,3,512,512]{3,2,1,0:T(8,128)} %get-tuple-element.145, s32[]{:T(128)S(6)} %select_n.78, f32[3,512]{1,0:T(4,128)S(1)} %bitcast.91, f32[512]{0:T(512)S(1)} %bitcast.94), kind=kLoop, calls=%fused_computation.18 | loop fusion | flops 2359296 | bytes 4726788 | tf_op jit(solution)/shard_map/convert_element_type | solution.py:133
  144.4 2.5 fusion.9
  146.9 87.9 %collective-permute-done.2 = bf16[512,4096]{1,0:T(8,128)(2,1)} collective-permute-done((bf16[512,4096]{1,0:T(8,128)(2,1)}, bf16[512,4096]{1,0:T(8,128)(2,1)}, u32[]{:S(2)}, u32[]{:S(2)}) %collective-permute-start.2) | collective-permute-done | bytes 4194336 | tf_op jit(solution)/shard_map/ppermute | solution.py:18
  234.8 4.6 %fusion.8 = f32[512,4096]{1,0:T(8,128)S(1)} fusion(bf16[512,4096]{1,0:T(8,128)(2,1)} %collective-permute-done.2, bf16[3,512,512]{2,1,0:T(8,128)(2,1)S(1)} %fusion.4), kind=kOutput, calls=%fused_computation.30 | convolution fusion | flops 2147483648 | bytes 13107200 | tf_op jit(solution)/shard_map/dot_general | solution.py:136
  239.4 0.0 collective-permute-done.3
  239.4 0.0 copy-start.1
  239.4 7.4 %add_convert_fusion = bf16[512,4096]{1,0:T(8,128)(2,1)} fusion(f32[512,4096]{1,0:T(8,128)S(1)} %fusion.9, f32[512,4096]{1,0:T(8,128)S(1)} %fusion.8, bf16[512,4096]{1,0:T(8,128)(2,1)} %collective-permute-done.3, bf16[3,512,512]{2,1,0:T(8,128)(2,1)S(1)} %fusion.4), kind=kOutput, calls=%fused_computation.14 | convolution fusion | flops 2153775104 | bytes 25690112 | tf_op jit(solution)/shard_map/dot_general | solution.py:137
  (84 shorter events, 0.8 us)
Async XLA Ops:
  0.0 1.6 copy-start
  3.5 4.6 %copy-start.6 = (s32[512]{0:T(512)S(1)}, s32[512]{0:T(512)}, u32[]{:S(2)}) copy-start(s32[512]{0:T(512)} %param.16) | copy-start | bytes 6148
  3.5 4.6 %copy-start.7 = (s32[512]{0:T(512)S(1)}, s32[512]{0:T(512)}, u32[]{:S(2)}) copy-start(s32[512]{0:T(512)} %param.15) | copy-start | bytes 6148
  3.5 4.9 %copy-start.8 = (s32[1,2]{1,0:T(1,128)S(1)}, s32[1,2]{1,0:T(1,128)}, u32[]{:S(2)}) copy-start(s32[1,2]{1,0:T(1,128)} %param.17) | copy-start | bytes 28
  7.6 2.3 collective-permute-start
  45.0 2.8 %collective-permute-start.1 = (bf16[8,528,128]{2,1,0:T(8,128)(2,1)S(1)}, bf16[8,528,128]{2,1,0:T(8,128)(2,1)}, u32[]{:S(2)}, u32[]{:S(2)}) collective-permute-start(bf16[8,528,128]{2,1,0:T(8,128)(2,1)S(1)} %all_to_all.5), channel_id=1, source_target_pairs={{0,1},{1,0},{2,3},{3,2},{4,5},{5,4},{6,7},{7,6},{8,9},{9,8},{10,11... | collective-permute-start | bytes 3244040 | tf_op jit(solution)/shard_map/ppermute | solution.py:63
  49.5 1.3 copy-start.4
  51.8 182.9 %collective-permute-start.2 = (bf16[512,4096]{1,0:T(8,128)(2,1)}, bf16[512,4096]{1,0:T(8,128)(2,1)}, u32[]{:S(2)}, u32[]{:S(2)}) collective-permute-start(bf16[512,4096]{1,0:T(8,128)(2,1)} %param.12), channel_id=1, source_target_pairs={{0,2},{2,4},{4,6},{6,8},{8,10},{10,12},{12,14},{1,3},{3,5},{5,7},{... | collective-permute-start | bytes 12582920 | tf_op jit(solution)/shard_map/ppermute | solution.py:18
  56.4 183.0 %collective-permute-start.3 = (bf16[512,4096]{1,0:T(8,128)(2,1)}, bf16[512,4096]{1,0:T(8,128)(2,1)}, u32[]{:S(2)}, u32[]{:S(2)}) collective-permute-start(bf16[512,4096]{1,0:T(8,128)(2,1)} %param.12), channel_id=1, source_target_pairs={{2,0},{4,2},{6,4},{8,6},{10,8},{12,10},{14,12},{3,1},{5,3},{7,5},{... | collective-permute-start | bytes 12582920 | tf_op jit(solution)/shard_map/ppermute | solution.py:18
  70.1 15.4 %copy-start.2 = (f32[8,3,512,512]{3,2,1,0:T(8,128)S(1)}, f32[8,3,512,512]{3,2,1,0:T(8,128)}, u32[]{:S(2)}) copy-start(f32[8,3,512,512]{3,2,1,0:T(8,128)} %get-tuple-element.142) | copy-start | bytes 75497472 | tf_op jit(solution)/shard_map/while
  79.9 7.9 %copy-start.5 = (f32[8,3,512]{2,0,1:T(8,128)}, f32[8,3,512]{2,0,1:T(8,128)S(1)}, u32[]{:S(2)}) copy-start(f32[8,3,512]{2,0,1:T(8,128)S(1)} %pad_maximum_fusion.10) | copy-start | bytes 147460 | tf_op jit(solution)/shard_map/while
  87.8 15.4 %copy-start.2 = (f32[8,3,512,512]{3,2,1,0:T(8,128)S(1)}, f32[8,3,512,512]{3,2,1,0:T(8,128)}, u32[]{:S(2)}) copy-start(f32[8,3,512,512]{3,2,1,0:T(8,128)} %get-tuple-element.142) | copy-start | bytes 75497472 | tf_op jit(solution)/shard_map/while
  97.6 7.9 %copy-start.5 = (f32[8,3,512]{2,0,1:T(8,128)}, f32[8,3,512]{2,0,1:T(8,128)S(1)}, u32[]{:S(2)}) copy-start(f32[8,3,512]{2,0,1:T(8,128)S(1)} %pad_maximum_fusion.10) | copy-start | bytes 147460 | tf_op jit(solution)/shard_map/while
  105.5 15.4 %copy-start.2 = (f32[8,3,512,512]{3,2,1,0:T(8,128)S(1)}, f32[8,3,512,512]{3,2,1,0:T(8,128)}, u32[]{:S(2)}) copy-start(f32[8,3,512,512]{3,2,1,0:T(8,128)} %get-tuple-element.142) | copy-start | bytes 75497472 | tf_op jit(solution)/shard_map/while
  115.3 7.9 %copy-start.5 = (f32[8,3,512]{2,0,1:T(8,128)}, f32[8,3,512]{2,0,1:T(8,128)S(1)}, u32[]{:S(2)}) copy-start(f32[8,3,512]{2,0,1:T(8,128)S(1)} %pad_maximum_fusion.10) | copy-start | bytes 147460 | tf_op jit(solution)/shard_map/while
  123.2 15.4 %copy-start.2 = (f32[8,3,512,512]{3,2,1,0:T(8,128)S(1)}, f32[8,3,512,512]{3,2,1,0:T(8,128)}, u32[]{:S(2)}) copy-start(f32[8,3,512,512]{3,2,1,0:T(8,128)} %get-tuple-element.142) | copy-start | bytes 75497472 | tf_op jit(solution)/shard_map/while
  133.0 7.9 %copy-start.5 = (f32[8,3,512]{2,0,1:T(8,128)}, f32[8,3,512]{2,0,1:T(8,128)S(1)}, u32[]{:S(2)}) copy-start(f32[8,3,512]{2,0,1:T(8,128)S(1)} %pad_maximum_fusion.10) | copy-start | bytes 147460 | tf_op jit(solution)/shard_map/while
  140.9 3.5 %copy-start.3 = (bf16[512,4096]{1,0:T(8,128)(2,1)S(1)}, bf16[512,4096]{1,0:T(8,128)(2,1)}, u32[]{:S(2)}) copy-start(bf16[512,4096]{1,0:T(8,128)(2,1)} %param.12) | copy-start | bytes 12582916
  239.4 7.4 %copy-start.1 = (bf16[512,2048]{1,0:T(8,128)(2,1)S(1)}, bf16[512,2048]{1,0:T(8,128)(2,1)}, u32[]{:S(2)}) copy-start(bf16[512,2048]{1,0:T(8,128)(2,1)} %param.11) | copy-start | bytes 6291460

commit v9 on v8

--- a/solution.py
+++ b/solution.py
@@ -89,9 +89,8 @@
     packed = jnp.concatenate([units, extra, jnp.zeros((pad, units.shape[1]), jnp.bfloat16)], 0)
     gathered = gather_halves(packed)
 
-    teacher_rows, gathered = lax.optimization_barrier((teacher_hidden, gathered))
-    left_rows = shifted(teacher_rows, "seq", 1)
-    right_rows = shifted(teacher_rows, "seq", -1)
+    left_rows = shifted(teacher_hidden, "seq", 1)
+    right_rows = shifted(teacher_hidden, "seq", -1)
 
     s_unit = gathered[:, :rows, :proj_width]
     t_unit = gathered[:, :rows, proj_width:]

time: 247 us -> 241 us (0.976)
  waiting for transfers between devices: 90.6 us -> 82.8 us
    ppermute x2, waiting for transfers between devices: 87.9 us -> 82.8 us  [shifted(): return lax.ppermute(block, axis, route)]
    ppermute x1, waiting for transfers between devices: 2.76 us -> 0.01 us  [gather_halves(): theirs = lax.ppermute(got, 'tgrp', [(0, 1), (1, 0)])]
  transfers between devices with their start and end apart: 4 -> 4, of which waited for: 2 -> 1; matrix products, arithmetic and copies ran while one was open for 29% -> 32% of each run, Pallas kernels for 0% -> 0%
where the time goes in v9:
time: 241 us; the launch traced here: 240 us
  waiting for transfers between devices  82.8 us (34%)
  other arithmetic  53.6 us (22%)
  blocking collectives  34.5 us (14%)
  matrix products  31.8 us (13%)
  local copies, waits for them, and re-layouts  30.1 us (12%)
  starting transfers between devices  6.54 us (3%)
    ppermute x2, waiting for transfers between devices, shifted(): return lax.ppermute(block, axis, route)  82.8 us
    reduce_sum x4, other arithmetic, iterate(): partial_cols = jnp.sum(row_scale[:, None, None, :] * kernel, axis=3)  38.4 us
    all_to_all x1, blocking collectives, gather_halves(): lax.all_to_all(jnp.broadcast_to(mine, (n,) + mine.shape), 'seq', 0, 0, ti...  34.5 us
    while x16, local copies, waits for them, and re-layouts  22.4 us
    dot_general x1, matrix products, body_local(): jnp.einsum('bkjp,bip->bkji', beside(t_unit), s_unit, preferred_element_ty...  11.5 us
    reduce_sum x4, other arithmetic, iterate(): row_scale = 1.0 / jnp.sum(kernel * col_scale[:, :, :, None], axis=(1, 2))  8.94 us
    dot_general x1, matrix products, body_local(): lax.dot_general(plan[2], right_rows, along_j, preferred_element_type=jnp....  7.35 us
    ppermute x2, starting transfers between devices, shifted(): return lax.ppermute(block, axis, route)  6.02 us
  transfers between devices with their start and end apart: 4, of which 1 were waited for; matrix products, arithmetic and copies ran while one was open for 32% of the time, Pallas kernels for 0%

profile of v9, /device:TPU:0, one launch (start us, length us, event | category | flops | bytes accessed | tf_op | source)
XLA Modules:
  0.0 240.3 jit_solution(7097775989028778952)
XLA Ops:
  0.0 0.0 copy-start
  0.0 1.6 copy-done
  1.6 1.9 fusion.27
  3.5 0.0 copy-start.7
  3.5 0.0 copy-start.8
  3.5 0.0 copy-start.9
  3.5 4.0 %fusion.28 = f32[512,128]{0,1:T(8,128)S(1)} fusion(bf16[512,4096]{1,0:T(8,128)(2,1)} %param.12, bf16[4096,128]{1,0:T(8,128)(2,1)} %param.14), kind=kOutput, calls=%fused_computation.97 | convolution fusion | flops 536870912 | bytes 5505024 | tf_op jit(solution)/shard_map/dot_general | solution.py:78
  7.6 0.5 collective-permute-start
  8.1 0.0 copy-done.7
  8.1 0.1 fusion.16
  8.2 0.1 copy.29
  8.4 0.1 copy.28
  8.5 0.1 pad.31.clone
  8.6 0.6 compare_reduce_fusion
  9.2 0.6 broadcast_select_fusion.3
  9.8 0.0 collective-permute-done
  9.9 0.1 fusion.20
  9.9 0.1 multiply_reduce_fusion.2
  10.0 0.1 multiply_convert_fusion
  10.1 0.1 fusion.11
  10.2 0.1 copy.30
  10.4 0.1 broadcast_in_dim.8
  10.5 34.5 %all_to_all.5 = bf16[8,528,128]{2,1,0:T(8,128)(2,1)S(1)} all-to-all(bf16[8,528,128]{2,1,0:T(8,128)(2,1)S(1)} %broadcast_in_dim.8), channel_id=1, replica_groups=mesh['groups'=2,'seq'=8,'tgrp'=2] {'seq'}, dimensions={0} | all-to-all | bytes 2162688 | tf_op jit(solution)/shard_map/all_to_all | solution.py:62
  45.0 0.0 collective-permute-start.1
  45.0 4.6 %collective-permute-start.2 = (bf16[512,4096]{1,0:T(8,128)(2,1)}, bf16[512,4096]{1,0:T(8,128)(2,1)}, u32[]{:S(2)}, u32[]{:S(2)}) collective-permute-start(bf16[512,4096]{1,0:T(8,128)(2,1)} %param.12), channel_id=1, source_target_pairs={{0,2},{2,4},{4,6},{6,8},{8,10},{10,12},{12,14},{1,3},{3,5},{5,7},{... | collective-permute-start | bytes 12582920 | tf_op jit(solution)/shard_map/ppermute | solution.py:18
  49.6 1.5 collective-permute-start.3
  51.1 0.1 pad.17.clone
  51.1 0.0 copy-done.4
  51.1 0.0 collective-permute-done.1
  51.1 1.7 broadcast_select_fusion.1
  52.9 1.2 fusion.23
  54.1 1.0 slice_bitcast_fusion.2
  55.2 0.1 reshape.405
  55.2 0.0 copy-start.6
  55.2 0.1 slice_add_fusion
  55.4 1.4 pad_bitcast_fusion.2
  56.8 0.1 pad_bitcast_fusion.3
  57.0 0.1 fusion.26
  57.1 0.1 pad_maximum_fusion.6
  57.2 11.5 %exponential_multiply_fusion = f32[8,3,512,512]{3,2,1,0:T(8,128)} fusion(f32[8,3]{1,0:T(8,128)S(1)} %pad_maximum_fusion.6, f32[8,3,512]{2,1,0:T(4,128)S(1)} %copy.34, f32[8,512]{1,0:T(8,128)S(1)} %bitcast.93, bf16[8,528,128]{2,1,0:T(8,128)(2,1)S(1)} %get-tuple-element.73, bf16[8,1,512,128]{3,2,0,1:T(8,128)(2,1)S(1)} %pad_bitcast_fusion.2, ...), kind=kOutput, calls=%fused_computation.13 | convolution fusion | flops 1651507200 | bytes 29446144 | tf_op jit(solution)/shard_map/bkjp,bip->bkji/dot_general | solution.py:104
  68.7 70.8 %while.14 = (s32[]{:T(128)}, f32[8,512]{1,0:T(8,128)S(1)}, f32[8,3,512]{2,0,1:T(8,128)}, f32[8,3,512,512]{3,2,1,0:T(8,128)}, s32[]{:T(128)}, /*index=5*/s32[]{:T(128)}) while((s32[]{:T(128)}, f32[8,512]{1,0:T(8,128)S(1)}, f32[8,3,512]{2,0,1:T(8,128)}, f32[8,3,512,512]{3,2,1,0:T(8,128)}, s32[]{:T(128)}, /*index=5*/s32[]{:T(128)}) %tuple.45), condition=%wide.region_6.7_spmd.clone, body=%wide.region_3.6_spmd.clone.sunk | while | flops 25194500 | bytes 151912576 | solution.py:123
  68.7 9.6 %multiply_reduce_fusion.6 = f32[8,3,512]{2,1,0:T(4,128)S(1)} fusion(f32[8,3,512,512]{3,2,1,0:T(8,128)} %get-tuple-element.138, f32[8,512]{1,0:T(8,128)S(1)} %broadcast_select_fusion.5), kind=kLoop, calls=%fused_computation.1.clone.1 | loop fusion | flops 12570624 | bytes 25231360 | tf_op jit(solution)/shard_map/while/body/eval_jaxpr/reduce_sum | solution.py:112
  78.4 0.0 copy-start.5
  78.5 5.6 %copy-done.2 = f32[8,3,512,512]{3,2,1,0:T(8,128)S(1)} copy-done((f32[8,3,512,512]{3,2,1,0:T(8,128)S(1)}, f32[8,3,512,512]{3,2,1,0:T(8,128)}, u32[]{:S(2)}) %copy-start.2) | copy-done | bytes 25165848 | tf_op jit(solution)/shard_map/while
  84.1 2.2 multiply_reduce_fusion.7
  86.3 0.0 copy-done.5
  86.4 9.6 %multiply_reduce_fusion.6 = f32[8,3,512]{2,1,0:T(4,128)S(1)} fusion(f32[8,3,512,512]{3,2,1,0:T(8,128)} %get-tuple-element.138, f32[8,512]{1,0:T(8,128)S(1)} %broadcast_select_fusion.5), kind=kLoop, calls=%fused_computation.1.clone.1 | loop fusion | flops 12570624 | bytes 25231360 | tf_op jit(solution)/shard_map/while/body/eval_jaxpr/reduce_sum | solution.py:112
  96.2 5.6 %copy-done.2 = f32[8,3,512,512]{3,2,1,0:T(8,128)S(1)} copy-done((f32[8,3,512,512]{3,2,1,0:T(8,128)S(1)}, f32[8,3,512,512]{3,2,1,0:T(8,128)}, u32[]{:S(2)}) %copy-start.2) | copy-done | bytes 25165848 | tf_op jit(solution)/shard_map/while
  101.8 2.2 multiply_reduce_fusion.7
  104.1 9.6 %multiply_reduce_fusion.6 = f32[8,3,512]{2,1,0:T(4,128)S(1)} fusion(f32[8,3,512,512]{3,2,1,0:T(8,128)} %get-tuple-element.138, f32[8,512]{1,0:T(8,128)S(1)} %broadcast_select_fusion.5), kind=kLoop, calls=%fused_computation.1.clone.1 | loop fusion | flops 12570624 | bytes 25231360 | tf_op jit(solution)/shard_map/while/body/eval_jaxpr/reduce_sum | solution.py:112
  113.9 5.6 %copy-done.2 = f32[8,3,512,512]{3,2,1,0:T(8,128)S(1)} copy-done((f32[8,3,512,512]{3,2,1,0:T(8,128)S(1)}, f32[8,3,512,512]{3,2,1,0:T(8,128)}, u32[]{:S(2)}) %copy-start.2) | copy-done | bytes 25165848 | tf_op jit(solution)/shard_map/while
  119.5 2.2 multiply_reduce_fusion.7
  121.8 9.6 %multiply_reduce_fusion.6 = f32[8,3,512]{2,1,0:T(4,128)S(1)} fusion(f32[8,3,512,512]{3,2,1,0:T(8,128)} %get-tuple-element.138, f32[8,512]{1,0:T(8,128)S(1)} %broadcast_select_fusion.5), kind=kLoop, calls=%fused_computation.1.clone.1 | loop fusion | flops 12570624 | bytes 25231360 | tf_op jit(solution)/shard_map/while/body/eval_jaxpr/reduce_sum | solution.py:112
  131.6 5.6 %copy-done.2 = f32[8,3,512,512]{3,2,1,0:T(8,128)S(1)} copy-done((f32[8,3,512,512]{3,2,1,0:T(8,128)S(1)}, f32[8,3,512,512]{3,2,1,0:T(8,128)}, u32[]{:S(2)}) %copy-start.2) | copy-done | bytes 25165848 | tf_op jit(solution)/shard_map/while
  137.2 2.2 multiply_reduce_fusion.7
  139.5 0.0 copy-start.3
  139.5 1.0 constant_dynamic-slice_fusion
  140.5 2.5 %fusion.4 = bf16[3,512,512]{2,1,0:T(8,128)(2,1)S(1)} fusion(f32[8,3,512,512]{3,2,1,0:T(8,128)} %get-tuple-element.141, s32[]{:T(128)S(6)} %select_n.78, f32[3,512]{1,0:T(4,128)S(1)} %bitcast.91, f32[512]{0:T(512)S(1)} %bitcast.94), kind=kLoop, calls=%fused_computation.18 | loop fusion | flops 2359296 | bytes 4726788 | tf_op jit(solution)/shard_map/convert_element_type | solution.py:132
  143.0 2.5 %fusion.7 = f32[512,4096]{1,0:T(8,128)S(1)} fusion(bf16[512,4096]{1,0:T(8,128)(2,1)S(1)} %copy-done.3, bf16[3,512,512]{2,1,0:T(8,128)(2,1)S(1)} %fusion.4), kind=kOutput, calls=%fused_computation.30 | convolution fusion | flops 2147483648 | bytes 13107200 | tf_op jit(solution)/shard_map/dot_general | solution.py:134
  145.5 82.8 %collective-permute-done.2 = bf16[512,4096]{1,0:T(8,128)(2,1)} collective-permute-done((bf16[512,4096]{1,0:T(8,128)(2,1)}, bf16[512,4096]{1,0:T(8,128)(2,1)}, u32[]{:S(2)}, u32[]{:S(2)}) %collective-permute-start.2) | collective-permute-done | bytes 4194336 | tf_op jit(solution)/shard_map/ppermute | solution.py:18
  228.3 4.6 %fusion.6 = f32[512,4096]{1,0:T(8,128)S(1)} fusion(bf16[512,4096]{1,0:T(8,128)(2,1)} %collective-permute-done.2, bf16[3,512,512]{2,1,0:T(8,128)(2,1)S(1)} %fusion.4), kind=kOutput, calls=%fused_computation.28 | convolution fusion | flops 2147483648 | bytes 13107200 | tf_op jit(solution)/shard_map/dot_general | solution.py:135
  232.9 0.0 collective-permute-done.3
  232.9 0.0 copy-start.1
  232.9 7.4 %add_convert_fusion = bf16[512,4096]{1,0:T(8,128)(2,1)} fusion(f32[512,4096]{1,0:T(8,128)S(1)} %fusion.7, f32[512,4096]{1,0:T(8,128)S(1)} %fusion.6, bf16[512,4096]{1,0:T(8,128)(2,1)} %collective-permute-done.3, bf16[3,512,512]{2,1,0:T(8,128)(2,1)S(1)} %fusion.4), kind=kOutput, calls=%fused_computation.14 | convolution fusion | flops 2153775104 | bytes 25690112 | tf_op jit(solution)/shard_map/dot_general | solution.py:136
  (85 shorter events, 0.9 us)
Async XLA Ops:
  0.0 1.6 copy-start
  3.5 4.6 %copy-start.7 = (s32[512]{0:T(512)S(1)}, s32[512]{0:T(512)}, u32[]{:S(2)}) copy-start(s32[512]{0:T(512)} %param.16) | copy-start | bytes 6148
  3.5 4.6 %copy-start.8 = (s32[512]{0:T(512)S(1)}, s32[512]{0:T(512)}, u32[]{:S(2)}) copy-start(s32[512]{0:T(512)} %param.15) | copy-start | bytes 6148
  3.5 4.9 %copy-start.9 = (s32[1,2]{1,0:T(1,128)S(1)}, s32[1,2]{1,0:T(1,128)}, u32[]{:S(2)}) copy-start(s32[1,2]{1,0:T(1,128)} %param.17) | copy-start | bytes 28
  7.6 2.3 collective-permute-start
  45.0 6.1 %copy-start.4 = (bf16[8,528,128]{2,1,0:T(8,128)(2,1)}, bf16[8,528,128]{2,1,0:T(8,128)(2,1)S(1)}, u32[]{:S(2)}) copy-start(bf16[8,528,128]{2,1,0:T(8,128)(2,1)S(1)} %all_to_all.5) | copy-start | bytes 3244036
  45.0 6.1 %collective-permute-start.1 = (bf16[8,528,128]{2,1,0:T(8,128)(2,1)S(1)}, bf16[8,528,128]{2,1,0:T(8,128)(2,1)}, u32[]{:S(2)}, u32[]{:S(2)}) collective-permute-start(bf16[8,528,128]{2,1,0:T(8,128)(2,1)S(1)} %all_to_all.5), channel_id=1, source_target_pairs={{0,1},{1,0},{2,3},{3,2},{4,5},{5,4},{6,7},{7,6},{8,9},{9,8},{10,11... | collective-permute-start | bytes 3244040 | tf_op jit(solution)/shard_map/ppermute | solution.py:63
  45.0 183.3 %collective-permute-start.2 = (bf16[512,4096]{1,0:T(8,128)(2,1)}, bf16[512,4096]{1,0:T(8,128)(2,1)}, u32[]{:S(2)}, u32[]{:S(2)}) collective-permute-start(bf16[512,4096]{1,0:T(8,128)(2,1)} %param.12), channel_id=1, source_target_pairs={{0,2},{2,4},{4,6},{6,8},{8,10},{10,12},{12,14},{1,3},{3,5},{5,7},{... | collective-permute-start | bytes 12582920 | tf_op jit(solution)/shard_map/ppermute | solution.py:18
  49.6 183.4 %collective-permute-start.3 = (bf16[512,4096]{1,0:T(8,128)(2,1)}, bf16[512,4096]{1,0:T(8,128)(2,1)}, u32[]{:S(2)}, u32[]{:S(2)}) collective-permute-start(bf16[512,4096]{1,0:T(8,128)(2,1)} %param.12), channel_id=1, source_target_pairs={{2,0},{4,2},{6,4},{8,6},{10,8},{12,10},{14,12},{3,1},{5,3},{7,5},{... | collective-permute-start | bytes 12582920 | tf_op jit(solution)/shard_map/ppermute | solution.py:18
  55.2 2.0 copy-start.6
  68.7 15.4 %copy-start.2 = (f32[8,3,512,512]{3,2,1,0:T(8,128)S(1)}, f32[8,3,512,512]{3,2,1,0:T(8,128)}, u32[]{:S(2)}) copy-start(f32[8,3,512,512]{3,2,1,0:T(8,128)} %get-tuple-element.138) | copy-start | bytes 75497472 | tf_op jit(solution)/shard_map/while
  78.4 7.9 %copy-start.5 = (f32[8,3,512]{2,0,1:T(8,128)}, f32[8,3,512]{2,0,1:T(8,128)S(1)}, u32[]{:S(2)}) copy-start(f32[8,3,512]{2,0,1:T(8,128)S(1)} %pad_maximum_fusion.10) | copy-start | bytes 147460 | tf_op jit(solution)/shard_map/while
  86.4 15.4 %copy-start.2 = (f32[8,3,512,512]{3,2,1,0:T(8,128)S(1)}, f32[8,3,512,512]{3,2,1,0:T(8,128)}, u32[]{:S(2)}) copy-start(f32[8,3,512,512]{3,2,1,0:T(8,128)} %get-tuple-element.138) | copy-start | bytes 75497472 | tf_op jit(solution)/shard_map/while
  96.1 7.9 %copy-start.5 = (f32[8,3,512]{2,0,1:T(8,128)}, f32[8,3,512]{2,0,1:T(8,128)S(1)}, u32[]{:S(2)}) copy-start(f32[8,3,512]{2,0,1:T(8,128)S(1)} %pad_maximum_fusion.10) | copy-start | bytes 147460 | tf_op jit(solution)/shard_map/while
  104.1 15.4 %copy-start.2 = (f32[8,3,512,512]{3,2,1,0:T(8,128)S(1)}, f32[8,3,512,512]{3,2,1,0:T(8,128)}, u32[]{:S(2)}) copy-start(f32[8,3,512,512]{3,2,1,0:T(8,128)} %get-tuple-element.138) | copy-start | bytes 75497472 | tf_op jit(solution)/shard_map/while
  113.8 7.9 %copy-start.5 = (f32[8,3,512]{2,0,1:T(8,128)}, f32[8,3,512]{2,0,1:T(8,128)S(1)}, u32[]{:S(2)}) copy-start(f32[8,3,512]{2,0,1:T(8,128)S(1)} %pad_maximum_fusion.10) | copy-start | bytes 147460 | tf_op jit(solution)/shard_map/while
  121.8 15.4 %copy-start.2 = (f32[8,3,512,512]{3,2,1,0:T(8,128)S(1)}, f32[8,3,512,512]{3,2,1,0:T(8,128)}, u32[]{:S(2)}) copy-start(f32[8,3,512,512]{3,2,1,0:T(8,128)} %get-tuple-element.138) | copy-start | bytes 75497472 | tf_op jit(solution)/shard_map/while
  131.6 7.9 %copy-start.5 = (f32[8,3,512]{2,0,1:T(8,128)}, f32[8,3,512]{2,0,1:T(8,128)S(1)}, u32[]{:S(2)}) copy-start(f32[8,3,512]{2,0,1:T(8,128)S(1)} %pad_maximum_fusion.10) | copy-start | bytes 147460 | tf_op jit(solution)/shard_map/while
  139.5 3.5 %copy-start.3 = (bf16[512,4096]{1,0:T(8,128)(2,1)S(1)}, bf16[512,4096]{1,0:T(8,128)(2,1)}, u32[]{:S(2)}) copy-start(bf16[512,4096]{1,0:T(8,128)(2,1)} %param.12) | copy-start | bytes 12582916
  232.9 7.4 %copy-start.1 = (bf16[512,2048]{1,0:T(8,128)(2,1)S(1)}, bf16[512,2048]{1,0:T(8,128)(2,1)}, u32[]{:S(2)}) copy-start(bf16[512,2048]{1,0:T(8,128)(2,1)} %param.11) | copy-start | bytes 6291460

commit v10 on v9

--- a/solution.py
+++ b/solution.py
@@ -132,8 +132,9 @@
     plan = (own_row[None, None, :] * own_kernel * own_col[:, :, None]).astype(jnp.bfloat16)
     along_j = (((0,), (0,)), ((), ()))
     aligned = lax.dot_general(plan[1], teacher_hidden, along_j, preferred_element_type=jnp.float32)
-    aligned = aligned + lax.dot_general(plan[0], left_rows, along_j, preferred_element_type=jnp.float32)
-    aligned = aligned + lax.dot_general(plan[2], right_rows, along_j, preferred_element_type=jnp.float32)
+    sides = jnp.concatenate([plan[0], plan[2]], 0)
+    near_rows = jnp.concatenate([left_rows, right_rows], 0)
+    aligned = aligned + lax.dot_general(sides, near_rows, along_j, preferred_element_type=jnp.float32)
     return aligned.astype(jnp.bfloat16)
 
 

time: 241 us -> 240 us (level)
    dot_general x2 -> x1, matrix products: 12 us -> 10.7 us  [body_local(): lax.dot_general(sides, near_rows, along_j, preferred_element_type=jnp.flo...]
  transfers between devices with their start and end apart: 4 -> 4, of which waited for: 1 -> 1; matrix products, arithmetic and copies ran while one was open for 32% -> 31% of each run, Pallas kernels for 0% -> 0%
where the time goes in v10:
time: 240 us; the launch traced here: 239 us
  waiting for transfers between devices  82 us (34%)
  other arithmetic  53.6 us (22%)
  blocking collectives  34.5 us (14%)
  local copies, waits for them, and re-layouts  31 us (13%)
  matrix products  30.5 us (13%)
  starting transfers between devices  6.5 us (3%)
    ppermute x2, waiting for transfers between devices, shifted(): return lax.ppermute(block, axis, route)  82 us
    reduce_sum x4, other arithmetic, iterate(): partial_cols = jnp.sum(row_scale[:, None, None, :] * kernel, axis=3)  38.4 us
    all_to_all x1, blocking collectives, gather_halves(): lax.all_to_all(jnp.broadcast_to(mine, (n,) + mine.shape), 'seq', 0, 0, ti...  34.5 us
    while x16, local copies, waits for them, and re-layouts  22.4 us
    dot_general x1, matrix products, body_local(): jnp.einsum('bkjp,bip->bkji', beside(t_unit), s_unit, preferred_element_ty...  11.5 us
    dot_general x1, matrix products, body_local(): lax.dot_general(sides, near_rows, along_j, preferred_element_type=jnp.flo...  10.7 us
    reduce_sum x4, other arithmetic, iterate(): row_scale = 1.0 / jnp.sum(kernel * col_scale[:, :, :, None], axis=(1, 2))  8.94 us
    ppermute x2, starting transfers between devices, shifted(): return lax.ppermute(block, axis, route)  5.98 us
  transfers between devices with their start and end apart: 4, of which 1 were waited for; matrix products, arithmetic and copies ran while one was open for 31% of the time, Pallas kernels for 0%

profile of v10, /device:TPU:0, one launch (start us, length us, event | category | flops | bytes accessed | tf_op | source)
XLA Modules:
  0.0 239.0 jit_solution(9946684229557803659)
XLA Ops:
  0.0 1.6 copy-done
  1.6 1.9 fusion.36
  3.5 0.0 copy-start.7
  3.5 0.0 copy-start.8
  3.5 0.0 copy-start.9
  3.5 4.0 %fusion.37 = f32[512,128]{0,1:T(8,128)S(1)} fusion(bf16[512,4096]{1,0:T(8,128)(2,1)} %param.12, bf16[4096,128]{1,0:T(8,128)(2,1)} %param.14), kind=kOutput, calls=%fused_computation.104 | convolution fusion | flops 536870912 | bytes 5505024 | tf_op jit(solution)/shard_map/dot_general | solution.py:78
  7.6 0.5 collective-permute-start
  8.1 0.1 fusion.24
  8.2 0.1 copy.29
  8.3 0.0 copy-done.9
  8.4 0.1 copy.28
  8.5 0.1 pad.35.clone
  8.6 0.6 compare_reduce_fusion
  9.2 0.6 broadcast_select_fusion.3
  9.8 0.0 collective-permute-done
  9.9 0.1 fusion.29
  9.9 0.1 multiply_reduce_fusion.2
  10.0 0.1 multiply_convert_fusion
  10.1 0.1 fusion.19
  10.2 0.1 copy.30
  10.4 0.1 broadcast_in_dim.8
  10.5 34.5 %all_to_all.5 = bf16[8,528,128]{2,1,0:T(8,128)(2,1)S(1)} all-to-all(bf16[8,528,128]{2,1,0:T(8,128)(2,1)S(1)} %broadcast_in_dim.8), channel_id=1, replica_groups=mesh['groups'=2,'seq'=8,'tgrp'=2] {'seq'}, dimensions={0} | all-to-all | bytes 2162688 | tf_op jit(solution)/shard_map/all_to_all | solution.py:62
  45.0 0.0 collective-permute-start.1
  45.0 4.5 %collective-permute-start.2 = (bf16[512,4096]{1,0:T(8,128)(2,1)}, bf16[512,4096]{1,0:T(8,128)(2,1)}, u32[]{:S(2)}, u32[]{:S(2)}) collective-permute-start(bf16[512,4096]{1,0:T(8,128)(2,1)} %param.12), channel_id=1, source_target_pairs={{0,2},{2,4},{4,6},{6,8},{8,10},{10,12},{12,14},{1,3},{3,5},{5,7},{... | collective-permute-start | bytes 12582920 | tf_op jit(solution)/shard_map/ppermute | solution.py:18
  49.5 1.5 collective-permute-start.3
  51.0 0.1 pad.21.clone
  51.1 0.0 copy-done.4
  51.1 0.0 collective-permute-done.1
  51.1 1.7 broadcast_select_fusion.1
  52.8 1.2 fusion.32
  54.1 1.0 slice_bitcast_fusion.2
  55.1 0.1 reshape.405
  55.2 0.0 copy-start.6
  55.2 0.1 slice_add_fusion
  55.4 1.4 pad_bitcast_fusion.2
  56.8 0.1 pad_bitcast_fusion.3
  57.0 0.1 fusion.35
  57.1 0.1 pad_maximum_fusion.6
  57.1 0.0 copy-done.6
  57.1 11.5 %exponential_multiply_fusion = f32[8,3,512,512]{3,2,1,0:T(8,128)} fusion(f32[8,3]{1,0:T(8,128)S(1)} %pad_maximum_fusion.6, f32[8,3,512]{2,1,0:T(4,128)S(1)} %copy.34, f32[8,512]{1,0:T(8,128)S(1)} %bitcast.89, bf16[8,528,128]{2,1,0:T(8,128)(2,1)S(1)} %get-tuple-element.73, bf16[8,1,512,128]{3,2,0,1:T(8,128)(2,1)S(1)} %pad_bitcast_fusion.2, ...), kind=kOutput, calls=%fused_computation.13 | convolution fusion | flops 1651507200 | bytes 29446144 | tf_op jit(solution)/shard_map/bkjp,bip->bkji/dot_general | solution.py:104
  68.7 70.8 %while.14 = (s32[]{:T(128)}, f32[8,512]{1,0:T(8,128)S(1)}, f32[8,3,512]{2,0,1:T(8,128)}, f32[8,3,512,512]{3,2,1,0:T(8,128)}, s32[]{:T(128)}, /*index=5*/s32[]{:T(128)}) while((s32[]{:T(128)}, f32[8,512]{1,0:T(8,128)S(1)}, f32[8,3,512]{2,0,1:T(8,128)}, f32[8,3,512,512]{3,2,1,0:T(8,128)}, s32[]{:T(128)}, /*index=5*/s32[]{:T(128)}) %tuple.46), condition=%wide.region_6.7_spmd.clone, body=%wide.region_3.6_spmd.clone.sunk | while | flops 25194500 | bytes 151912576 | solution.py:123
  68.7 9.6 %multiply_reduce_fusion.6 = f32[8,3,512]{2,1,0:T(4,128)S(1)} fusion(f32[8,3,512,512]{3,2,1,0:T(8,128)} %get-tuple-element.140, f32[8,512]{1,0:T(8,128)S(1)} %broadcast_select_fusion.5), kind=kLoop, calls=%fused_computation.1.clone.1 | loop fusion | flops 12570624 | bytes 25231360 | tf_op jit(solution)/shard_map/while/body/eval_jaxpr/reduce_sum | solution.py:112
  78.5 5.6 %copy-done.2 = f32[8,3,512,512]{3,2,1,0:T(8,128)S(1)} copy-done((f32[8,3,512,512]{3,2,1,0:T(8,128)S(1)}, f32[8,3,512,512]{3,2,1,0:T(8,128)}, u32[]{:S(2)}) %copy-start.2) | copy-done | bytes 25165848 | tf_op jit(solution)/shard_map/while
  84.1 2.2 multiply_reduce_fusion.7
  86.4 0.0 copy-start.2
  86.4 9.6 %multiply_reduce_fusion.6 = f32[8,3,512]{2,1,0:T(4,128)S(1)} fusion(f32[8,3,512,512]{3,2,1,0:T(8,128)} %get-tuple-element.140, f32[8,512]{1,0:T(8,128)S(1)} %broadcast_select_fusion.5), kind=kLoop, calls=%fused_computation.1.clone.1 | loop fusion | flops 12570624 | bytes 25231360 | tf_op jit(solution)/shard_map/while/body/eval_jaxpr/reduce_sum | solution.py:112
  96.2 5.6 %copy-done.2 = f32[8,3,512,512]{3,2,1,0:T(8,128)S(1)} copy-done((f32[8,3,512,512]{3,2,1,0:T(8,128)S(1)}, f32[8,3,512,512]{3,2,1,0:T(8,128)}, u32[]{:S(2)}) %copy-start.2) | copy-done | bytes 25165848 | tf_op jit(solution)/shard_map/while
  101.8 2.2 multiply_reduce_fusion.7
  104.1 0.0 copy-start.2
  104.1 9.6 %multiply_reduce_fusion.6 = f32[8,3,512]{2,1,0:T(4,128)S(1)} fusion(f32[8,3,512,512]{3,2,1,0:T(8,128)} %get-tuple-element.140, f32[8,512]{1,0:T(8,128)S(1)} %broadcast_select_fusion.5), kind=kLoop, calls=%fused_computation.1.clone.1 | loop fusion | flops 12570624 | bytes 25231360 | tf_op jit(solution)/shard_map/while/body/eval_jaxpr/reduce_sum | solution.py:112
  113.8 0.0 copy-start.5
  113.9 5.6 %copy-done.2 = f32[8,3,512,512]{3,2,1,0:T(8,128)S(1)} copy-done((f32[8,3,512,512]{3,2,1,0:T(8,128)S(1)}, f32[8,3,512,512]{3,2,1,0:T(8,128)}, u32[]{:S(2)}) %copy-start.2) | copy-done | bytes 25165848 | tf_op jit(solution)/shard_map/while
  119.5 2.2 multiply_reduce_fusion.7
  121.8 9.6 %multiply_reduce_fusion.6 = f32[8,3,512]{2,1,0:T(4,128)S(1)} fusion(f32[8,3,512,512]{3,2,1,0:T(8,128)} %get-tuple-element.140, f32[8,512]{1,0:T(8,128)S(1)} %broadcast_select_fusion.5), kind=kLoop, calls=%fused_computation.1.clone.1 | loop fusion | flops 12570624 | bytes 25231360 | tf_op jit(solution)/shard_map/while/body/eval_jaxpr/reduce_sum | solution.py:112
  131.6 5.6 %copy-done.2 = f32[8,3,512,512]{3,2,1,0:T(8,128)S(1)} copy-done((f32[8,3,512,512]{3,2,1,0:T(8,128)S(1)}, f32[8,3,512,512]{3,2,1,0:T(8,128)}, u32[]{:S(2)}) %copy-start.2) | copy-done | bytes 25165848 | tf_op jit(solution)/shard_map/while
  137.2 2.2 multiply_reduce_fusion.7
  139.5 0.0 copy-start.3
  139.5 1.0 constant_dynamic-slice_fusion
  140.5 2.5 %fusion.10 = bf16[3,512,512]{2,1,0:T(8,128)(2,1)S(1)} fusion(f32[8,3,512,512]{3,2,1,0:T(8,128)} %get-tuple-element.143, s32[]{:T(128)S(6)} %select_n.78, f32[3,512]{1,0:T(4,128)S(1)} %bitcast.87, f32[512]{0:T(512)S(1)} %bitcast.90), kind=kLoop, calls=%fused_computation.22 | loop fusion | flops 2359296 | bytes 4726788 | tf_op jit(solution)/shard_map/convert_element_type | solution.py:132
  143.0 0.9 slice_bitcast_fusion.4
  143.8 2.4 %fusion.15 = f32[512,4096]{1,0:T(8,128)S(1)} fusion(bf16[512,4096]{1,0:T(8,128)(2,1)S(1)} %copy-done.3, bf16[3,512,512]{2,1,0:T(8,128)(2,1)S(1)} %fusion.10), kind=kOutput, calls=%fused_computation.36 | convolution fusion | flops 2147483648 | bytes 13107200 | tf_op jit(solution)/shard_map/dot_general | solution.py:134
  146.3 82.0 %collective-permute-done.2 = bf16[512,4096]{1,0:T(8,128)(2,1)} collective-permute-done((bf16[512,4096]{1,0:T(8,128)(2,1)}, bf16[512,4096]{1,0:T(8,128)(2,1)}, u32[]{:S(2)}, u32[]{:S(2)}) %collective-permute-start.2) | collective-permute-done | bytes 4194336 | tf_op jit(solution)/shard_map/ppermute | solution.py:18
  228.3 0.0 collective-permute-done.3
  228.3 10.7 %add_convert_fusion = bf16[512,4096]{1,0:T(8,128)(2,1)} fusion(f32[512,4096]{1,0:T(8,128)S(1)} %fusion.15, bf16[512,4096]{1,0:T(8,128)(2,1)} %collective-permute-done.3, bf16[512,4096]{1,0:T(8,128)(2,1)} %collective-permute-done.2, bf16[512,512]{1,0:T(8,128)(2,1)} %get-tuple-element.76, bf16[512,512]{1,0:T(8,128)(2,1)S(1)} %get-tuple-element.75), kind=kOutput, calls=%fused_computation.18 | convolution fusion | flops 4318035968 | bytes 22020096 | tf_op jit(solution)/shard_map/dot_general | solution.py:137
  (85 shorter events, 0.9 us)
Async XLA Ops:
  0.0 1.6 copy-start
  3.5 4.6 %copy-start.7 = (s32[512]{0:T(512)S(1)}, s32[512]{0:T(512)}, u32[]{:S(2)}) copy-start(s32[512]{0:T(512)} %param.16) | copy-start | bytes 6148
  3.5 4.6 %copy-start.8 = (s32[512]{0:T(512)S(1)}, s32[512]{0:T(512)}, u32[]{:S(2)}) copy-start(s32[512]{0:T(512)} %param.15) | copy-start | bytes 6148
  3.5 4.9 %copy-start.9 = (s32[1,2]{1,0:T(1,128)S(1)}, s32[1,2]{1,0:T(1,128)}, u32[]{:S(2)}) copy-start(s32[1,2]{1,0:T(1,128)} %param.17) | copy-start | bytes 28
  7.6 2.3 collective-permute-start
  45.0 6.1 %copy-start.4 = (bf16[8,528,128]{2,1,0:T(8,128)(2,1)}, bf16[8,528,128]{2,1,0:T(8,128)(2,1)S(1)}, u32[]{:S(2)}) copy-start(bf16[8,528,128]{2,1,0:T(8,128)(2,1)S(1)} %all_to_all.5) | copy-start | bytes 3244036
  45.0 6.1 %collective-permute-start.1 = (bf16[8,528,128]{2,1,0:T(8,128)(2,1)S(1)}, bf16[8,528,128]{2,1,0:T(8,128)(2,1)}, u32[]{:S(2)}, u32[]{:S(2)}) collective-permute-start(bf16[8,528,128]{2,1,0:T(8,128)(2,1)S(1)} %all_to_all.5), channel_id=1, source_target_pairs={{0,1},{1,0},{2,3},{3,2},{4,5},{5,4},{6,7},{7,6},{8,9},{9,8},{10,11... | collective-permute-start | bytes 3244040 | tf_op jit(solution)/shard_map/ppermute | solution.py:63
  45.0 183.3 %collective-permute-start.2 = (bf16[512,4096]{1,0:T(8,128)(2,1)}, bf16[512,4096]{1,0:T(8,128)(2,1)}, u32[]{:S(2)}, u32[]{:S(2)}) collective-permute-start(bf16[512,4096]{1,0:T(8,128)(2,1)} %param.12), channel_id=1, source_target_pairs={{0,2},{2,4},{4,6},{6,8},{8,10},{10,12},{12,14},{1,3},{3,5},{5,7},{... | collective-permute-start | bytes 12582920 | tf_op jit(solution)/shard_map/ppermute | solution.py:18
  49.5 178.8 %collective-permute-start.3 = (bf16[512,4096]{1,0:T(8,128)(2,1)}, bf16[512,4096]{1,0:T(8,128)(2,1)}, u32[]{:S(2)}, u32[]{:S(2)}) collective-permute-start(bf16[512,4096]{1,0:T(8,128)(2,1)} %param.12), channel_id=1, source_target_pairs={{2,0},{4,2},{6,4},{8,6},{10,8},{12,10},{14,12},{3,1},{5,3},{7,5},{... | collective-permute-start | bytes 12582920 | tf_op jit(solution)/shard_map/ppermute | solution.py:18
  55.2 2.0 copy-start.6
  68.7 15.4 %copy-start.2 = (f32[8,3,512,512]{3,2,1,0:T(8,128)S(1)}, f32[8,3,512,512]{3,2,1,0:T(8,128)}, u32[]{:S(2)}) copy-start(f32[8,3,512,512]{3,2,1,0:T(8,128)} %get-tuple-element.140) | copy-start | bytes 75497472 | tf_op jit(solution)/shard_map/while
  78.4 7.9 %copy-start.5 = (f32[8,3,512]{2,0,1:T(8,128)}, f32[8,3,512]{2,0,1:T(8,128)S(1)}, u32[]{:S(2)}) copy-start(f32[8,3,512]{2,0,1:T(8,128)S(1)} %pad_maximum_fusion.10) | copy-start | bytes 147460 | tf_op jit(solution)/shard_map/while
  86.4 15.4 %copy-start.2 = (f32[8,3,512,512]{3,2,1,0:T(8,128)S(1)}, f32[8,3,512,512]{3,2,1,0:T(8,128)}, u32[]{:S(2)}) copy-start(f32[8,3,512,512]{3,2,1,0:T(8,128)} %get-tuple-element.140) | copy-start | bytes 75497472 | tf_op jit(solution)/shard_map/while
  96.1 7.9 %copy-start.5 = (f32[8,3,512]{2,0,1:T(8,128)}, f32[8,3,512]{2,0,1:T(8,128)S(1)}, u32[]{:S(2)}) copy-start(f32[8,3,512]{2,0,1:T(8,128)S(1)} %pad_maximum_fusion.10) | copy-start | bytes 147460 | tf_op jit(solution)/shard_map/while
  104.1 15.4 %copy-start.2 = (f32[8,3,512,512]{3,2,1,0:T(8,128)S(1)}, f32[8,3,512,512]{3,2,1,0:T(8,128)}, u32[]{:S(2)}) copy-start(f32[8,3,512,512]{3,2,1,0:T(8,128)} %get-tuple-element.140) | copy-start | bytes 75497472 | tf_op jit(solution)/shard_map/while
  113.8 7.9 %copy-start.5 = (f32[8,3,512]{2,0,1:T(8,128)}, f32[8,3,512]{2,0,1:T(8,128)S(1)}, u32[]{:S(2)}) copy-start(f32[8,3,512]{2,0,1:T(8,128)S(1)} %pad_maximum_fusion.10) | copy-start | bytes 147460 | tf_op jit(solution)/shard_map/while
  121.8 15.4 %copy-start.2 = (f32[8,3,512,512]{3,2,1,0:T(8,128)S(1)}, f32[8,3,512,512]{3,2,1,0:T(8,128)}, u32[]{:S(2)}) copy-start(f32[8,3,512,512]{3,2,1,0:T(8,128)} %get-tuple-element.140) | copy-start | bytes 75497472 | tf_op jit(solution)/shard_map/while
  131.5 7.9 %copy-start.5 = (f32[8,3,512]{2,0,1:T(8,128)}, f32[8,3,512]{2,0,1:T(8,128)S(1)}, u32[]{:S(2)}) copy-start(f32[8,3,512]{2,0,1:T(8,128)S(1)} %pad_maximum_fusion.10) | copy-start | bytes 147460 | tf_op jit(solution)/shard_map/while
  139.5 4.4 %copy-start.3 = (bf16[512,4096]{1,0:T(8,128)(2,1)S(1)}, bf16[512,4096]{1,0:T(8,128)(2,1)}, u32[]{:S(2)}) copy-start(bf16[512,4096]{1,0:T(8,128)(2,1)} %param.12) | copy-start | bytes 12582916
  228.3 10.7 %copy-start.1 = (bf16[512,2048]{1,0:T(8,128)(2,1)S(1)}, bf16[512,2048]{1,0:T(8,128)(2,1)}, u32[]{:S(2)}) copy-start(bf16[512,2048]{1,0:T(8,128)(2,1)} %param.11) | copy-start | bytes 6291460

commit v11 on v9

--- a/solution.py
+++ b/solution.py
@@ -89,8 +89,13 @@
     packed = jnp.concatenate([units, extra, jnp.zeros((pad, units.shape[1]), jnp.bfloat16)], 0)
     gathered = gather_halves(packed)
 
-    left_rows = shifted(teacher_hidden, "seq", 1)
-    right_rows = shifted(teacher_hidden, "seq", -1)
+    pieces = 2 if rows % 16 == 0 else 1
+    cut = rows // pieces
+    near_pieces = [
+        (shifted(teacher_hidden[p * cut : (p + 1) * cut], "seq", 1),
+         shifted(teacher_hidden[p * cut : (p + 1) * cut], "seq", -1))
+        for p in range(pieces)
+    ]
 
     s_unit = gathered[:, :rows, :proj_width]
     t_unit = gathered[:, :rows, proj_width:]
@@ -132,8 +137,12 @@
     plan = (own_row[None, None, :] * own_kernel * own_col[:, :, None]).astype(jnp.bfloat16)
     along_j = (((0,), (0,)), ((), ()))
     aligned = lax.dot_general(plan[1], teacher_hidden, along_j, preferred_element_type=jnp.float32)
-    aligned = aligned + lax.dot_general(plan[0], left_rows, along_j, preferred_element_type=jnp.float32)
-    aligned = aligned + lax.dot_general(plan[2], right_rows, along_j, preferred_element_type=jnp.float32)
+    for p, (left_rows, right_rows) in enumerate(near_pieces):
+        if p:
+            left_rows, right_rows, aligned = lax.optimization_barrier((left_rows, right_rows, aligned))
+        sides = jnp.concatenate([plan[0, p * cut : (p + 1) * cut], plan[2, p * cut : (p + 1) * cut]], 0)
+        near_rows = jnp.concatenate([left_rows, right_rows], 0)
+        aligned = aligned + lax.dot_general(sides, near_rows, along_j, preferred_element_type=jnp.float32)
     return aligned.astype(jnp.bfloat16)
 
 

time: 241 us -> 251 us (1.041)
  waiting for transfers between devices: 82.8 us -> 67.9 us
  other arithmetic: 53.6 us -> 62.7 us
  starting transfers between devices: 6.54 us -> 13.1 us
  local copies, waits for them, and re-layouts: 30.1 us -> 35.4 us
  matrix products: 31.8 us -> 35.6 us
    ppermute x2 -> x4, waiting for transfers between devices: 82.8 us -> 67.9 us  [shifted(): return lax.ppermute(block, axis, route)]
    convert_element_type x0 -> x1, other arithmetic: none -> 9.16 us  [body_local(): return aligned.astype(jnp.bfloat16)]
    ppermute x2 -> x4, starting transfers between devices: 6.02 us -> 12.6 us  [shifted(): return lax.ppermute(block, axis, route)]
    slice x0 -> x1, local copies, waits for them, and re-layouts: none -> 5.17 us  [body_local(): teacher_hidden[p * cut:(p + 1) * cut]]
    dot_general x2, matrix products: 12 us -> 15.7 us  [body_local(): lax.dot_general(sides, near_rows, along_j, preferred_element_type=jnp.flo...]
  transfers between devices with their start and end apart: 4 -> 6, of which waited for: 1 -> 2; matrix products, arithmetic and copies ran while one was open for 32% -> 34% of each run, Pallas kernels for 0% -> 0%
where the time goes in v11:
time: 251 us; the launch traced here: 250 us
  waiting for transfers between devices  67.9 us (27%)
  other arithmetic  62.7 us (25%)
  matrix products  35.6 us (14%)
  local copies, waits for them, and re-layouts  35.4 us (14%)
  blocking collectives  34.5 us (14%)
  starting transfers between devices  13.1 us (5%)
    ppermute x4, waiting for transfers between devices, shifted(): return lax.ppermute(block, axis, route)  67.9 us
    reduce_sum x4, other arithmetic, iterate(): partial_cols = jnp.sum(row_scale[:, None, None, :] * kernel, axis=3)  38.4 us
    all_to_all x1, blocking collectives, gather_halves(): lax.all_to_all(jnp.broadcast_to(mine, (n,) + mine.shape), 'seq', 0, 0, ti...  34.5 us
    while x16, local copies, waits for them, and re-layouts  22.4 us
    dot_general x2, matrix products, body_local(): lax.dot_general(sides, near_rows, along_j, preferred_element_type=jnp.flo...  15.7 us
    ppermute x4, starting transfers between devices, shifted(): return lax.ppermute(block, axis, route)  12.6 us
    dot_general x1, matrix products, body_local(): jnp.einsum('bkjp,bip->bkji', beside(t_unit), s_unit, preferred_element_ty...  11.6 us
    convert_element_type x1, other arithmetic, body_local(): return aligned.astype(jnp.bfloat16)  9.16 us
  transfers between devices with their start and end apart: 6, of which 2 were waited for; matrix products, arithmetic and copies ran while one was open for 34% of the time, Pallas kernels for 0%

profile of v11, /device:TPU:0, one launch (start us, length us, event | category | flops | bytes accessed | tf_op | source)
XLA Modules:
  0.0 250.1 jit_solution(10132231835493613029)
XLA Ops:
  0.0 1.6 copy-done
  1.6 1.9 fusion.42
  3.5 0.0 copy-start.7
  3.5 0.0 copy-start.8
  3.5 0.0 copy-start.9
  3.5 4.0 %fusion.43 = f32[512,128]{0,1:T(8,128)S(1)} fusion(bf16[512,4096]{1,0:T(8,128)(2,1)} %param.12, bf16[4096,128]{1,0:T(8,128)(2,1)} %param.14), kind=kOutput, calls=%fused_computation.115 | convolution fusion | flops 536870912 | bytes 5505024 | tf_op jit(solution)/shard_map/dot_general | solution.py:78
  7.6 0.5 collective-permute-start.2
  8.1 0.1 fusion.28
  8.2 0.1 copy.29
  8.4 0.1 copy.28
  8.5 0.1 pad.39.clone
  8.6 0.6 compare_reduce_fusion
  9.2 0.6 broadcast_select_fusion.3
  9.8 0.0 collective-permute-done.2
  9.9 0.1 fusion.34
  9.9 0.1 multiply_reduce_fusion.2
  10.0 0.1 multiply_convert_fusion
  10.1 0.1 fusion.23
  10.2 0.1 copy.30
  10.4 0.1 broadcast_in_dim.8
  10.5 34.5 %all_to_all.5 = bf16[8,528,128]{2,1,0:T(8,128)(2,1)S(1)} all-to-all(bf16[8,528,128]{2,1,0:T(8,128)(2,1)S(1)} %broadcast_in_dim.8), channel_id=1, replica_groups=mesh['groups'=2,'seq'=8,'tgrp'=2] {'seq'}, dimensions={0} | all-to-all | bytes 2162688 | tf_op jit(solution)/shard_map/all_to_all | solution.py:62
  45.0 0.0 collective-permute-start.3
  45.0 5.2 %fusion.37 = (bf16[256,4096]{1,0:T(8,128)(2,1)}, bf16[256,4096]{1,0:T(8,128)(2,1)}) fusion(bf16[512,4096]{1,0:T(8,128)(2,1)} %param.12), kind=kLoop, calls=%fused_computation.109 | loop fusion | bytes 8388608 | tf_op jit(solution)/shard_map/slice | solution.py:95
  50.2 3.9 %collective-permute-start.4 = (bf16[256,4096]{1,0:T(8,128)(2,1)}, bf16[256,4096]{1,0:T(8,128)(2,1)}, u32[]{:S(2)}, u32[]{:S(2)}) collective-permute-start(bf16[256,4096]{1,0:T(8,128)(2,1)} %get-tuple-element.79), channel_id=1, source_target_pairs={{0,2},{2,4},{4,6},{6,8},{8,10},{10,12},{12,14},{1,3},{3,5},{5,7},{... | collective-permute-start | bytes 6291464 | tf_op jit(solution)/shard_map/ppermute | solution.py:18
  54.1 1.3 collective-permute-start.5
  55.4 5.9 %collective-permute-start = (bf16[256,4096]{1,0:T(8,128)(2,1)}, bf16[256,4096]{1,0:T(8,128)(2,1)}, u32[]{:S(2)}, u32[]{:S(2)}) collective-permute-start(bf16[256,4096]{1,0:T(8,128)(2,1)} %get-tuple-element.80), channel_id=1, source_target_pairs={{0,2},{2,4},{4,6},{6,8},{8,10},{10,12},{12,14},{1,3},{3,5},{5,7},{... | collective-permute-start | bytes 6291464 | tf_op jit(solution)/shard_map/ppermute | solution.py:18
  61.3 1.5 collective-permute-start.1
  62.8 0.1 pad.25.clone
  62.9 0.0 collective-permute-done.3
  62.9 1.7 broadcast_select_fusion.1
  64.6 1.3 fusion.38
  65.9 1.0 slice_bitcast_fusion.2
  66.9 0.1 reshape.405
  67.0 0.1 slice_add_fusion
  67.2 1.4 pad_bitcast_fusion.2
  68.6 0.1 pad_bitcast_fusion.3
  68.8 0.1 fusion.41
  68.9 0.1 pad_maximum_fusion.6
  68.9 11.6 %exponential_multiply_fusion = f32[8,3,512,512]{3,2,1,0:T(8,128)} fusion(f32[8,3]{1,0:T(8,128)S(1)} %pad_maximum_fusion.6, f32[8,3,512]{2,1,0:T(4,128)S(1)} %copy.34, f32[8,512]{1,0:T(8,128)S(1)} %bitcast.93, bf16[8,528,128]{2,1,0:T(8,128)(2,1)S(1)} %get-tuple-element.81, bf16[8,1,512,128]{3,2,0,1:T(8,128)(2,1)S(1)} %pad_bitcast_fusion.2, ...), kind=kOutput, calls=%fused_computation.13 | convolution fusion | flops 1651507200 | bytes 29446144 | tf_op jit(solution)/shard_map/bkjp,bip->bkji/dot_general | solution.py:109
  80.5 70.8 %while.14 = (s32[]{:T(128)}, f32[8,512]{1,0:T(8,128)S(1)}, f32[8,3,512]{2,0,1:T(8,128)}, f32[8,3,512,512]{3,2,1,0:T(8,128)}, s32[]{:T(128)}, /*index=5*/s32[]{:T(128)}) while((s32[]{:T(128)}, f32[8,512]{1,0:T(8,128)S(1)}, f32[8,3,512]{2,0,1:T(8,128)}, f32[8,3,512,512]{3,2,1,0:T(8,128)}, s32[]{:T(128)}, /*index=5*/s32[]{:T(128)}) %tuple.51), condition=%wide.region_6.7_spmd.clone, body=%wide.region_3.6_spmd.clone.sunk | while | flops 25194500 | bytes 151912576 | solution.py:128
  80.5 9.6 %multiply_reduce_fusion.6 = f32[8,3,512]{2,1,0:T(4,128)S(1)} fusion(f32[8,3,512,512]{3,2,1,0:T(8,128)} %get-tuple-element.150, f32[8,512]{1,0:T(8,128)S(1)} %broadcast_select_fusion.5), kind=kLoop, calls=%fused_computation.1.clone.1 | loop fusion | flops 12570624 | bytes 25231360 | tf_op jit(solution)/shard_map/while/body/eval_jaxpr/reduce_sum | solution.py:117
  90.3 5.6 %copy-done.2 = f32[8,3,512,512]{3,2,1,0:T(8,128)S(1)} copy-done((f32[8,3,512,512]{3,2,1,0:T(8,128)S(1)}, f32[8,3,512,512]{3,2,1,0:T(8,128)}, u32[]{:S(2)}) %copy-start.2) | copy-done | bytes 25165848 | tf_op jit(solution)/shard_map/while
  95.9 2.2 multiply_reduce_fusion.7
  98.2 9.6 %multiply_reduce_fusion.6 = f32[8,3,512]{2,1,0:T(4,128)S(1)} fusion(f32[8,3,512,512]{3,2,1,0:T(8,128)} %get-tuple-element.150, f32[8,512]{1,0:T(8,128)S(1)} %broadcast_select_fusion.5), kind=kLoop, calls=%fused_computation.1.clone.1 | loop fusion | flops 12570624 | bytes 25231360 | tf_op jit(solution)/shard_map/while/body/eval_jaxpr/reduce_sum | solution.py:117
  108.0 5.6 %copy-done.2 = f32[8,3,512,512]{3,2,1,0:T(8,128)S(1)} copy-done((f32[8,3,512,512]{3,2,1,0:T(8,128)S(1)}, f32[8,3,512,512]{3,2,1,0:T(8,128)}, u32[]{:S(2)}) %copy-start.2) | copy-done | bytes 25165848 | tf_op jit(solution)/shard_map/while
  113.6 2.2 multiply_reduce_fusion.7
  115.9 9.6 %multiply_reduce_fusion.6 = f32[8,3,512]{2,1,0:T(4,128)S(1)} fusion(f32[8,3,512,512]{3,2,1,0:T(8,128)} %get-tuple-element.150, f32[8,512]{1,0:T(8,128)S(1)} %broadcast_select_fusion.5), kind=kLoop, calls=%fused_computation.1.clone.1 | loop fusion | flops 12570624 | bytes 25231360 | tf_op jit(solution)/shard_map/while/body/eval_jaxpr/reduce_sum | solution.py:117
  125.7 5.6 %copy-done.2 = f32[8,3,512,512]{3,2,1,0:T(8,128)S(1)} copy-done((f32[8,3,512,512]{3,2,1,0:T(8,128)S(1)}, f32[8,3,512,512]{3,2,1,0:T(8,128)}, u32[]{:S(2)}) %copy-start.2) | copy-done | bytes 25165848 | tf_op jit(solution)/shard_map/while
  131.3 2.2 multiply_reduce_fusion.7
  133.6 9.6 %multiply_reduce_fusion.6 = f32[8,3,512]{2,1,0:T(4,128)S(1)} fusion(f32[8,3,512,512]{3,2,1,0:T(8,128)} %get-tuple-element.150, f32[8,512]{1,0:T(8,128)S(1)} %broadcast_select_fusion.5), kind=kLoop, calls=%fused_computation.1.clone.1 | loop fusion | flops 12570624 | bytes 25231360 | tf_op jit(solution)/shard_map/while/body/eval_jaxpr/reduce_sum | solution.py:117
  143.4 5.6 %copy-done.2 = f32[8,3,512,512]{3,2,1,0:T(8,128)S(1)} copy-done((f32[8,3,512,512]{3,2,1,0:T(8,128)S(1)}, f32[8,3,512,512]{3,2,1,0:T(8,128)}, u32[]{:S(2)}) %copy-start.2) | copy-done | bytes 25165848 | tf_op jit(solution)/shard_map/while
  149.0 2.2 multiply_reduce_fusion.7
  151.3 0.0 copy-start.3
  151.3 1.0 constant_dynamic-slice_fusion
  152.3 2.5 fusion.11
  154.8 0.1 slice_bitcast_fusion.6
  154.9 2.5 fusion.13
  157.3 31.6 %collective-permute-done.4 = bf16[256,4096]{1,0:T(8,128)(2,1)} collective-permute-done((bf16[256,4096]{1,0:T(8,128)(2,1)}, bf16[256,4096]{1,0:T(8,128)(2,1)}, u32[]{:S(2)}, u32[]{:S(2)}) %collective-permute-start.4) | collective-permute-done | bytes 2097184 | tf_op jit(solution)/shard_map/ppermute | solution.py:18
  189.0 0.0 collective-permute-done.5
  189.0 7.8 %convolution_add_fusion = f32[512,4096]{1,0:T(8,128)} fusion(f32[512,4096]{1,0:T(8,128)S(1)} %fusion.13, bf16[256,4096]{1,0:T(8,128)(2,1)} %collective-permute-done.5, bf16[256,4096]{1,0:T(8,128)(2,1)} %collective-permute-done.4, bf16[256,512]{1,0:T(8,128)(2,1)S(1)} %get-tuple-element.85, bf16[256,512]{1,0:T(8,128)(2,1)S(1)} %get-tuple-element.86), kind=kOutput, calls=%fused_computation.15 | convolution fusion | flops 2159017984 | bytes 21495808 | tf_op jit(solution)/shard_map/dot_general | solution.py:145
  196.8 36.3 %collective-permute-done = bf16[256,4096]{1,0:T(8,128)(2,1)} collective-permute-done((bf16[256,4096]{1,0:T(8,128)(2,1)}, bf16[256,4096]{1,0:T(8,128)(2,1)}, u32[]{:S(2)}, u32[]{:S(2)}) %collective-permute-start) | collective-permute-done | bytes 2097184 | tf_op jit(solution)/shard_map/ppermute | solution.py:18
  233.1 0.0 collective-permute-done.1
  233.1 7.8 %fusion.6 = f32[512,4096]{1,0:T(8,128)} fusion(bf16[256,4096]{1,0:T(8,128)(2,1)} %collective-permute-done.1, bf16[256,4096]{1,0:T(8,128)(2,1)} %collective-permute-done, bf16[256,512]{1,0:T(8,128)(2,1)S(1)} %get-tuple-element.84, bf16[256,512]{1,0:T(8,128)(2,1)S(1)} %get-tuple-element.83), kind=kOutput, calls=%fused_computation.19 | convolution fusion | flops 2156920832 | bytes 13107200 | tf_op jit(solution)/shard_map/dot_general | solution.py:145
  240.9 9.2 %add_convert_fusion = bf16[512,4096]{1,0:T(8,128)(2,1)} fusion(f32[512,4096]{1,0:T(8,128)} %convolution_add_fusion, f32[512,4096]{1,0:T(8,128)} %fusion.6), kind=kLoop, calls=%fused_computation.14 | loop fusion | flops 4194304 | bytes 20971520 | tf_op jit(solution)/shard_map/convert_element_type | solution.py:146
  (92 shorter events, 0.9 us)
Async XLA Ops:
  0.0 1.6 copy-start
  3.5 4.6 %copy-start.7 = (s32[512]{0:T(512)S(1)}, s32[512]{0:T(512)}, u32[]{:S(2)}) copy-start(s32[512]{0:T(512)} %param.16) | copy-start | bytes 6148
  3.5 4.6 %copy-start.8 = (s32[512]{0:T(512)S(1)}, s32[512]{0:T(512)}, u32[]{:S(2)}) copy-start(s32[512]{0:T(512)} %param.15) | copy-start | bytes 6148
  3.5 4.9 %copy-start.9 = (s32[1,2]{1,0:T(1,128)S(1)}, s32[1,2]{1,0:T(1,128)}, u32[]{:S(2)}) copy-start(s32[1,2]{1,0:T(1,128)} %param.17) | copy-start | bytes 28
  7.6 2.3 collective-permute-start.2
  45.0 5.2 %copy-start.4 = (bf16[8,528,128]{2,1,0:T(8,128)(2,1)}, bf16[8,528,128]{2,1,0:T(8,128)(2,1)S(1)}, u32[]{:S(2)}) copy-start(bf16[8,528,128]{2,1,0:T(8,128)(2,1)S(1)} %all_to_all.5) | copy-start | bytes 3244036
  45.0 17.9 %collective-permute-start.3 = (bf16[8,528,128]{2,1,0:T(8,128)(2,1)S(1)}, bf16[8,528,128]{2,1,0:T(8,128)(2,1)}, u32[]{:S(2)}, u32[]{:S(2)}) collective-permute-start(bf16[8,528,128]{2,1,0:T(8,128)(2,1)S(1)} %all_to_all.5), channel_id=1, source_target_pairs={{0,1},{1,0},{2,3},{3,2},{4,5},{5,4},{6,7},{7,6},{8,9},{9,8},{10,11... | collective-permute-start | bytes 3244040 | tf_op jit(solution)/shard_map/ppermute | solution.py:63
  50.2 138.8 %collective-permute-start.4 = (bf16[256,4096]{1,0:T(8,128)(2,1)}, bf16[256,4096]{1,0:T(8,128)(2,1)}, u32[]{:S(2)}, u32[]{:S(2)}) collective-permute-start(bf16[256,4096]{1,0:T(8,128)(2,1)} %get-tuple-element.79), channel_id=1, source_target_pairs={{0,2},{2,4},{4,6},{6,8},{8,10},{10,12},{12,14},{1,3},{3,5},{5,7},{... | collective-permute-start | bytes 6291464 | tf_op jit(solution)/shard_map/ppermute | solution.py:18
  54.1 134.9 %collective-permute-start.5 = (bf16[256,4096]{1,0:T(8,128)(2,1)}, bf16[256,4096]{1,0:T(8,128)(2,1)}, u32[]{:S(2)}, u32[]{:S(2)}) collective-permute-start(bf16[256,4096]{1,0:T(8,128)(2,1)} %get-tuple-element.79), channel_id=1, source_target_pairs={{2,0},{4,2},{6,4},{8,6},{10,8},{12,10},{14,12},{3,1},{5,3},{7,5},{... | collective-permute-start | bytes 6291464 | tf_op jit(solution)/shard_map/ppermute | solution.py:18
  55.4 177.7 %collective-permute-start = (bf16[256,4096]{1,0:T(8,128)(2,1)}, bf16[256,4096]{1,0:T(8,128)(2,1)}, u32[]{:S(2)}, u32[]{:S(2)}) collective-permute-start(bf16[256,4096]{1,0:T(8,128)(2,1)} %get-tuple-element.80), channel_id=1, source_target_pairs={{0,2},{2,4},{4,6},{6,8},{8,10},{10,12},{12,14},{1,3},{3,5},{5,7},{... | collective-permute-start | bytes 6291464 | tf_op jit(solution)/shard_map/ppermute | solution.py:18
  61.3 171.8 %collective-permute-start.1 = (bf16[256,4096]{1,0:T(8,128)(2,1)}, bf16[256,4096]{1,0:T(8,128)(2,1)}, u32[]{:S(2)}, u32[]{:S(2)}) collective-permute-start(bf16[256,4096]{1,0:T(8,128)(2,1)} %get-tuple-element.80), channel_id=1, source_target_pairs={{2,0},{4,2},{6,4},{8,6},{10,8},{12,10},{14,12},{3,1},{5,3},{7,5},{... | collective-permute-start | bytes 6291464 | tf_op jit(solution)/shard_map/ppermute | solution.py:18
  67.0 2.0 copy-start.6
  80.5 15.4 %copy-start.2 = (f32[8,3,512,512]{3,2,1,0:T(8,128)S(1)}, f32[8,3,512,512]{3,2,1,0:T(8,128)}, u32[]{:S(2)}) copy-start(f32[8,3,512,512]{3,2,1,0:T(8,128)} %get-tuple-element.150) | copy-start | bytes 75497472 | tf_op jit(solution)/shard_map/while
  90.2 7.9 %copy-start.5 = (f32[8,3,512]{2,0,1:T(8,128)}, f32[8,3,512]{2,0,1:T(8,128)S(1)}, u32[]{:S(2)}) copy-start(f32[8,3,512]{2,0,1:T(8,128)S(1)} %pad_maximum_fusion.10) | copy-start | bytes 147460 | tf_op jit(solution)/shard_map/while
  98.2 15.4 %copy-start.2 = (f32[8,3,512,512]{3,2,1,0:T(8,128)S(1)}, f32[8,3,512,512]{3,2,1,0:T(8,128)}, u32[]{:S(2)}) copy-start(f32[8,3,512,512]{3,2,1,0:T(8,128)} %get-tuple-element.150) | copy-start | bytes 75497472 | tf_op jit(solution)/shard_map/while
  108.0 7.9 %copy-start.5 = (f32[8,3,512]{2,0,1:T(8,128)}, f32[8,3,512]{2,0,1:T(8,128)S(1)}, u32[]{:S(2)}) copy-start(f32[8,3,512]{2,0,1:T(8,128)S(1)} %pad_maximum_fusion.10) | copy-start | bytes 147460 | tf_op jit(solution)/shard_map/while
  115.9 15.4 %copy-start.2 = (f32[8,3,512,512]{3,2,1,0:T(8,128)S(1)}, f32[8,3,512,512]{3,2,1,0:T(8,128)}, u32[]{:S(2)}) copy-start(f32[8,3,512,512]{3,2,1,0:T(8,128)} %get-tuple-element.150) | copy-start | bytes 75497472 | tf_op jit(solution)/shard_map/while
  125.7 7.9 %copy-start.5 = (f32[8,3,512]{2,0,1:T(8,128)}, f32[8,3,512]{2,0,1:T(8,128)S(1)}, u32[]{:S(2)}) copy-start(f32[8,3,512]{2,0,1:T(8,128)S(1)} %pad_maximum_fusion.10) | copy-start | bytes 147460 | tf_op jit(solution)/shard_map/while
  133.6 15.4 %copy-start.2 = (f32[8,3,512,512]{3,2,1,0:T(8,128)S(1)}, f32[8,3,512,512]{3,2,1,0:T(8,128)}, u32[]{:S(2)}) copy-start(f32[8,3,512,512]{3,2,1,0:T(8,128)} %get-tuple-element.150) | copy-start | bytes 75497472 | tf_op jit(solution)/shard_map/while
  143.4 7.9 %copy-start.5 = (f32[8,3,512]{2,0,1:T(8,128)}, f32[8,3,512]{2,0,1:T(8,128)S(1)}, u32[]{:S(2)}) copy-start(f32[8,3,512]{2,0,1:T(8,128)S(1)} %pad_maximum_fusion.10) | copy-start | bytes 147460 | tf_op jit(solution)/shard_map/while
  151.3 3.6 %copy-start.3 = (bf16[512,4096]{1,0:T(8,128)(2,1)S(1)}, bf16[512,4096]{1,0:T(8,128)(2,1)}, u32[]{:S(2)}) copy-start(bf16[512,4096]{1,0:T(8,128)(2,1)} %param.12) | copy-start | bytes 12582916
  240.9 9.2 %copy-start.1 = (bf16[512,2048]{1,0:T(8,128)(2,1)S(1)}, bf16[512,2048]{1,0:T(8,128)(2,1)}, u32[]{:S(2)}) copy-start(bf16[512,2048]{1,0:T(8,128)(2,1)} %param.11) | copy-start | bytes 6291460

commit v12 on v9

--- a/solution.py
+++ b/solution.py
@@ -90,7 +90,8 @@
     gathered = gather_halves(packed)
 
     left_rows = shifted(teacher_hidden, "seq", 1)
-    right_rows = shifted(teacher_hidden, "seq", -1)
+    second_rows, left_rows = lax.optimization_barrier((teacher_hidden, left_rows))
+    right_rows = shifted(second_rows, "seq", -1)
 
     s_unit = gathered[:, :rows, :proj_width]
     t_unit = gathered[:, :rows, proj_width:]

time: 241 us -> 241 us (level)
  local copies, waits for them, and re-layouts: 30.1 us -> 26.7 us
  transfers between devices with their start and end apart: 4 -> 4, of which waited for: 1 -> 2; matrix products, arithmetic and copies ran while one was open for 32% -> 32% of each run, Pallas kernels for 0% -> 0%
where the time goes in v12:
time: 241 us
  waiting for transfers between devices  85 us (35%)
  other arithmetic  53.3 us (22%)
  blocking collectives  34.5 us (14%)
  matrix products  34 us (14%)
  local copies, waits for them, and re-layouts  26.7 us (11%)
  starting transfers between devices  6.55 us (3%)
    ppermute x2, waiting for transfers between devices, shifted(): return lax.ppermute(block, axis, route)  85 us
    reduce_sum x4, other arithmetic, iterate(): partial_cols = jnp.sum(row_scale[:, None, None, :] * kernel, axis=3)  38.4 us
    all_to_all x1, blocking collectives, gather_halves(): lax.all_to_all(jnp.broadcast_to(mine, (n,) + mine.shape), 'seq', 0, 0, ti...  34.5 us
    while x16, local copies, waits for them, and re-layouts  22.4 us
    dot_general x1, matrix products, body_local(): jnp.einsum('bkjp,bip->bkji', beside(t_unit), s_unit, preferred_element_ty...  11.6 us
    reduce_sum x4, other arithmetic, iterate(): row_scale = 1.0 / jnp.sum(kernel * col_scale[:, :, :, None], axis=(1, 2))  8.94 us
    dot_general x1, matrix products, body_local(): lax.dot_general(plan[2], right_rows, along_j, preferred_element_type=jnp....  7.35 us
    ppermute x2, starting transfers between devices, shifted(): return lax.ppermute(block, axis, route)  6.03 us
  transfers between devices with their start and end apart: 4, of which 2 were waited for; matrix products, arithmetic and copies ran while one was open for 32% of the time, Pallas kernels for 0%

profile of v12, /device:TPU:0, one launch (start us, length us, event | category | flops | bytes accessed | tf_op | source)
XLA Modules:
  0.0 240.9 jit_solution(106058631500771781)
XLA Ops:
  0.0 0.0 copy-start
  0.0 1.6 copy-done
  1.6 1.9 fusion.27
  3.5 0.0 copy-start.5
  3.5 0.0 copy-start.6
  3.5 0.0 copy-start.7
  3.5 4.0 %fusion.28 = f32[512,128]{0,1:T(8,128)S(1)} fusion(bf16[512,4096]{1,0:T(8,128)(2,1)} %param.12, bf16[4096,128]{1,0:T(8,128)(2,1)} %param.14), kind=kOutput, calls=%fused_computation.97 | convolution fusion | flops 536870912 | bytes 5505024 | tf_op jit(solution)/shard_map/dot_general | solution.py:78
  7.6 0.5 collective-permute-start
  8.1 0.0 copy-done.5
  8.1 0.0 copy-done.6
  8.1 0.1 fusion.16
  8.2 0.1 copy.29
  8.3 0.0 copy-done.7
  8.4 0.1 copy.28
  8.5 0.1 pad.31.clone
  8.6 0.6 compare_reduce_fusion
  9.2 0.6 broadcast_select_fusion.3
  9.8 0.0 collective-permute-done
  9.9 0.1 fusion.20
  9.9 0.1 multiply_reduce_fusion.2
  10.0 0.1 multiply_convert_fusion
  10.1 0.1 fusion.11
  10.2 0.1 copy.30
  10.4 0.1 broadcast_in_dim.8
  10.5 34.5 %all_to_all.5 = bf16[8,528,128]{2,1,0:T(8,128)(2,1)S(1)} all-to-all(bf16[8,528,128]{2,1,0:T(8,128)(2,1)S(1)} %broadcast_in_dim.8), channel_id=1, replica_groups=mesh['groups'=2,'seq'=8,'tgrp'=2] {'seq'}, dimensions={0} | all-to-all | bytes 2162688 | tf_op jit(solution)/shard_map/all_to_all | solution.py:62
  45.0 0.0 collective-permute-start.1
  45.0 4.6 %collective-permute-start.2 = (bf16[512,4096]{1,0:T(8,128)(2,1)}, bf16[512,4096]{1,0:T(8,128)(2,1)}, u32[]{:S(2)}, u32[]{:S(2)}) collective-permute-start(bf16[512,4096]{1,0:T(8,128)(2,1)} %param.12), channel_id=1, source_target_pairs={{0,2},{2,4},{4,6},{6,8},{8,10},{10,12},{12,14},{1,3},{3,5},{5,7},{... | collective-permute-start | bytes 12582920 | tf_op jit(solution)/shard_map/ppermute | solution.py:18
  49.6 0.1 pad.17.clone
  49.7 0.0 copy-done.3
  49.7 0.0 collective-permute-done.1
  49.7 1.7 broadcast_select_fusion.1
  51.4 0.1 reshape.405
  51.5 0.1 slice_add_fusion
  51.8 0.2 fusion.23
  52.0 0.1 pad_bitcast_fusion.2
  52.1 0.1 pad_bitcast_fusion.3
  52.2 0.1 fusion.26
  52.3 0.1 pad_maximum_fusion.6
  52.3 0.1 slice_bitcast_fusion.2
  52.4 11.6 %exponential_multiply_fusion = f32[8,3,512,512]{3,2,1,0:T(8,128)} fusion(f32[8,3]{1,0:T(8,128)S(1)} %pad_maximum_fusion.6, f32[8,3,512]{2,1,0:T(4,128)S(1)} %copy.34, f32[8,512]{1,0:T(8,128)S(1)} %bitcast.93, bf16[8,528,128]{2,1,0:T(8,128)(2,1)S(1)} %get-tuple-element.77, bf16[8,1,512,128]{3,2,0,1:T(8,128)(2,1)S(1)} %pad_bitcast_fusion.2, ...), kind=kOutput, calls=%fused_computation.13 | convolution fusion | flops 1651507200 | bytes 29446144 | tf_op jit(solution)/shard_map/bkjp,bip->bkji/dot_general | solution.py:105
  64.0 74.4 %collective-permute-done.2 = bf16[512,4096]{1,0:T(8,128)(2,1)} collective-permute-done((bf16[512,4096]{1,0:T(8,128)(2,1)}, bf16[512,4096]{1,0:T(8,128)(2,1)}, u32[]{:S(2)}, u32[]{:S(2)}) %collective-permute-start.2) | collective-permute-done | bytes 4194336 | tf_op jit(solution)/shard_map/ppermute | solution.py:18
  138.4 1.5 collective-permute-start.3
  139.9 70.8 %while.14 = (s32[]{:T(128)}, f32[8,512]{1,0:T(8,128)S(1)}, f32[8,3,512]{2,0,1:T(8,128)}, f32[8,3,512,512]{3,2,1,0:T(8,128)}, s32[]{:T(128)}, /*index=5*/s32[]{:T(128)}) while((s32[]{:T(128)}, f32[8,512]{1,0:T(8,128)S(1)}, f32[8,3,512]{2,0,1:T(8,128)}, f32[8,3,512,512]{3,2,1,0:T(8,128)}, s32[]{:T(128)}, /*index=5*/s32[]{:T(128)}) %tuple.47), condition=%wide.region_6.7_spmd.clone, body=%wide.region_3.6_spmd.clone.sunk | while | flops 25194500 | bytes 151912576 | solution.py:124
  139.9 9.6 %multiply_reduce_fusion.6 = f32[8,3,512]{2,1,0:T(4,128)S(1)} fusion(f32[8,3,512,512]{3,2,1,0:T(8,128)} %get-tuple-element.142, f32[8,512]{1,0:T(8,128)S(1)} %broadcast_select_fusion.5), kind=kLoop, calls=%fused_computation.1.clone.1 | loop fusion | flops 12570624 | bytes 25231360 | tf_op jit(solution)/shard_map/while/body/eval_jaxpr/reduce_sum | solution.py:113
  149.7 5.6 %copy-done.2 = f32[8,3,512,512]{3,2,1,0:T(8,128)S(1)} copy-done((f32[8,3,512,512]{3,2,1,0:T(8,128)S(1)}, f32[8,3,512,512]{3,2,1,0:T(8,128)}, u32[]{:S(2)}) %copy-start.2) | copy-done | bytes 25165848 | tf_op jit(solution)/shard_map/while
  155.3 2.2 multiply_reduce_fusion.7
  157.6 9.6 %multiply_reduce_fusion.6 = f32[8,3,512]{2,1,0:T(4,128)S(1)} fusion(f32[8,3,512,512]{3,2,1,0:T(8,128)} %get-tuple-element.142, f32[8,512]{1,0:T(8,128)S(1)} %broadcast_select_fusion.5), kind=kLoop, calls=%fused_computation.1.clone.1 | loop fusion | flops 12570624 | bytes 25231360 | tf_op jit(solution)/shard_map/while/body/eval_jaxpr/reduce_sum | solution.py:113
  167.4 5.6 %copy-done.2 = f32[8,3,512,512]{3,2,1,0:T(8,128)S(1)} copy-done((f32[8,3,512,512]{3,2,1,0:T(8,128)S(1)}, f32[8,3,512,512]{3,2,1,0:T(8,128)}, u32[]{:S(2)}) %copy-start.2) | copy-done | bytes 25165848 | tf_op jit(solution)/shard_map/while
  173.0 2.2 multiply_reduce_fusion.7
  175.3 0.0 copy-start.2
  175.3 9.6 %multiply_reduce_fusion.6 = f32[8,3,512]{2,1,0:T(4,128)S(1)} fusion(f32[8,3,512,512]{3,2,1,0:T(8,128)} %get-tuple-element.142, f32[8,512]{1,0:T(8,128)S(1)} %broadcast_select_fusion.5), kind=kLoop, calls=%fused_computation.1.clone.1 | loop fusion | flops 12570624 | bytes 25231360 | tf_op jit(solution)/shard_map/while/body/eval_jaxpr/reduce_sum | solution.py:113
  185.1 5.6 %copy-done.2 = f32[8,3,512,512]{3,2,1,0:T(8,128)S(1)} copy-done((f32[8,3,512,512]{3,2,1,0:T(8,128)S(1)}, f32[8,3,512,512]{3,2,1,0:T(8,128)}, u32[]{:S(2)}) %copy-start.2) | copy-done | bytes 25165848 | tf_op jit(solution)/shard_map/while
  190.7 2.2 multiply_reduce_fusion.7
  193.0 0.0 copy-start.2
  193.0 9.6 %multiply_reduce_fusion.6 = f32[8,3,512]{2,1,0:T(4,128)S(1)} fusion(f32[8,3,512,512]{3,2,1,0:T(8,128)} %get-tuple-element.142, f32[8,512]{1,0:T(8,128)S(1)} %broadcast_select_fusion.5), kind=kLoop, calls=%fused_computation.1.clone.1 | loop fusion | flops 12570624 | bytes 25231360 | tf_op jit(solution)/shard_map/while/body/eval_jaxpr/reduce_sum | solution.py:113
  202.8 0.0 copy-start.4
  202.8 5.6 %copy-done.2 = f32[8,3,512,512]{3,2,1,0:T(8,128)S(1)} copy-done((f32[8,3,512,512]{3,2,1,0:T(8,128)S(1)}, f32[8,3,512,512]{3,2,1,0:T(8,128)}, u32[]{:S(2)}) %copy-start.2) | copy-done | bytes 25165848 | tf_op jit(solution)/shard_map/while
  208.4 2.2 multiply_reduce_fusion.7
  210.7 0.8 constant_dynamic-slice_fusion
  211.5 2.2 fusion.4
  213.8 4.6 %fusion.7 = f32[512,4096]{1,0:T(8,128)S(1)} fusion(bf16[512,4096]{1,0:T(8,128)(2,1)} %param.12, bf16[3,512,512]{2,1,0:T(8,128)(2,1)S(1)} %fusion.4), kind=kOutput, calls=%fused_computation.30 | convolution fusion | flops 2147483648 | bytes 13107200 | tf_op jit(solution)/shard_map/dot_general | solution.py:135
  218.4 4.6 %fusion.6 = f32[512,4096]{1,0:T(8,128)S(1)} fusion(bf16[512,4096]{1,0:T(8,128)(2,1)} %collective-permute-done.2, bf16[3,512,512]{2,1,0:T(8,128)(2,1)S(1)} %fusion.4), kind=kOutput, calls=%fused_computation.28 | convolution fusion | flops 2147483648 | bytes 13107200 | tf_op jit(solution)/shard_map/dot_general | solution.py:136
  223.0 10.5 %collective-permute-done.3 = bf16[512,4096]{1,0:T(8,128)(2,1)} collective-permute-done((bf16[512,4096]{1,0:T(8,128)(2,1)}, bf16[512,4096]{1,0:T(8,128)(2,1)}, u32[]{:S(2)}, u32[]{:S(2)}) %collective-permute-start.3) | collective-permute-done | bytes 4194336 | tf_op jit(solution)/shard_map/ppermute | solution.py:18
  233.6 7.4 %add_convert_fusion = bf16[512,4096]{1,0:T(8,128)(2,1)} fusion(f32[512,4096]{1,0:T(8,128)S(1)} %fusion.7, f32[512,4096]{1,0:T(8,128)S(1)} %fusion.6, bf16[512,4096]{1,0:T(8,128)(2,1)} %collective-permute-done.3, bf16[3,512,512]{2,1,0:T(8,128)(2,1)S(1)} %fusion.4), kind=kOutput, calls=%fused_computation.14 | convolution fusion | flops 2153775104 | bytes 25690112 | tf_op jit(solution)/shard_map/dot_general | solution.py:137
  (81 shorter events, 0.8 us)
Async XLA Ops:
  0.0 1.6 copy-start
  3.5 4.6 %copy-start.5 = (s32[512]{0:T(512)S(1)}, s32[512]{0:T(512)}, u32[]{:S(2)}) copy-start(s32[512]{0:T(512)} %param.16) | copy-start | bytes 6148
  3.5 4.6 %copy-start.6 = (s32[512]{0:T(512)S(1)}, s32[512]{0:T(512)}, u32[]{:S(2)}) copy-start(s32[512]{0:T(512)} %param.15) | copy-start | bytes 6148
  3.5 4.9 %copy-start.7 = (s32[1,2]{1,0:T(1,128)S(1)}, s32[1,2]{1,0:T(1,128)}, u32[]{:S(2)}) copy-start(s32[1,2]{1,0:T(1,128)} %param.17) | copy-start | bytes 28
  7.6 2.3 collective-permute-start
  45.0 4.7 %copy-start.3 = (bf16[8,528,128]{2,1,0:T(8,128)(2,1)}, bf16[8,528,128]{2,1,0:T(8,128)(2,1)S(1)}, u32[]{:S(2)}) copy-start(bf16[8,528,128]{2,1,0:T(8,128)(2,1)S(1)} %all_to_all.5) | copy-start | bytes 3244036
  45.0 4.7 %collective-permute-start.1 = (bf16[8,528,128]{2,1,0:T(8,128)(2,1)S(1)}, bf16[8,528,128]{2,1,0:T(8,128)(2,1)}, u32[]{:S(2)}, u32[]{:S(2)}) collective-permute-start(bf16[8,528,128]{2,1,0:T(8,128)(2,1)S(1)} %all_to_all.5), channel_id=1, source_target_pairs={{0,1},{1,0},{2,3},{3,2},{4,5},{5,4},{6,7},{7,6},{8,9},{9,8},{10,11... | collective-permute-start | bytes 3244040 | tf_op jit(solution)/shard_map/ppermute | solution.py:63
  45.0 93.4 %collective-permute-start.2 = (bf16[512,4096]{1,0:T(8,128)(2,1)}, bf16[512,4096]{1,0:T(8,128)(2,1)}, u32[]{:S(2)}, u32[]{:S(2)}) collective-permute-start(bf16[512,4096]{1,0:T(8,128)(2,1)} %param.12), channel_id=1, source_target_pairs={{0,2},{2,4},{4,6},{6,8},{8,10},{10,12},{12,14},{1,3},{3,5},{5,7},{... | collective-permute-start | bytes 12582920 | tf_op jit(solution)/shard_map/ppermute | solution.py:18
  138.4 95.2 %collective-permute-start.3 = (bf16[512,4096]{1,0:T(8,128)(2,1)}, bf16[512,4096]{1,0:T(8,128)(2,1)}, u32[]{:S(2)}, u32[]{:S(2)}) collective-permute-start(bf16[512,4096]{1,0:T(8,128)(2,1)} %param.12), channel_id=1, source_target_pairs={{2,0},{4,2},{6,4},{8,6},{10,8},{12,10},{14,12},{3,1},{5,3},{7,5},{... | collective-permute-start | bytes 12582920 | tf_op jit(solution)/shard_map/ppermute | solution.py:18
  139.9 15.4 %copy-start.2 = (f32[8,3,512,512]{3,2,1,0:T(8,128)S(1)}, f32[8,3,512,512]{3,2,1,0:T(8,128)}, u32[]{:S(2)}) copy-start(f32[8,3,512,512]{3,2,1,0:T(8,128)} %get-tuple-element.142) | copy-start | bytes 75497472 | tf_op jit(solution)/shard_map/while
  149.7 7.9 %copy-start.4 = (f32[8,3,512]{2,0,1:T(8,128)}, f32[8,3,512]{2,0,1:T(8,128)S(1)}, u32[]{:S(2)}) copy-start(f32[8,3,512]{2,0,1:T(8,128)S(1)} %pad_maximum_fusion.10) | copy-start | bytes 147460 | tf_op jit(solution)/shard_map/while
  157.6 15.4 %copy-start.2 = (f32[8,3,512,512]{3,2,1,0:T(8,128)S(1)}, f32[8,3,512,512]{3,2,1,0:T(8,128)}, u32[]{:S(2)}) copy-start(f32[8,3,512,512]{3,2,1,0:T(8,128)} %get-tuple-element.142) | copy-start | bytes 75497472 | tf_op jit(solution)/shard_map/while
  167.4 7.9 %copy-start.4 = (f32[8,3,512]{2,0,1:T(8,128)}, f32[8,3,512]{2,0,1:T(8,128)S(1)}, u32[]{:S(2)}) copy-start(f32[8,3,512]{2,0,1:T(8,128)S(1)} %pad_maximum_fusion.10) | copy-start | bytes 147460 | tf_op jit(solution)/shard_map/while
  175.3 15.4 %copy-start.2 = (f32[8,3,512,512]{3,2,1,0:T(8,128)S(1)}, f32[8,3,512,512]{3,2,1,0:T(8,128)}, u32[]{:S(2)}) copy-start(f32[8,3,512,512]{3,2,1,0:T(8,128)} %get-tuple-element.142) | copy-start | bytes 75497472 | tf_op jit(solution)/shard_map/while
  185.1 7.9 %copy-start.4 = (f32[8,3,512]{2,0,1:T(8,128)}, f32[8,3,512]{2,0,1:T(8,128)S(1)}, u32[]{:S(2)}) copy-start(f32[8,3,512]{2,0,1:T(8,128)S(1)} %pad_maximum_fusion.10) | copy-start | bytes 147460 | tf_op jit(solution)/shard_map/while
  193.0 15.4 %copy-start.2 = (f32[8,3,512,512]{3,2,1,0:T(8,128)S(1)}, f32[8,3,512,512]{3,2,1,0:T(8,128)}, u32[]{:S(2)}) copy-start(f32[8,3,512,512]{3,2,1,0:T(8,128)} %get-tuple-element.142) | copy-start | bytes 75497472 | tf_op jit(solution)/shard_map/while
  202.8 7.9 %copy-start.4 = (f32[8,3,512]{2,0,1:T(8,128)}, f32[8,3,512]{2,0,1:T(8,128)S(1)}, u32[]{:S(2)}) copy-start(f32[8,3,512]{2,0,1:T(8,128)S(1)} %pad_maximum_fusion.10) | copy-start | bytes 147460 | tf_op jit(solution)/shard_map/while
  233.6 7.4 %copy-start.1 = (bf16[512,2048]{1,0:T(8,128)(2,1)S(1)}, bf16[512,2048]{1,0:T(8,128)(2,1)}, u32[]{:S(2)}) copy-start(bf16[512,2048]{1,0:T(8,128)(2,1)} %param.11) | copy-start | bytes 6291460

commit v13 on v4

--- a/solution.py
+++ b/solution.py
@@ -36,13 +36,29 @@
     return lax.psum(value, "tgrp")
 
 
+SEQ = ("z", "y")
+
+
+def seq_shifted(block, distance):
+    devices = range(lax.axis_size("z") * lax.axis_size("y"))
+    route = [(i - distance, i) for i in devices if i - distance in devices]
+    return lax.ppermute(block, SEQ, route)
+
+
+def gather_pairs(mine):
+    partner = lax.ppermute(mine, "y", [(0, 1), (1, 0)])
+    second = lax.axis_index("y") == 1
+    pair = jnp.stack([jnp.where(second, partner, mine), jnp.where(second, mine, partner)])
+    z_size = lax.axis_size("z")
+    got = lax.all_to_all(jnp.broadcast_to(pair, (z_size,) + pair.shape), "z", 0, 0, tiled=False)
+    return got.reshape((z_size * 2,) + mine.shape)
+
+
 def gather_halves(packed):
-    if lax.axis_size("tgrp") != 2:
-        return lax.all_gather(packed, "seq")
     half = packed.shape[1] // 2
     core = lax.axis_index("tgrp")
     mine = lax.dynamic_slice_in_dim(packed, core * half, half, 1)
-    got = lax.all_gather(mine, "seq")
+    got = gather_pairs(mine)
     theirs = lax.ppermute(got, "tgrp", [(0, 1), (1, 0)])
     first = jnp.where(core == 0, got, theirs)
     second = jnp.where(core == 0, theirs, got)
@@ -54,8 +70,8 @@
 ):
     rows = student_hidden.shape[0]
     proj_width = student_proj.shape[1]
-    blocks = lax.axis_size("seq")
-    me = lax.axis_index("seq")
+    blocks = lax.axis_size("z") * lax.axis_size("y")
+    me = lax.axis_index("z") * lax.axis_size("y") + lax.axis_index("y")
 
     s_part = jnp.dot(student_hidden, student_proj, preferred_element_type=jnp.float32)
     t_part = jnp.dot(teacher_hidden, teacher_proj, preferred_element_type=jnp.float32)
@@ -72,9 +88,8 @@
     packed = jnp.concatenate([units, extra, jnp.zeros((pad, units.shape[1]), jnp.bfloat16)], 0)
     gathered = gather_halves(packed)
 
-    teacher_rows, gathered = lax.optimization_barrier((teacher_hidden, gathered))
-    left_rows = shifted(teacher_rows, "seq", 1)
-    right_rows = shifted(teacher_rows, "seq", -1)
+    left_rows = seq_shifted(teacher_hidden, 1)
+    right_rows = seq_shifted(teacher_hidden, -1)
 
     s_unit = gathered[:, :rows, :proj_width]
     t_unit = gathered[:, :rows, proj_width:]
@@ -116,8 +131,9 @@
     plan = (own_row[None, None, :] * own_kernel * own_col[:, :, None]).astype(jnp.bfloat16)
     along_j = (((0,), (0,)), ((), ()))
     aligned = lax.dot_general(plan[1], teacher_hidden, along_j, preferred_element_type=jnp.float32)
-    aligned = aligned + lax.dot_general(plan[0], left_rows, along_j, preferred_element_type=jnp.float32)
-    aligned = aligned + lax.dot_general(plan[2], right_rows, along_j, preferred_element_type=jnp.float32)
+    sides = jnp.concatenate([plan[0], plan[2]], 0)
+    near_rows = jnp.concatenate([left_rows, right_rows], 0)
+    aligned = aligned + lax.dot_general(sides, near_rows, along_j, preferred_element_type=jnp.float32)
     return aligned.astype(jnp.bfloat16)
 
 
@@ -169,27 +185,41 @@
     return aligned.astype(jnp.bfloat16)
 
 
+def specs(seq):
+    return dict(
+        in_specs=(
+            P(("groups",) + seq, "tgrp"),
+            P(("groups",) + seq, "tgrp"),
+            P("tgrp", None),
+            P("tgrp", None),
+            P(("groups",) + seq),
+            P(("groups",) + seq),
+            P(("groups",) + seq, None),
+        ),
+        out_specs=P(("groups",) + seq, "tgrp"),
+    )
+
+
 def solution(mesh):
     blocks = mesh.shape["seq"]
-
-    def body(*args):
-        rows = args[0].shape[0]
-        if blocks * 3 * rows * rows * 4 <= LOCAL_KERNEL_BYTES:
-            return body_local(*args)
-        return body_banded(*args)
-
-    return jax.shard_map(
-        body,
-        mesh=mesh,
-        in_specs=(
-            P(("groups", "seq"), "tgrp"),
-            P(("groups", "seq"), "tgrp"),
-            P("tgrp", None),
-            P("tgrp", None),
-            P(("groups", "seq")),
-            P(("groups", "seq")),
-            P(("groups", "seq"), None),
-        ),
-        out_specs=P(("groups", "seq"), "tgrp"),
-        check_vma=False,
-    )
+    sizes = dict(mesh.shape)
+
+    def fits(rows):
+        return blocks * 3 * rows * rows * 4 <= LOCAL_KERNEL_BYTES
+
+    local = blocks % 2 == 0 and sizes["tgrp"] == 2
+    if local:
+        view = jax.sharding.Mesh(
+            mesh.devices.reshape(sizes["groups"], blocks // 2, 2, sizes["tgrp"]),
+            ("groups", "z", "y", "tgrp"),
+        )
+        local_fn = jax.shard_map(body_local, mesh=view, check_vma=False, **specs(SEQ))
+    banded_fn = jax.shard_map(body_banded, mesh=mesh, check_vma=False, **specs(("seq",)))
+
+    def run(*args):
+        rows = args[0].shape[0] // (sizes["groups"] * blocks)
+        if local and fits(rows):
+            return local_fn(*args)
+        return banded_fn(*args)
+
+    return run

time: 269 us -> 244 us (0.907)
  waiting for transfers between devices: 134 us -> 86.7 us
  blocking collectives: 0 us -> 31 us
  between operations: 13.8 us -> 0.37 us
  starting transfers between devices: 6.42 us -> 10.1 us
  local copies, waits for them, and re-layouts: 28.4 us -> 31.1 us
    all_gather x1 -> x0, waiting for transfers between devices: 42.9 us -> none  [gather_halves(): got = lax.all_gather(mine, 'seq')]
    all_to_all x0 -> x1, blocking collectives: none -> 31 us  [gather_pairs(): lax.all_to_all(jnp.broadcast_to(pair, (z_size,) + pair.shape), 'z', 0, 0,...]
    ppermute x2 -> x3, starting transfers between devices: 5.89 us -> 9.54 us  [the longest x2 6.82 us: seq_shifted(): return lax.ppermute(block, SEQ, route)]
    ppermute x1, waiting for transfers between devices: 2.84 us -> 0.01 us  [gather_halves(): theirs = lax.ppermute(got, 'tgrp', [(0, 1), (1, 0)])]
    dot_general x2 -> x1, matrix products: 12 us -> 10.7 us  [body_local(): lax.dot_general(sides, near_rows, along_j, preferred_element_type=jnp.flo...]
    ppermute x2 -> x3, waiting for transfers between devices: 87.9 us -> 86.7 us  [the longest x2 82 us: seq_shifted(): return lax.ppermute(block, SEQ, route)]
  transfers between devices with their start and end apart: 5 -> 5, of which waited for: 3 -> 2; matrix products, arithmetic and copies ran while one was open for 27% -> 30% of each run, Pallas kernels for 0% -> 0%
where the time goes in v13:
time: 244 us
  waiting for transfers between devices  86.7 us (36%)
  other arithmetic  53.7 us (22%)
  local copies, waits for them, and re-layouts  31.1 us (13%)
  blocking collectives  31 us (13%)
  matrix products  30.5 us (12%)
  starting transfers between devices  10.1 us (4%)
    ppermute x2, waiting for transfers between devices, seq_shifted(): return lax.ppermute(block, SEQ, route)  82 us
    reduce_sum x4, other arithmetic, iterate(): partial_cols = jnp.sum(row_scale[:, None, None, :] * kernel, axis=3)  38.4 us
    all_to_all x1, blocking collectives, gather_pairs(): lax.all_to_all(jnp.broadcast_to(pair, (z_size,) + pair.shape), 'z', 0, 0,...  31 us
    while x16, local copies, waits for them, and re-layouts  22.4 us
    dot_general x1, matrix products, body_local(): jnp.einsum('bkjp,bip->bkji', beside(t_unit), s_unit, preferred_element_ty...  11.5 us
    dot_general x1, matrix products, body_local(): lax.dot_general(sides, near_rows, along_j, preferred_element_type=jnp.flo...  10.7 us
    reduce_sum x4, other arithmetic, iterate(): row_scale = 1.0 / jnp.sum(kernel * col_scale[:, :, :, None], axis=(1, 2))  8.94 us
    ppermute x2, starting transfers between devices, seq_shifted(): return lax.ppermute(block, SEQ, route)  6.82 us
  transfers between devices with their start and end apart: 5, of which 2 were waited for; matrix products, arithmetic and copies ran while one was open for 30% of the time, Pallas kernels for 0%

profile of v13, /device:TPU:0, one launch (start us, length us, event | category | flops | bytes accessed | tf_op | source)
XLA Modules:
  0.0 244.0 jit_solution(13515642888111258803)
XLA Ops:
  0.0 0.0 copy-start
  0.0 1.6 copy-done
  1.6 1.9 fusion.36
  3.5 0.0 copy-start.7
  3.5 0.0 copy-start.8
  3.5 0.0 copy-start.9
  3.5 4.0 %fusion.37 = f32[512,128]{0,1:T(8,128)S(1)} fusion(bf16[512,4096]{1,0:T(8,128)(2,1)} %param.12, bf16[4096,128]{1,0:T(8,128)(2,1)} %param.14), kind=kOutput, calls=%fused_computation.107 | convolution fusion | flops 536870912 | bytes 5505024 | tf_op jit(solution)/shard_map/dot_general | solution.py:77
  7.6 0.5 collective-permute-start
  8.1 0.0 copy-done.7
  8.1 0.1 fusion.24
  8.2 0.1 copy.29
  8.4 0.1 copy.28
  8.5 0.1 pad.37.clone
  8.6 0.6 compare_reduce_fusion
  9.2 0.6 broadcast_select_fusion.3
  9.8 0.0 collective-permute-done
  9.9 0.1 fusion.29
  9.9 0.1 multiply_reduce_fusion.2
  10.0 0.1 multiply_convert_fusion
  10.1 0.1 fusion.19
  10.2 2.7 %collective-permute-start.1 = (bf16[528,128]{0,1:T(8,128)(2,1)S(1)}, bf16[528,128]{0,1:T(8,128)(2,1)S(1)}, u32[]{:S(2)}, u32[]{:S(2)}) collective-permute-start(bf16[528,128]{0,1:T(8,128)(2,1)S(1)} %fusion.19), channel_id=1, source_target_pairs={{0,2},{2,0},{1,3},{3,1},{4,6},{6,4},{5,7},{7,5},{8,10},{10,8},{9,1... | collective-permute-start | bytes 405512 | tf_op jit(solution)/shard_map/ppermute | solution.py:49
  13.0 4.7 %collective-permute-done.1 = bf16[528,128]{0,1:T(8,128)(2,1)S(1)} collective-permute-done((bf16[528,128]{0,1:T(8,128)(2,1)S(1)}, bf16[528,128]{0,1:T(8,128)(2,1)S(1)}, u32[]{:S(2)}, u32[]{:S(2)}) %collective-permute-start.1) | collective-permute-done | bytes 135200 | tf_op jit(solution)/shard_map/ppermute | solution.py:49
  17.7 0.1 pad_maximum_fusion.3
  17.8 0.2 copy.30
  18.0 0.1 broadcast_in_dim.8
  18.1 31.0 %all_to_all.5 = bf16[4,2,528,128]{3,2,1,0:T(8,128)(2,1)S(1)} all-to-all(bf16[4,2,528,128]{3,2,1,0:T(8,128)(2,1)S(1)} %broadcast_in_dim.8), channel_id=1, replica_groups=mesh['groups'=2,'z'=4,'y'=2,'tgrp'=2] {'z'}, dimensions={0} | all-to-all | bytes 2162688 | tf_op jit(solution)/shard_map/all_to_all | solution.py:53
  49.2 0.0 collective-permute-start.2
  49.2 5.4 %collective-permute-start.3 = (bf16[512,4096]{1,0:T(8,128)(2,1)}, bf16[512,4096]{1,0:T(8,128)(2,1)}, u32[]{:S(2)}, u32[]{:S(2)}) collective-permute-start(bf16[512,4096]{1,0:T(8,128)(2,1)} %param.12), channel_id=1, source_target_pairs={{0,2},{2,4},{4,6},{6,8},{8,10},{10,12},{12,14},{1,3},{3,5},{5,7},{... | collective-permute-start | bytes 12582920 | tf_op jit(solution)/shard_map/ppermute | solution.py:45
  54.6 1.5 collective-permute-start.4
  56.1 0.1 pad.21.clone
  56.1 0.0 collective-permute-done.2
  56.1 1.7 broadcast_select_fusion.1
  57.8 1.2 fusion.32
  59.1 1.0 slice_bitcast_fusion.2
  60.1 0.1 reshape.409
  60.2 0.0 copy-start.6
  60.2 0.1 slice_add_fusion
  60.4 1.4 pad_bitcast_fusion.2
  61.8 0.1 pad_bitcast_fusion.3
  62.0 0.1 fusion.35
  62.1 0.1 pad_maximum_fusion.7
  62.2 11.5 %exponential_multiply_fusion = f32[8,3,512,512]{3,2,1,0:T(8,128)} fusion(f32[8,3]{1,0:T(8,128)S(1)} %pad_maximum_fusion.7, f32[8,3,512]{2,1,0:T(4,128)S(1)} %copy.34, f32[8,512]{1,0:T(8,128)S(1)} %bitcast.97, bf16[8,528,128]{2,1,0:T(8,128)(2,1)S(1)} %get-tuple-element.73, bf16[8,1,512,128]{3,2,0,1:T(8,128)(2,1)S(1)} %pad_bitcast_fusion.2, ...), kind=kOutput, calls=%fused_computation.13 | convolution fusion | flops 1651507200 | bytes 29446144 | tf_op jit(solution)/shard_map/bkjp,bip->bkji/dot_general | solution.py:103
  73.7 70.8 %while.14 = (s32[]{:T(128)}, f32[8,512]{1,0:T(8,128)S(1)}, f32[8,3,512]{2,0,1:T(8,128)}, f32[8,3,512,512]{3,2,1,0:T(8,128)}, s32[]{:T(128)}, /*index=5*/s32[]{:T(128)}) while((s32[]{:T(128)}, f32[8,512]{1,0:T(8,128)S(1)}, f32[8,3,512]{2,0,1:T(8,128)}, f32[8,3,512,512]{3,2,1,0:T(8,128)}, s32[]{:T(128)}, /*index=5*/s32[]{:T(128)}) %tuple.47), condition=%wide.region_6.7_spmd.clone, body=%wide.region_3.6_spmd.clone.sunk | while | flops 25194500 | bytes 151912576 | solution.py:122
  73.7 9.6 %multiply_reduce_fusion.6 = f32[8,3,512]{2,1,0:T(4,128)S(1)} fusion(f32[8,3,512,512]{3,2,1,0:T(8,128)} %get-tuple-element.142, f32[8,512]{1,0:T(8,128)S(1)} %broadcast_select_fusion.5), kind=kLoop, calls=%fused_computation.1.clone.1 | loop fusion | flops 12570624 | bytes 25231360 | tf_op jit(solution)/shard_map/while/body/eval_jaxpr/reduce_sum | solution.py:111
  83.4 0.0 copy-start.5
  83.5 5.6 %copy-done.2 = f32[8,3,512,512]{3,2,1,0:T(8,128)S(1)} copy-done((f32[8,3,512,512]{3,2,1,0:T(8,128)S(1)}, f32[8,3,512,512]{3,2,1,0:T(8,128)}, u32[]{:S(2)}) %copy-start.2) | copy-done | bytes 25165848 | tf_op jit(solution)/shard_map/while
  89.1 2.2 multiply_reduce_fusion.7
  91.4 9.6 %multiply_reduce_fusion.6 = f32[8,3,512]{2,1,0:T(4,128)S(1)} fusion(f32[8,3,512,512]{3,2,1,0:T(8,128)} %get-tuple-element.142, f32[8,512]{1,0:T(8,128)S(1)} %broadcast_select_fusion.5), kind=kLoop, calls=%fused_computation.1.clone.1 | loop fusion | flops 12570624 | bytes 25231360 | tf_op jit(solution)/shard_map/while/body/eval_jaxpr/reduce_sum | solution.py:111
  101.2 5.6 %copy-done.2 = f32[8,3,512,512]{3,2,1,0:T(8,128)S(1)} copy-done((f32[8,3,512,512]{3,2,1,0:T(8,128)S(1)}, f32[8,3,512,512]{3,2,1,0:T(8,128)}, u32[]{:S(2)}) %copy-start.2) | copy-done | bytes 25165848 | tf_op jit(solution)/shard_map/while
  106.8 2.2 multiply_reduce_fusion.7
  109.1 9.6 %multiply_reduce_fusion.6 = f32[8,3,512]{2,1,0:T(4,128)S(1)} fusion(f32[8,3,512,512]{3,2,1,0:T(8,128)} %get-tuple-element.142, f32[8,512]{1,0:T(8,128)S(1)} %broadcast_select_fusion.5), kind=kLoop, calls=%fused_computation.1.clone.1 | loop fusion | flops 12570624 | bytes 25231360 | tf_op jit(solution)/shard_map/while/body/eval_jaxpr/reduce_sum | solution.py:111
  118.9 5.6 %copy-done.2 = f32[8,3,512,512]{3,2,1,0:T(8,128)S(1)} copy-done((f32[8,3,512,512]{3,2,1,0:T(8,128)S(1)}, f32[8,3,512,512]{3,2,1,0:T(8,128)}, u32[]{:S(2)}) %copy-start.2) | copy-done | bytes 25165848 | tf_op jit(solution)/shard_map/while
  124.5 2.2 multiply_reduce_fusion.7
  126.8 9.6 %multiply_reduce_fusion.6 = f32[8,3,512]{2,1,0:T(4,128)S(1)} fusion(f32[8,3,512,512]{3,2,1,0:T(8,128)} %get-tuple-element.142, f32[8,512]{1,0:T(8,128)S(1)} %broadcast_select_fusion.5), kind=kLoop, calls=%fused_computation.1.clone.1 | loop fusion | flops 12570624 | bytes 25231360 | tf_op jit(solution)/shard_map/while/body/eval_jaxpr/reduce_sum | solution.py:111
  136.6 5.6 %copy-done.2 = f32[8,3,512,512]{3,2,1,0:T(8,128)S(1)} copy-done((f32[8,3,512,512]{3,2,1,0:T(8,128)S(1)}, f32[8,3,512,512]{3,2,1,0:T(8,128)}, u32[]{:S(2)}) %copy-start.2) | copy-done | bytes 25165848 | tf_op jit(solution)/shard_map/while
  142.2 2.2 multiply_reduce_fusion.7
  144.5 0.0 copy-start.3
  144.5 1.0 constant_dynamic-slice_fusion
  145.5 2.5 %fusion.10 = bf16[3,512,512]{2,1,0:T(8,128)(2,1)S(1)} fusion(f32[8,3,512,512]{3,2,1,0:T(8,128)} %get-tuple-element.145, s32[]{:T(128)S(6)} %select_n.93, f32[3,512]{1,0:T(4,128)S(1)} %bitcast.95, f32[512]{0:T(512)S(1)} %bitcast.98), kind=kLoop, calls=%fused_computation.22 | loop fusion | flops 2359296 | bytes 4726788 | tf_op jit(solution)/shard_map/convert_element_type | solution.py:131
  148.0 0.9 slice_bitcast_fusion.4
  148.9 2.4 %fusion.15 = f32[512,4096]{1,0:T(8,128)S(1)} fusion(bf16[512,4096]{1,0:T(8,128)(2,1)S(1)} %copy-done.3, bf16[3,512,512]{2,1,0:T(8,128)(2,1)S(1)} %fusion.10), kind=kOutput, calls=%fused_computation.36 | convolution fusion | flops 2147483648 | bytes 13107200 | tf_op jit(solution)/shard_map/dot_general | solution.py:133
  151.3 82.0 %collective-permute-done.3 = bf16[512,4096]{1,0:T(8,128)(2,1)} collective-permute-done((bf16[512,4096]{1,0:T(8,128)(2,1)}, bf16[512,4096]{1,0:T(8,128)(2,1)}, u32[]{:S(2)}, u32[]{:S(2)}) %collective-permute-start.3) | collective-permute-done | bytes 4194336 | tf_op jit(solution)/shard_map/ppermute | solution.py:45
  233.3 0.0 collective-permute-done.4
  233.3 10.7 %add_convert_fusion = bf16[512,4096]{1,0:T(8,128)(2,1)} fusion(f32[512,4096]{1,0:T(8,128)S(1)} %fusion.15, bf16[512,4096]{1,0:T(8,128)(2,1)} %collective-permute-done.4, bf16[512,4096]{1,0:T(8,128)(2,1)} %collective-permute-done.3, bf16[512,512]{1,0:T(8,128)(2,1)} %get-tuple-element.76, bf16[512,512]{1,0:T(8,128)(2,1)S(1)} %get-tuple-element.75), kind=kOutput, calls=%fused_computation.18 | convolution fusion | flops 4318035968 | bytes 22020096 | tf_op jit(solution)/shard_map/dot_general | solution.py:136
  (89 shorter events, 0.9 us)
Async XLA Ops:
  0.0 1.6 copy-start
  3.5 4.6 %copy-start.7 = (s32[512]{0:T(512)S(1)}, s32[512]{0:T(512)}, u32[]{:S(2)}) copy-start(s32[512]{0:T(512)} %param.16) | copy-start | bytes 6148
  3.5 4.6 %copy-start.8 = (s32[512]{0:T(512)S(1)}, s32[512]{0:T(512)}, u32[]{:S(2)}) copy-start(s32[512]{0:T(512)} %param.15) | copy-start | bytes 6148
  3.5 4.9 %copy-start.9 = (s32[1,2]{1,0:T(1,128)S(1)}, s32[1,2]{1,0:T(1,128)}, u32[]{:S(2)}) copy-start(s32[1,2]{1,0:T(1,128)} %param.17) | copy-start | bytes 28
  7.6 2.3 collective-permute-start
  10.2 7.5 %collective-permute-start.1 = (bf16[528,128]{0,1:T(8,128)(2,1)S(1)}, bf16[528,128]{0,1:T(8,128)(2,1)S(1)}, u32[]{:S(2)}, u32[]{:S(2)}) collective-permute-start(bf16[528,128]{0,1:T(8,128)(2,1)S(1)} %fusion.19), channel_id=1, source_target_pairs={{0,2},{2,0},{1,3},{3,1},{4,6},{6,4},{5,7},{7,5},{8,10},{10,8},{9,1... | collective-permute-start | bytes 405512 | tf_op jit(solution)/shard_map/ppermute | solution.py:49
  49.2 6.9 %copy-start.4 = (bf16[4,2,528,128]{3,2,1,0:T(8,128)(2,1)}, bf16[4,2,528,128]{3,2,1,0:T(8,128)(2,1)S(1)}, u32[]{:S(2)}) copy-start(bf16[4,2,528,128]{3,2,1,0:T(8,128)(2,1)S(1)} %all_to_all.5) | copy-start | bytes 3244036
  49.2 6.9 %collective-permute-start.2 = (bf16[8,528,128]{2,1,0:T(8,128)(2,1)S(1)}, bf16[8,528,128]{2,1,0:T(8,128)(2,1)}, u32[]{:S(2)}, u32[]{:S(2)}) collective-permute-start(bf16[8,528,128]{2,1,0:T(8,128)(2,1)S(1)} %bitcast.90), channel_id=1, source_target_pairs={{0,1},{1,0},{2,3},{3,2},{4,5},{5,4},{6,7},{7,6},{8,9},{9,8},{10,11... | collective-permute-start | bytes 3244040 | tf_op jit(solution)/shard_map/ppermute | solution.py:62
  49.2 184.1 %collective-permute-start.3 = (bf16[512,4096]{1,0:T(8,128)(2,1)}, bf16[512,4096]{1,0:T(8,128)(2,1)}, u32[]{:S(2)}, u32[]{:S(2)}) collective-permute-start(bf16[512,4096]{1,0:T(8,128)(2,1)} %param.12), channel_id=1, source_target_pairs={{0,2},{2,4},{4,6},{6,8},{8,10},{10,12},{12,14},{1,3},{3,5},{5,7},{... | collective-permute-start | bytes 12582920 | tf_op jit(solution)/shard_map/ppermute | solution.py:45
  54.6 178.8 %collective-permute-start.4 = (bf16[512,4096]{1,0:T(8,128)(2,1)}, bf16[512,4096]{1,0:T(8,128)(2,1)}, u32[]{:S(2)}, u32[]{:S(2)}) collective-permute-start(bf16[512,4096]{1,0:T(8,128)(2,1)} %param.12), channel_id=1, source_target_pairs={{2,0},{4,2},{6,4},{8,6},{10,8},{12,10},{14,12},{3,1},{5,3},{7,5},{... | collective-permute-start | bytes 12582920 | tf_op jit(solution)/shard_map/ppermute | solution.py:45
  60.2 2.0 copy-start.6
  73.7 15.4 %copy-start.2 = (f32[8,3,512,512]{3,2,1,0:T(8,128)S(1)}, f32[8,3,512,512]{3,2,1,0:T(8,128)}, u32[]{:S(2)}) copy-start(f32[8,3,512,512]{3,2,1,0:T(8,128)} %get-tuple-element.142) | copy-start | bytes 75497472 | tf_op jit(solution)/shard_map/while
  83.4 7.9 %copy-start.5 = (f32[8,3,512]{2,0,1:T(8,128)}, f32[8,3,512]{2,0,1:T(8,128)S(1)}, u32[]{:S(2)}) copy-start(f32[8,3,512]{2,0,1:T(8,128)S(1)} %pad_maximum_fusion.11) | copy-start | bytes 147460 | tf_op jit(solution)/shard_map/while
  91.4 15.4 %copy-start.2 = (f32[8,3,512,512]{3,2,1,0:T(8,128)S(1)}, f32[8,3,512,512]{3,2,1,0:T(8,128)}, u32[]{:S(2)}) copy-start(f32[8,3,512,512]{3,2,1,0:T(8,128)} %get-tuple-element.142) | copy-start | bytes 75497472 | tf_op jit(solution)/shard_map/while
  101.2 7.9 %copy-start.5 = (f32[8,3,512]{2,0,1:T(8,128)}, f32[8,3,512]{2,0,1:T(8,128)S(1)}, u32[]{:S(2)}) copy-start(f32[8,3,512]{2,0,1:T(8,128)S(1)} %pad_maximum_fusion.11) | copy-start | bytes 147460 | tf_op jit(solution)/shard_map/while
  109.1 15.4 %copy-start.2 = (f32[8,3,512,512]{3,2,1,0:T(8,128)S(1)}, f32[8,3,512,512]{3,2,1,0:T(8,128)}, u32[]{:S(2)}) copy-start(f32[8,3,512,512]{3,2,1,0:T(8,128)} %get-tuple-element.142) | copy-start | bytes 75497472 | tf_op jit(solution)/shard_map/while
  118.9 7.9 %copy-start.5 = (f32[8,3,512]{2,0,1:T(8,128)}, f32[8,3,512]{2,0,1:T(8,128)S(1)}, u32[]{:S(2)}) copy-start(f32[8,3,512]{2,0,1:T(8,128)S(1)} %pad_maximum_fusion.11) | copy-start | bytes 147460 | tf_op jit(solution)/shard_map/while
  126.8 15.4 %copy-start.2 = (f32[8,3,512,512]{3,2,1,0:T(8,128)S(1)}, f32[8,3,512,512]{3,2,1,0:T(8,128)}, u32[]{:S(2)}) copy-start(f32[8,3,512,512]{3,2,1,0:T(8,128)} %get-tuple-element.142) | copy-start | bytes 75497472 | tf_op jit(solution)/shard_map/while
  136.6 7.9 %copy-start.5 = (f32[8,3,512]{2,0,1:T(8,128)}, f32[8,3,512]{2,0,1:T(8,128)S(1)}, u32[]{:S(2)}) copy-start(f32[8,3,512]{2,0,1:T(8,128)S(1)} %pad_maximum_fusion.11) | copy-start | bytes 147460 | tf_op jit(solution)/shard_map/while
  144.5 4.4 %copy-start.3 = (bf16[512,4096]{1,0:T(8,128)(2,1)S(1)}, bf16[512,4096]{1,0:T(8,128)(2,1)}, u32[]{:S(2)}) copy-start(bf16[512,4096]{1,0:T(8,128)(2,1)} %param.12) | copy-start | bytes 12582916
  233.3 10.7 %copy-start.1 = (bf16[512,2048]{1,0:T(8,128)(2,1)S(1)}, bf16[512,2048]{1,0:T(8,128)(2,1)}, u32[]{:S(2)}) copy-start(bf16[512,2048]{1,0:T(8,128)(2,1)} %param.11) | copy-start | bytes 6291460

commit v14 on v13

--- a/solution.py
+++ b/solution.py
@@ -46,11 +46,11 @@
 
 
 def gather_pairs(mine):
-    partner = lax.ppermute(mine, "y", [(0, 1), (1, 0)])
+    z_size = lax.axis_size("z")
+    row = lax.all_to_all(jnp.broadcast_to(mine, (z_size,) + mine.shape), "z", 0, 0, tiled=False)
+    other = lax.ppermute(row, "y", [(0, 1), (1, 0)])
     second = lax.axis_index("y") == 1
-    pair = jnp.stack([jnp.where(second, partner, mine), jnp.where(second, mine, partner)])
-    z_size = lax.axis_size("z")
-    got = lax.all_to_all(jnp.broadcast_to(pair, (z_size,) + pair.shape), "z", 0, 0, tiled=False)
+    got = jnp.stack([jnp.where(second, other, row), jnp.where(second, row, other)], 1)
     return got.reshape((z_size * 2,) + mine.shape)
 
 

time: 244 us -> 241 us (0.988)
  blocking collectives: 31 us -> 21.2 us
  waiting for transfers between devices: 86.7 us -> 92.1 us
    all_to_all x1, blocking collectives: 31 us -> 21.2 us  [gather_pairs(): lax.all_to_all(jnp.broadcast_to(mine, (z_size,) + mine.shape), 'z', 0, 0,...]
    ppermute x1, waiting for transfers between devices: 4.73 us -> 11.9 us  [gather_pairs(): other = lax.ppermute(row, 'y', [(0, 1), (1, 0)])]
  transfers between devices with their start and end apart: 5 -> 5, of which waited for: 2 -> 2; matrix products, arithmetic and copies ran while one was open for 30% -> 32% of each run, Pallas kernels for 0% -> 0%
where the time goes in v14:
time: 241 us; the launch traced here: 240 us
  waiting for transfers between devices  92.1 us (38%)
  other arithmetic  53.5 us (22%)
  matrix products  32.7 us (14%)
  local copies, waits for them, and re-layouts  30.8 us (13%)
  blocking collectives  21.2 us (9%)
  starting transfers between devices  8.93 us (4%)
    ppermute x2, waiting for transfers between devices, seq_shifted(): return lax.ppermute(block, SEQ, route)  80.2 us
    reduce_sum x4, other arithmetic, iterate(): partial_cols = jnp.sum(row_scale[:, None, None, :] * kernel, axis=3)  38.4 us
    while x16, local copies, waits for them, and re-layouts  22.4 us
    all_to_all x1, blocking collectives, gather_pairs(): lax.all_to_all(jnp.broadcast_to(mine, (z_size,) + mine.shape), 'z', 0, 0,...  21.2 us
    ppermute x1, waiting for transfers between devices, gather_pairs(): other = lax.ppermute(row, 'y', [(0, 1), (1, 0)])  11.9 us
    dot_general x1, matrix products, body_local(): jnp.einsum('bkjp,bip->bkji', beside(t_unit), s_unit, preferred_element_ty...  11.5 us
    dot_general x1, matrix products, body_local(): lax.dot_general(sides, near_rows, along_j, preferred_element_type=jnp.flo...  10.7 us
    reduce_sum x4, other arithmetic, iterate(): row_scale = 1.0 / jnp.sum(kernel * col_scale[:, :, :, None], axis=(1, 2))  8.94 us
  transfers between devices with their start and end apart: 5, of which 2 were waited for; matrix products, arithmetic and copies ran while one was open for 32% of the time, Pallas kernels for 0%

profile of v14, /device:TPU:0, one launch (start us, length us, event | category | flops | bytes accessed | tf_op | source)
XLA Modules:
  0.0 240.1 jit_solution(15368842508739779372)
XLA Ops:
  0.0 1.6 copy-done
  1.6 1.9 fusion.36
  3.5 0.0 copy-start.6
  3.5 0.0 copy-start.7
  3.5 0.0 copy-start.8
  3.5 4.0 %fusion.37 = f32[512,128]{0,1:T(8,128)S(1)} fusion(bf16[512,4096]{1,0:T(8,128)(2,1)} %param.12, bf16[4096,128]{1,0:T(8,128)(2,1)} %param.14), kind=kOutput, calls=%fused_computation.107 | convolution fusion | flops 536870912 | bytes 5505024 | tf_op jit(solution)/shard_map/dot_general | solution.py:77
  7.6 0.5 collective-permute-start
  8.1 0.0 copy-done.7
  8.1 0.1 fusion.24
  8.2 0.1 copy.31
  8.4 0.1 copy.30
  8.5 0.1 pad.37.clone
  8.6 0.6 compare_reduce_fusion
  9.2 0.6 broadcast_select_fusion.3
  9.8 0.0 collective-permute-done
  9.9 0.1 fusion.29
  9.9 0.1 multiply_reduce_fusion.2
  10.0 0.1 multiply_convert_fusion
  10.1 0.1 fusion.19
  10.2 0.1 copy.32
  10.4 0.1 broadcast_in_dim.8
  10.4 21.2 %all_to_all.5 = bf16[4,528,128]{2,1,0:T(8,128)(2,1)S(1)} all-to-all(bf16[4,528,128]{2,1,0:T(8,128)(2,1)S(1)} %broadcast_in_dim.8), channel_id=1, replica_groups=mesh['groups'=2,'z'=4,'y'=2,'tgrp'=2] {'z'}, dimensions={0} | all-to-all | bytes 1081344 | tf_op jit(solution)/shard_map/all_to_all | solution.py:50
  31.6 1.5 collective-permute-start.1
  33.1 11.9 %collective-permute-done.1 = bf16[4,528,128]{2,1,0:T(8,128)(2,1)S(1)} collective-permute-done((bf16[4,528,128]{2,1,0:T(8,128)(2,1)S(1)}, bf16[4,528,128]{2,1,0:T(8,128)(2,1)S(1)}, u32[]{:S(2)}, u32[]{:S(2)}) %collective-permute-start.1) | collective-permute-done | bytes 540704 | tf_op jit(solution)/shard_map/ppermute | solution.py:51
  45.0 0.1 select_bitcast_fusion.1
  45.1 0.1 pad_maximum_fusion.2
  45.2 0.0 copy-start.3
  45.2 0.1 collective-permute-start.2
  45.3 5.4 %collective-permute-start.3 = (bf16[512,4096]{1,0:T(8,128)(2,1)}, bf16[512,4096]{1,0:T(8,128)(2,1)}, u32[]{:S(2)}, u32[]{:S(2)}) collective-permute-start(bf16[512,4096]{1,0:T(8,128)(2,1)} %param.12), channel_id=1, source_target_pairs={{0,2},{2,4},{4,6},{6,8},{8,10},{10,12},{12,14},{1,3},{3,5},{5,7},{... | collective-permute-start | bytes 12582920 | tf_op jit(solution)/shard_map/ppermute | solution.py:45
  50.7 1.5 collective-permute-start.4
  52.2 0.1 pad.21.clone
  52.3 0.0 collective-permute-done.2
  52.3 1.7 broadcast_select_fusion.1
  54.0 1.3 fusion.32
  55.2 1.0 slice_bitcast_fusion.2
  56.3 0.1 reshape.409
  56.3 0.0 copy-start.5
  56.4 0.1 slice_add_fusion
  56.6 1.4 pad_bitcast_fusion.2
  57.9 0.1 pad_bitcast_fusion.3
  58.2 0.1 fusion.35
  58.2 0.1 pad_maximum_fusion.7
  58.3 11.5 %exponential_multiply_fusion = f32[8,3,512,512]{3,2,1,0:T(8,128)} fusion(f32[8,3]{1,0:T(8,128)S(1)} %pad_maximum_fusion.7, f32[8,3,512]{2,1,0:T(4,128)S(1)} %copy.37, f32[8,512]{1,0:T(8,128)S(1)} %bitcast.99, bf16[8,528,128]{2,1,0:T(8,128)(2,1)S(1)} %get-tuple-element.73, bf16[8,1,512,128]{3,2,0,1:T(8,128)(2,1)S(1)} %pad_bitcast_fusion.2, ...), kind=kOutput, calls=%fused_computation.13 | convolution fusion | flops 1651507200 | bytes 29446144 | tf_op jit(solution)/shard_map/bkjp,bip->bkji/dot_general | solution.py:103
  69.8 70.8 %while.14 = (s32[]{:T(128)}, f32[8,512]{1,0:T(8,128)S(1)}, f32[8,3,512]{2,0,1:T(8,128)}, f32[8,3,512,512]{3,2,1,0:T(8,128)}, s32[]{:T(128)}, /*index=5*/s32[]{:T(128)}) while((s32[]{:T(128)}, f32[8,512]{1,0:T(8,128)S(1)}, f32[8,3,512]{2,0,1:T(8,128)}, f32[8,3,512,512]{3,2,1,0:T(8,128)}, s32[]{:T(128)}, /*index=5*/s32[]{:T(128)}) %tuple.47), condition=%wide.region_6.7_spmd.clone, body=%wide.region_3.6_spmd.clone.sunk | while | flops 25194500 | bytes 151912576 | solution.py:122
  69.9 9.6 %multiply_reduce_fusion.6 = f32[8,3,512]{2,1,0:T(4,128)S(1)} fusion(f32[8,3,512,512]{3,2,1,0:T(8,128)} %get-tuple-element.142, f32[8,512]{1,0:T(8,128)S(1)} %broadcast_select_fusion.5), kind=kLoop, calls=%fused_computation.1.clone.1 | loop fusion | flops 12570624 | bytes 25231360 | tf_op jit(solution)/shard_map/while/body/eval_jaxpr/reduce_sum | solution.py:111
  79.6 5.6 %copy-done.2 = f32[8,3,512,512]{3,2,1,0:T(8,128)S(1)} copy-done((f32[8,3,512,512]{3,2,1,0:T(8,128)S(1)}, f32[8,3,512,512]{3,2,1,0:T(8,128)}, u32[]{:S(2)}) %copy-start.2) | copy-done | bytes 25165848 | tf_op jit(solution)/shard_map/while
  85.3 2.2 multiply_reduce_fusion.7
  87.6 9.6 %multiply_reduce_fusion.6 = f32[8,3,512]{2,1,0:T(4,128)S(1)} fusion(f32[8,3,512,512]{3,2,1,0:T(8,128)} %get-tuple-element.142, f32[8,512]{1,0:T(8,128)S(1)} %broadcast_select_fusion.5), kind=kLoop, calls=%fused_computation.1.clone.1 | loop fusion | flops 12570624 | bytes 25231360 | tf_op jit(solution)/shard_map/while/body/eval_jaxpr/reduce_sum | solution.py:111
  97.4 5.6 %copy-done.2 = f32[8,3,512,512]{3,2,1,0:T(8,128)S(1)} copy-done((f32[8,3,512,512]{3,2,1,0:T(8,128)S(1)}, f32[8,3,512,512]{3,2,1,0:T(8,128)}, u32[]{:S(2)}) %copy-start.2) | copy-done | bytes 25165848 | tf_op jit(solution)/shard_map/while
  103.0 2.2 multiply_reduce_fusion.7
  105.3 0.0 copy-start.2
  105.3 9.6 %multiply_reduce_fusion.6 = f32[8,3,512]{2,1,0:T(4,128)S(1)} fusion(f32[8,3,512,512]{3,2,1,0:T(8,128)} %get-tuple-element.142, f32[8,512]{1,0:T(8,128)S(1)} %broadcast_select_fusion.5), kind=kLoop, calls=%fused_computation.1.clone.1 | loop fusion | flops 12570624 | bytes 25231360 | tf_op jit(solution)/shard_map/while/body/eval_jaxpr/reduce_sum | solution.py:111
  115.1 5.6 %copy-done.2 = f32[8,3,512,512]{3,2,1,0:T(8,128)S(1)} copy-done((f32[8,3,512,512]{3,2,1,0:T(8,128)S(1)}, f32[8,3,512,512]{3,2,1,0:T(8,128)}, u32[]{:S(2)}) %copy-start.2) | copy-done | bytes 25165848 | tf_op jit(solution)/shard_map/while
  120.7 2.2 multiply_reduce_fusion.7
  123.0 9.6 %multiply_reduce_fusion.6 = f32[8,3,512]{2,1,0:T(4,128)S(1)} fusion(f32[8,3,512,512]{3,2,1,0:T(8,128)} %get-tuple-element.142, f32[8,512]{1,0:T(8,128)S(1)} %broadcast_select_fusion.5), kind=kLoop, calls=%fused_computation.1.clone.1 | loop fusion | flops 12570624 | bytes 25231360 | tf_op jit(solution)/shard_map/while/body/eval_jaxpr/reduce_sum | solution.py:111
  132.8 5.6 %copy-done.2 = f32[8,3,512,512]{3,2,1,0:T(8,128)S(1)} copy-done((f32[8,3,512,512]{3,2,1,0:T(8,128)S(1)}, f32[8,3,512,512]{3,2,1,0:T(8,128)}, u32[]{:S(2)}) %copy-start.2) | copy-done | bytes 25165848 | tf_op jit(solution)/shard_map/while
  138.4 2.2 multiply_reduce_fusion.7
  140.6 0.8 constant_dynamic-slice_fusion
  141.5 2.2 fusion.10
  143.7 0.9 slice_bitcast_fusion.4
  144.6 4.6 %fusion.15 = f32[512,4096]{1,0:T(8,128)S(1)} fusion(bf16[512,4096]{1,0:T(8,128)(2,1)} %param.12, bf16[3,512,512]{2,1,0:T(8,128)(2,1)S(1)} %fusion.10), kind=kOutput, calls=%fused_computation.39 | convolution fusion | flops 2147483648 | bytes 13107200 | tf_op jit(solution)/shard_map/dot_general | solution.py:133
  149.2 80.2 %collective-permute-done.3 = bf16[512,4096]{1,0:T(8,128)(2,1)} collective-permute-done((bf16[512,4096]{1,0:T(8,128)(2,1)}, bf16[512,4096]{1,0:T(8,128)(2,1)}, u32[]{:S(2)}, u32[]{:S(2)}) %collective-permute-start.3) | collective-permute-done | bytes 4194336 | tf_op jit(solution)/shard_map/ppermute | solution.py:45
  229.4 0.0 collective-permute-done.4
  229.4 10.7 %add_convert_fusion = bf16[512,4096]{1,0:T(8,128)(2,1)} fusion(f32[512,4096]{1,0:T(8,128)S(1)} %fusion.15, bf16[512,4096]{1,0:T(8,128)(2,1)} %collective-permute-done.4, bf16[512,4096]{1,0:T(8,128)(2,1)} %collective-permute-done.3, bf16[512,512]{1,0:T(8,128)(2,1)} %get-tuple-element.76, bf16[512,512]{1,0:T(8,128)(2,1)S(1)} %get-tuple-element.75), kind=kOutput, calls=%fused_computation.18 | convolution fusion | flops 4318035968 | bytes 22020096 | tf_op jit(solution)/shard_map/dot_general | solution.py:136
  (87 shorter events, 0.9 us)
Async XLA Ops:
  0.0 1.6 copy-start
  3.5 4.6 %copy-start.6 = (s32[512]{0:T(512)S(1)}, s32[512]{0:T(512)}, u32[]{:S(2)}) copy-start(s32[512]{0:T(512)} %param.16) | copy-start | bytes 6148
  3.5 4.6 %copy-start.7 = (s32[512]{0:T(512)S(1)}, s32[512]{0:T(512)}, u32[]{:S(2)}) copy-start(s32[512]{0:T(512)} %param.15) | copy-start | bytes 6148
  3.5 4.9 %copy-start.8 = (s32[1,2]{1,0:T(1,128)S(1)}, s32[1,2]{1,0:T(1,128)}, u32[]{:S(2)}) copy-start(s32[1,2]{1,0:T(1,128)} %param.17) | copy-start | bytes 28
  7.6 2.3 collective-permute-start
  31.6 13.4 %collective-permute-start.1 = (bf16[4,528,128]{2,1,0:T(8,128)(2,1)S(1)}, bf16[4,528,128]{2,1,0:T(8,128)(2,1)S(1)}, u32[]{:S(2)}, u32[]{:S(2)}) collective-permute-start(bf16[4,528,128]{2,1,0:T(8,128)(2,1)S(1)} %all_to_all.5), channel_id=1, source_target_pairs={{0,2},{2,0},{1,3},{3,1},{4,6},{6,4},{5,7},{7,5},{8,10},{10,8},{9,1... | collective-permute-start | bytes 1622024 | tf_op jit(solution)/shard_map/ppermute | solution.py:51
  45.2 7.0 %copy-start.3 = (bf16[4,2,528,128]{3,2,1,0:T(8,128)(2,1)}, bf16[4,2,528,128]{3,2,1,0:T(8,128)(2,1)S(1)}, u32[]{:S(2)}) copy-start(bf16[4,2,528,128]{3,2,1,0:T(8,128)(2,1)S(1)} %pad_maximum_fusion.2) | copy-start | bytes 3244036
  45.2 7.0 %collective-permute-start.2 = (bf16[8,528,128]{2,1,0:T(8,128)(2,1)S(1)}, bf16[8,528,128]{2,1,0:T(8,128)(2,1)}, u32[]{:S(2)}, u32[]{:S(2)}) collective-permute-start(bf16[8,528,128]{2,1,0:T(8,128)(2,1)S(1)} %bitcast.92), channel_id=1, source_target_pairs={{0,1},{1,0},{2,3},{3,2},{4,5},{5,4},{6,7},{7,6},{8,9},{9,8},{10,11... | collective-permute-start | bytes 3244040 | tf_op jit(solution)/shard_map/ppermute | solution.py:62
  45.3 184.1 %collective-permute-start.3 = (bf16[512,4096]{1,0:T(8,128)(2,1)}, bf16[512,4096]{1,0:T(8,128)(2,1)}, u32[]{:S(2)}, u32[]{:S(2)}) collective-permute-start(bf16[512,4096]{1,0:T(8,128)(2,1)} %param.12), channel_id=1, source_target_pairs={{0,2},{2,4},{4,6},{6,8},{8,10},{10,12},{12,14},{1,3},{3,5},{5,7},{... | collective-permute-start | bytes 12582920 | tf_op jit(solution)/shard_map/ppermute | solution.py:45
  50.7 178.7 %collective-permute-start.4 = (bf16[512,4096]{1,0:T(8,128)(2,1)}, bf16[512,4096]{1,0:T(8,128)(2,1)}, u32[]{:S(2)}, u32[]{:S(2)}) collective-permute-start(bf16[512,4096]{1,0:T(8,128)(2,1)} %param.12), channel_id=1, source_target_pairs={{2,0},{4,2},{6,4},{8,6},{10,8},{12,10},{14,12},{3,1},{5,3},{7,5},{... | collective-permute-start | bytes 12582920 | tf_op jit(solution)/shard_map/ppermute | solution.py:45
  56.3 2.0 copy-start.5
  69.8 15.4 %copy-start.2 = (f32[8,3,512,512]{3,2,1,0:T(8,128)S(1)}, f32[8,3,512,512]{3,2,1,0:T(8,128)}, u32[]{:S(2)}) copy-start(f32[8,3,512,512]{3,2,1,0:T(8,128)} %get-tuple-element.142) | copy-start | bytes 75497472 | tf_op jit(solution)/shard_map/while
  79.6 7.9 %copy-start.4 = (f32[8,3,512]{2,0,1:T(8,128)}, f32[8,3,512]{2,0,1:T(8,128)S(1)}, u32[]{:S(2)}) copy-start(f32[8,3,512]{2,0,1:T(8,128)S(1)} %pad_maximum_fusion.11) | copy-start | bytes 147460 | tf_op jit(solution)/shard_map/while
  87.6 15.4 %copy-start.2 = (f32[8,3,512,512]{3,2,1,0:T(8,128)S(1)}, f32[8,3,512,512]{3,2,1,0:T(8,128)}, u32[]{:S(2)}) copy-start(f32[8,3,512,512]{3,2,1,0:T(8,128)} %get-tuple-element.142) | copy-start | bytes 75497472 | tf_op jit(solution)/shard_map/while
  97.3 7.9 %copy-start.4 = (f32[8,3,512]{2,0,1:T(8,128)}, f32[8,3,512]{2,0,1:T(8,128)S(1)}, u32[]{:S(2)}) copy-start(f32[8,3,512]{2,0,1:T(8,128)S(1)} %pad_maximum_fusion.11) | copy-start | bytes 147460 | tf_op jit(solution)/shard_map/while
  105.3 15.4 %copy-start.2 = (f32[8,3,512,512]{3,2,1,0:T(8,128)S(1)}, f32[8,3,512,512]{3,2,1,0:T(8,128)}, u32[]{:S(2)}) copy-start(f32[8,3,512,512]{3,2,1,0:T(8,128)} %get-tuple-element.142) | copy-start | bytes 75497472 | tf_op jit(solution)/shard_map/while
  115.0 7.9 %copy-start.4 = (f32[8,3,512]{2,0,1:T(8,128)}, f32[8,3,512]{2,0,1:T(8,128)S(1)}, u32[]{:S(2)}) copy-start(f32[8,3,512]{2,0,1:T(8,128)S(1)} %pad_maximum_fusion.11) | copy-start | bytes 147460 | tf_op jit(solution)/shard_map/while
  123.0 15.4 %copy-start.2 = (f32[8,3,512,512]{3,2,1,0:T(8,128)S(1)}, f32[8,3,512,512]{3,2,1,0:T(8,128)}, u32[]{:S(2)}) copy-start(f32[8,3,512,512]{3,2,1,0:T(8,128)} %get-tuple-element.142) | copy-start | bytes 75497472 | tf_op jit(solution)/shard_map/while
  132.7 7.9 %copy-start.4 = (f32[8,3,512]{2,0,1:T(8,128)}, f32[8,3,512]{2,0,1:T(8,128)S(1)}, u32[]{:S(2)}) copy-start(f32[8,3,512]{2,0,1:T(8,128)S(1)} %pad_maximum_fusion.11) | copy-start | bytes 147460 | tf_op jit(solution)/shard_map/while
  229.4 10.7 %copy-start.1 = (bf16[512,2048]{1,0:T(8,128)(2,1)S(1)}, bf16[512,2048]{1,0:T(8,128)(2,1)}, u32[]{:S(2)}) copy-start(bf16[512,2048]{1,0:T(8,128)(2,1)} %param.11) | copy-start | bytes 6291460

commit v15 on v10

--- a/solution.py
+++ b/solution.py
@@ -74,9 +74,10 @@
     blocks = lax.axis_size("seq")
     me = lax.axis_index("seq")
 
-    s_part = jnp.dot(student_hidden, student_proj, preferred_element_type=jnp.float32)
-    t_part = jnp.dot(teacher_hidden, teacher_proj, preferred_element_type=jnp.float32)
-    feats = tgrp_sum(jnp.concatenate([s_part, t_part], 1))
+    along_width = (((0,), (1,)), ((), ()))
+    s_part = lax.dot_general(student_proj, student_hidden, along_width, preferred_element_type=jnp.float32)
+    t_part = lax.dot_general(teacher_proj, teacher_hidden, along_width, preferred_element_type=jnp.float32)
+    feats = tgrp_sum(jnp.concatenate([s_part, t_part], 0).T)
     units = jnp.concatenate(
         [unit_rows(feats[:, :proj_width]), unit_rows(feats[:, proj_width:])], 1
     )

time: 240 us -> 240 us (level)
  no operation moved by 1% of the time
where the time goes in v15:
time: 240 us; the launch traced here: 239 us
  waiting for transfers between devices  82 us (34%)
  other arithmetic  53.6 us (22%)
  blocking collectives  34.5 us (14%)
  local copies, waits for them, and re-layouts  31 us (13%)
  matrix products  30.6 us (13%)
  starting transfers between devices  6.5 us (3%)
    ppermute x2, waiting for transfers between devices, shifted(): return lax.ppermute(block, axis, route)  82 us
    reduce_sum x4, other arithmetic, iterate(): partial_cols = jnp.sum(row_scale[:, None, None, :] * kernel, axis=3)  38.4 us
    all_to_all x1, blocking collectives, gather_halves(): lax.all_to_all(jnp.broadcast_to(mine, (n,) + mine.shape), 'seq', 0, 0, ti...  34.5 us
    while x16, local copies, waits for them, and re-layouts  22.4 us
    dot_general x1, matrix products, body_local(): jnp.einsum('bkjp,bip->bkji', beside(t_unit), s_unit, preferred_element_ty...  11.5 us
    dot_general x1, matrix products, body_local(): lax.dot_general(sides, near_rows, along_j, preferred_element_type=jnp.flo...  10.7 us
    reduce_sum x4, other arithmetic, iterate(): row_scale = 1.0 / jnp.sum(kernel * col_scale[:, :, :, None], axis=(1, 2))  8.94 us
    ppermute x2, starting transfers between devices, shifted(): return lax.ppermute(block, axis, route)  5.98 us
  transfers between devices with their start and end apart: 4, of which 1 were waited for; matrix products, arithmetic and copies ran while one was open for 31% of the time, Pallas kernels for 0%

profile of v15, /device:TPU:0, one launch (start us, length us, event | category | flops | bytes accessed | tf_op | source)
XLA Modules:
  0.0 239.0 jit_solution(9190293282250785169)
XLA Ops:
  0.0 0.0 copy-start
  0.0 1.6 copy-done
  1.6 1.9 fusion.36
  3.5 4.0 %fusion.37 = f32[128,512]{1,0:T(8,128)S(1)} fusion(bf16[4096,128]{1,0:T(8,128)(2,1)} %param.14, bf16[512,4096]{1,0:T(8,128)(2,1)} %param.12), kind=kOutput, calls=%fused_computation.104 | convolution fusion | flops 536870912 | bytes 5505024 | tf_op jit(solution)/shard_map/dot_general | solution.py:79
  7.6 0.5 collective-permute-start
  8.1 0.0 copy-done.8
  8.1 0.0 copy-done.7
  8.1 0.1 fusion.24
  8.2 0.1 copy.29
  8.4 0.0 copy-done.9
  8.4 0.1 copy.28
  8.5 0.1 pad.35.clone
  8.6 0.6 compare_reduce_fusion
  9.2 0.6 broadcast_select_fusion.3
  9.9 0.0 collective-permute-done
  9.9 0.1 fusion.29
  10.0 0.1 multiply_reduce_fusion.2
  10.0 0.1 multiply_convert_fusion
  10.1 0.1 fusion.19
  10.2 0.1 copy.30
  10.4 0.1 broadcast_in_dim.8
  10.5 34.5 %all_to_all.5 = bf16[8,528,128]{2,1,0:T(8,128)(2,1)S(1)} all-to-all(bf16[8,528,128]{2,1,0:T(8,128)(2,1)S(1)} %broadcast_in_dim.8), channel_id=1, replica_groups=mesh['groups'=2,'seq'=8,'tgrp'=2] {'seq'}, dimensions={0} | all-to-all | bytes 2162688 | tf_op jit(solution)/shard_map/all_to_all | solution.py:62
  45.0 0.0 collective-permute-start.1
  45.0 4.5 %collective-permute-start.2 = (bf16[512,4096]{1,0:T(8,128)(2,1)}, bf16[512,4096]{1,0:T(8,128)(2,1)}, u32[]{:S(2)}, u32[]{:S(2)}) collective-permute-start(bf16[512,4096]{1,0:T(8,128)(2,1)} %param.12), channel_id=1, source_target_pairs={{0,2},{2,4},{4,6},{6,8},{8,10},{10,12},{12,14},{1,3},{3,5},{5,7},{... | collective-permute-start | bytes 12582920 | tf_op jit(solution)/shard_map/ppermute | solution.py:18
  49.6 1.5 collective-permute-start.3
  51.1 0.1 pad.21.clone
  51.1 0.0 copy-done.4
  51.1 0.0 collective-permute-done.1
  51.1 1.7 broadcast_select_fusion.1
  52.8 1.2 fusion.32
  54.1 1.0 slice_bitcast_fusion.2
  55.1 0.1 reshape.405
  55.2 0.0 copy-start.6
  55.2 0.1 slice_add_fusion
  55.4 1.4 pad_bitcast_fusion.2
  56.8 0.1 pad_bitcast_fusion.3
  57.0 0.1 fusion.35
  57.1 0.1 pad_maximum_fusion.5
  57.2 0.0 copy-done.6
  57.2 11.5 %exponential_multiply_fusion = f32[8,3,512,512]{3,2,1,0:T(8,128)} fusion(f32[8,3]{1,0:T(8,128)S(1)} %pad_maximum_fusion.5, f32[8,3,512]{2,1,0:T(4,128)S(1)} %copy.34, f32[8,512]{1,0:T(8,128)S(1)} %bitcast.93, bf16[8,528,128]{2,1,0:T(8,128)(2,1)S(1)} %get-tuple-element.73, bf16[8,1,512,128]{3,2,0,1:T(8,128)(2,1)S(1)} %pad_bitcast_fusion.2, ...), kind=kOutput, calls=%fused_computation.13 | convolution fusion | flops 1651507200 | bytes 29446144 | tf_op jit(solution)/shard_map/bkjp,bip->bkji/dot_general | solution.py:105
  68.7 70.8 %while.14 = (s32[]{:T(128)}, f32[8,512]{1,0:T(8,128)S(1)}, f32[8,3,512]{2,0,1:T(8,128)}, f32[8,3,512,512]{3,2,1,0:T(8,128)}, s32[]{:T(128)}, /*index=5*/s32[]{:T(128)}) while((s32[]{:T(128)}, f32[8,512]{1,0:T(8,128)S(1)}, f32[8,3,512]{2,0,1:T(8,128)}, f32[8,3,512,512]{3,2,1,0:T(8,128)}, s32[]{:T(128)}, /*index=5*/s32[]{:T(128)}) %tuple.46), condition=%wide.region_6.7_spmd.clone, body=%wide.region_3.6_spmd.clone.sunk | while | flops 25194500 | bytes 151912576 | solution.py:124
  68.7 9.6 %multiply_reduce_fusion.6 = f32[8,3,512]{2,1,0:T(4,128)S(1)} fusion(f32[8,3,512,512]{3,2,1,0:T(8,128)} %get-tuple-element.140, f32[8,512]{1,0:T(8,128)S(1)} %broadcast_select_fusion.5), kind=kLoop, calls=%fused_computation.1.clone.1 | loop fusion | flops 12570624 | bytes 25231360 | tf_op jit(solution)/shard_map/while/body/eval_jaxpr/reduce_sum | solution.py:113
  78.4 0.0 copy-start.5
  78.5 5.6 %copy-done.2 = f32[8,3,512,512]{3,2,1,0:T(8,128)S(1)} copy-done((f32[8,3,512,512]{3,2,1,0:T(8,128)S(1)}, f32[8,3,512,512]{3,2,1,0:T(8,128)}, u32[]{:S(2)}) %copy-start.2) | copy-done | bytes 25165848 | tf_op jit(solution)/shard_map/while
  84.1 2.2 multiply_reduce_fusion.7
  86.4 9.6 %multiply_reduce_fusion.6 = f32[8,3,512]{2,1,0:T(4,128)S(1)} fusion(f32[8,3,512,512]{3,2,1,0:T(8,128)} %get-tuple-element.140, f32[8,512]{1,0:T(8,128)S(1)} %broadcast_select_fusion.5), kind=kLoop, calls=%fused_computation.1.clone.1 | loop fusion | flops 12570624 | bytes 25231360 | tf_op jit(solution)/shard_map/while/body/eval_jaxpr/reduce_sum | solution.py:113
  96.2 0.0 copy-start.5
  96.2 5.6 %copy-done.2 = f32[8,3,512,512]{3,2,1,0:T(8,128)S(1)} copy-done((f32[8,3,512,512]{3,2,1,0:T(8,128)S(1)}, f32[8,3,512,512]{3,2,1,0:T(8,128)}, u32[]{:S(2)}) %copy-start.2) | copy-done | bytes 25165848 | tf_op jit(solution)/shard_map/while
  101.8 2.2 multiply_reduce_fusion.7
  104.1 9.6 %multiply_reduce_fusion.6 = f32[8,3,512]{2,1,0:T(4,128)S(1)} fusion(f32[8,3,512,512]{3,2,1,0:T(8,128)} %get-tuple-element.140, f32[8,512]{1,0:T(8,128)S(1)} %broadcast_select_fusion.5), kind=kLoop, calls=%fused_computation.1.clone.1 | loop fusion | flops 12570624 | bytes 25231360 | tf_op jit(solution)/shard_map/while/body/eval_jaxpr/reduce_sum | solution.py:113
  113.9 5.6 %copy-done.2 = f32[8,3,512,512]{3,2,1,0:T(8,128)S(1)} copy-done((f32[8,3,512,512]{3,2,1,0:T(8,128)S(1)}, f32[8,3,512,512]{3,2,1,0:T(8,128)}, u32[]{:S(2)}) %copy-start.2) | copy-done | bytes 25165848 | tf_op jit(solution)/shard_map/while
  119.5 2.2 multiply_reduce_fusion.7
  121.8 0.0 copy-done.5
  121.8 9.6 %multiply_reduce_fusion.6 = f32[8,3,512]{2,1,0:T(4,128)S(1)} fusion(f32[8,3,512,512]{3,2,1,0:T(8,128)} %get-tuple-element.140, f32[8,512]{1,0:T(8,128)S(1)} %broadcast_select_fusion.5), kind=kLoop, calls=%fused_computation.1.clone.1 | loop fusion | flops 12570624 | bytes 25231360 | tf_op jit(solution)/shard_map/while/body/eval_jaxpr/reduce_sum | solution.py:113
  131.6 5.6 %copy-done.2 = f32[8,3,512,512]{3,2,1,0:T(8,128)S(1)} copy-done((f32[8,3,512,512]{3,2,1,0:T(8,128)S(1)}, f32[8,3,512,512]{3,2,1,0:T(8,128)}, u32[]{:S(2)}) %copy-start.2) | copy-done | bytes 25165848 | tf_op jit(solution)/shard_map/while
  137.2 2.2 multiply_reduce_fusion.7
  139.5 0.0 copy-start.3
  139.5 1.0 constant_dynamic-slice_fusion
  140.5 2.5 %fusion.10 = bf16[3,512,512]{2,1,0:T(8,128)(2,1)S(1)} fusion(f32[8,3,512,512]{3,2,1,0:T(8,128)} %get-tuple-element.143, s32[]{:T(128)S(6)} %select_n.78, f32[3,512]{1,0:T(4,128)S(1)} %bitcast.91, f32[512]{0:T(512)S(1)} %bitcast.94), kind=kLoop, calls=%fused_computation.22 | loop fusion | flops 2359296 | bytes 4726788 | tf_op jit(solution)/shard_map/convert_element_type | solution.py:133
  143.0 0.9 slice_bitcast_fusion.4
  143.9 2.4 %fusion.15 = f32[512,4096]{1,0:T(8,128)S(1)} fusion(bf16[512,4096]{1,0:T(8,128)(2,1)S(1)} %copy-done.3, bf16[3,512,512]{2,1,0:T(8,128)(2,1)S(1)} %fusion.10), kind=kOutput, calls=%fused_computation.36 | convolution fusion | flops 2147483648 | bytes 13107200 | tf_op jit(solution)/shard_map/dot_general | solution.py:135
  146.3 82.0 %collective-permute-done.2 = bf16[512,4096]{1,0:T(8,128)(2,1)} collective-permute-done((bf16[512,4096]{1,0:T(8,128)(2,1)}, bf16[512,4096]{1,0:T(8,128)(2,1)}, u32[]{:S(2)}, u32[]{:S(2)}) %collective-permute-start.2) | collective-permute-done | bytes 4194336 | tf_op jit(solution)/shard_map/ppermute | solution.py:18
  228.3 0.0 collective-permute-done.3
  228.3 10.7 %add_convert_fusion = bf16[512,4096]{1,0:T(8,128)(2,1)} fusion(f32[512,4096]{1,0:T(8,128)S(1)} %fusion.15, bf16[512,4096]{1,0:T(8,128)(2,1)} %collective-permute-done.3, bf16[512,4096]{1,0:T(8,128)(2,1)} %collective-permute-done.2, bf16[512,512]{1,0:T(8,128)(2,1)} %get-tuple-element.76, bf16[512,512]{1,0:T(8,128)(2,1)S(1)} %get-tuple-element.75), kind=kOutput, calls=%fused_computation.18 | convolution fusion | flops 4318035968 | bytes 22020096 | tf_op jit(solution)/shard_map/dot_general | solution.py:138
  (85 shorter events, 0.9 us)
Async XLA Ops:
  0.0 1.6 copy-start
  0.0 8.1 %copy-start.8 = (s32[512]{0:T(512)S(1)}, s32[512]{0:T(512)}, u32[]{:S(2)}) copy-start(s32[512]{0:T(512)} %param.15) | copy-start | bytes 6148
  0.0 8.1 %copy-start.7 = (s32[512]{0:T(512)S(1)}, s32[512]{0:T(512)}, u32[]{:S(2)}) copy-start(s32[512]{0:T(512)} %param.16) | copy-start | bytes 6148
  1.6 6.8 %copy-start.9 = (s32[1,2]{1,0:T(1,128)S(1)}, s32[1,2]{1,0:T(1,128)}, u32[]{:S(2)}) copy-start(s32[1,2]{1,0:T(1,128)} %param.17) | copy-start | bytes 28
  7.6 2.3 collective-permute-start
  45.0 6.1 %copy-start.4 = (bf16[8,528,128]{2,1,0:T(8,128)(2,1)}, bf16[8,528,128]{2,1,0:T(8,128)(2,1)S(1)}, u32[]{:S(2)}) copy-start(bf16[8,528,128]{2,1,0:T(8,128)(2,1)S(1)} %all_to_all.5) | copy-start | bytes 3244036
  45.0 6.1 %collective-permute-start.1 = (bf16[8,528,128]{2,1,0:T(8,128)(2,1)S(1)}, bf16[8,528,128]{2,1,0:T(8,128)(2,1)}, u32[]{:S(2)}, u32[]{:S(2)}) collective-permute-start(bf16[8,528,128]{2,1,0:T(8,128)(2,1)S(1)} %all_to_all.5), channel_id=1, source_target_pairs={{0,1},{1,0},{2,3},{3,2},{4,5},{5,4},{6,7},{7,6},{8,9},{9,8},{10,11... | collective-permute-start | bytes 3244040 | tf_op jit(solution)/shard_map/ppermute | solution.py:63
  45.0 183.3 %collective-permute-start.2 = (bf16[512,4096]{1,0:T(8,128)(2,1)}, bf16[512,4096]{1,0:T(8,128)(2,1)}, u32[]{:S(2)}, u32[]{:S(2)}) collective-permute-start(bf16[512,4096]{1,0:T(8,128)(2,1)} %param.12), channel_id=1, source_target_pairs={{0,2},{2,4},{4,6},{6,8},{8,10},{10,12},{12,14},{1,3},{3,5},{5,7},{... | collective-permute-start | bytes 12582920 | tf_op jit(solution)/shard_map/ppermute | solution.py:18
  49.6 178.8 %collective-permute-start.3 = (bf16[512,4096]{1,0:T(8,128)(2,1)}, bf16[512,4096]{1,0:T(8,128)(2,1)}, u32[]{:S(2)}, u32[]{:S(2)}) collective-permute-start(bf16[512,4096]{1,0:T(8,128)(2,1)} %param.12), channel_id=1, source_target_pairs={{2,0},{4,2},{6,4},{8,6},{10,8},{12,10},{14,12},{3,1},{5,3},{7,5},{... | collective-permute-start | bytes 12582920 | tf_op jit(solution)/shard_map/ppermute | solution.py:18
  55.2 2.0 copy-start.6
  68.7 15.4 %copy-start.2 = (f32[8,3,512,512]{3,2,1,0:T(8,128)S(1)}, f32[8,3,512,512]{3,2,1,0:T(8,128)}, u32[]{:S(2)}) copy-start(f32[8,3,512,512]{3,2,1,0:T(8,128)} %get-tuple-element.140) | copy-start | bytes 75497472 | tf_op jit(solution)/shard_map/while
  78.4 7.9 %copy-start.5 = (f32[8,3,512]{2,0,1:T(8,128)}, f32[8,3,512]{2,0,1:T(8,128)S(1)}, u32[]{:S(2)}) copy-start(f32[8,3,512]{2,0,1:T(8,128)S(1)} %pad_maximum_fusion.9) | copy-start | bytes 147460 | tf_op jit(solution)/shard_map/while
  86.4 15.4 %copy-start.2 = (f32[8,3,512,512]{3,2,1,0:T(8,128)S(1)}, f32[8,3,512,512]{3,2,1,0:T(8,128)}, u32[]{:S(2)}) copy-start(f32[8,3,512,512]{3,2,1,0:T(8,128)} %get-tuple-element.140) | copy-start | bytes 75497472 | tf_op jit(solution)/shard_map/while
  96.2 7.9 %copy-start.5 = (f32[8,3,512]{2,0,1:T(8,128)}, f32[8,3,512]{2,0,1:T(8,128)S(1)}, u32[]{:S(2)}) copy-start(f32[8,3,512]{2,0,1:T(8,128)S(1)} %pad_maximum_fusion.9) | copy-start | bytes 147460 | tf_op jit(solution)/shard_map/while
  104.1 15.4 %copy-start.2 = (f32[8,3,512,512]{3,2,1,0:T(8,128)S(1)}, f32[8,3,512,512]{3,2,1,0:T(8,128)}, u32[]{:S(2)}) copy-start(f32[8,3,512,512]{3,2,1,0:T(8,128)} %get-tuple-element.140) | copy-start | bytes 75497472 | tf_op jit(solution)/shard_map/while
  113.9 7.9 %copy-start.5 = (f32[8,3,512]{2,0,1:T(8,128)}, f32[8,3,512]{2,0,1:T(8,128)S(1)}, u32[]{:S(2)}) copy-start(f32[8,3,512]{2,0,1:T(8,128)S(1)} %pad_maximum_fusion.9) | copy-start | bytes 147460 | tf_op jit(solution)/shard_map/while
  121.8 15.4 %copy-start.2 = (f32[8,3,512,512]{3,2,1,0:T(8,128)S(1)}, f32[8,3,512,512]{3,2,1,0:T(8,128)}, u32[]{:S(2)}) copy-start(f32[8,3,512,512]{3,2,1,0:T(8,128)} %get-tuple-element.140) | copy-start | bytes 75497472 | tf_op jit(solution)/shard_map/while
  131.6 7.9 %copy-start.5 = (f32[8,3,512]{2,0,1:T(8,128)}, f32[8,3,512]{2,0,1:T(8,128)S(1)}, u32[]{:S(2)}) copy-start(f32[8,3,512]{2,0,1:T(8,128)S(1)} %pad_maximum_fusion.9) | copy-start | bytes 147460 | tf_op jit(solution)/shard_map/while
  139.5 4.4 %copy-start.3 = (bf16[512,4096]{1,0:T(8,128)(2,1)S(1)}, bf16[512,4096]{1,0:T(8,128)(2,1)}, u32[]{:S(2)}) copy-start(bf16[512,4096]{1,0:T(8,128)(2,1)} %param.12) | copy-start | bytes 12582916
  228.3 10.7 %copy-start.1 = (bf16[512,2048]{1,0:T(8,128)(2,1)S(1)}, bf16[512,2048]{1,0:T(8,128)(2,1)}, u32[]{:S(2)}) copy-start(bf16[512,2048]{1,0:T(8,128)(2,1)} %param.11) | copy-start | bytes 6291460

commit v16 on v14

--- a/solution.py
+++ b/solution.py
@@ -45,24 +45,26 @@
     return lax.ppermute(block, SEQ, route)
 
 
-def gather_pairs(mine):
-    z_size = lax.axis_size("z")
-    row = lax.all_to_all(jnp.broadcast_to(mine, (z_size,) + mine.shape), "z", 0, 0, tiled=False)
-    other = lax.ppermute(row, "y", [(0, 1), (1, 0)])
-    second = lax.axis_index("y") == 1
-    got = jnp.stack([jnp.where(second, other, row), jnp.where(second, row, other)], 1)
-    return got.reshape((z_size * 2,) + mine.shape)
-
-
 def gather_halves(packed):
     half = packed.shape[1] // 2
     core = lax.axis_index("tgrp")
     mine = lax.dynamic_slice_in_dim(packed, core * half, half, 1)
-    got = gather_pairs(mine)
-    theirs = lax.ppermute(got, "tgrp", [(0, 1), (1, 0)])
-    first = jnp.where(core == 0, got, theirs)
-    second = jnp.where(core == 0, theirs, got)
-    return jnp.concatenate([first, second], 2)
+    z_size = lax.axis_size("z")
+    row = lax.all_to_all(jnp.broadcast_to(mine, (z_size,) + mine.shape), "z", 0, 0, tiled=False)
+    row_other_core = lax.ppermute(row, "tgrp", [(0, 1), (1, 0)])
+    other_y = lax.ppermute(row, "y", [(0, 1), (1, 0)])
+    other_y_other_core = lax.ppermute(row, ("y", "tgrp"), [(i, 3 - i) for i in range(4)])
+    first_core = core == 0
+    same_y = jnp.concatenate(
+        [jnp.where(first_core, row, row_other_core), jnp.where(first_core, row_other_core, row)], 2
+    )
+    across_y = jnp.concatenate(
+        [jnp.where(first_core, other_y, other_y_other_core), jnp.where(first_core, other_y_other_core, other_y)],
+        2,
+    )
+    second_y = lax.axis_index("y") == 1
+    got = jnp.stack([jnp.where(second_y, across_y, same_y), jnp.where(second_y, same_y, across_y)], 1)
+    return got.reshape((z_size * 2,) + packed.shape)
 
 
 def body_local(

time: 241 us -> 251 us (1.041)
  waiting for transfers between devices: 92.1 us -> 107 us
    ppermute x2 -> x3, waiting for transfers between devices: 11.9 us -> 107 us  [the longest x1 95.1 us: gather_halves(): other_y = lax.ppermute(row, 'y', [(0, 1), (1, 0)])]
    ppermute x2, waiting for transfers between devices: 80.2 us -> 0.01 us  [seq_shifted(): return lax.ppermute(block, SEQ, route)]
  transfers between devices with their start and end apart: 5 -> 6, of which waited for: 2 -> 2; matrix products, arithmetic and copies ran while one was open for 32% -> 28% of each run, Pallas kernels for 0% -> 0%
where the time goes in v16:
time: 251 us; the launch traced here: 250 us
  waiting for transfers between devices  107 us (43%)
  other arithmetic  53.4 us (21%)
  matrix products  30.5 us (12%)
  local copies, waits for them, and re-layouts  28.5 us (11%)
  blocking collectives  21.2 us (8%)
  starting transfers between devices  9.21 us (4%)
    ppermute x1, waiting for transfers between devices, gather_halves(): other_y = lax.ppermute(row, 'y', [(0, 1), (1, 0)])  95.1 us
    reduce_sum x4, other arithmetic, iterate(): partial_cols = jnp.sum(row_scale[:, None, None, :] * kernel, axis=3)  38.4 us
    while x16, local copies, waits for them, and re-layouts  22.4 us
    all_to_all x1, blocking collectives, gather_halves(): lax.all_to_all(jnp.broadcast_to(mine, (z_size,) + mine.shape), 'z', 0, 0,...  21.2 us
    dot_general x1, matrix products, body_local(): jnp.einsum('bkjp,bip->bkji', beside(t_unit), s_unit, preferred_element_ty...  11.8 us
    ppermute x1, waiting for transfers between devices, gather_halves(): lax.ppermute(row, ('y', 'tgrp'), [(i, 3 - i) for i in range(4)])  11.6 us
    dot_general x1, matrix products, body_local(): lax.dot_general(sides, near_rows, along_j, preferred_element_type=jnp.flo...  10.7 us
    reduce_sum x4, other arithmetic, iterate(): row_scale = 1.0 / jnp.sum(kernel * col_scale[:, :, :, None], axis=(1, 2))  8.94 us
  transfers between devices with their start and end apart: 6, of which 2 were waited for; matrix products, arithmetic and copies ran while one was open for 28% of the time, Pallas kernels for 0%

profile of v16, /device:TPU:0, one launch (start us, length us, event | category | flops | bytes accessed | tf_op | source)
XLA Modules:
  0.0 250.5 jit_solution(1327968285471827842)
XLA Ops:
  0.0 1.6 copy-done
  1.6 1.9 fusion.35
  3.5 0.0 copy-start.7
  3.5 0.0 copy-start.8
  3.5 0.0 copy-start.9
  3.5 3.7 %fusion.36 = f32[512,128]{0,1:T(8,128)S(1)} fusion(bf16[512,4096]{1,0:T(8,128)(2,1)} %param.12, bf16[4096,128]{1,0:T(8,128)(2,1)S(1)} %copy-done.6), kind=kOutput, calls=%fused_computation.110 | convolution fusion | flops 536870912 | bytes 5505024 | tf_op jit(solution)/shard_map/dot_general | solution.py:79
  7.3 0.5 collective-permute-start
  7.8 0.1 fusion.23
  7.9 0.1 copy.35
  8.1 0.1 copy.34
  8.2 0.1 pad.39.clone
  8.3 0.6 compare_reduce_fusion
  8.9 0.6 broadcast_select_fusion.3
  9.6 0.0 collective-permute-done
  9.6 0.1 fusion.28
  9.7 0.1 multiply_reduce_fusion.2
  9.7 0.1 multiply_convert_fusion
  9.8 0.1 fusion.19
  9.9 0.1 copy.36
  10.1 0.1 broadcast_in_dim.8
  10.2 21.2 %all_to_all.5 = bf16[4,528,128]{2,1,0:T(8,128)(2,1)S(1)} all-to-all(bf16[4,528,128]{2,1,0:T(8,128)(2,1)S(1)} %broadcast_in_dim.8), channel_id=1, replica_groups=mesh['groups'=2,'z'=4,'y'=2,'tgrp'=2] {'z'}, dimensions={0} | all-to-all | bytes 1081344 | tf_op jit(solution)/shard_map/all_to_all | solution.py:53
  31.3 1.5 collective-permute-start.1
  32.9 0.3 collective-permute-start.2
  33.2 5.4 %collective-permute-start.4 = (bf16[512,4096]{1,0:T(8,128)(2,1)}, bf16[512,4096]{1,0:T(8,128)(2,1)}, u32[]{:S(2)}, u32[]{:S(2)}) collective-permute-start(bf16[512,4096]{1,0:T(8,128)(2,1)} %param.12), channel_id=1, source_target_pairs={{0,2},{2,4},{4,6},{6,8},{8,10},{10,12},{12,14},{1,3},{3,5},{5,7},{... | collective-permute-start | bytes 12582920 | tf_op jit(solution)/shard_map/ppermute | solution.py:45
  38.6 1.5 collective-permute-start.5
  40.1 0.1 pad.21.clone
  40.1 0.1 select_bitcast_fusion.1
  40.2 95.1 %collective-permute-done.1 = bf16[4,528,128]{2,1,0:T(8,128)(2,1)S(1)} collective-permute-done((bf16[4,528,128]{2,1,0:T(8,128)(2,1)S(1)}, bf16[4,528,128]{2,1,0:T(8,128)(2,1)S(1)}, u32[]{:S(2)}, u32[]{:S(2)}) %collective-permute-start.1) | collective-permute-done | bytes 540704 | tf_op jit(solution)/shard_map/ppermute | solution.py:55
  135.3 11.6 %collective-permute-done.2 = bf16[4,528,128]{2,1,0:T(8,128)(2,1)S(1)} collective-permute-done((bf16[4,528,128]{2,1,0:T(8,128)(2,1)S(1)}, bf16[4,528,128]{2,1,0:T(8,128)(2,1)S(1)}, u32[]{:S(2)}, u32[]{:S(2)}) %collective-permute-start.2) | collective-permute-done | bytes 540704 | tf_op jit(solution)/shard_map/ppermute | solution.py:56
  146.9 0.1 select_bitcast_fusion.3
  147.0 0.5 broadcast_select_fusion.2
  147.5 0.2 pad_maximum_fusion.2
  147.7 0.0 copy-start.4
  147.7 0.4 fusion.31
  148.1 0.2 slice_bitcast_fusion.2
  148.3 0.8 copy-done.4
  149.1 0.1 reshape.519
  149.1 0.1 slice_add_fusion
  149.3 0.8 slice_convert_fusion.1
  150.1 0.1 pad_bitcast_fusion.2
  150.2 0.1 pad_bitcast_fusion.3
  150.4 0.1 fusion.34
  150.5 0.1 pad_maximum_fusion.8
  150.6 11.8 %exponential_multiply_fusion = f32[8,3,512,512]{3,2,1,0:T(8,128)} fusion(f32[8,3]{1,0:T(8,128)S(1)} %pad_maximum_fusion.8, f32[8,3,512]{2,1,0:T(4,128)S(1)} %copy.43, f32[8,512]{1,0:T(8,128)S(1)} %bitcast.109, bf16[8,528,256]{2,1,0:T(8,128)(2,1)} %bitcast.101, bf16[8,1,512,128]{3,2,0,1:T(8,128)(2,1)S(1)} %pad_bitcast_fusion.2, ...), kind=kOutput, calls=%fused_computation.13 | convolution fusion | flops 1651507200 | bytes 29425760 | tf_op jit(solution)/shard_map/bkjp,bip->bkji/dot_general | solution.py:105
  162.4 70.8 %while.14 = (s32[]{:T(128)}, f32[8,512]{1,0:T(8,128)S(1)}, f32[8,3,512]{2,0,1:T(8,128)}, f32[8,3,512,512]{3,2,1,0:T(8,128)}, s32[]{:T(128)}, /*index=5*/s32[]{:T(128)}) while((s32[]{:T(128)}, f32[8,512]{1,0:T(8,128)S(1)}, f32[8,3,512]{2,0,1:T(8,128)}, f32[8,3,512,512]{3,2,1,0:T(8,128)}, s32[]{:T(128)}, /*index=5*/s32[]{:T(128)}) %tuple.48), condition=%wide.region_6.7_spmd.clone, body=%wide.region_3.6_spmd.clone.sunk | while | flops 25194500 | bytes 151912576 | solution.py:124
  162.4 9.6 %multiply_reduce_fusion.6 = f32[8,3,512]{2,1,0:T(4,128)S(1)} fusion(f32[8,3,512,512]{3,2,1,0:T(8,128)} %get-tuple-element.144, f32[8,512]{1,0:T(8,128)S(1)} %broadcast_select_fusion.5), kind=kLoop, calls=%fused_computation.1.clone.1 | loop fusion | flops 12570624 | bytes 25231360 | tf_op jit(solution)/shard_map/while/body/eval_jaxpr/reduce_sum | solution.py:113
  172.2 5.6 %copy-done.2 = f32[8,3,512,512]{3,2,1,0:T(8,128)S(1)} copy-done((f32[8,3,512,512]{3,2,1,0:T(8,128)S(1)}, f32[8,3,512,512]{3,2,1,0:T(8,128)}, u32[]{:S(2)}) %copy-start.2) | copy-done | bytes 25165848 | tf_op jit(solution)/shard_map/while
  177.8 2.2 multiply_reduce_fusion.7
  180.1 9.6 %multiply_reduce_fusion.6 = f32[8,3,512]{2,1,0:T(4,128)S(1)} fusion(f32[8,3,512,512]{3,2,1,0:T(8,128)} %get-tuple-element.144, f32[8,512]{1,0:T(8,128)S(1)} %broadcast_select_fusion.5), kind=kLoop, calls=%fused_computation.1.clone.1 | loop fusion | flops 12570624 | bytes 25231360 | tf_op jit(solution)/shard_map/while/body/eval_jaxpr/reduce_sum | solution.py:113
  189.9 5.6 %copy-done.2 = f32[8,3,512,512]{3,2,1,0:T(8,128)S(1)} copy-done((f32[8,3,512,512]{3,2,1,0:T(8,128)S(1)}, f32[8,3,512,512]{3,2,1,0:T(8,128)}, u32[]{:S(2)}) %copy-start.2) | copy-done | bytes 25165848 | tf_op jit(solution)/shard_map/while
  195.5 2.2 multiply_reduce_fusion.7
  197.8 9.6 %multiply_reduce_fusion.6 = f32[8,3,512]{2,1,0:T(4,128)S(1)} fusion(f32[8,3,512,512]{3,2,1,0:T(8,128)} %get-tuple-element.144, f32[8,512]{1,0:T(8,128)S(1)} %broadcast_select_fusion.5), kind=kLoop, calls=%fused_computation.1.clone.1 | loop fusion | flops 12570624 | bytes 25231360 | tf_op jit(solution)/shard_map/while/body/eval_jaxpr/reduce_sum | solution.py:113
  207.6 5.6 %copy-done.2 = f32[8,3,512,512]{3,2,1,0:T(8,128)S(1)} copy-done((f32[8,3,512,512]{3,2,1,0:T(8,128)S(1)}, f32[8,3,512,512]{3,2,1,0:T(8,128)}, u32[]{:S(2)}) %copy-start.2) | copy-done | bytes 25165848 | tf_op jit(solution)/shard_map/while
  213.2 2.2 multiply_reduce_fusion.7
  215.5 9.6 %multiply_reduce_fusion.6 = f32[8,3,512]{2,1,0:T(4,128)S(1)} fusion(f32[8,3,512,512]{3,2,1,0:T(8,128)} %get-tuple-element.144, f32[8,512]{1,0:T(8,128)S(1)} %broadcast_select_fusion.5), kind=kLoop, calls=%fused_computation.1.clone.1 | loop fusion | flops 12570624 | bytes 25231360 | tf_op jit(solution)/shard_map/while/body/eval_jaxpr/reduce_sum | solution.py:113
  225.3 5.6 %copy-done.2 = f32[8,3,512,512]{3,2,1,0:T(8,128)S(1)} copy-done((f32[8,3,512,512]{3,2,1,0:T(8,128)S(1)}, f32[8,3,512,512]{3,2,1,0:T(8,128)}, u32[]{:S(2)}) %copy-start.2) | copy-done | bytes 25165848 | tf_op jit(solution)/shard_map/while
  230.9 2.2 multiply_reduce_fusion.7
  233.2 0.8 constant_dynamic-slice_fusion
  234.0 0.0 copy-start.3
  234.0 2.4 fusion.10
  236.4 0.9 slice_bitcast_fusion.4
  237.3 2.4 fusion.15
  239.8 0.0 copy-start.1
  239.8 10.7 %add_convert_fusion = bf16[512,4096]{1,0:T(8,128)(2,1)} fusion(f32[512,4096]{1,0:T(8,128)S(1)} %fusion.15, bf16[512,4096]{1,0:T(8,128)(2,1)} %collective-permute-done.5, bf16[512,4096]{1,0:T(8,128)(2,1)} %collective-permute-done.4, bf16[512,512]{1,0:T(8,128)(2,1)} %get-tuple-element.78, bf16[512,512]{1,0:T(8,128)(2,1)S(1)} %get-tuple-element.77), kind=kOutput, calls=%fused_computation.18 | convolution fusion | flops 4318035968 | bytes 22020096 | tf_op jit(solution)/shard_map/dot_general | solution.py:138
  (92 shorter events, 0.9 us)
Async XLA Ops:
  0.0 1.6 copy-start
  0.0 3.5 %copy-start.6 = (bf16[4096,128]{1,0:T(8,128)(2,1)S(1)}, bf16[4096,128]{1,0:T(8,128)(2,1)}, u32[]{:S(2)}) copy-start(bf16[4096,128]{1,0:T(8,128)(2,1)} %param.14) | copy-start | bytes 3145732
  3.5 4.3 %copy-start.7 = (s32[512]{0:T(512)S(1)}, s32[512]{0:T(512)}, u32[]{:S(2)}) copy-start(s32[512]{0:T(512)} %param.16) | copy-start | bytes 6148
  3.5 4.3 %copy-start.8 = (s32[512]{0:T(512)S(1)}, s32[512]{0:T(512)}, u32[]{:S(2)}) copy-start(s32[512]{0:T(512)} %param.15) | copy-start | bytes 6148
  3.5 4.6 %copy-start.9 = (s32[1,2]{1,0:T(1,128)S(1)}, s32[1,2]{1,0:T(1,128)}, u32[]{:S(2)}) copy-start(s32[1,2]{1,0:T(1,128)} %param.17) | copy-start | bytes 28
  7.3 2.3 collective-permute-start
  31.3 8.8 %collective-permute-start.3 = (bf16[4,528,128]{2,1,0:T(8,128)(2,1)S(1)}, bf16[4,528,128]{2,1,0:T(8,128)(2,1)S(1)}, u32[]{:S(2)}, u32[]{:S(2)}) collective-permute-start(bf16[4,528,128]{2,1,0:T(8,128)(2,1)S(1)} %all_to_all.5), channel_id=1, source_target_pairs={{0,1},{1,0},{2,3},{3,2},{4,5},{5,4},{6,7},{7,6},{8,9},{9,8},{10,11... | collective-permute-start | bytes 1622024 | tf_op jit(solution)/shard_map/ppermute | solution.py:54
  31.3 104.0 %collective-permute-start.1 = (bf16[4,528,128]{2,1,0:T(8,128)(2,1)S(1)}, bf16[4,528,128]{2,1,0:T(8,128)(2,1)S(1)}, u32[]{:S(2)}, u32[]{:S(2)}) collective-permute-start(bf16[4,528,128]{2,1,0:T(8,128)(2,1)S(1)} %all_to_all.5), channel_id=1, source_target_pairs={{0,2},{2,0},{1,3},{3,1},{4,6},{6,4},{5,7},{7,5},{8,10},{10,8},{9,1... | collective-permute-start | bytes 1622024 | tf_op jit(solution)/shard_map/ppermute | solution.py:55
  32.9 114.1 %collective-permute-start.2 = (bf16[4,528,128]{2,1,0:T(8,128)(2,1)S(1)}, bf16[4,528,128]{2,1,0:T(8,128)(2,1)S(1)}, u32[]{:S(2)}, u32[]{:S(2)}) collective-permute-start(bf16[4,528,128]{2,1,0:T(8,128)(2,1)S(1)} %all_to_all.5), channel_id=1, source_target_pairs={{0,3},{1,2},{2,1},{3,0},{4,7},{5,6},{6,5},{7,4},{8,11},{9,10},{10,... | collective-permute-start | bytes 1622024 | tf_op jit(solution)/shard_map/ppermute | solution.py:56
  33.2 206.6 %collective-permute-start.4 = (bf16[512,4096]{1,0:T(8,128)(2,1)}, bf16[512,4096]{1,0:T(8,128)(2,1)}, u32[]{:S(2)}, u32[]{:S(2)}) collective-permute-start(bf16[512,4096]{1,0:T(8,128)(2,1)} %param.12), channel_id=1, source_target_pairs={{0,2},{2,4},{4,6},{6,8},{8,10},{10,12},{12,14},{1,3},{3,5},{5,7},{... | collective-permute-start | bytes 12582920 | tf_op jit(solution)/shard_map/ppermute | solution.py:45
  38.6 201.2 %collective-permute-start.5 = (bf16[512,4096]{1,0:T(8,128)(2,1)}, bf16[512,4096]{1,0:T(8,128)(2,1)}, u32[]{:S(2)}, u32[]{:S(2)}) collective-permute-start(bf16[512,4096]{1,0:T(8,128)(2,1)} %param.12), channel_id=1, source_target_pairs={{2,0},{4,2},{6,4},{8,6},{10,8},{12,10},{14,12},{3,1},{5,3},{7,5},{... | collective-permute-start | bytes 12582920 | tf_op jit(solution)/shard_map/ppermute | solution.py:45
  147.7 1.3 copy-start.4
  162.4 15.4 %copy-start.2 = (f32[8,3,512,512]{3,2,1,0:T(8,128)S(1)}, f32[8,3,512,512]{3,2,1,0:T(8,128)}, u32[]{:S(2)}) copy-start(f32[8,3,512,512]{3,2,1,0:T(8,128)} %get-tuple-element.144) | copy-start | bytes 75497472 | tf_op jit(solution)/shard_map/while
  172.1 7.9 %copy-start.5 = (f32[8,3,512]{2,0,1:T(8,128)}, f32[8,3,512]{2,0,1:T(8,128)S(1)}, u32[]{:S(2)}) copy-start(f32[8,3,512]{2,0,1:T(8,128)S(1)} %pad_maximum_fusion.12) | copy-start | bytes 147460 | tf_op jit(solution)/shard_map/while
  180.1 15.4 %copy-start.2 = (f32[8,3,512,512]{3,2,1,0:T(8,128)S(1)}, f32[8,3,512,512]{3,2,1,0:T(8,128)}, u32[]{:S(2)}) copy-start(f32[8,3,512,512]{3,2,1,0:T(8,128)} %get-tuple-element.144) | copy-start | bytes 75497472 | tf_op jit(solution)/shard_map/while
  189.9 7.9 %copy-start.5 = (f32[8,3,512]{2,0,1:T(8,128)}, f32[8,3,512]{2,0,1:T(8,128)S(1)}, u32[]{:S(2)}) copy-start(f32[8,3,512]{2,0,1:T(8,128)S(1)} %pad_maximum_fusion.12) | copy-start | bytes 147460 | tf_op jit(solution)/shard_map/while
  197.8 15.4 %copy-start.2 = (f32[8,3,512,512]{3,2,1,0:T(8,128)S(1)}, f32[8,3,512,512]{3,2,1,0:T(8,128)}, u32[]{:S(2)}) copy-start(f32[8,3,512,512]{3,2,1,0:T(8,128)} %get-tuple-element.144) | copy-start | bytes 75497472 | tf_op jit(solution)/shard_map/while
  207.6 7.9 %copy-start.5 = (f32[8,3,512]{2,0,1:T(8,128)}, f32[8,3,512]{2,0,1:T(8,128)S(1)}, u32[]{:S(2)}) copy-start(f32[8,3,512]{2,0,1:T(8,128)S(1)} %pad_maximum_fusion.12) | copy-start | bytes 147460 | tf_op jit(solution)/shard_map/while
  215.5 15.4 %copy-start.2 = (f32[8,3,512,512]{3,2,1,0:T(8,128)S(1)}, f32[8,3,512,512]{3,2,1,0:T(8,128)}, u32[]{:S(2)}) copy-start(f32[8,3,512,512]{3,2,1,0:T(8,128)} %get-tuple-element.144) | copy-start | bytes 75497472 | tf_op jit(solution)/shard_map/while
  225.3 7.9 %copy-start.5 = (f32[8,3,512]{2,0,1:T(8,128)}, f32[8,3,512]{2,0,1:T(8,128)S(1)}, u32[]{:S(2)}) copy-start(f32[8,3,512]{2,0,1:T(8,128)S(1)} %pad_maximum_fusion.12) | copy-start | bytes 147460 | tf_op jit(solution)/shard_map/while
  234.0 3.3 %copy-start.3 = (bf16[512,4096]{1,0:T(8,128)(2,1)S(1)}, bf16[512,4096]{1,0:T(8,128)(2,1)}, u32[]{:S(2)}) copy-start(bf16[512,4096]{1,0:T(8,128)(2,1)} %param.12) | copy-start | bytes 12582916
  239.8 10.7 %copy-start.1 = (bf16[512,2048]{1,0:T(8,128)(2,1)S(1)}, bf16[512,2048]{1,0:T(8,128)(2,1)}, u32[]{:S(2)}) copy-start(bf16[512,2048]{1,0:T(8,128)(2,1)} %param.11) | copy-start | bytes 6291460

commit v17 on v14

--- a/solution.py
+++ b/solution.py
@@ -47,10 +47,16 @@
 
 def gather_pairs(mine):
     z_size = lax.axis_size("z")
-    row = lax.all_to_all(jnp.broadcast_to(mine, (z_size,) + mine.shape), "z", 0, 0, tiled=False)
-    other = lax.ppermute(row, "y", [(0, 1), (1, 0)])
+    cut = mine.shape[1] // 2
+    part_a, part_b = mine[:, :cut], mine[:, cut:]
     second = lax.axis_index("y") == 1
-    got = jnp.stack([jnp.where(second, other, row), jnp.where(second, row, other)], 1)
+    row_a = lax.all_to_all(jnp.broadcast_to(part_a, (z_size,) + part_a.shape), "z", 0, 0, tiled=False)
+    partner_b = lax.ppermute(part_b, "y", [(0, 1), (1, 0)])
+    pair_b = jnp.stack([jnp.where(second, partner_b, part_b), jnp.where(second, part_b, partner_b)])
+    other_a = lax.ppermute(row_a, "y", [(0, 1), (1, 0)])
+    got_b = lax.all_to_all(jnp.broadcast_to(pair_b, (z_size,) + pair_b.shape), "z", 0, 0, tiled=False)
+    got_a = jnp.stack([jnp.where(second, other_a, row_a), jnp.where(second, row_a, other_a)], 1)
+    got = jnp.concatenate([got_a, got_b], -1)
     return got.reshape((z_size * 2,) + mine.shape)
 
 

time: 241 us -> 248 us (1.029)
  blocking collectives: 21.2 us -> 0 us
  waiting for transfers between devices: 92.1 us -> 109 us
  starting transfers between devices: 8.93 us -> 20.3 us
    all_to_all x1 -> x0, blocking collectives: 21.2 us -> none  [gather_pairs(): lax.all_to_all(jnp.broadcast_to(mine, (z_size,) + mine.shape), 'z', 0, 0,...]
    all_to_all x0 -> x2, waiting for transfers between devices: none -> 18 us  [the longest x1 10 us: gather_pairs(): lax.all_to_all(jnp.broadcast_to(part_a, (z_size,) + part_a.shape), 'z', 0...]
    all_to_all x0 -> x2, starting transfers between devices: none -> 8.58 us  [the longest x1 5.09 us: gather_pairs(): lax.all_to_all(jnp.broadcast_to(part_a, (z_size,) + part_a.shape), 'z', 0...]
    ppermute x1 -> x2, waiting for transfers between devices: 11.9 us -> 8.95 us  [the longest x1 5.98 us: gather_pairs(): other_a = lax.ppermute(row_a, 'y', [(0, 1), (1, 0)])]
    ppermute x1 -> x2, starting transfers between devices: 1.52 us -> 4.31 us  [the longest x1 2.72 us: gather_pairs(): partner_b = lax.ppermute(part_b, 'y', [(0, 1), (1, 0)])]
  transfers between devices with their start and end apart: 5 -> 8, of which waited for: 2 -> 5; matrix products, arithmetic and copies ran while one was open for 32% -> 30% of each run, Pallas kernels for 0% -> 0%
where the time goes in v17:
time: 248 us; the launch traced here: 247 us
  waiting for transfers between devices  109 us (44%)
  other arithmetic  53.7 us (22%)
  local copies, waits for them, and re-layouts  33 us (13%)
  matrix products  30.3 us (12%)
  starting transfers between devices  20.3 us (8%)
    ppermute x2, waiting for transfers between devices, seq_shifted(): return lax.ppermute(block, SEQ, route)  82.2 us
    reduce_sum x4, other arithmetic, iterate(): partial_cols = jnp.sum(row_scale[:, None, None, :] * kernel, axis=3)  38.4 us
    while x16, local copies, waits for them, and re-layouts  22.4 us
    dot_general x1, matrix products, body_local(): jnp.einsum('bkjp,bip->bkji', beside(t_unit), s_unit, preferred_element_ty...  11.6 us
    dot_general x1, matrix products, body_local(): lax.dot_general(sides, near_rows, along_j, preferred_element_type=jnp.flo...  10.7 us
    all_to_all x1, waiting for transfers between devices, gather_pairs(): lax.all_to_all(jnp.broadcast_to(part_a, (z_size,) + part_a.shape), 'z', 0...  10 us
    reduce_sum x4, other arithmetic, iterate(): row_scale = 1.0 / jnp.sum(kernel * col_scale[:, :, :, None], axis=(1, 2))  8.94 us
    all_to_all x1, waiting for transfers between devices, gather_pairs(): lax.all_to_all(jnp.broadcast_to(pair_b, (z_size,) + pair_b.shape), 'z', 0...  7.96 us
  transfers between devices with their start and end apart: 8, of which 5 were waited for; matrix products, arithmetic and copies ran while one was open for 30% of the time, Pallas kernels for 0%

profile of v17, /device:TPU:0, one launch (start us, length us, event | category | flops | bytes accessed | tf_op | source)
XLA Modules:
  0.0 247.4 jit_solution(14013726180692106807)
XLA Ops:
  0.0 1.6 copy-done
  1.6 1.9 fusion.36
  3.5 0.0 copy-start.8
  3.5 0.0 copy-start.9
  3.5 3.7 %fusion.37 = f32[512,128]{0,1:T(8,128)S(1)} fusion(bf16[512,4096]{1,0:T(8,128)(2,1)} %param.12, bf16[4096,128]{1,0:T(8,128)(2,1)S(1)} %copy-done.7), kind=kOutput, calls=%fused_computation.110 | convolution fusion | flops 536870912 | bytes 5505024 | tf_op jit(solution)/shard_map/dot_general | solution.py:83
  7.3 0.5 collective-permute-start
  7.8 0.1 fusion.24
  7.9 0.1 copy.33
  8.1 0.1 copy.32
  8.2 0.1 pad.40.clone
  8.3 0.6 compare_reduce_fusion
  8.9 0.6 broadcast_select_fusion.3
  9.6 0.1 fusion.29
  9.7 0.1 multiply_reduce_fusion.2
  9.7 0.1 multiply_convert_fusion
  9.8 0.1 fusion.19
  10.0 2.7 %collective-permute-start.2 = (bf16[528,64]{0,1:T(8,128)(2,1)S(1)}, bf16[528,64]{0,1:T(8,128)(2,1)S(1)}, u32[]{:S(2)}, u32[]{:S(2)}) collective-permute-start(bf16[528,64]{0,1:T(8,128)(2,1)S(1)} %slice.144), channel_id=1, source_target_pairs={{0,2},{2,0},{1,3},{3,1},{4,6},{6,4},{5,7},{7,5},{8,10},{10,8},{9,1... | collective-permute-start | bytes 202760 | tf_op jit(solution)/shard_map/ppermute | solution.py:54
  12.7 3.0 %collective-permute-done.2 = bf16[528,64]{0,1:T(8,128)(2,1)S(1)} collective-permute-done((bf16[528,64]{0,1:T(8,128)(2,1)S(1)}, bf16[528,64]{0,1:T(8,128)(2,1)S(1)}, u32[]{:S(2)}, u32[]{:S(2)}) %collective-permute-start.2) | collective-permute-done | bytes 67616 | tf_op jit(solution)/shard_map/ppermute | solution.py:54
  15.7 0.8 broadcast_in_dim.10
  16.4 5.1 %all-to-all-start = ((bf16[4,528,64]{1,2,0:T(8,128)(2,1)}), bf16[4,528,64]{1,2,0:T(8,128)(2,1)S(1)}, u32[]{:S(2)}, u32[]{:S(2)}) async-start(bf16[4,528,64]{1,2,0:T(8,128)(2,1)} %broadcast_in_dim.10), calls=%async_computation | async-start | bytes 655360 | tf_op jit(solution)/shard_map/all_to_all | solution.py:53
  21.6 10.0 %all-to-all-done = bf16[4,528,64]{1,2,0:T(8,128)(2,1)S(1)} async-done(((bf16[4,528,64]{1,2,0:T(8,128)(2,1)}), bf16[4,528,64]{1,2,0:T(8,128)(2,1)S(1)}, u32[]{:S(2)}, u32[]{:S(2)}) %all-to-all-start) | async-done | bytes 270368 | tf_op jit(solution)/shard_map/all_to_all | solution.py:53
  31.6 0.9 broadcast_in_dim.11
  32.5 3.5 %all-to-all-start.1 = ((bf16[4,2,528,64]{2,3,1,0:T(8,128)(2,1)}), bf16[4,2,528,64]{2,3,1,0:T(8,128)(2,1)S(1)}, u32[]{:S(2)}, u32[]{:S(2)}) async-start(bf16[4,2,528,64]{2,3,1,0:T(8,128)(2,1)} %broadcast_in_dim.11), calls=%async_computation.1 | async-start | bytes 1310720 | tf_op jit(solution)/shard_map/all_to_all | solution.py:57
  36.0 1.6 collective-permute-start.1
  37.5 6.0 %collective-permute-done.1 = bf16[4,528,64]{1,2,0:T(8,128)(2,1)S(1)} collective-permute-done((bf16[4,528,64]{1,2,0:T(8,128)(2,1)S(1)}, bf16[4,528,64]{1,2,0:T(8,128)(2,1)S(1)}, u32[]{:S(2)}, u32[]{:S(2)}) %collective-permute-start.1) | collective-permute-done | bytes 270368 | tf_op jit(solution)/shard_map/ppermute | solution.py:56
  43.5 0.1 select_bitcast_fusion.1
  43.6 8.0 %all-to-all-done.1 = bf16[4,2,528,64]{2,3,1,0:T(8,128)(2,1)S(1)} async-done(((bf16[4,2,528,64]{2,3,1,0:T(8,128)(2,1)}), bf16[4,2,528,64]{2,3,1,0:T(8,128)(2,1)S(1)}, u32[]{:S(2)}, u32[]{:S(2)}) %all-to-all-start.1) | async-done | bytes 540704 | tf_op jit(solution)/shard_map/all_to_all | solution.py:57
  51.5 0.1 pad_maximum_fusion.2
  51.7 0.8 copy.35
  52.5 0.0 copy-start.4
  52.5 0.1 collective-permute-start.3
  52.6 5.4 %collective-permute-start.4 = (bf16[512,4096]{1,0:T(8,128)(2,1)}, bf16[512,4096]{1,0:T(8,128)(2,1)}, u32[]{:S(2)}, u32[]{:S(2)}) collective-permute-start(bf16[512,4096]{1,0:T(8,128)(2,1)} %param.12), channel_id=1, source_target_pairs={{0,2},{2,4},{4,6},{6,8},{8,10},{10,12},{12,14},{1,3},{3,5},{5,7},{... | collective-permute-start | bytes 12582920 | tf_op jit(solution)/shard_map/ppermute | solution.py:45
  57.9 1.5 collective-permute-start.5
  59.4 0.1 pad.21.clone
  59.5 1.7 broadcast_select_fusion.1
  61.2 1.3 fusion.32
  62.5 1.0 slice_bitcast_fusion.2
  63.5 0.1 reshape.409
  63.6 0.1 slice_add_fusion
  63.8 0.0 copy-start.6
  63.8 1.3 pad_bitcast_fusion.2
  65.2 0.1 pad_bitcast_fusion.3
  65.4 0.1 fusion.35
  65.5 0.1 pad_maximum_fusion.8
  65.5 11.6 %exponential_multiply_fusion = f32[8,3,512,512]{3,2,1,0:T(8,128)} fusion(f32[8,3]{1,0:T(8,128)S(1)} %pad_maximum_fusion.8, f32[8,3,512]{2,1,0:T(4,128)S(1)} %copy.39, f32[8,512]{1,0:T(8,128)S(1)} %bitcast.101, bf16[8,528,128]{2,1,0:T(8,128)(2,1)S(1)} %get-tuple-element.73, bf16[8,1,512,128]{3,2,0,1:T(8,128)(2,1)S(1)} %pad_bitcast_fusion.2, ...), kind=kOutput, calls=%fused_computation.13 | convolution fusion | flops 1651507200 | bytes 29446144 | tf_op jit(solution)/shard_map/bkjp,bip->bkji/dot_general | solution.py:109
  77.1 70.8 %while.14 = (s32[]{:T(128)}, f32[8,512]{1,0:T(8,128)S(1)}, f32[8,3,512]{2,0,1:T(8,128)}, f32[8,3,512,512]{3,2,1,0:T(8,128)}, s32[]{:T(128)}, /*index=5*/s32[]{:T(128)}) while((s32[]{:T(128)}, f32[8,512]{1,0:T(8,128)S(1)}, f32[8,3,512]{2,0,1:T(8,128)}, f32[8,3,512,512]{3,2,1,0:T(8,128)}, s32[]{:T(128)}, /*index=5*/s32[]{:T(128)}) %tuple.49), condition=%wide.region_6.7_spmd.clone, body=%wide.region_3.6_spmd.clone.sunk | while | flops 25194500 | bytes 151912576 | solution.py:128
  77.1 9.6 %multiply_reduce_fusion.6 = f32[8,3,512]{2,1,0:T(4,128)S(1)} fusion(f32[8,3,512,512]{3,2,1,0:T(8,128)} %get-tuple-element.145, f32[8,512]{1,0:T(8,128)S(1)} %broadcast_select_fusion.5), kind=kLoop, calls=%fused_computation.1.clone.1 | loop fusion | flops 12570624 | bytes 25231360 | tf_op jit(solution)/shard_map/while/body/eval_jaxpr/reduce_sum | solution.py:117
  86.9 5.6 %copy-done.2 = f32[8,3,512,512]{3,2,1,0:T(8,128)S(1)} copy-done((f32[8,3,512,512]{3,2,1,0:T(8,128)S(1)}, f32[8,3,512,512]{3,2,1,0:T(8,128)}, u32[]{:S(2)}) %copy-start.2) | copy-done | bytes 25165848 | tf_op jit(solution)/shard_map/while
  92.5 2.2 multiply_reduce_fusion.7
  94.8 9.6 %multiply_reduce_fusion.6 = f32[8,3,512]{2,1,0:T(4,128)S(1)} fusion(f32[8,3,512,512]{3,2,1,0:T(8,128)} %get-tuple-element.145, f32[8,512]{1,0:T(8,128)S(1)} %broadcast_select_fusion.5), kind=kLoop, calls=%fused_computation.1.clone.1 | loop fusion | flops 12570624 | bytes 25231360 | tf_op jit(solution)/shard_map/while/body/eval_jaxpr/reduce_sum | solution.py:117
  104.6 5.6 %copy-done.2 = f32[8,3,512,512]{3,2,1,0:T(8,128)S(1)} copy-done((f32[8,3,512,512]{3,2,1,0:T(8,128)S(1)}, f32[8,3,512,512]{3,2,1,0:T(8,128)}, u32[]{:S(2)}) %copy-start.2) | copy-done | bytes 25165848 | tf_op jit(solution)/shard_map/while
  110.2 2.2 multiply_reduce_fusion.7
  112.5 9.6 %multiply_reduce_fusion.6 = f32[8,3,512]{2,1,0:T(4,128)S(1)} fusion(f32[8,3,512,512]{3,2,1,0:T(8,128)} %get-tuple-element.145, f32[8,512]{1,0:T(8,128)S(1)} %broadcast_select_fusion.5), kind=kLoop, calls=%fused_computation.1.clone.1 | loop fusion | flops 12570624 | bytes 25231360 | tf_op jit(solution)/shard_map/while/body/eval_jaxpr/reduce_sum | solution.py:117
  122.3 5.6 %copy-done.2 = f32[8,3,512,512]{3,2,1,0:T(8,128)S(1)} copy-done((f32[8,3,512,512]{3,2,1,0:T(8,128)S(1)}, f32[8,3,512,512]{3,2,1,0:T(8,128)}, u32[]{:S(2)}) %copy-start.2) | copy-done | bytes 25165848 | tf_op jit(solution)/shard_map/while
  127.9 2.2 multiply_reduce_fusion.7
  130.3 9.6 %multiply_reduce_fusion.6 = f32[8,3,512]{2,1,0:T(4,128)S(1)} fusion(f32[8,3,512,512]{3,2,1,0:T(8,128)} %get-tuple-element.145, f32[8,512]{1,0:T(8,128)S(1)} %broadcast_select_fusion.5), kind=kLoop, calls=%fused_computation.1.clone.1 | loop fusion | flops 12570624 | bytes 25231360 | tf_op jit(solution)/shard_map/while/body/eval_jaxpr/reduce_sum | solution.py:117
  140.1 5.6 %copy-done.2 = f32[8,3,512,512]{3,2,1,0:T(8,128)S(1)} copy-done((f32[8,3,512,512]{3,2,1,0:T(8,128)S(1)}, f32[8,3,512,512]{3,2,1,0:T(8,128)}, u32[]{:S(2)}) %copy-start.2) | copy-done | bytes 25165848 | tf_op jit(solution)/shard_map/while
  145.6 2.2 multiply_reduce_fusion.7
  147.9 0.8 constant_dynamic-slice_fusion
  148.8 2.4 fusion.10
  151.2 0.9 slice_bitcast_fusion.4
  152.0 2.4 fusion.15
  154.5 82.2 %collective-permute-done.4 = bf16[512,4096]{1,0:T(8,128)(2,1)} collective-permute-done((bf16[512,4096]{1,0:T(8,128)(2,1)}, bf16[512,4096]{1,0:T(8,128)(2,1)}, u32[]{:S(2)}, u32[]{:S(2)}) %collective-permute-start.4) | collective-permute-done | bytes 4194336 | tf_op jit(solution)/shard_map/ppermute | solution.py:45
  236.7 10.7 %add_convert_fusion = bf16[512,4096]{1,0:T(8,128)(2,1)} fusion(f32[512,4096]{1,0:T(8,128)S(1)} %fusion.15, bf16[512,4096]{1,0:T(8,128)(2,1)} %collective-permute-done.5, bf16[512,4096]{1,0:T(8,128)(2,1)} %collective-permute-done.4, bf16[512,512]{1,0:T(8,128)(2,1)} %get-tuple-element.76, bf16[512,512]{1,0:T(8,128)(2,1)S(1)} %get-tuple-element.75), kind=kOutput, calls=%fused_computation.18 | convolution fusion | flops 4318035968 | bytes 22020096 | tf_op jit(solution)/shard_map/dot_general | solution.py:142
  (100 shorter events, 0.9 us)
Async XLA Ops:
  0.0 1.6 copy-start
  0.0 3.5 %copy-start.7 = (bf16[4096,128]{1,0:T(8,128)(2,1)S(1)}, bf16[4096,128]{1,0:T(8,128)(2,1)}, u32[]{:S(2)}) copy-start(bf16[4096,128]{1,0:T(8,128)(2,1)} %param.14) | copy-start | bytes 3145732
  3.5 4.3 %copy-start.8 = (s32[512]{0:T(512)S(1)}, s32[512]{0:T(512)}, u32[]{:S(2)}) copy-start(s32[512]{0:T(512)} %param.16) | copy-start | bytes 6148
  3.5 4.3 %copy-start.9 = (s32[512]{0:T(512)S(1)}, s32[512]{0:T(512)}, u32[]{:S(2)}) copy-start(s32[512]{0:T(512)} %param.15) | copy-start | bytes 6148
  3.5 4.6 %copy-start.10 = (s32[1,2]{1,0:T(1,128)S(1)}, s32[1,2]{1,0:T(1,128)}, u32[]{:S(2)}) copy-start(s32[1,2]{1,0:T(1,128)} %param.17) | copy-start | bytes 28
  7.3 2.3 collective-permute-start
  10.0 5.7 %collective-permute-start.2 = (bf16[528,64]{0,1:T(8,128)(2,1)S(1)}, bf16[528,64]{0,1:T(8,128)(2,1)S(1)}, u32[]{:S(2)}, u32[]{:S(2)}) collective-permute-start(bf16[528,64]{0,1:T(8,128)(2,1)S(1)} %slice.144), channel_id=1, source_target_pairs={{0,2},{2,0},{1,3},{3,1},{4,6},{6,4},{5,7},{7,5},{8,10},{10,8},{9,1... | collective-permute-start | bytes 202760 | tf_op jit(solution)/shard_map/ppermute | solution.py:54
  16.4 15.1 %all-to-all-start = ((bf16[4,528,64]{1,2,0:T(8,128)(2,1)}), bf16[4,528,64]{1,2,0:T(8,128)(2,1)S(1)}, u32[]{:S(2)}, u32[]{:S(2)}) async-start(bf16[4,528,64]{1,2,0:T(8,128)(2,1)} %broadcast_in_dim.10), calls=%async_computation | async-start | bytes 655360 | tf_op jit(solution)/shard_map/all_to_all | solution.py:53
  32.5 19.1 %all-to-all-start.1 = ((bf16[4,2,528,64]{2,3,1,0:T(8,128)(2,1)}), bf16[4,2,528,64]{2,3,1,0:T(8,128)(2,1)S(1)}, u32[]{:S(2)}, u32[]{:S(2)}) async-start(bf16[4,2,528,64]{2,3,1,0:T(8,128)(2,1)} %broadcast_in_dim.11), calls=%async_computation.1 | async-start | bytes 1310720 | tf_op jit(solution)/shard_map/all_to_all | solution.py:57
  36.0 7.6 %collective-permute-start.1 = (bf16[4,528,64]{1,2,0:T(8,128)(2,1)S(1)}, bf16[4,528,64]{1,2,0:T(8,128)(2,1)S(1)}, u32[]{:S(2)}, u32[]{:S(2)}) collective-permute-start(bf16[4,528,64]{1,2,0:T(8,128)(2,1)S(1)} %all-to-all-done), channel_id=1, source_target_pairs={{0,2},{2,0},{1,3},{3,1},{4,6},{6,4},{5,7},{7,5},{8,10},{10,8},{9,1... | collective-permute-start | bytes 811016 | tf_op jit(solution)/shard_map/ppermute | solution.py:56
  52.5 7.0 %copy-start.4 = (bf16[4,2,528,128]{3,2,1,0:T(8,128)(2,1)}, bf16[4,2,528,128]{3,2,1,0:T(8,128)(2,1)S(1)}, u32[]{:S(2)}) copy-start(bf16[4,2,528,128]{3,2,1,0:T(8,128)(2,1)S(1)} %copy.35) | copy-start | bytes 3244036
  52.5 7.0 %collective-permute-start.3 = (bf16[8,528,128]{2,1,0:T(8,128)(2,1)S(1)}, bf16[8,528,128]{2,1,0:T(8,128)(2,1)}, u32[]{:S(2)}, u32[]{:S(2)}) collective-permute-start(bf16[8,528,128]{2,1,0:T(8,128)(2,1)S(1)} %bitcast.94), channel_id=1, source_target_pairs={{0,1},{1,0},{2,3},{3,2},{4,5},{5,4},{6,7},{7,6},{8,9},{9,8},{10,11... | collective-permute-start | bytes 3244040 | tf_op jit(solution)/shard_map/ppermute | solution.py:68
  52.6 184.1 %collective-permute-start.4 = (bf16[512,4096]{1,0:T(8,128)(2,1)}, bf16[512,4096]{1,0:T(8,128)(2,1)}, u32[]{:S(2)}, u32[]{:S(2)}) collective-permute-start(bf16[512,4096]{1,0:T(8,128)(2,1)} %param.12), channel_id=1, source_target_pairs={{0,2},{2,4},{4,6},{6,8},{8,10},{10,12},{12,14},{1,3},{3,5},{5,7},{... | collective-permute-start | bytes 12582920 | tf_op jit(solution)/shard_map/ppermute | solution.py:45
  57.9 178.7 %collective-permute-start.5 = (bf16[512,4096]{1,0:T(8,128)(2,1)}, bf16[512,4096]{1,0:T(8,128)(2,1)}, u32[]{:S(2)}, u32[]{:S(2)}) collective-permute-start(bf16[512,4096]{1,0:T(8,128)(2,1)} %param.12), channel_id=1, source_target_pairs={{2,0},{4,2},{6,4},{8,6},{10,8},{12,10},{14,12},{3,1},{5,3},{7,5},{... | collective-permute-start | bytes 12582920 | tf_op jit(solution)/shard_map/ppermute | solution.py:45
  63.8 1.8 copy-start.6
  77.1 15.4 %copy-start.2 = (f32[8,3,512,512]{3,2,1,0:T(8,128)S(1)}, f32[8,3,512,512]{3,2,1,0:T(8,128)}, u32[]{:S(2)}) copy-start(f32[8,3,512,512]{3,2,1,0:T(8,128)} %get-tuple-element.145) | copy-start | bytes 75497472 | tf_op jit(solution)/shard_map/while
  86.9 7.9 %copy-start.5 = (f32[8,3,512]{2,0,1:T(8,128)}, f32[8,3,512]{2,0,1:T(8,128)S(1)}, u32[]{:S(2)}) copy-start(f32[8,3,512]{2,0,1:T(8,128)S(1)} %pad_maximum_fusion.12) | copy-start | bytes 147460 | tf_op jit(solution)/shard_map/while
  94.8 15.4 %copy-start.2 = (f32[8,3,512,512]{3,2,1,0:T(8,128)S(1)}, f32[8,3,512,512]{3,2,1,0:T(8,128)}, u32[]{:S(2)}) copy-start(f32[8,3,512,512]{3,2,1,0:T(8,128)} %get-tuple-element.145) | copy-start | bytes 75497472 | tf_op jit(solution)/shard_map/while
  104.6 7.9 %copy-start.5 = (f32[8,3,512]{2,0,1:T(8,128)}, f32[8,3,512]{2,0,1:T(8,128)S(1)}, u32[]{:S(2)}) copy-start(f32[8,3,512]{2,0,1:T(8,128)S(1)} %pad_maximum_fusion.12) | copy-start | bytes 147460 | tf_op jit(solution)/shard_map/while
  112.5 15.4 %copy-start.2 = (f32[8,3,512,512]{3,2,1,0:T(8,128)S(1)}, f32[8,3,512,512]{3,2,1,0:T(8,128)}, u32[]{:S(2)}) copy-start(f32[8,3,512,512]{3,2,1,0:T(8,128)} %get-tuple-element.145) | copy-start | bytes 75497472 | tf_op jit(solution)/shard_map/while
  122.3 7.9 %copy-start.5 = (f32[8,3,512]{2,0,1:T(8,128)}, f32[8,3,512]{2,0,1:T(8,128)S(1)}, u32[]{:S(2)}) copy-start(f32[8,3,512]{2,0,1:T(8,128)S(1)} %pad_maximum_fusion.12) | copy-start | bytes 147460 | tf_op jit(solution)/shard_map/while
  130.2 15.4 %copy-start.2 = (f32[8,3,512,512]{3,2,1,0:T(8,128)S(1)}, f32[8,3,512,512]{3,2,1,0:T(8,128)}, u32[]{:S(2)}) copy-start(f32[8,3,512,512]{3,2,1,0:T(8,128)} %get-tuple-element.145) | copy-start | bytes 75497472 | tf_op jit(solution)/shard_map/while
  140.0 7.9 %copy-start.5 = (f32[8,3,512]{2,0,1:T(8,128)}, f32[8,3,512]{2,0,1:T(8,128)S(1)}, u32[]{:S(2)}) copy-start(f32[8,3,512]{2,0,1:T(8,128)S(1)} %pad_maximum_fusion.12) | copy-start | bytes 147460 | tf_op jit(solution)/shard_map/while
  148.8 3.3 %copy-start.3 = (bf16[512,4096]{1,0:T(8,128)(2,1)S(1)}, bf16[512,4096]{1,0:T(8,128)(2,1)}, u32[]{:S(2)}) copy-start(bf16[512,4096]{1,0:T(8,128)(2,1)} %param.12) | copy-start | bytes 12582916
  236.7 10.7 %copy-start.1 = (bf16[512,2048]{1,0:T(8,128)(2,1)S(1)}, bf16[512,2048]{1,0:T(8,128)(2,1)}, u32[]{:S(2)}) copy-start(bf16[512,2048]{1,0:T(8,128)(2,1)} %param.11) | copy-start | bytes 6291460

commit v18 on v10

--- a/solution.py
+++ b/solution.py
@@ -83,7 +83,9 @@
     digits = jnp.stack([student_chars, teacher_chars])
     digits = jnp.stack([digits // 4096, digits // 64 % 64, digits % 64], 1)
     digit_rows = digits.reshape(-1, units.shape[1]).astype(jnp.bfloat16)
-    flag_row = jnp.zeros((1, units.shape[1]), jnp.bfloat16).at[0, :2].set(band[0].astype(jnp.bfloat16))
+    flag_row = jnp.concatenate(
+        [band[0].astype(jnp.bfloat16), jnp.zeros((units.shape[1] - 2,), jnp.bfloat16)]
+    )[None]
     extra = jnp.concatenate([digit_rows, flag_row], 0)
     pad = -(rows + extra.shape[0]) % 16
     packed = jnp.concatenate([units, extra, jnp.zeros((pad, units.shape[1]), jnp.bfloat16)], 0)

time: 240 us -> 240 us (level)
  transfers between devices with their start and end apart: 4 -> 4, of which waited for: 1 -> 2; matrix products, arithmetic and copies ran while one was open for 31% -> 30% of each run, Pallas kernels for 0% -> 0%
where the time goes in v18:
time: 240 us; the launch traced here: 239 us
  waiting for transfers between devices  83 us (35%)
  other arithmetic  52.4 us (22%)
  blocking collectives  34.5 us (14%)
  local copies, waits for them, and re-layouts  31 us (13%)
  matrix products  30.5 us (13%)
  starting transfers between devices  6.53 us (3%)
    ppermute x2, waiting for transfers between devices, shifted(): return lax.ppermute(block, axis, route)  82 us
    reduce_sum x4, other arithmetic, iterate(): partial_cols = jnp.sum(row_scale[:, None, None, :] * kernel, axis=3)  38.4 us
    all_to_all x1, blocking collectives, gather_halves(): lax.all_to_all(jnp.broadcast_to(mine, (n,) + mine.shape), 'seq', 0, 0, ti...  34.5 us
    while x16, local copies, waits for them, and re-layouts  22.4 us
    dot_general x1, matrix products, body_local(): jnp.einsum('bkjp,bip->bkji', beside(t_unit), s_unit, preferred_element_ty...  11.6 us
    dot_general x1, matrix products, body_local(): lax.dot_general(sides, near_rows, along_j, preferred_element_type=jnp.flo...  10.7 us
    reduce_sum x4, other arithmetic, iterate(): row_scale = 1.0 / jnp.sum(kernel * col_scale[:, :, :, None], axis=(1, 2))  8.94 us
    ppermute x2, starting transfers between devices, shifted(): return lax.ppermute(block, axis, route)  6.01 us
  transfers between devices with their start and end apart: 4, of which 2 were waited for; matrix products, arithmetic and copies ran while one was open for 30% of the time, Pallas kernels for 0%

profile of v18, /device:TPU:0, one launch (start us, length us, event | category | flops | bytes accessed | tf_op | source)
XLA Modules:
  0.0 238.8 jit_solution(9426896821671654076)
XLA Ops:
  0.0 0.0 copy-start
  0.0 1.6 copy-done
  1.6 1.9 fusion.34
  3.5 0.0 copy-start.7
  3.5 0.0 copy-start.8
  3.5 0.0 copy-start.9
  3.5 4.0 %fusion.35 = f32[512,128]{0,1:T(8,128)S(1)} fusion(bf16[512,4096]{1,0:T(8,128)(2,1)} %param.10, bf16[4096,128]{1,0:T(8,128)(2,1)} %param.12), kind=kOutput, calls=%fused_computation.99 | convolution fusion | flops 536870912 | bytes 5505024 | tf_op jit(solution)/shard_map/dot_general | solution.py:78
  7.6 0.5 collective-permute-start
  8.1 0.0 copy-done.7
  8.1 0.1 fusion.22
  8.2 0.1 copy.27
  8.4 0.1 broadcast_in_dim.14
  8.5 0.1 pad.31.clone
  8.6 1.0 collective-permute-done
  9.6 0.1 fusion.27
  9.7 0.1 multiply_reduce_fusion.2
  9.8 0.1 multiply_convert_fusion
  9.8 0.2 fusion.19
  10.1 0.1 copy.29
  10.2 0.1 broadcast_in_dim.11
  10.3 34.5 %all_to_all.5 = bf16[8,528,128]{2,1,0:T(8,128)(2,1)S(1)} all-to-all(bf16[8,528,128]{2,1,0:T(8,128)(2,1)S(1)} %broadcast_in_dim.11), channel_id=1, replica_groups=mesh['groups'=2,'seq'=8,'tgrp'=2] {'seq'}, dimensions={0} | all-to-all | bytes 2162688 | tf_op jit(solution)/shard_map/all_to_all | solution.py:62
  44.8 0.0 collective-permute-start.1
  44.8 4.5 %collective-permute-start.2 = (bf16[512,4096]{1,0:T(8,128)(2,1)}, bf16[512,4096]{1,0:T(8,128)(2,1)}, u32[]{:S(2)}, u32[]{:S(2)}) collective-permute-start(bf16[512,4096]{1,0:T(8,128)(2,1)} %param.10), channel_id=1, source_target_pairs={{0,2},{2,4},{4,6},{6,8},{8,10},{10,12},{12,14},{1,3},{3,5},{5,7},{... | collective-permute-start | bytes 12582920 | tf_op jit(solution)/shard_map/ppermute | solution.py:18
  49.4 1.5 collective-permute-start.3
  50.9 0.1 pad.17.clone
  51.0 0.0 collective-permute-done.1
  51.0 1.7 broadcast_select_fusion.1
  52.7 1.2 fusion.30
  53.9 1.0 slice_bitcast_fusion.2
  55.0 0.1 reshape.378
  55.0 0.0 copy-start.6
  55.0 0.1 slice_add_fusion
  55.2 1.4 pad_bitcast_fusion.2
  56.6 0.1 pad_bitcast_fusion.3
  56.8 0.1 fusion.33
  56.9 0.1 pad_maximum_fusion.6
  57.0 11.6 %exponential_multiply_fusion = f32[8,3,512,512]{3,2,1,0:T(8,128)} fusion(f32[8,3]{1,0:T(8,128)S(1)} %pad_maximum_fusion.6, f32[8,3,512]{2,1,0:T(4,128)S(1)} %copy.33, f32[8,512]{1,0:T(8,128)S(1)} %bitcast.91, bf16[8,528,128]{2,1,0:T(8,128)(2,1)S(1)} %get-tuple-element.61, bf16[8,1,512,128]{3,2,0,1:T(8,128)(2,1)S(1)} %pad_bitcast_fusion.2, ...), kind=kOutput, calls=%fused_computation.13 | convolution fusion | flops 1651507200 | bytes 29446144 | tf_op jit(solution)/shard_map/bkjp,bip->bkji/dot_general | solution.py:106
  68.5 70.8 %while.13 = (s32[]{:T(128)}, f32[8,512]{1,0:T(8,128)S(1)}, f32[8,3,512]{2,0,1:T(8,128)}, f32[8,3,512,512]{3,2,1,0:T(8,128)}, s32[]{:T(128)}, /*index=5*/s32[]{:T(128)}) while((s32[]{:T(128)}, f32[8,512]{1,0:T(8,128)S(1)}, f32[8,3,512]{2,0,1:T(8,128)}, f32[8,3,512,512]{3,2,1,0:T(8,128)}, s32[]{:T(128)}, /*index=5*/s32[]{:T(128)}) %tuple.42), condition=%wide.region_5.6_spmd.clone, body=%wide.region_2.5_spmd.clone.sunk | while | flops 25194500 | bytes 151912576 | solution.py:125
  68.5 9.6 %multiply_reduce_fusion.6 = f32[8,3,512]{2,1,0:T(4,128)S(1)} fusion(f32[8,3,512,512]{3,2,1,0:T(8,128)} %get-tuple-element.128, f32[8,512]{1,0:T(8,128)S(1)} %broadcast_select_fusion.4), kind=kLoop, calls=%fused_computation.1.clone.1 | loop fusion | flops 12570624 | bytes 25231360 | tf_op jit(solution)/shard_map/while/body/eval_jaxpr/reduce_sum | solution.py:114
  78.3 0.0 copy-start.5
  78.3 5.6 %copy-done.2 = f32[8,3,512,512]{3,2,1,0:T(8,128)S(1)} copy-done((f32[8,3,512,512]{3,2,1,0:T(8,128)S(1)}, f32[8,3,512,512]{3,2,1,0:T(8,128)}, u32[]{:S(2)}) %copy-start.2) | copy-done | bytes 25165848 | tf_op jit(solution)/shard_map/while
  83.9 2.2 multiply_reduce_fusion.7
  86.2 0.0 copy-done.5
  86.3 9.6 %multiply_reduce_fusion.6 = f32[8,3,512]{2,1,0:T(4,128)S(1)} fusion(f32[8,3,512,512]{3,2,1,0:T(8,128)} %get-tuple-element.128, f32[8,512]{1,0:T(8,128)S(1)} %broadcast_select_fusion.4), kind=kLoop, calls=%fused_computation.1.clone.1 | loop fusion | flops 12570624 | bytes 25231360 | tf_op jit(solution)/shard_map/while/body/eval_jaxpr/reduce_sum | solution.py:114
  96.0 5.6 %copy-done.2 = f32[8,3,512,512]{3,2,1,0:T(8,128)S(1)} copy-done((f32[8,3,512,512]{3,2,1,0:T(8,128)S(1)}, f32[8,3,512,512]{3,2,1,0:T(8,128)}, u32[]{:S(2)}) %copy-start.2) | copy-done | bytes 25165848 | tf_op jit(solution)/shard_map/while
  101.6 2.2 multiply_reduce_fusion.7
  104.0 9.6 %multiply_reduce_fusion.6 = f32[8,3,512]{2,1,0:T(4,128)S(1)} fusion(f32[8,3,512,512]{3,2,1,0:T(8,128)} %get-tuple-element.128, f32[8,512]{1,0:T(8,128)S(1)} %broadcast_select_fusion.4), kind=kLoop, calls=%fused_computation.1.clone.1 | loop fusion | flops 12570624 | bytes 25231360 | tf_op jit(solution)/shard_map/while/body/eval_jaxpr/reduce_sum | solution.py:114
  113.8 5.6 %copy-done.2 = f32[8,3,512,512]{3,2,1,0:T(8,128)S(1)} copy-done((f32[8,3,512,512]{3,2,1,0:T(8,128)S(1)}, f32[8,3,512,512]{3,2,1,0:T(8,128)}, u32[]{:S(2)}) %copy-start.2) | copy-done | bytes 25165848 | tf_op jit(solution)/shard_map/while
  119.4 2.2 multiply_reduce_fusion.7
  121.6 0.0 copy-start.2
  121.7 9.6 %multiply_reduce_fusion.6 = f32[8,3,512]{2,1,0:T(4,128)S(1)} fusion(f32[8,3,512,512]{3,2,1,0:T(8,128)} %get-tuple-element.128, f32[8,512]{1,0:T(8,128)S(1)} %broadcast_select_fusion.4), kind=kLoop, calls=%fused_computation.1.clone.1 | loop fusion | flops 12570624 | bytes 25231360 | tf_op jit(solution)/shard_map/while/body/eval_jaxpr/reduce_sum | solution.py:114
  131.4 0.0 copy-start.5
  131.5 5.6 %copy-done.2 = f32[8,3,512,512]{3,2,1,0:T(8,128)S(1)} copy-done((f32[8,3,512,512]{3,2,1,0:T(8,128)S(1)}, f32[8,3,512,512]{3,2,1,0:T(8,128)}, u32[]{:S(2)}) %copy-start.2) | copy-done | bytes 25165848 | tf_op jit(solution)/shard_map/while
  137.1 2.2 multiply_reduce_fusion.7
  139.3 0.0 copy-start.3
  139.3 1.0 constant_dynamic-slice_fusion
  140.3 2.5 %fusion.10 = bf16[3,512,512]{2,1,0:T(8,128)(2,1)S(1)} fusion(f32[8,3,512,512]{3,2,1,0:T(8,128)} %get-tuple-element.131, s32[]{:T(128)S(6)} %select_n.78, f32[3,512]{1,0:T(4,128)S(1)} %bitcast.89, f32[512]{0:T(512)S(1)} %bitcast.92), kind=kLoop, calls=%fused_computation.22 | loop fusion | flops 2359296 | bytes 4726788 | tf_op jit(solution)/shard_map/convert_element_type | solution.py:134
  142.8 0.9 slice_bitcast_fusion.4
  143.7 0.0 copy-done.3
  143.7 2.4 %fusion.15 = f32[512,4096]{1,0:T(8,128)S(1)} fusion(bf16[512,4096]{1,0:T(8,128)(2,1)S(1)} %copy-done.3, bf16[3,512,512]{2,1,0:T(8,128)(2,1)S(1)} %fusion.10), kind=kOutput, calls=%fused_computation.36 | convolution fusion | flops 2147483648 | bytes 13107200 | tf_op jit(solution)/shard_map/dot_general | solution.py:136
  146.1 82.0 %collective-permute-done.2 = bf16[512,4096]{1,0:T(8,128)(2,1)} collective-permute-done((bf16[512,4096]{1,0:T(8,128)(2,1)}, bf16[512,4096]{1,0:T(8,128)(2,1)}, u32[]{:S(2)}, u32[]{:S(2)}) %collective-permute-start.2) | collective-permute-done | bytes 4194336 | tf_op jit(solution)/shard_map/ppermute | solution.py:18
  228.1 0.0 collective-permute-done.3
  228.1 10.7 %add_convert_fusion = bf16[512,4096]{1,0:T(8,128)(2,1)} fusion(f32[512,4096]{1,0:T(8,128)S(1)} %fusion.15, bf16[512,4096]{1,0:T(8,128)(2,1)} %collective-permute-done.3, bf16[512,4096]{1,0:T(8,128)(2,1)} %collective-permute-done.2, bf16[512,512]{1,0:T(8,128)(2,1)} %get-tuple-element.64, bf16[512,512]{1,0:T(8,128)(2,1)S(1)} %get-tuple-element.63), kind=kOutput, calls=%fused_computation.18 | convolution fusion | flops 4318035968 | bytes 22020096 | tf_op jit(solution)/shard_map/dot_general | solution.py:139
  238.8 0.0 copy-done.1
  (84 shorter events, 0.9 us)
Async XLA Ops:
  0.0 1.6 copy-start
  3.5 4.6 %copy-start.7 = (s32[512]{0:T(512)S(1)}, s32[512]{0:T(512)}, u32[]{:S(2)}) copy-start(s32[512]{0:T(512)} %param.14) | copy-start | bytes 6148
  3.5 4.6 %copy-start.8 = (s32[512]{0:T(512)S(1)}, s32[512]{0:T(512)}, u32[]{:S(2)}) copy-start(s32[512]{0:T(512)} %param.13) | copy-start | bytes 6148
  3.5 4.9 %copy-start.9 = (s32[1,2]{1,0:T(1,128)S(1)}, s32[1,2]{1,0:T(1,128)}, u32[]{:S(2)}) copy-start(s32[1,2]{1,0:T(1,128)} %param.15) | copy-start | bytes 28
  7.6 2.1 collective-permute-start
  44.8 6.1 %copy-start.4 = (bf16[8,528,128]{2,1,0:T(8,128)(2,1)}, bf16[8,528,128]{2,1,0:T(8,128)(2,1)S(1)}, u32[]{:S(2)}) copy-start(bf16[8,528,128]{2,1,0:T(8,128)(2,1)S(1)} %all_to_all.5) | copy-start | bytes 3244036
  44.8 6.1 %collective-permute-start.1 = (bf16[8,528,128]{2,1,0:T(8,128)(2,1)S(1)}, bf16[8,528,128]{2,1,0:T(8,128)(2,1)}, u32[]{:S(2)}, u32[]{:S(2)}) collective-permute-start(bf16[8,528,128]{2,1,0:T(8,128)(2,1)S(1)} %all_to_all.5), channel_id=1, source_target_pairs={{0,1},{1,0},{2,3},{3,2},{4,5},{5,4},{6,7},{7,6},{8,9},{9,8},{10,11... | collective-permute-start | bytes 3244040 | tf_op jit(solution)/shard_map/ppermute | solution.py:63
  44.8 183.3 %collective-permute-start.2 = (bf16[512,4096]{1,0:T(8,128)(2,1)}, bf16[512,4096]{1,0:T(8,128)(2,1)}, u32[]{:S(2)}, u32[]{:S(2)}) collective-permute-start(bf16[512,4096]{1,0:T(8,128)(2,1)} %param.10), channel_id=1, source_target_pairs={{0,2},{2,4},{4,6},{6,8},{8,10},{10,12},{12,14},{1,3},{3,5},{5,7},{... | collective-permute-start | bytes 12582920 | tf_op jit(solution)/shard_map/ppermute | solution.py:18
  49.4 178.7 %collective-permute-start.3 = (bf16[512,4096]{1,0:T(8,128)(2,1)}, bf16[512,4096]{1,0:T(8,128)(2,1)}, u32[]{:S(2)}, u32[]{:S(2)}) collective-permute-start(bf16[512,4096]{1,0:T(8,128)(2,1)} %param.10), channel_id=1, source_target_pairs={{2,0},{4,2},{6,4},{8,6},{10,8},{12,10},{14,12},{3,1},{5,3},{7,5},{... | collective-permute-start | bytes 12582920 | tf_op jit(solution)/shard_map/ppermute | solution.py:18
  55.0 2.0 copy-start.6
  68.5 15.4 %copy-start.2 = (f32[8,3,512,512]{3,2,1,0:T(8,128)S(1)}, f32[8,3,512,512]{3,2,1,0:T(8,128)}, u32[]{:S(2)}) copy-start(f32[8,3,512,512]{3,2,1,0:T(8,128)} %get-tuple-element.128) | copy-start | bytes 75497472 | tf_op jit(solution)/shard_map/while
  78.3 7.9 %copy-start.5 = (f32[8,3,512]{2,0,1:T(8,128)}, f32[8,3,512]{2,0,1:T(8,128)S(1)}, u32[]{:S(2)}) copy-start(f32[8,3,512]{2,0,1:T(8,128)S(1)} %pad_maximum_fusion.10) | copy-start | bytes 147460 | tf_op jit(solution)/shard_map/while
  86.2 15.4 %copy-start.2 = (f32[8,3,512,512]{3,2,1,0:T(8,128)S(1)}, f32[8,3,512,512]{3,2,1,0:T(8,128)}, u32[]{:S(2)}) copy-start(f32[8,3,512,512]{3,2,1,0:T(8,128)} %get-tuple-element.128) | copy-start | bytes 75497472 | tf_op jit(solution)/shard_map/while
  96.0 7.9 %copy-start.5 = (f32[8,3,512]{2,0,1:T(8,128)}, f32[8,3,512]{2,0,1:T(8,128)S(1)}, u32[]{:S(2)}) copy-start(f32[8,3,512]{2,0,1:T(8,128)S(1)} %pad_maximum_fusion.10) | copy-start | bytes 147460 | tf_op jit(solution)/shard_map/while
  103.9 15.4 %copy-start.2 = (f32[8,3,512,512]{3,2,1,0:T(8,128)S(1)}, f32[8,3,512,512]{3,2,1,0:T(8,128)}, u32[]{:S(2)}) copy-start(f32[8,3,512,512]{3,2,1,0:T(8,128)} %get-tuple-element.128) | copy-start | bytes 75497472 | tf_op jit(solution)/shard_map/while
  113.7 7.9 %copy-start.5 = (f32[8,3,512]{2,0,1:T(8,128)}, f32[8,3,512]{2,0,1:T(8,128)S(1)}, u32[]{:S(2)}) copy-start(f32[8,3,512]{2,0,1:T(8,128)S(1)} %pad_maximum_fusion.10) | copy-start | bytes 147460 | tf_op jit(solution)/shard_map/while
  121.6 15.4 %copy-start.2 = (f32[8,3,512,512]{3,2,1,0:T(8,128)S(1)}, f32[8,3,512,512]{3,2,1,0:T(8,128)}, u32[]{:S(2)}) copy-start(f32[8,3,512,512]{3,2,1,0:T(8,128)} %get-tuple-element.128) | copy-start | bytes 75497472 | tf_op jit(solution)/shard_map/while
  131.4 7.9 %copy-start.5 = (f32[8,3,512]{2,0,1:T(8,128)}, f32[8,3,512]{2,0,1:T(8,128)S(1)}, u32[]{:S(2)}) copy-start(f32[8,3,512]{2,0,1:T(8,128)S(1)} %pad_maximum_fusion.10) | copy-start | bytes 147460 | tf_op jit(solution)/shard_map/while
  139.3 4.4 %copy-start.3 = (bf16[512,4096]{1,0:T(8,128)(2,1)S(1)}, bf16[512,4096]{1,0:T(8,128)(2,1)}, u32[]{:S(2)}) copy-start(bf16[512,4096]{1,0:T(8,128)(2,1)} %param.10) | copy-start | bytes 12582916
  228.1 10.7 %copy-start.1 = (bf16[512,2048]{1,0:T(8,128)(2,1)S(1)}, bf16[512,2048]{1,0:T(8,128)(2,1)}, u32[]{:S(2)}) copy-start(bf16[512,2048]{1,0:T(8,128)(2,1)} %param.9) | copy-start | bytes 6291460

commit v19 on v18

--- a/solution.py
+++ b/solution.py
@@ -76,10 +76,11 @@
 
     s_part = jnp.dot(student_hidden, student_proj, preferred_element_type=jnp.float32)
     t_part = jnp.dot(teacher_hidden, teacher_proj, preferred_element_type=jnp.float32)
-    feats = tgrp_sum(jnp.concatenate([s_part, t_part], 1))
-    units = jnp.concatenate(
-        [unit_rows(feats[:, :proj_width]), unit_rows(feats[:, proj_width:])], 1
-    )
+    first_core = lax.axis_index("tgrp") == 0
+    own_part = jnp.where(first_core, s_part, t_part)
+    their_part = jnp.where(first_core, t_part, s_part)
+    own_units = unit_rows(own_part + lax.ppermute(their_part, "tgrp", [(0, 1), (1, 0)]))
+    units = jnp.concatenate([own_units, own_units], 1)
     digits = jnp.stack([student_chars, teacher_chars])
     digits = jnp.stack([digits // 4096, digits // 64 % 64, digits % 64], 1)
     digit_rows = digits.reshape(-1, units.shape[1]).astype(jnp.bfloat16)

time: 240 us -> 239 us (level)
  no operation moved by 1% of the time
where the time goes in v19:
time: 239 us; the launch traced here: 238 us
  waiting for transfers between devices  84.1 us (35%)
  other arithmetic  52.2 us (22%)
  blocking collectives  34.5 us (14%)
  matrix products  30.6 us (13%)
  local copies, waits for them, and re-layouts  29.5 us (12%)
  starting transfers between devices  6.52 us (3%)
    ppermute x2, waiting for transfers between devices, shifted(): return lax.ppermute(block, axis, route)  83.5 us
    reduce_sum x4, other arithmetic, iterate(): partial_cols = jnp.sum(row_scale[:, None, None, :] * kernel, axis=3)  38.4 us
    all_to_all x1, blocking collectives, gather_halves(): lax.all_to_all(jnp.broadcast_to(mine, (n,) + mine.shape), 'seq', 0, 0, ti...  34.5 us
    while x16, local copies, waits for them, and re-layouts  22.4 us
    dot_general x1, matrix products, body_local(): jnp.einsum('bkjp,bip->bkji', beside(t_unit), s_unit, preferred_element_ty...  11.6 us
    dot_general x1, matrix products, body_local(): lax.dot_general(sides, near_rows, along_j, preferred_element_type=jnp.flo...  10.7 us
    reduce_sum x4, other arithmetic, iterate(): row_scale = 1.0 / jnp.sum(kernel * col_scale[:, :, :, None], axis=(1, 2))  8.94 us
    ppermute x2, starting transfers between devices, shifted(): return lax.ppermute(block, axis, route)  6 us
  transfers between devices with their start and end apart: 4, of which 2 were waited for; matrix products, arithmetic and copies ran while one was open for 30% of the time, Pallas kernels for 0%

profile of v19, /device:TPU:0, one launch (start us, length us, event | category | flops | bytes accessed | tf_op | source)
XLA Modules:
  0.0 238.3 jit_solution(16715784484941621226)
XLA Ops:
  0.0 0.0 copy-start
  0.0 1.6 copy-done
  1.6 1.9 fusion.33
  3.5 0.0 copy-start.7
  3.5 0.0 copy-start.8
  3.5 0.0 copy-start.9
  3.5 4.0 %broadcast_select_fusion.3 = (f32[512,128]{0,1:T(8,128)S(1)}, f32[512,128]{0,1:T(8,128)S(1)}) fusion(f32[512,128]{0,1:T(8,128)S(1)} %fusion.33, pred[]{:T(512)S(6)} %eq.8, bf16[512,4096]{1,0:T(8,128)(2,1)} %param.10, bf16[4096,128]{1,0:T(8,128)(2,1)} %param.12), kind=kOutput, calls=%fused_computation.48 | convolution fusion | flops 536936448 | bytes 6029313 | tf_op jit(solution)/shard_map/dot_general | solution.py:78
  7.5 0.5 collective-permute-start
  8.0 0.0 copy-done.7
  8.0 0.0 copy-done.8
  8.0 0.1 fusion.22
  8.2 0.1 copy.27
  8.3 0.0 copy-done.9
  8.3 0.1 broadcast_in_dim.14
  8.4 0.1 pad.31.clone
  8.5 0.7 collective-permute-done
  9.2 0.1 multiply_reduce_fusion.2
  9.3 0.2 fusion.19
  9.5 0.1 copy.29
  9.6 0.1 broadcast_in_dim.13
  9.8 34.5 %all_to_all.5 = bf16[8,528,128]{2,1,0:T(8,128)(2,1)S(1)} all-to-all(bf16[8,528,128]{2,1,0:T(8,128)(2,1)S(1)} %broadcast_in_dim.13), channel_id=1, replica_groups=mesh['groups'=2,'seq'=8,'tgrp'=2] {'seq'}, dimensions={0} | all-to-all | bytes 2162688 | tf_op jit(solution)/shard_map/all_to_all | solution.py:62
  44.3 0.0 collective-permute-start.1
  44.3 4.5 %collective-permute-start.2 = (bf16[512,4096]{1,0:T(8,128)(2,1)}, bf16[512,4096]{1,0:T(8,128)(2,1)}, u32[]{:S(2)}, u32[]{:S(2)}) collective-permute-start(bf16[512,4096]{1,0:T(8,128)(2,1)} %param.10), channel_id=1, source_target_pairs={{0,2},{2,4},{4,6},{6,8},{8,10},{10,12},{12,14},{1,3},{3,5},{5,7},{... | collective-permute-start | bytes 12582920 | tf_op jit(solution)/shard_map/ppermute | solution.py:18
  48.8 1.5 collective-permute-start.3
  50.3 0.1 pad.17.clone
  50.4 0.0 copy-done.4
  50.4 0.0 collective-permute-done.1
  50.4 1.7 broadcast_select_fusion.1
  52.1 1.2 fusion.29
  53.4 0.1 reshape.370
  53.4 0.0 copy-start.5
  53.5 0.1 slice_add_fusion
  53.6 0.1 slice_bitcast_fusion.2
  53.9 0.1 fusion.32
  53.9 0.7 copy-done.5
  54.6 0.2 pad_bitcast_fusion.2
  54.8 0.1 pad_maximum_fusion.5
  54.9 11.6 %exponential_multiply_fusion = f32[8,3,512,512]{3,2,1,0:T(8,128)} fusion(f32[8,3]{1,0:T(8,128)S(1)} %pad_maximum_fusion.5, f32[8,3,512]{2,1,0:T(4,128)S(1)} %copy.33, f32[8,512]{1,0:T(8,128)S(1)} %bitcast.87, bf16[8,528,128]{2,1,0:T(8,128)(2,1)S(1)} %get-tuple-element.61, bf16[8,1,512,128]{3,2,0,1:T(8,128)(2,1)S(1)} %get-tuple-element.78, ...), kind=kOutput, calls=%fused_computation.13 | convolution fusion | flops 1651507200 | bytes 29446144 | tf_op jit(solution)/shard_map/bkjp,bip->bkji/dot_general | solution.py:107
  66.5 70.8 %while.13 = (s32[]{:T(128)}, f32[8,512]{1,0:T(8,128)S(1)}, f32[8,3,512]{2,0,1:T(8,128)}, f32[8,3,512,512]{3,2,1,0:T(8,128)}, s32[]{:T(128)}, /*index=5*/s32[]{:T(128)}) while((s32[]{:T(128)}, f32[8,512]{1,0:T(8,128)S(1)}, f32[8,3,512]{2,0,1:T(8,128)}, f32[8,3,512,512]{3,2,1,0:T(8,128)}, s32[]{:T(128)}, /*index=5*/s32[]{:T(128)}) %tuple.43), condition=%wide.region_4.5_spmd.clone, body=%wide.region_1.4_spmd.clone.sunk | while | flops 25194500 | bytes 151912576 | solution.py:126
  66.5 9.6 %multiply_reduce_fusion.5 = f32[8,3,512]{2,1,0:T(4,128)S(1)} fusion(f32[8,3,512,512]{3,2,1,0:T(8,128)} %get-tuple-element.130, f32[8,512]{1,0:T(8,128)S(1)} %broadcast_select_fusion.5), kind=kLoop, calls=%fused_computation.1.clone.1 | loop fusion | flops 12570624 | bytes 25231360 | tf_op jit(solution)/shard_map/while/body/eval_jaxpr/reduce_sum | solution.py:115
  76.2 0.0 copy-start.6
  76.3 5.6 %copy-done.2 = f32[8,3,512,512]{3,2,1,0:T(8,128)S(1)} copy-done((f32[8,3,512,512]{3,2,1,0:T(8,128)S(1)}, f32[8,3,512,512]{3,2,1,0:T(8,128)}, u32[]{:S(2)}) %copy-start.2) | copy-done | bytes 25165848 | tf_op jit(solution)/shard_map/while
  81.9 2.2 multiply_reduce_fusion.6
  84.2 9.6 %multiply_reduce_fusion.5 = f32[8,3,512]{2,1,0:T(4,128)S(1)} fusion(f32[8,3,512,512]{3,2,1,0:T(8,128)} %get-tuple-element.130, f32[8,512]{1,0:T(8,128)S(1)} %broadcast_select_fusion.5), kind=kLoop, calls=%fused_computation.1.clone.1 | loop fusion | flops 12570624 | bytes 25231360 | tf_op jit(solution)/shard_map/while/body/eval_jaxpr/reduce_sum | solution.py:115
  94.0 5.6 %copy-done.2 = f32[8,3,512,512]{3,2,1,0:T(8,128)S(1)} copy-done((f32[8,3,512,512]{3,2,1,0:T(8,128)S(1)}, f32[8,3,512,512]{3,2,1,0:T(8,128)}, u32[]{:S(2)}) %copy-start.2) | copy-done | bytes 25165848 | tf_op jit(solution)/shard_map/while
  99.6 2.2 multiply_reduce_fusion.6
  101.9 0.0 copy-start.2
  101.9 9.6 %multiply_reduce_fusion.5 = f32[8,3,512]{2,1,0:T(4,128)S(1)} fusion(f32[8,3,512,512]{3,2,1,0:T(8,128)} %get-tuple-element.130, f32[8,512]{1,0:T(8,128)S(1)} %broadcast_select_fusion.5), kind=kLoop, calls=%fused_computation.1.clone.1 | loop fusion | flops 12570624 | bytes 25231360 | tf_op jit(solution)/shard_map/while/body/eval_jaxpr/reduce_sum | solution.py:115
  111.7 5.6 %copy-done.2 = f32[8,3,512,512]{3,2,1,0:T(8,128)S(1)} copy-done((f32[8,3,512,512]{3,2,1,0:T(8,128)S(1)}, f32[8,3,512,512]{3,2,1,0:T(8,128)}, u32[]{:S(2)}) %copy-start.2) | copy-done | bytes 25165848 | tf_op jit(solution)/shard_map/while
  117.3 2.2 multiply_reduce_fusion.6
  119.6 0.0 copy-start.2
  119.6 9.6 %multiply_reduce_fusion.5 = f32[8,3,512]{2,1,0:T(4,128)S(1)} fusion(f32[8,3,512,512]{3,2,1,0:T(8,128)} %get-tuple-element.130, f32[8,512]{1,0:T(8,128)S(1)} %broadcast_select_fusion.5), kind=kLoop, calls=%fused_computation.1.clone.1 | loop fusion | flops 12570624 | bytes 25231360 | tf_op jit(solution)/shard_map/while/body/eval_jaxpr/reduce_sum | solution.py:115
  129.4 0.0 copy-start.6
  129.4 5.6 %copy-done.2 = f32[8,3,512,512]{3,2,1,0:T(8,128)S(1)} copy-done((f32[8,3,512,512]{3,2,1,0:T(8,128)S(1)}, f32[8,3,512,512]{3,2,1,0:T(8,128)}, u32[]{:S(2)}) %copy-start.2) | copy-done | bytes 25165848 | tf_op jit(solution)/shard_map/while
  135.0 2.2 multiply_reduce_fusion.6
  137.3 0.0 copy-start.3
  137.3 1.0 constant_dynamic-slice_fusion
  138.3 2.5 %fusion.10 = bf16[3,512,512]{2,1,0:T(8,128)(2,1)S(1)} fusion(f32[8,3,512,512]{3,2,1,0:T(8,128)} %get-tuple-element.133, s32[]{:T(128)S(6)} %select_n.93, f32[3,512]{1,0:T(4,128)S(1)} %bitcast.85, f32[512]{0:T(512)S(1)} %bitcast.88), kind=kLoop, calls=%fused_computation.22 | loop fusion | flops 2359296 | bytes 4726788 | tf_op jit(solution)/shard_map/convert_element_type | solution.py:135
  140.8 0.9 slice_bitcast_fusion.4
  141.7 0.0 copy-done.3
  141.7 2.4 %fusion.15 = f32[512,4096]{1,0:T(8,128)S(1)} fusion(bf16[512,4096]{1,0:T(8,128)(2,1)S(1)} %copy-done.3, bf16[3,512,512]{2,1,0:T(8,128)(2,1)S(1)} %fusion.10), kind=kOutput, calls=%fused_computation.36 | convolution fusion | flops 2147483648 | bytes 13107200 | tf_op jit(solution)/shard_map/dot_general | solution.py:137
  144.1 83.5 %collective-permute-done.2 = bf16[512,4096]{1,0:T(8,128)(2,1)} collective-permute-done((bf16[512,4096]{1,0:T(8,128)(2,1)}, bf16[512,4096]{1,0:T(8,128)(2,1)}, u32[]{:S(2)}, u32[]{:S(2)}) %collective-permute-start.2) | collective-permute-done | bytes 4194336 | tf_op jit(solution)/shard_map/ppermute | solution.py:18
  227.6 0.0 collective-permute-done.3
  227.6 10.7 %add_convert_fusion = bf16[512,4096]{1,0:T(8,128)(2,1)} fusion(f32[512,4096]{1,0:T(8,128)S(1)} %fusion.15, bf16[512,4096]{1,0:T(8,128)(2,1)} %collective-permute-done.3, bf16[512,4096]{1,0:T(8,128)(2,1)} %collective-permute-done.2, bf16[512,512]{1,0:T(8,128)(2,1)} %get-tuple-element.64, bf16[512,512]{1,0:T(8,128)(2,1)S(1)} %get-tuple-element.63), kind=kOutput, calls=%fused_computation.18 | convolution fusion | flops 4318035968 | bytes 22020096 | tf_op jit(solution)/shard_map/dot_general | solution.py:140
  (80 shorter events, 0.8 us)
Async XLA Ops:
  0.0 1.6 copy-start
  3.5 4.6 %copy-start.7 = (s32[512]{0:T(512)S(1)}, s32[512]{0:T(512)}, u32[]{:S(2)}) copy-start(s32[512]{0:T(512)} %param.14) | copy-start | bytes 6148
  3.5 4.5 %copy-start.8 = (s32[512]{0:T(512)S(1)}, s32[512]{0:T(512)}, u32[]{:S(2)}) copy-start(s32[512]{0:T(512)} %param.13) | copy-start | bytes 6148
  3.5 4.8 %copy-start.9 = (s32[1,2]{1,0:T(1,128)S(1)}, s32[1,2]{1,0:T(1,128)}, u32[]{:S(2)}) copy-start(s32[1,2]{1,0:T(1,128)} %param.15) | copy-start | bytes 28
  7.5 1.7 collective-permute-start
  44.3 6.1 %copy-start.4 = (bf16[8,528,128]{2,1,0:T(8,128)(2,1)}, bf16[8,528,128]{2,1,0:T(8,128)(2,1)S(1)}, u32[]{:S(2)}) copy-start(bf16[8,528,128]{2,1,0:T(8,128)(2,1)S(1)} %all_to_all.5) | copy-start | bytes 3244036
  44.3 6.1 %collective-permute-start.1 = (bf16[8,528,128]{2,1,0:T(8,128)(2,1)S(1)}, bf16[8,528,128]{2,1,0:T(8,128)(2,1)}, u32[]{:S(2)}, u32[]{:S(2)}) collective-permute-start(bf16[8,528,128]{2,1,0:T(8,128)(2,1)S(1)} %all_to_all.5), channel_id=1, source_target_pairs={{0,1},{1,0},{2,3},{3,2},{4,5},{5,4},{6,7},{7,6},{8,9},{9,8},{10,11... | collective-permute-start | bytes 3244040 | tf_op jit(solution)/shard_map/ppermute | solution.py:63
  44.3 183.3 %collective-permute-start.2 = (bf16[512,4096]{1,0:T(8,128)(2,1)}, bf16[512,4096]{1,0:T(8,128)(2,1)}, u32[]{:S(2)}, u32[]{:S(2)}) collective-permute-start(bf16[512,4096]{1,0:T(8,128)(2,1)} %param.10), channel_id=1, source_target_pairs={{0,2},{2,4},{4,6},{6,8},{8,10},{10,12},{12,14},{1,3},{3,5},{5,7},{... | collective-permute-start | bytes 12582920 | tf_op jit(solution)/shard_map/ppermute | solution.py:18
  48.8 178.7 %collective-permute-start.3 = (bf16[512,4096]{1,0:T(8,128)(2,1)}, bf16[512,4096]{1,0:T(8,128)(2,1)}, u32[]{:S(2)}, u32[]{:S(2)}) collective-permute-start(bf16[512,4096]{1,0:T(8,128)(2,1)} %param.10), channel_id=1, source_target_pairs={{2,0},{4,2},{6,4},{8,6},{10,8},{12,10},{14,12},{3,1},{5,3},{7,5},{... | collective-permute-start | bytes 12582920 | tf_op jit(solution)/shard_map/ppermute | solution.py:18
  53.4 1.2 copy-start.5
  66.5 15.4 %copy-start.2 = (f32[8,3,512,512]{3,2,1,0:T(8,128)S(1)}, f32[8,3,512,512]{3,2,1,0:T(8,128)}, u32[]{:S(2)}) copy-start(f32[8,3,512,512]{3,2,1,0:T(8,128)} %get-tuple-element.130) | copy-start | bytes 75497472 | tf_op jit(solution)/shard_map/while
  76.2 7.9 %copy-start.6 = (f32[8,3,512]{2,0,1:T(8,128)}, f32[8,3,512]{2,0,1:T(8,128)S(1)}, u32[]{:S(2)}) copy-start(f32[8,3,512]{2,0,1:T(8,128)S(1)} %pad_maximum_fusion.9) | copy-start | bytes 147460 | tf_op jit(solution)/shard_map/while
  84.2 15.4 %copy-start.2 = (f32[8,3,512,512]{3,2,1,0:T(8,128)S(1)}, f32[8,3,512,512]{3,2,1,0:T(8,128)}, u32[]{:S(2)}) copy-start(f32[8,3,512,512]{3,2,1,0:T(8,128)} %get-tuple-element.130) | copy-start | bytes 75497472 | tf_op jit(solution)/shard_map/while
  94.0 7.9 %copy-start.6 = (f32[8,3,512]{2,0,1:T(8,128)}, f32[8,3,512]{2,0,1:T(8,128)S(1)}, u32[]{:S(2)}) copy-start(f32[8,3,512]{2,0,1:T(8,128)S(1)} %pad_maximum_fusion.9) | copy-start | bytes 147460 | tf_op jit(solution)/shard_map/while
  101.9 15.4 %copy-start.2 = (f32[8,3,512,512]{3,2,1,0:T(8,128)S(1)}, f32[8,3,512,512]{3,2,1,0:T(8,128)}, u32[]{:S(2)}) copy-start(f32[8,3,512,512]{3,2,1,0:T(8,128)} %get-tuple-element.130) | copy-start | bytes 75497472 | tf_op jit(solution)/shard_map/while
  111.7 7.9 %copy-start.6 = (f32[8,3,512]{2,0,1:T(8,128)}, f32[8,3,512]{2,0,1:T(8,128)S(1)}, u32[]{:S(2)}) copy-start(f32[8,3,512]{2,0,1:T(8,128)S(1)} %pad_maximum_fusion.9) | copy-start | bytes 147460 | tf_op jit(solution)/shard_map/while
  119.6 15.4 %copy-start.2 = (f32[8,3,512,512]{3,2,1,0:T(8,128)S(1)}, f32[8,3,512,512]{3,2,1,0:T(8,128)}, u32[]{:S(2)}) copy-start(f32[8,3,512,512]{3,2,1,0:T(8,128)} %get-tuple-element.130) | copy-start | bytes 75497472 | tf_op jit(solution)/shard_map/while
  129.4 7.9 %copy-start.6 = (f32[8,3,512]{2,0,1:T(8,128)}, f32[8,3,512]{2,0,1:T(8,128)S(1)}, u32[]{:S(2)}) copy-start(f32[8,3,512]{2,0,1:T(8,128)S(1)} %pad_maximum_fusion.9) | copy-start | bytes 147460 | tf_op jit(solution)/shard_map/while
  137.3 4.4 %copy-start.3 = (bf16[512,4096]{1,0:T(8,128)(2,1)S(1)}, bf16[512,4096]{1,0:T(8,128)(2,1)}, u32[]{:S(2)}) copy-start(bf16[512,4096]{1,0:T(8,128)(2,1)} %param.10) | copy-start | bytes 12582916
  227.6 10.7 %copy-start.1 = (bf16[512,2048]{1,0:T(8,128)(2,1)S(1)}, bf16[512,2048]{1,0:T(8,128)(2,1)}, u32[]{:S(2)}) copy-start(bf16[512,2048]{1,0:T(8,128)(2,1)} %param.9) | copy-start | bytes 6291460

commit v20 on v19

--- a/solution.py
+++ b/solution.py
@@ -74,8 +74,9 @@
     blocks = lax.axis_size("seq")
     me = lax.axis_index("seq")
 
-    s_part = jnp.dot(student_hidden, student_proj, preferred_element_type=jnp.float32)
     t_part = jnp.dot(teacher_hidden, teacher_proj, preferred_element_type=jnp.float32)
+    student_rows, t_part = lax.optimization_barrier((student_hidden, t_part))
+    s_part = jnp.dot(student_rows, student_proj, preferred_element_type=jnp.float32)
     first_core = lax.axis_index("tgrp") == 0
     own_part = jnp.where(first_core, s_part, t_part)
     their_part = jnp.where(first_core, t_part, s_part)

time: 239 us -> 236 us (0.987)
  waiting for transfers between devices: 84.1 us -> 81.1 us
    ppermute x2, waiting for transfers between devices: 83.5 us -> 80.3 us  [shifted(): return lax.ppermute(block, axis, route)]
  transfers between devices with their start and end apart: 4 -> 4, of which waited for: 2 -> 2; matrix products, arithmetic and copies ran while one was open for 30% -> 31% of each run, Pallas kernels for 0% -> 0%
where the time goes in v20:
time: 236 us; the launch traced here: 235 us
  waiting for transfers between devices  81.1 us (34%)
  other arithmetic  52.1 us (22%)
  blocking collectives  34.5 us (15%)
  matrix products  31.5 us (13%)
  local copies, waits for them, and re-layouts  28.8 us (12%)
  starting transfers between devices  6.54 us (3%)
    ppermute x2, waiting for transfers between devices, shifted(): return lax.ppermute(block, axis, route)  80.3 us
    reduce_sum x4, other arithmetic, iterate(): partial_cols = jnp.sum(row_scale[:, None, None, :] * kernel, axis=3)  38.4 us
    all_to_all x1, blocking collectives, gather_halves(): lax.all_to_all(jnp.broadcast_to(mine, (n,) + mine.shape), 'seq', 0, 0, ti...  34.5 us
    while x16, local copies, waits for them, and re-layouts  22.4 us
    dot_general x1, matrix products, body_local(): jnp.einsum('bkjp,bip->bkji', beside(t_unit), s_unit, preferred_element_ty...  11.6 us
    dot_general x1, matrix products, body_local(): lax.dot_general(sides, near_rows, along_j, preferred_element_type=jnp.flo...  10.7 us
    reduce_sum x4, other arithmetic, iterate(): row_scale = 1.0 / jnp.sum(kernel * col_scale[:, :, :, None], axis=(1, 2))  8.94 us
    ppermute x2, starting transfers between devices, shifted(): return lax.ppermute(block, axis, route)  6 us
  transfers between devices with their start and end apart: 4, of which 2 were waited for; matrix products, arithmetic and copies ran while one was open for 31% of the time, Pallas kernels for 0%

profile of v20, /device:TPU:0, one launch (start us, length us, event | category | flops | bytes accessed | tf_op | source)
XLA Modules:
  0.0 235.4 jit_solution(1066819716038702231)
XLA Ops:
  0.0 0.0 copy-start
  0.0 0.0 copy-start.9
  0.0 3.9 %fusion.33 = f32[512,128]{1,0:T(8,128)S(1)} fusion(bf16[512,4096]{1,0:T(8,128)(2,1)} %param.10, bf16[4096,128]{1,0:T(8,128)(2,1)} %param.12), kind=kOutput, calls=%fused_computation.95 | convolution fusion | flops 536870912 | bytes 5505024 | tf_op jit(solution)/shard_map/dot_general | solution.py:77
  3.9 0.0 copy-done
  3.9 0.0 copy-done.6
  3.9 0.7 broadcast_select_fusion.3
  4.7 0.5 collective-permute-start
  5.2 0.0 copy-done.7
  5.2 0.0 copy-done.8
  5.2 0.1 fusion.22
  5.3 0.0 copy-done.9
  5.4 0.1 pad.31.clone
  5.5 0.9 collective-permute-done
  6.3 0.1 multiply_reduce_fusion.2
  6.5 0.1 multiply_convert_fusion
  6.7 0.1 fusion.19
  6.8 0.1 broadcast_in_dim.13
  7.0 34.5 %all_to_all.5 = bf16[8,528,128]{2,1,0:T(8,128)(2,1)S(1)} all-to-all(bf16[8,528,128]{2,1,0:T(8,128)(2,1)S(1)} %broadcast_in_dim.13), channel_id=1, replica_groups=mesh['groups'=2,'seq'=8,'tgrp'=2] {'seq'}, dimensions={0} | all-to-all | bytes 2162688 | tf_op jit(solution)/shard_map/all_to_all | solution.py:62
  41.4 0.0 collective-permute-start.1
  41.4 4.5 %collective-permute-start.2 = (bf16[512,4096]{1,0:T(8,128)(2,1)}, bf16[512,4096]{1,0:T(8,128)(2,1)}, u32[]{:S(2)}, u32[]{:S(2)}) collective-permute-start(bf16[512,4096]{1,0:T(8,128)(2,1)} %param.10), channel_id=1, source_target_pairs={{0,2},{2,4},{4,6},{6,8},{8,10},{10,12},{12,14},{1,3},{3,5},{5,7},{... | collective-permute-start | bytes 12582920 | tf_op jit(solution)/shard_map/ppermute | solution.py:18
  46.0 1.5 collective-permute-start.3
  47.5 0.1 pad.17.clone
  47.6 0.0 copy-done.3
  47.6 0.0 collective-permute-done.1
  47.6 1.7 broadcast_select_fusion.1
  49.3 1.3 fusion.29
  50.5 1.0 slice_bitcast_fusion.2
  51.6 0.1 reshape.370
  51.6 0.0 copy-start.5
  51.7 0.1 slice_add_fusion
  52.0 0.1 fusion.32
  52.0 1.4 pad_bitcast_fusion.2
  53.4 0.1 pad_maximum_fusion.5
  53.5 0.0 copy-done.5
  53.5 11.6 %exponential_multiply_fusion = f32[8,3,512,512]{3,2,1,0:T(8,128)} fusion(f32[8,3]{1,0:T(8,128)S(1)} %pad_maximum_fusion.5, f32[8,3,512]{2,1,0:T(4,128)S(1)} %copy.32, f32[8,512]{1,0:T(8,128)S(1)} %bitcast.87, bf16[8,528,128]{2,1,0:T(8,128)(2,1)S(1)} %get-tuple-element.65, bf16[8,1,512,128]{3,2,0,1:T(8,128)(2,1)S(1)} %get-tuple-element.82, ...), kind=kOutput, calls=%fused_computation.13 | convolution fusion | flops 1651507200 | bytes 29446144 | tf_op jit(solution)/shard_map/bkjp,bip->bkji/dot_general | solution.py:108
  65.1 70.8 %while.13 = (s32[]{:T(128)}, f32[8,512]{1,0:T(8,128)S(1)}, f32[8,3,512]{2,0,1:T(8,128)}, f32[8,3,512,512]{3,2,1,0:T(8,128)}, s32[]{:T(128)}, /*index=5*/s32[]{:T(128)}) while((s32[]{:T(128)}, f32[8,512]{1,0:T(8,128)S(1)}, f32[8,3,512]{2,0,1:T(8,128)}, f32[8,3,512,512]{3,2,1,0:T(8,128)}, s32[]{:T(128)}, /*index=5*/s32[]{:T(128)}) %tuple.45), condition=%wide.region_4.5_spmd.clone, body=%wide.region_1.4_spmd.clone.sunk | while | flops 25194500 | bytes 151912576 | solution.py:127
  65.1 9.6 %multiply_reduce_fusion.5 = f32[8,3,512]{2,1,0:T(4,128)S(1)} fusion(f32[8,3,512,512]{3,2,1,0:T(8,128)} %get-tuple-element.134, f32[8,512]{1,0:T(8,128)S(1)} %broadcast_select_fusion.5), kind=kLoop, calls=%fused_computation.1.clone.1 | loop fusion | flops 12570624 | bytes 25231360 | tf_op jit(solution)/shard_map/while/body/eval_jaxpr/reduce_sum | solution.py:116
  74.8 0.0 copy-start.4
  74.9 5.6 %copy-done.2 = f32[8,3,512,512]{3,2,1,0:T(8,128)S(1)} copy-done((f32[8,3,512,512]{3,2,1,0:T(8,128)S(1)}, f32[8,3,512,512]{3,2,1,0:T(8,128)}, u32[]{:S(2)}) %copy-start.2) | copy-done | bytes 25165848 | tf_op jit(solution)/shard_map/while
  80.5 2.2 multiply_reduce_fusion.6
  82.7 0.0 copy-done.4
  82.8 0.0 copy-start.2
  82.8 9.6 %multiply_reduce_fusion.5 = f32[8,3,512]{2,1,0:T(4,128)S(1)} fusion(f32[8,3,512,512]{3,2,1,0:T(8,128)} %get-tuple-element.134, f32[8,512]{1,0:T(8,128)S(1)} %broadcast_select_fusion.5), kind=kLoop, calls=%fused_computation.1.clone.1 | loop fusion | flops 12570624 | bytes 25231360 | tf_op jit(solution)/shard_map/while/body/eval_jaxpr/reduce_sum | solution.py:116
  92.5 0.0 copy-start.4
  92.6 5.6 %copy-done.2 = f32[8,3,512,512]{3,2,1,0:T(8,128)S(1)} copy-done((f32[8,3,512,512]{3,2,1,0:T(8,128)S(1)}, f32[8,3,512,512]{3,2,1,0:T(8,128)}, u32[]{:S(2)}) %copy-start.2) | copy-done | bytes 25165848 | tf_op jit(solution)/shard_map/while
  98.2 2.2 multiply_reduce_fusion.6
  100.4 0.0 copy-done.4
  100.5 0.0 copy-start.2
  100.5 9.6 %multiply_reduce_fusion.5 = f32[8,3,512]{2,1,0:T(4,128)S(1)} fusion(f32[8,3,512,512]{3,2,1,0:T(8,128)} %get-tuple-element.134, f32[8,512]{1,0:T(8,128)S(1)} %broadcast_select_fusion.5), kind=kLoop, calls=%fused_computation.1.clone.1 | loop fusion | flops 12570624 | bytes 25231360 | tf_op jit(solution)/shard_map/while/body/eval_jaxpr/reduce_sum | solution.py:116
  110.3 0.0 copy-start.4
  110.3 5.6 %copy-done.2 = f32[8,3,512,512]{3,2,1,0:T(8,128)S(1)} copy-done((f32[8,3,512,512]{3,2,1,0:T(8,128)S(1)}, f32[8,3,512,512]{3,2,1,0:T(8,128)}, u32[]{:S(2)}) %copy-start.2) | copy-done | bytes 25165848 | tf_op jit(solution)/shard_map/while
  115.9 2.2 multiply_reduce_fusion.6
  118.1 0.0 copy-done.4
  118.2 9.6 %multiply_reduce_fusion.5 = f32[8,3,512]{2,1,0:T(4,128)S(1)} fusion(f32[8,3,512,512]{3,2,1,0:T(8,128)} %get-tuple-element.134, f32[8,512]{1,0:T(8,128)S(1)} %broadcast_select_fusion.5), kind=kLoop, calls=%fused_computation.1.clone.1 | loop fusion | flops 12570624 | bytes 25231360 | tf_op jit(solution)/shard_map/while/body/eval_jaxpr/reduce_sum | solution.py:116
  128.0 5.6 %copy-done.2 = f32[8,3,512,512]{3,2,1,0:T(8,128)S(1)} copy-done((f32[8,3,512,512]{3,2,1,0:T(8,128)S(1)}, f32[8,3,512,512]{3,2,1,0:T(8,128)}, u32[]{:S(2)}) %copy-start.2) | copy-done | bytes 25165848 | tf_op jit(solution)/shard_map/while
  133.6 2.2 multiply_reduce_fusion.6
  135.9 0.0 copy-done.4
  135.9 0.8 constant_dynamic-slice_fusion
  136.7 2.2 fusion.10
  139.0 0.9 slice_bitcast_fusion.4
  139.8 4.6 %fusion.15 = f32[512,4096]{1,0:T(8,128)S(1)} fusion(bf16[512,4096]{1,0:T(8,128)(2,1)} %param.10, bf16[3,512,512]{2,1,0:T(8,128)(2,1)S(1)} %fusion.10), kind=kOutput, calls=%fused_computation.36 | convolution fusion | flops 2147483648 | bytes 13107200 | tf_op jit(solution)/shard_map/dot_general | solution.py:138
  144.5 80.3 %collective-permute-done.2 = bf16[512,4096]{1,0:T(8,128)(2,1)} collective-permute-done((bf16[512,4096]{1,0:T(8,128)(2,1)}, bf16[512,4096]{1,0:T(8,128)(2,1)}, u32[]{:S(2)}, u32[]{:S(2)}) %collective-permute-start.2) | collective-permute-done | bytes 4194336 | tf_op jit(solution)/shard_map/ppermute | solution.py:18
  224.7 0.0 collective-permute-done.3
  224.7 10.7 %add_convert_fusion = bf16[512,4096]{1,0:T(8,128)(2,1)} fusion(f32[512,4096]{1,0:T(8,128)S(1)} %fusion.15, bf16[512,4096]{1,0:T(8,128)(2,1)} %collective-permute-done.3, bf16[512,4096]{1,0:T(8,128)(2,1)} %collective-permute-done.2, bf16[512,512]{1,0:T(8,128)(2,1)} %get-tuple-element.68, bf16[512,512]{1,0:T(8,128)(2,1)S(1)} %get-tuple-element.67), kind=kOutput, calls=%fused_computation.18 | convolution fusion | flops 4318035968 | bytes 22020096 | tf_op jit(solution)/shard_map/dot_general | solution.py:141
  (78 shorter events, 0.8 us)
Async XLA Ops:
  0.0 3.9 %copy-start = (bf16[512,2048]{1,0:T(8,128)(2,1)S(1)}, bf16[512,2048]{1,0:T(8,128)(2,1)}, u32[]{:S(2)}) copy-start(bf16[512,2048]{1,0:T(8,128)(2,1)} %param.9) | copy-start | bytes 6291460
  0.0 3.9 %copy-start.6 = (bf16[2048,128]{1,0:T(8,128)(2,1)S(1)}, bf16[2048,128]{1,0:T(8,128)(2,1)}, u32[]{:S(2)}) copy-start(bf16[2048,128]{1,0:T(8,128)(2,1)} %param.11) | copy-start | bytes 1572868
  0.0 5.2 %copy-start.7 = (s32[512]{0:T(512)S(1)}, s32[512]{0:T(512)}, u32[]{:S(2)}) copy-start(s32[512]{0:T(512)} %param.14) | copy-start | bytes 6148
  0.0 5.2 %copy-start.8 = (s32[512]{0:T(512)S(1)}, s32[512]{0:T(512)}, u32[]{:S(2)}) copy-start(s32[512]{0:T(512)} %param.13) | copy-start | bytes 6148
  0.0 5.3 %copy-start.9 = (s32[1,2]{1,0:T(1,128)S(1)}, s32[1,2]{1,0:T(1,128)}, u32[]{:S(2)}) copy-start(s32[1,2]{1,0:T(1,128)} %param.15) | copy-start | bytes 28
  4.7 1.7 collective-permute-start
  41.4 6.1 %copy-start.3 = (bf16[8,528,128]{2,1,0:T(8,128)(2,1)}, bf16[8,528,128]{2,1,0:T(8,128)(2,1)S(1)}, u32[]{:S(2)}) copy-start(bf16[8,528,128]{2,1,0:T(8,128)(2,1)S(1)} %all_to_all.5) | copy-start | bytes 3244036
  41.4 6.1 %collective-permute-start.1 = (bf16[8,528,128]{2,1,0:T(8,128)(2,1)S(1)}, bf16[8,528,128]{2,1,0:T(8,128)(2,1)}, u32[]{:S(2)}, u32[]{:S(2)}) collective-permute-start(bf16[8,528,128]{2,1,0:T(8,128)(2,1)S(1)} %all_to_all.5), channel_id=1, source_target_pairs={{0,1},{1,0},{2,3},{3,2},{4,5},{5,4},{6,7},{7,6},{8,9},{9,8},{10,11... | collective-permute-start | bytes 3244040 | tf_op jit(solution)/shard_map/ppermute | solution.py:63
  41.4 183.3 %collective-permute-start.2 = (bf16[512,4096]{1,0:T(8,128)(2,1)}, bf16[512,4096]{1,0:T(8,128)(2,1)}, u32[]{:S(2)}, u32[]{:S(2)}) collective-permute-start(bf16[512,4096]{1,0:T(8,128)(2,1)} %param.10), channel_id=1, source_target_pairs={{0,2},{2,4},{4,6},{6,8},{8,10},{10,12},{12,14},{1,3},{3,5},{5,7},{... | collective-permute-start | bytes 12582920 | tf_op jit(solution)/shard_map/ppermute | solution.py:18
  46.0 178.7 %collective-permute-start.3 = (bf16[512,4096]{1,0:T(8,128)(2,1)}, bf16[512,4096]{1,0:T(8,128)(2,1)}, u32[]{:S(2)}, u32[]{:S(2)}) collective-permute-start(bf16[512,4096]{1,0:T(8,128)(2,1)} %param.10), channel_id=1, source_target_pairs={{2,0},{4,2},{6,4},{8,6},{10,8},{12,10},{14,12},{3,1},{5,3},{7,5},{... | collective-permute-start | bytes 12582920 | tf_op jit(solution)/shard_map/ppermute | solution.py:18
  51.6 1.9 copy-start.5
  65.1 15.4 %copy-start.2 = (f32[8,3,512,512]{3,2,1,0:T(8,128)S(1)}, f32[8,3,512,512]{3,2,1,0:T(8,128)}, u32[]{:S(2)}) copy-start(f32[8,3,512,512]{3,2,1,0:T(8,128)} %get-tuple-element.134) | copy-start | bytes 75497472 | tf_op jit(solution)/shard_map/while
  74.8 7.9 %copy-start.4 = (f32[8,3,512]{2,0,1:T(8,128)}, f32[8,3,512]{2,0,1:T(8,128)S(1)}, u32[]{:S(2)}) copy-start(f32[8,3,512]{2,0,1:T(8,128)S(1)} %pad_maximum_fusion.9) | copy-start | bytes 147460 | tf_op jit(solution)/shard_map/while
  82.8 15.4 %copy-start.2 = (f32[8,3,512,512]{3,2,1,0:T(8,128)S(1)}, f32[8,3,512,512]{3,2,1,0:T(8,128)}, u32[]{:S(2)}) copy-start(f32[8,3,512,512]{3,2,1,0:T(8,128)} %get-tuple-element.134) | copy-start | bytes 75497472 | tf_op jit(solution)/shard_map/while
  92.5 7.9 %copy-start.4 = (f32[8,3,512]{2,0,1:T(8,128)}, f32[8,3,512]{2,0,1:T(8,128)S(1)}, u32[]{:S(2)}) copy-start(f32[8,3,512]{2,0,1:T(8,128)S(1)} %pad_maximum_fusion.9) | copy-start | bytes 147460 | tf_op jit(solution)/shard_map/while
  100.5 15.4 %copy-start.2 = (f32[8,3,512,512]{3,2,1,0:T(8,128)S(1)}, f32[8,3,512,512]{3,2,1,0:T(8,128)}, u32[]{:S(2)}) copy-start(f32[8,3,512,512]{3,2,1,0:T(8,128)} %get-tuple-element.134) | copy-start | bytes 75497472 | tf_op jit(solution)/shard_map/while
  110.3 7.9 %copy-start.4 = (f32[8,3,512]{2,0,1:T(8,128)}, f32[8,3,512]{2,0,1:T(8,128)S(1)}, u32[]{:S(2)}) copy-start(f32[8,3,512]{2,0,1:T(8,128)S(1)} %pad_maximum_fusion.9) | copy-start | bytes 147460 | tf_op jit(solution)/shard_map/while
  118.2 15.4 %copy-start.2 = (f32[8,3,512,512]{3,2,1,0:T(8,128)S(1)}, f32[8,3,512,512]{3,2,1,0:T(8,128)}, u32[]{:S(2)}) copy-start(f32[8,3,512,512]{3,2,1,0:T(8,128)} %get-tuple-element.134) | copy-start | bytes 75497472 | tf_op jit(solution)/shard_map/while
  128.0 7.9 %copy-start.4 = (f32[8,3,512]{2,0,1:T(8,128)}, f32[8,3,512]{2,0,1:T(8,128)S(1)}, u32[]{:S(2)}) copy-start(f32[8,3,512]{2,0,1:T(8,128)S(1)} %pad_maximum_fusion.9) | copy-start | bytes 147460 | tf_op jit(solution)/shard_map/while
  224.7 10.7 %copy-start.1 = (bf16[512,2048]{1,0:T(8,128)(2,1)S(1)}, bf16[512,2048]{1,0:T(8,128)(2,1)}, u32[]{:S(2)}) copy-start(bf16[512,2048]{1,0:T(8,128)(2,1)} %param.9) | copy-start | bytes 6291460
